TPU v7x, 32 devices: a whole 2x2x4 slice. The times are simulated.
32 devices in a mesh: groups: 2 (over y), dom: 4 (over z), cols: 4 (over x, core).
Axes of the slice: x: 2, y: 2, z: 4, core: 2. Of those that a mesh axis runs over, the one named last changes fastest.
Arguments:
- features: bfloat16 [32768, 768], P(('groups', 'dom'), 'cols'), parts along dimension 0, may hold values from -6 to 6
- edge_source: int32 [8, 4, 1024], P(('groups', 'dom')), parts along dimension 0, may hold values from 0 to 4095, as said below
- edge_target: int32 [8, 4, 1024], P(('groups', 'dom')), parts along dimension 0, may hold values from 0 to 1024, as said below
- neigh_weight: bfloat16 [768, 1024], P('cols'), may hold values from -0.21875 to 0.21875
- self_weight: bfloat16 [768, 1024], P('cols'), may hold values from -0.21875 to 0.21875
- bias_one: float32 [1024], replicated, may hold values from -3 to 3
- upper_weight: bfloat16 [1024, 1024], P('cols'), may hold values from -0.375 to 0.375
- bias_two: float32 [1024], replicated, may hold values from -3 to 3
- upper_neighbours: int32 [8192, 15], P(('groups', 'dom', 'cols')), parts along dimension 0, may hold values from 0 to 255
- out_cotangent: bfloat16 [8192, 1024], P(('groups', 'dom', 'cols')), parts along dimension 0, may hold values from -6 to 6
Outputs:
- hidden_two: bfloat16 [8192, 1024], P(('groups', 'dom', 'cols')), parts along dimension 0
- grad_neigh: float32 [1536, 1024], P(('groups', 'cols'), 'dom'), parts along dimension 0
- grad_self: float32 [1536, 1024], P(('groups', 'cols'), 'dom'), parts along dimension 0
- grad_upper: float32 [2048, 1024], P(('groups', 'cols')), parts along dimension 0
There are 2 independent parts, one for each index of `groups`. A program takes and returns all parts, laid end to end along the dimension named above; an argument that names none is the same for every part. Nothing has to cross between parts.
Inputs may be any that keep to these rules, and one draw needn't show every extreme that they name: `edge_source`: for each pair (s, o) the live slots are the first ones, 1 to 1024 of them, and some pair has all 1024 live; busy owners receive more edges; dead slots hold 0. edge_target[o, s, k] belongs to the same edge as edge_source[s, o, k]; dead slots hold 1024.
All inputs are finite; a program needn't handle non-finite values.
Results may differ from a plain program's by a relative error of at most 0.015.
Values may be sent and summed in bfloat16 or wider, within the bound.
No kernel may reach another device: no remote copies, remote signals or barrier semaphores. Data moves between devices by JAX's collectives and lax.ppermute only.
A program may use at most 128 MiB of HBM per device.

v0:
```python
import jax
import jax.numpy as jnp
from jax import lax
from jax.sharding import PartitionSpec as P

TGT_DEV = 1024


def swish_slope(preact):
    gate_val = jax.nn.sigmoid(preact)
    return gate_val * (1.0 + preact * (1.0 - gate_val))


def mixing(neighbours, block_len):
    positions = jnp.arange(block_len, dtype=jnp.int32)
    neighbour_hits = jnp.sum(
        (neighbours[:, :, None] == positions[None, None, :]).astype(jnp.float32), axis=1
    )
    return (jnp.eye(block_len, dtype=jnp.float32) + neighbour_hits) / (neighbours.shape[1] + 1.0)


def contract_rows(left_mat, right_mat):
    return lax.dot_general(
        left_mat, right_mat, (((0,), (0,)), ((), ())), preferred_element_type=jnp.float32
    )


def local(
    features,
    edge_source,
    edge_target,
    neigh_weight,
    self_weight,
    bias_one,
    upper_weight,
    bias_two,
    upper_neighbours,
    out_cotangent,
):
    partitions = lax.axis_size("dom")
    capacity = edge_source.shape[2]
    slice_width = features.shape[1]
    outgoing = jnp.take(features, edge_source[0].reshape(-1), axis=0).reshape(
        partitions, capacity, slice_width
    )
    received = lax.all_to_all(outgoing, "dom", split_axis=0, concat_axis=0, tiled=True).reshape(
        partitions * capacity, slice_width
    )
    targets_of = edge_target[0].reshape(-1)
    summed = jax.ops.segment_sum(received.astype(jnp.float32), targets_of, TGT_DEV + 1)[:TGT_DEV]
    counts = jax.ops.segment_sum(jnp.ones(targets_of.shape, jnp.float32), targets_of, TGT_DEV + 1)[
        :TGT_DEV
    ]
    mean_feats = (summed / jnp.maximum(counts, 1.0)[:, None]).astype(jnp.bfloat16)
    own_feats = features[:TGT_DEV]
    partial_value = jnp.dot(mean_feats, neigh_weight, preferred_element_type=jnp.float32)
    partial_value = partial_value + jnp.dot(
        own_feats, self_weight, preferred_element_type=jnp.float32
    )
    pre_one = (
        lax.psum_scatter(
            partial_value.astype(jnp.bfloat16), "cols", scatter_dimension=0, tiled=True
        ).astype(jnp.float32)
        + bias_one
    )
    hidden_one = jax.nn.silu(pre_one).astype(jnp.bfloat16)
    full_upper = lax.all_gather(upper_weight, "cols", axis=0, tiled=True)
    mix_matrix = mixing(upper_neighbours, hidden_one.shape[0])
    upper_input = jnp.dot(
        mix_matrix, hidden_one.astype(jnp.float32), precision=lax.Precision.HIGHEST
    ).astype(jnp.bfloat16)
    pre_two = jnp.dot(upper_input, full_upper, preferred_element_type=jnp.float32) + bias_two
    hidden_two = jax.nn.silu(pre_two).astype(jnp.bfloat16)
    slope_two = (out_cotangent.astype(jnp.float32) * swish_slope(pre_two)).astype(jnp.bfloat16)
    share_rows = upper_weight.shape[0]
    column = lax.axis_index("cols")
    local_grad = contract_rows(upper_input, slope_two)
    summed_grad = lax.psum(local_grad, ("dom", "cols"))
    grad_upper = lax.dynamic_slice_in_dim(summed_grad, column * share_rows, share_rows, 0)
    back_mixed = lax.dot_general(
        slope_two, full_upper, (((1,), (1,)), ((), ())), preferred_element_type=jnp.float32
    )
    back_one = jnp.dot(mix_matrix.T, back_mixed, precision=lax.Precision.HIGHEST)
    slope_one = (back_one * swish_slope(pre_one)).astype(jnp.bfloat16)
    slab_rows = lax.all_gather(slope_one, "cols", axis=0, tiled=True)
    neigh_total = contract_rows(mean_feats, slab_rows)
    self_total = contract_rows(own_feats, slab_rows)
    grad_neigh, grad_self = (
        lax.psum_scatter(
            neigh_total.astype(jnp.bfloat16), "dom", scatter_dimension=1, tiled=True
        ).astype(jnp.float32),
        lax.psum_scatter(
            self_total.astype(jnp.bfloat16), "dom", scatter_dimension=1, tiled=True
        ).astype(jnp.float32),
    )
    return (hidden_two, grad_neigh, grad_self, grad_upper)


def solution(mesh):
    in_specs = (
        P(("groups", "dom"), "cols"),
        P(("groups", "dom"), None, None),
        P(("groups", "dom"), None, None),
        P("cols", None),
        P("cols", None),
        P(),
        P("cols", None),
        P(),
        P(("groups", "dom", "cols"), None),
        P(("groups", "dom", "cols"), None),
    )
    out_specs = (
        P(("groups", "dom", "cols"), None),
        P(("groups", "cols"), "dom"),
        P(("groups", "cols"), "dom"),
        P(("groups", "cols"), None),
    )
    return jax.shard_map(local, mesh=mesh, in_specs=in_specs, out_specs=out_specs, check_vma=False)
```

profile of v0, /device:TPU:0, one launch (start us, length us, event | category | flops | bytes accessed | tf_op | source)
XLA Modules:
  0.0 358.2 jit_solution(6167018570598169652)
XLA Ops:
  7.2 3.2 copy.28
  10.5 16.9 %gather_fusion = bf16[4096,192]{1,0:T(8,128)(2,1)} fusion(bf16[4096,192]{1,0:T(8,128)(2,1)S(1)} %copy.28, s32[4096]{0:T(1024)S(1)} %broadcast_clamp_fusion), kind=kCustom, calls=%fused_computation | custom fusion | bytes 3162112 | tf_op jit(solution)/shard_map/jit(_take)/gather | solution.py:43
  27.4 2.9 copy.29
  30.4 1.3 broadcast_select_fusion
  31.7 6.4 %all-to-all-start = ((bf16[4,1024,192]{1,2,0:T(8,128)(2,1)}), bf16[4,1024,192]{1,2,0:T(8,128)(2,1)S(1)}, u32[]{:S(2)}, u32[]{:S(2)}) async-start(bf16[4,1024,192]{1,2,0:T(8,128)(2,1)} %broadcast_select_fusion), calls=%async_computation | async-start | bytes 3145728 | tf_op jit(solution)/shard_map/all_to_all | solution.py:46
  38.2 28.8 %scatter_custom_fusion.1 = f32[1025]{0:T(1024)S(1)} fusion(s32[4096]{0:T(1024)S(1)} %bitcast.31, f32[4096]{0:T(1024)S(1)} %broadcast.40, f32[]{:T(128)} %constant.10.clone.1), kind=kCustom, calls=%fused_computation.38 | custom fusion | flops 4096 | bytes 4104 | tf_op jit(solution)/shard_map/scatter-add | solution.py:51
  67.0 8.1 %all-to-all-done = bf16[4,1024,192]{1,2,0:T(8,128)(2,1)S(1)} async-done(((bf16[4,1024,192]{1,2,0:T(8,128)(2,1)}), bf16[4,1024,192]{1,2,0:T(8,128)(2,1)S(1)}, u32[]{:S(2)}, u32[]{:S(2)}) %all-to-all-start) | async-done | bytes 1572896 | tf_op jit(solution)/shard_map/all_to_all | solution.py:46
  75.1 2.9 copy.32
  78.0 24.3 %scatter_custom_fusion = f32[1025,192]{1,0:T(8,128)S(1)} fusion(s32[4096]{0:T(1024)S(1)} %bitcast.32, f32[4096,192]{1,0:T(8,128)} %bitcast.26, f32[]{:T(128)} %constant.10.clone.1), kind=kCustom, calls=%fused_computation.22 | custom fusion | flops 786432 | bytes 787712 | tf_op jit(solution)/shard_map/scatter-add | solution.py:50
  102.4 0.8 fusion.17
  103.2 0.6 copy-done.1
  103.9 2.1 add_convert_fusion
  106.0 0.7 all-gather.3.cloned.1.call-update
  106.8 1.5 convert_reduce_fusion
  108.3 29.2 %reduce-scatter.4.cloned.1.call-done = bf16[256,1024]{1,0:T(8,128)(2,1)} async-done(((bf16[1024,1024]{1,0:T(8,128)(2,1)}), bf16[256,1024]{1,0:T(8,128)(2,1)}) %reduce-scatter.4.cloned.1.call-update) | async-done | bytes 524304 | tf_op jit(solution)/shard_map/reduce_scatter | solution.py:61
  137.5 1.9 convolution_convert_fusion
  139.4 22.3 %all-gather.3.cloned.1.call-done = bf16[1024,1024]{1,0:T(8,128)(2,1)} async-done(((bf16[256,1024]{1,0:T(8,128)(2,1)}), bf16[1024,1024]{1,0:T(8,128)(2,1)}) %all-gather.3.cloned.1.call-update) | async-done | bytes 2097168 | tf_op jit(solution)/shard_map/all_gather | solution.py:67
  161.7 3.4 multiply_convert_fusion.1
  165.2 0.9 fusion.20
  166.1 0.2 copy-done.5
  166.3 0.4 copy-done.10
  166.7 2.2 fusion
  168.9 4.3 %fusion.19 = f32[1024,1024]{1,0:T(8,128)} fusion(bf16[256,1024]{1,0:T(8,128)(2,1)S(1)} %convolution_convert_fusion, f32[256,1024]{1,0:T(8,128)} %copy-done.2, bf16[256,1024]{1,0:T(8,128)(2,1)} %param.19), kind=kOutput, calls=%fused_computation.45 | convolution fusion | flops 539492352 | bytes 6291456 | tf_op jit(solution)/shard_map/dot_general | solution.py:23
  173.2 18.4 %all-gather.5.cloned.1.call-done = bf16[1024,1024]{1,0:T(8,128)(2,1)} async-done(((bf16[256,1024]{1,0:T(8,128)(2,1)}), bf16[1024,1024]{1,0:T(8,128)(2,1)}) %all-gather.5.cloned.1.call-update) | async-done | bytes 2097168 | tf_op jit(solution)/shard_map/all_gather | solution.py:85
  191.6 3.2 convolution_convert_fusion.2
  194.9 2.9 fusion.1
  197.9 109.1 %all-reduce.2.cloned.1.call-done = f32[1024,1024]{1,0:T(8,128)} async-done(((f32[1024,1024]{1,0:T(8,128)}), f32[1024,1024]{1,0:T(8,128)}) %all-reduce.2.cloned.1.call-update) | async-done | bytes 4194320 | tf_op jit(solution)/shard_map/psum | solution.py:78
  307.0 2.3 constant_dynamic-slice_fusion
  309.3 19.4 %reduce-scatter.6.cloned.1.call-done = bf16[192,256]{1,0:T(8,128)(2,1)} async-done(((bf16[192,1024]{1,0:T(8,128)(2,1)}), bf16[192,256]{1,0:T(8,128)(2,1)}) %reduce-scatter.6.cloned.1.call-update) | async-done | bytes 98320 | tf_op jit(solution)/shard_map/reduce_scatter | solution.py:89
  328.7 1.6 convert_element_type.69
  330.3 19.6 %reduce-scatter.8.cloned.1.call-done = bf16[192,256]{1,0:T(8,128)(2,1)} async-done(((bf16[192,1024]{1,0:T(8,128)(2,1)}), bf16[192,256]{1,0:T(8,128)(2,1)}) %reduce-scatter.8.cloned.1.call-update) | async-done | bytes 98320 | tf_op jit(solution)/shard_map/reduce_scatter | solution.py:92
  349.8 1.6 convert_element_type.72
  (41 shorter events, 0.5 us)
Async XLA Ops:
  7.2 95.2 %copy-start = (bf16[192,1024]{1,0:T(8,128)(2,1)S(1)}, bf16[192,1024]{1,0:T(8,128)(2,1)}, u32[]{:S(2)}) copy-start(bf16[192,1024]{1,0:T(8,128)(2,1)} %param.13) | copy-start | bytes 1179652
  7.2 3.2 copy-start.6
  31.7 6.5 %copy-start.8 = (s32[1,4,1024]{2,1,0:T(4,128)S(1)}, s32[1,4,1024]{2,1,0:T(4,128)}, u32[]{:S(2)}) copy-start(s32[1,4,1024]{2,1,0:T(4,128)} %param.12) | copy-start | bytes 49156
  31.7 43.4 %all-to-all-start = ((bf16[4,1024,192]{1,2,0:T(8,128)(2,1)}), bf16[4,1024,192]{1,2,0:T(8,128)(2,1)S(1)}, u32[]{:S(2)}, u32[]{:S(2)}) async-start(bf16[4,1024,192]{1,2,0:T(8,128)(2,1)} %broadcast_select_fusion), calls=%async_computation | async-start | bytes 3145728 | tf_op jit(solution)/shard_map/all_to_all | solution.py:46
  38.2 99.3 %reduce-scatter.4.cloned.1.call-start = ((), (), s32[]{:S(2)}) async-start(), calls=%async_computation.4 | async-start | bytes 2621440 | tf_op jit(solution)/shard_map/reduce_scatter | solution.py:61
  102.4 1.4 copy-start.1
  102.4 1.5 copy-start.4
  106.0 0.8 copy-start.7
  106.0 55.8 %all-gather.3.cloned.1.call-start = ((), (), s32[]{:S(2)}) async-start(), calls=%async_computation.5 | async-start | bytes 2621440 | tf_op jit(solution)/shard_map/all_gather | solution.py:67
  106.7 84.9 %all-gather.5.cloned.1.call-start = ((), (), s32[]{:S(2)}) async-start(), calls=%async_computation.6 | async-start | bytes 2621440 | tf_op jit(solution)/shard_map/all_gather | solution.py:85
  108.3 53.5 %copy-start.11 = (f32[1024]{0:T(1024)S(1)}, f32[1024]{0:T(1024)}, u32[]{:S(2)}) copy-start(f32[1024]{0:T(1024)} %param.17) | copy-start | bytes 12292
  161.7 3.4 copy-start.3
  161.7 3.4 copy-start.9
  165.1 1.0 copy-start.2
  165.2 1.1 copy-start.5
  165.2 1.5 copy-start.10
  165.2 1.5 copy-start.12
  168.9 138.2 %all-reduce.2.cloned.1.call-start = ((), (), s32[]{:S(2)}) async-start(), calls=%async_computation.9 | async-start | bytes 8388608 | tf_op jit(solution)/shard_map/psum | solution.py:78
  173.2 155.5 %reduce-scatter.6.cloned.1.call-start = ((), (), s32[]{:S(2)}) async-start(), calls=%async_computation.7 | async-start | bytes 491520 | tf_op jit(solution)/shard_map/reduce_scatter | solution.py:89
  194.9 155.0 %reduce-scatter.8.cloned.1.call-start = ((), (), s32[]{:S(2)}) async-start(), calls=%async_computation.8 | async-start | bytes 491520 | tf_op jit(solution)/shard_map/reduce_scatter | solution.py:92
Sparse Core Ops, SparseCore 0:
  106.1 31.3 reduce-scatter.3
  139.1 22.5 all-gather.2
  169.0 22.5 all-gather.4
  195.6 111.3 all-reduce.1
  309.1 19.4 reduce-scatter.5
  330.9 18.8 reduce-scatter.7
where the time goes:
time: 360 us; the launch traced here: 358 us
  waiting for transfers between devices  227 us (63%)
  other arithmetic  59.1 us (16%)
  local copies, waits for them, and re-layouts  29.6 us (8%)
  matrix products  21.7 us (6%)
  between operations  14.3 us (4%)
  starting transfers between devices  6.66 us (2%)
    psum x1, waiting for transfers between devices, local(): summed_grad = lax.psum(local_grad, ('dom', 'cols'))  109 us
    reduce_scatter x1, waiting for transfers between devices, local(): lax.psum_scatter(partial_value.astype(jnp.bfloat16), 'cols', scatter_dime...  29.2 us
    scatter-add x1, other arithmetic, local(): jax.ops.segment_sum(jnp.ones(targets_of.shape, jnp.float32), targets_of,...  28.8 us
    scatter-add x1, other arithmetic, local(): jax.ops.segment_sum(received.astype(jnp.float32), targets_of, TGT_DEV + 1)  24.3 us
    all_gather x1, waiting for transfers between devices, local(): full_upper = lax.all_gather(upper_weight, 'cols', axis=0, tiled=True)  22.3 us
    gather x2, local copies, waits for them, and re-layouts, local(): jnp.take(features, edge_source[0].reshape(-1), axis=0)  19.9 us
    reduce_scatter x1, waiting for transfers between devices, local(): lax.psum_scatter(self_total.astype(jnp.bfloat16), 'dom', scatter_dimensio...  19.6 us
    reduce_scatter x1, waiting for transfers between devices, local(): lax.psum_scatter(neigh_total.astype(jnp.bfloat16), 'dom', scatter_dimensi...  19.4 us
  transfers between devices with their start and end apart: 7, of which 7 were waited for; matrix products, arithmetic and copies ran while one was open for 13% of the time, Pallas kernels for 0%

commit v1 on v0

v1 whole, which is shorter than its diff:
```python
import jax
import jax.numpy as jnp
from jax import lax
from jax.experimental import pallas as pl
from jax.experimental.pallas import tpu as pltpu
from jax.sharding import PartitionSpec as P


def swish_slope(preact):
    gate_val = jax.nn.sigmoid(preact)
    return gate_val * (1.0 + preact * (1.0 - gate_val))


def mixing(neighbours, block_len):
    positions = jnp.arange(block_len, dtype=jnp.int32)
    neighbour_hits = jnp.sum(
        (neighbours[:, :, None] == positions[None, None, :]).astype(jnp.float32), axis=1
    )
    return (jnp.eye(block_len, dtype=jnp.float32) + neighbour_hits) / (neighbours.shape[1] + 1.0)


def contract_rows(left_mat, right_mat):
    return lax.dot_general(
        left_mat, right_mat, (((0,), (0,)), ((), ())), preferred_element_type=jnp.float32
    )


def _aggregate_kernel(tgt_ref, rec_ref, sum_ref, cnt_ref):
    step = pl.program_id(0)

    @pl.when(step == 0)
    def _():
        sum_ref[...] = jnp.zeros_like(sum_ref)
        cnt_ref[...] = jnp.zeros_like(cnt_ref)

    targets = tgt_ref[0]
    n_tgt = sum_ref.shape[0]
    rows = lax.broadcasted_iota(jnp.int32, (n_tgt, targets.shape[1]), 0)
    hot = (rows == targets).astype(jnp.bfloat16)
    sum_ref[...] += jnp.dot(hot, rec_ref[0], preferred_element_type=jnp.float32)
    ones = jnp.ones((targets.shape[1], cnt_ref.shape[1]), jnp.bfloat16)
    cnt_ref[...] += jnp.dot(hot, ones, preferred_element_type=jnp.float32)


def aggregate(targets, received, n_tgt):
    n_src, cap = targets.shape
    width = received.shape[-1]
    targets = targets.reshape(n_src, 1, cap)
    received = received.reshape(n_src, cap, width)
    return pl.pallas_call(
        _aggregate_kernel,
        grid=(n_src,),
        in_specs=[
            pl.BlockSpec((1, 1, cap), lambda s: (s, 0, 0)),
            pl.BlockSpec((1, cap, width), lambda s: (s, 0, 0)),
        ],
        out_specs=[
            pl.BlockSpec((n_tgt, width), lambda s: (0, 0)),
            pl.BlockSpec((n_tgt, 128), lambda s: (0, 0)),
        ],
        out_shape=[
            jax.ShapeDtypeStruct((n_tgt, width), jnp.float32),
            jax.ShapeDtypeStruct((n_tgt, 128), jnp.float32),
        ],
        cost_estimate=pl.CostEstimate(
            flops=2 * n_src * n_tgt * cap * (width + 128),
            transcendentals=0,
            bytes_accessed=n_src * cap * (width * 2 + 4) + n_tgt * (width + 128) * 4,
        ),
    )(targets, received)


def local(
    features,
    edge_source,
    edge_target,
    neigh_weight,
    self_weight,
    bias_one,
    upper_weight,
    bias_two,
    upper_neighbours,
    out_cotangent,
):
    n_dom = lax.axis_size("dom")
    n_cols = lax.axis_size("cols")
    capacity = edge_source.shape[2]
    width = features.shape[1]
    hidden = upper_weight.shape[1]
    tgt_loc = upper_neighbours.shape[0]
    tgt_dev = tgt_loc * n_cols
    w_rows = neigh_weight.shape[0]
    up_rows = upper_weight.shape[0]

    packed = jnp.concatenate([neigh_weight, self_weight, upper_weight], axis=0)
    gathered = lax.all_gather(packed, "cols", axis=0, tiled=False)
    neigh_full = gathered[:, :w_rows]
    self_full = gathered[:, w_rows : 2 * w_rows]
    full_upper = gathered[:, 2 * w_rows :].reshape(n_cols * up_rows, hidden)

    outgoing = jnp.take(features, edge_source[0].reshape(-1), axis=0)
    received = lax.all_to_all(outgoing, "dom", split_axis=0, concat_axis=0, tiled=True)
    summed, counts = aggregate(edge_target[0], received, tgt_dev)
    mean_feats = (summed / jnp.maximum(counts[:, :1], 1.0)).astype(jnp.bfloat16)
    own_feats = features[:tgt_dev]

    both = jnp.concatenate([mean_feats, own_feats], axis=1)
    got = lax.all_to_all(both, "cols", split_axis=0, concat_axis=0, tiled=True).reshape(
        n_cols, tgt_loc, 2 * width
    )
    pre_one = (
        jnp.einsum(
            "ctf,cfh->th", got[:, :, :width], neigh_full, preferred_element_type=jnp.float32
        )
        + jnp.einsum(
            "ctf,cfh->th", got[:, :, width:], self_full, preferred_element_type=jnp.float32
        )
        + bias_one
    )
    hidden_one = jax.nn.silu(pre_one).astype(jnp.bfloat16)
    mix_matrix = mixing(upper_neighbours, tgt_loc)
    upper_input = jnp.dot(
        mix_matrix, hidden_one.astype(jnp.float32), precision=lax.Precision.HIGHEST
    ).astype(jnp.bfloat16)
    pre_two = jnp.dot(upper_input, full_upper, preferred_element_type=jnp.float32) + bias_two
    hidden_two = jax.nn.silu(pre_two).astype(jnp.bfloat16)
    slope_two = (out_cotangent.astype(jnp.float32) * swish_slope(pre_two)).astype(jnp.bfloat16)

    local_grad = contract_rows(upper_input, slope_two).astype(jnp.bfloat16)
    col_parts = lax.all_to_all(local_grad, "cols", split_axis=0, concat_axis=0, tiled=True)
    col_sum = jnp.sum(
        col_parts.reshape(n_cols, up_rows, hidden).astype(jnp.float32), axis=0
    )
    grad_upper = lax.psum(col_sum, "dom")

    back_mixed = lax.dot_general(
        slope_two, full_upper, (((1,), (1,)), ((), ())), preferred_element_type=jnp.float32
    )
    back_one = jnp.dot(mix_matrix.T, back_mixed, precision=lax.Precision.HIGHEST)
    slope_one = (back_one * swish_slope(pre_one)).astype(jnp.bfloat16)
    slab_rows = lax.all_to_all(
        jnp.broadcast_to(slope_one[None], (n_cols, tgt_loc, hidden)).reshape(
            n_cols * tgt_loc, hidden
        ),
        "cols",
        split_axis=0,
        concat_axis=0,
        tiled=True,
    )
    neigh_total = contract_rows(mean_feats, slab_rows)
    self_total = contract_rows(own_feats, slab_rows)
    stacked = jnp.concatenate([neigh_total, self_total], axis=0).astype(jnp.bfloat16)
    dom_cols = hidden // n_dom
    dom_parts = lax.all_to_all(stacked, "dom", split_axis=1, concat_axis=0, tiled=True)
    dom_sum = jnp.sum(
        dom_parts.reshape(n_dom, 2 * w_rows, dom_cols).astype(jnp.float32), axis=0
    )
    grad_neigh = dom_sum[:w_rows]
    grad_self = dom_sum[w_rows:]
    return (hidden_two, grad_neigh, grad_self, grad_upper)


def solution(mesh):
    in_specs = (
        P(("groups", "dom"), "cols"),
        P(("groups", "dom"), None, None),
        P(("groups", "dom"), None, None),
        P("cols", None),
        P("cols", None),
        P(),
        P("cols", None),
        P(),
        P(("groups", "dom", "cols"), None),
        P(("groups", "dom", "cols"), None),
    )
    out_specs = (
        P(("groups", "dom", "cols"), None),
        P(("groups", "cols"), "dom"),
        P(("groups", "cols"), "dom"),
        P(("groups", "cols"), None),
    )
    return jax.shard_map(local, mesh=mesh, in_specs=in_specs, out_specs=out_specs, check_vma=False)
```

time: 360 us -> 258 us (0.72)
  waiting for transfers between devices: 227 us -> 141 us
  other arithmetic: 59.1 us -> 13.9 us
  starting transfers between devices: 6.66 us -> 21.8 us
  local copies, waits for them, and re-layouts: 29.6 us -> 42.9 us
  Pallas kernels: 0 us -> 7.4 us
  matrix products: 21.7 us -> 15.7 us
    psum x1, waiting for transfers between devices: 109 us -> 30.3 us  [local(): grad_upper = lax.psum(col_sum, 'dom')]
    all_to_all x0 -> x4, waiting for transfers between devices: none -> 74 us  [the longest x1 28.9 us: local(): lax.all_to_all(stacked, 'dom', split_axis=1, concat_axis=0, tiled=True)]
    reduce_scatter x3 -> x0, waiting for transfers between devices: 68.1 us -> none  [the longest x1 29.2 us: local(): lax.psum_scatter(partial_value.astype(jnp.bfloat16), 'cols', scatter_dime...]
    scatter-add x2 -> x0, other arithmetic: 53.1 us -> none  [the longest x1 28.8 us: local(): jax.ops.segment_sum(jnp.ones(targets_of.shape, jnp.float32), targets_of,...]
    all_gather x2 -> x1, waiting for transfers between devices: 40.7 us -> 0.01 us  [local(): gathered = lax.all_gather(packed, 'cols', axis=0, tiled=False)]
    all_to_all x1, waiting for transfers between devices: 8.15 us -> 36.4 us  [local(): lax.all_to_all(outgoing, 'dom', split_axis=0, concat_axis=0, tiled=True)]
    all_to_all x0 -> x4, starting transfers between devices: none -> 15.2 us  [the longest x1 4.63 us: local(): lax.all_to_all(local_grad, 'cols', split_axis=0, concat_axis=0, tiled=True)]
    all_to_all x0 -> x3, local copies, waits for them, and re-layouts: none -> 7.49 us  [the longest x1 3.76 us: local(): lax.all_to_all(outgoing, 'dom', split_axis=0, concat_axis=0, tiled=True)]
  transfers between devices with their start and end apart: 7 -> 7, of which waited for: 7 -> 6; matrix products, arithmetic and copies ran while one was open for 13% -> 22% of each run, Pallas kernels for 0% -> 3%
where the time goes in v1:
time: 258 us; the launch traced here: 257 us
  waiting for transfers between devices  141 us (55%)
  local copies, waits for them, and re-layouts  42.9 us (17%)
  starting transfers between devices  21.8 us (8%)
  matrix products  15.7 us (6%)
  between operations  14.3 us (6%)
  other arithmetic  13.9 us (5%)
  Pallas kernels  7.4 us (3%)
    all_to_all x1, waiting for transfers between devices, local(): lax.all_to_all(outgoing, 'dom', split_axis=0, concat_axis=0, tiled=True)  36.4 us
    psum x1, waiting for transfers between devices, local(): grad_upper = lax.psum(col_sum, 'dom')  30.3 us
    all_to_all x1, waiting for transfers between devices, local(): lax.all_to_all(stacked, 'dom', split_axis=1, concat_axis=0, tiled=True)  28.9 us
    all_to_all x1, waiting for transfers between devices, local(): lax.all_to_all(jnp.broadcast_to(slope_one[None], (n_cols, tgt_loc, hidden...  22 us
    gather x2, local copies, waits for them, and re-layouts, local(): outgoing = jnp.take(features, edge_source[0].reshape(-1), axis=0)  20.9 us
    all_to_all x1, waiting for transfers between devices, local(): lax.all_to_all(local_grad, 'cols', split_axis=0, concat_axis=0, tiled=True)  14.7 us
    all_to_all x1, waiting for transfers between devices, local(): lax.all_to_all(both, 'cols', split_axis=0, concat_axis=0, tiled=True)  8.35 us
    pallas_call x1, Pallas kernels, aggregate(): pl.pallas_call(_aggregate_kernel, grid=(n_src,), in_specs=[pl.BlockSpec((...  7.4 us
  transfers between devices with their start and end apart: 7, of which 6 were waited for; matrix products, arithmetic and copies ran while one was open for 22% of the time, Pallas kernels for 3%

profile of v1, /device:TPU:0, one launch (start us, length us, event | category | flops | bytes accessed | tf_op | source)
XLA Modules:
  0.0 256.7 jit_solution(7686713818203817418)
XLA Ops:
  7.2 2.5 pad_maximum_fusion
  9.7 3.2 %copy.47 = bf16[4096,192]{1,0:T(8,128)(2,1)S(1)} copy(bf16[4096,192]{0,1:T(8,128)(2,1)} %param.10) | data formatting | bytes 3145728 | tf_op args[0]
  13.0 17.0 %gather_fusion = bf16[4096,192]{1,0:T(8,128)(2,1)} fusion(bf16[4096,192]{1,0:T(8,128)(2,1)S(1)} %copy.47, s32[4096]{0:T(1024)S(1)} %broadcast_clamp_fusion), kind=kCustom, calls=%fused_computation | custom fusion | bytes 3162112 | tf_op jit(solution)/shard_map/jit(_take)/gather | solution.py:101
  30.0 3.9 %copy.48 = bf16[4,1024,192]{1,2,0:T(8,128)(2,1)} copy(bf16[4,1024,192]{2,1,0:T(8,128)(2,1)} %bitcast.43) | data formatting | bytes 3145728 | tf_op jit(solution)/shard_map/jit(_take)/gather | solution.py:101
  33.9 2.7 %broadcast_select_fusion = bf16[4,1024,192]{1,2,0:T(8,128)(2,1)} fusion(bf16[4,1024,192]{1,2,0:T(8,128)(2,1)} %copy.48, pred[4,1024]{1,0:T(4,128)(4,1)S(1)} %compare_and_fusion), kind=kLoop, calls=%fused_computation.10 | loop fusion | flops 786432 | bytes 3149824 | tf_op jit(solution)/shard_map/jit(_take)/select_n | solution.py:101
  36.7 6.4 %all-to-all-start = ((bf16[4,1024,192]{1,2,0:T(8,128)(2,1)}), bf16[4,1024,192]{1,2,0:T(8,128)(2,1)}, u32[]{:S(2)}, u32[]{:S(2)}) async-start(bf16[4,1024,192]{1,2,0:T(8,128)(2,1)} %broadcast_select_fusion), calls=%async_computation | async-start | bytes 3145728 | tf_op jit(solution)/shard_map/all_to_all | solution.py:102
  43.7 36.4 %all-to-all-done = bf16[4,1024,192]{1,2,0:T(8,128)(2,1)} async-done(((bf16[4,1024,192]{1,2,0:T(8,128)(2,1)}), bf16[4,1024,192]{1,2,0:T(8,128)(2,1)}, u32[]{:S(2)}, u32[]{:S(2)}) %all-to-all-start) | async-done | bytes 1572896 | tf_op jit(solution)/shard_map/all_to_all | solution.py:102
  80.2 3.8 %copy.49.rec_ref = bf16[4,1024,192]{2,1,0:T(8,128)(2,1)} copy(bf16[4,1024,192]{1,2,0:T(8,128)(2,1)} %all-to-all-done) | data formatting | bytes 3145728 | tf_op jit(solution)/shard_map/all_to_all | solution.py:102
  83.9 7.4 %shard_map.129 = (f32[1024,192]{1,0:T(8,128)}, f32[1024,128]{1,0:T(8,128)}) custom-call(s32[4,1,1024]{2,1,0:T(1,128)} %reshape_squeeze.8.tgt_ref, bf16[4,1024,192]{2,1,0:T(8,128)(2,1)} %copy.49.rec_ref), custom_call_target="tpu_custom_call" | custom-call | flops 2684354560 | bytes 2899968 | tf_op jit(solution)/shard_map/pallas_call | solution.py:50
  92.6 1.4 divide_convert_fusion
  95.6 3.5 %all-to-all-start.1 = ((bf16[4,256,384]{1,2,0:T(8,128)(2,1)}), bf16[4,256,384]{1,2,0:T(8,128)(2,1)S(1)}, u32[]{:S(2)}, u32[]{:S(2)}) async-start(bf16[4,256,384]{1,2,0:T(8,128)(2,1)} %copy.51), calls=%async_computation.1 | async-start | bytes 1572864 | tf_op jit(solution)/shard_map/all_to_all | solution.py:108
  99.1 1.5 convert_reduce_fusion.1
  100.6 1.8 slice.43
  102.3 8.4 %all-to-all-done.1 = bf16[4,256,384]{1,2,0:T(8,128)(2,1)S(1)} async-done(((bf16[4,256,384]{1,2,0:T(8,128)(2,1)}), bf16[4,256,384]{1,2,0:T(8,128)(2,1)S(1)}, u32[]{:S(2)}, u32[]{:S(2)}) %all-to-all-start.1) | async-done | bytes 786464 | tf_op jit(solution)/shard_map/all_to_all | solution.py:108
  110.7 2.0 fusion.4
  112.7 2.1 fusion.13
  115.7 1.7 multiply_convert_fusion.1
  118.3 1.3 fusion.16
  119.9 1.5 broadcast_in_dim.22
  121.3 3.6 %all-to-all-start.2 = ((bf16[4,256,1024]{1,2,0:T(8,128)(2,1)}), bf16[4,256,1024]{1,2,0:T(8,128)(2,1)S(1)}, u32[]{:S(2)}, u32[]{:S(2)}) async-start(bf16[4,256,1024]{1,2,0:T(8,128)(2,1)} %broadcast_in_dim.22), calls=%async_computation.2 | async-start | bytes 4194304 | tf_op jit(solution)/shard_map/all_to_all | solution.py:141
  124.9 3.6 %convolution_convert_fusion = bf16[1024,1024]{1,0:T(8,128)(2,1)} fusion(bf16[256,1024]{1,0:T(8,128)(2,1)} %copy-done.11, f32[256,1024]{1,0:T(8,128)} %copy-done.10, bf16[256,1024]{1,0:T(8,128)(2,1)S(1)} %copy-done.7), kind=kOutput, calls=%fused_computation.4 | convolution fusion | flops 540540928 | bytes 4194304 | tf_op jit(solution)/shard_map/dot_general | solution.py:23
  128.6 22.0 %all-to-all-done.2 = bf16[4,256,1024]{1,2,0:T(8,128)(2,1)S(1)} async-done(((bf16[4,256,1024]{1,2,0:T(8,128)(2,1)}), bf16[4,256,1024]{1,2,0:T(8,128)(2,1)S(1)}, u32[]{:S(2)}, u32[]{:S(2)}) %all-to-all-start.2) | async-done | bytes 2097184 | tf_op jit(solution)/shard_map/all_to_all | solution.py:141
  150.6 4.6 %all-to-all-start.4 = ((bf16[4,256,1024]{2,1,0:T(8,128)(2,1)}), bf16[4,256,1024]{2,1,0:T(8,128)(2,1)}, u32[]{:S(2)}, u32[]{:S(2)}) async-start(bf16[4,256,1024]{2,1,0:T(8,128)(2,1)} %bitcast.45), calls=%async_computation.4 | async-start | bytes 4194304 | tf_op jit(solution)/shard_map/all_to_all | solution.py:130
  155.2 2.6 %copy.53 = bf16[4,256,1024]{2,1,0:T(8,128)(2,1)} copy(bf16[4,256,1024]{1,2,0:T(8,128)(2,1)S(1)} %all-to-all-done.2) | data formatting | bytes 4194304 | tf_op jit(solution)/shard_map/all_to_all | solution.py:141
  157.8 4.1 %copy.54 = bf16[1024,1024]{1,0:T(8,128)(2,1)} copy(bf16[1024,1024]{0,1:T(8,128)(2,1)} %bitcast.41) | data formatting | bytes 4194304 | tf_op jit(solution)/shard_map/dot_general | solution.py:23
  161.9 2.4 convolution_convert_fusion.2
  166.1 14.7 %all-to-all-done.4 = bf16[4,256,1024]{2,1,0:T(8,128)(2,1)} async-done(((bf16[4,256,1024]{2,1,0:T(8,128)(2,1)}), bf16[4,256,1024]{2,1,0:T(8,128)(2,1)}, u32[]{:S(2)}, u32[]{:S(2)}) %all-to-all-start.4) | async-done | bytes 2097184 | tf_op jit(solution)/shard_map/all_to_all | solution.py:130
  180.8 3.5 %all-to-all-start.3 = ((bf16[384,4,256]{2,0,1:T(8,128)(2,1)}), bf16[384,4,256]{2,0,1:T(8,128)(2,1)S(1)}, u32[]{:S(2)}, u32[]{:S(2)}) async-start(bf16[384,4,256]{2,0,1:T(8,128)(2,1)} %pad_maximum_fusion.2), calls=%async_computation.3 | async-start | bytes 1572864 | tf_op jit(solution)/shard_map/all_to_all | solution.py:154
  184.4 3.0 %convert_reduce_fusion = f32[256,1024]{1,0:T(8,128)} fusion(bf16[4,256,1024]{2,1,0:T(8,128)(2,1)} %all-to-all-done.4), kind=kLoop, calls=%fused_computation.1 | loop fusion | flops 1835008 | bytes 3145728 | tf_op jit(solution)/shard_map/reduce_sum | solution.py:131
  187.4 28.9 %all-to-all-done.3 = bf16[384,4,256]{2,0,1:T(8,128)(2,1)S(1)} async-done(((bf16[384,4,256]{2,0,1:T(8,128)(2,1)}), bf16[384,4,256]{2,0,1:T(8,128)(2,1)S(1)}, u32[]{:S(2)}, u32[]{:S(2)}) %all-to-all-start.3) | async-done | bytes 786464 | tf_op jit(solution)/shard_map/all_to_all | solution.py:154
  217.2 30.3 %all-reduce.2.cloned.1.call-done = f32[256,1024]{1,0:T(8,128)} async-done(((f32[256,1024]{1,0:T(8,128)}), f32[256,1024]{1,0:T(8,128)}) %all-reduce.2.cloned.1.call-update) | async-done | bytes 1048592 | tf_op jit(solution)/shard_map/psum | solution.py:134
  247.5 2.3 copy.64
  (47 shorter events, 8.3 us)
Async XLA Ops:
  7.2 93.4 %all-gather.3.cloned.1.call-start = ((), (), s32[]{:S(2)}) async-start(), calls=%async_computation.6 | async-start | bytes 6553600 | tf_op jit(solution)/shard_map/all_gather | solution.py:96
  9.7 3.2 %copy-start.4 = (s32[1,4,1024]{2,1,0:T(4,128)S(1)}, s32[1,4,1024]{2,1,0:T(4,128)}, u32[]{:S(2)}) copy-start(s32[1,4,1024]{2,1,0:T(4,128)} %param.11) | copy-start | bytes 49156
  12.9 30.2 %copy-start = (bf16[4096,192]{1,0:T(8,128)(2,1)}, bf16[4096,192]{1,0:T(8,128)(2,1)S(1)}, u32[]{:S(2)}) copy-start(bf16[4096,192]{1,0:T(8,128)(2,1)S(1)} %copy.47) | copy-start | bytes 4718596
  36.7 6.5 %copy-start.6 = (s32[1,4,1024]{2,1,0:T(4,128)S(1)}, s32[1,4,1024]{2,1,0:T(4,128)}, u32[]{:S(2)}) copy-start(s32[1,4,1024]{2,1,0:T(4,128)} %param.12) | copy-start | bytes 49156
  36.7 43.5 %all-to-all-start = ((bf16[4,1024,192]{1,2,0:T(8,128)(2,1)}), bf16[4,1024,192]{1,2,0:T(8,128)(2,1)}, u32[]{:S(2)}, u32[]{:S(2)}) async-start(bf16[4,1024,192]{1,2,0:T(8,128)(2,1)} %broadcast_select_fusion), calls=%async_computation | async-start | bytes 3145728 | tf_op jit(solution)/shard_map/all_to_all | solution.py:102
  91.3 2.8 %slice-start = ((bf16[4096,192]{1,0:T(8,128)(2,1)}), bf16[1024,192]{1,0:T(8,128)(2,1)S(1)}, s32[]{:S(2)}) async-start(bf16[4096,192]{1,0:T(8,128)(2,1)} %copy-done), calls=%async_computation.7 | async-start | bytes 1048576 | tf_op jit(solution)/shard_map/slice | solution.py:105
  94.1 5.0 %copy-start.5 = (s32[256,15]{0,1:T(8,128)S(1)}, s32[256,15]{0,1:T(8,128)}, u32[]{:S(2)}) copy-start(s32[256,15]{0,1:T(8,128)} %param.18) | copy-start | bytes 46084
  95.6 15.1 %all-to-all-start.1 = ((bf16[4,256,384]{1,2,0:T(8,128)(2,1)}), bf16[4,256,384]{1,2,0:T(8,128)(2,1)S(1)}, u32[]{:S(2)}, u32[]{:S(2)}) async-start(bf16[4,256,384]{1,2,0:T(8,128)(2,1)} %copy.51), calls=%async_computation.1 | async-start | bytes 1572864 | tf_op jit(solution)/shard_map/all_to_all | solution.py:108
  102.3 10.4 %copy-start.8 = (f32[1024]{0:T(1024)S(1)}, f32[1024]{0:T(1024)}, u32[]{:S(2)}) copy-start(f32[1024]{0:T(1024)} %param.15) | copy-start | bytes 12292
  112.7 2.1 copy-start.3
  114.8 0.8 copy-start.9
  115.6 1.7 copy-start.11
  115.6 1.7 copy-start.7
  117.3 1.0 copy-start.10
  121.3 29.3 %all-to-all-start.2 = ((bf16[4,256,1024]{1,2,0:T(8,128)(2,1)}), bf16[4,256,1024]{1,2,0:T(8,128)(2,1)S(1)}, u32[]{:S(2)}, u32[]{:S(2)}) async-start(bf16[4,256,1024]{1,2,0:T(8,128)(2,1)} %broadcast_in_dim.22), calls=%async_computation.2 | async-start | bytes 4194304 | tf_op jit(solution)/shard_map/all_to_all | solution.py:141
  150.6 30.2 %all-to-all-start.4 = ((bf16[4,256,1024]{2,1,0:T(8,128)(2,1)}), bf16[4,256,1024]{2,1,0:T(8,128)(2,1)}, u32[]{:S(2)}, u32[]{:S(2)}) async-start(bf16[4,256,1024]{2,1,0:T(8,128)(2,1)} %bitcast.45), calls=%async_computation.4 | async-start | bytes 4194304 | tf_op jit(solution)/shard_map/all_to_all | solution.py:130
  157.8 4.1 %copy-start.1 = (bf16[4096,192]{1,0:T(8,128)(2,1)S(1)}, bf16[4096,192]{1,0:T(8,128)(2,1)}, u32[]{:S(2)}) copy-start(bf16[4096,192]{1,0:T(8,128)(2,1)} %copy-done) | copy-start | bytes 4718596
  161.9 2.4 copy-start.2
  180.8 35.5 %all-to-all-start.3 = ((bf16[384,4,256]{2,0,1:T(8,128)(2,1)}), bf16[384,4,256]{2,0,1:T(8,128)(2,1)S(1)}, u32[]{:S(2)}, u32[]{:S(2)}) async-start(bf16[384,4,256]{2,0,1:T(8,128)(2,1)} %pad_maximum_fusion.2), calls=%async_computation.3 | async-start | bytes 1572864 | tf_op jit(solution)/shard_map/all_to_all | solution.py:154
  184.3 63.2 %all-reduce.2.cloned.1.call-start = ((), (), s32[]{:S(2)}) async-start(), calls=%async_computation.5 | async-start | bytes 2097152 | tf_op jit(solution)/shard_map/psum | solution.py:134
Sparse Core Ops, SparseCore 0:
  9.8 43.1 all-gather.2
  188.1 59.3 all-reduce.1

commit v2 on v1

v2 whole, which is shorter than its diff:
```python
import jax
import jax.numpy as jnp
from jax import lax
from jax.experimental import pallas as pl
from jax.experimental.pallas import tpu as pltpu
from jax.sharding import PartitionSpec as P


def swish_slope(preact):
    gate_val = jax.nn.sigmoid(preact)
    return gate_val * (1.0 + preact * (1.0 - gate_val))


def mixing(neighbours, block_len):
    positions = jnp.arange(block_len, dtype=jnp.int32)
    neighbour_hits = jnp.sum(
        (neighbours[:, :, None] == positions[None, None, :]).astype(jnp.float32), axis=1
    )
    return (jnp.eye(block_len, dtype=jnp.float32) + neighbour_hits) / (neighbours.shape[1] + 1.0)


def contract_rows(left_mat, right_mat):
    return lax.dot_general(
        left_mat, right_mat, (((0,), (0,)), ((), ())), preferred_element_type=jnp.float32
    )


def _aggregate_kernel(tgt_ref, rec_ref, sum_ref, cnt_ref):
    step = pl.program_id(0)

    @pl.when(step == 0)
    def _():
        sum_ref[...] = jnp.zeros_like(sum_ref)
        cnt_ref[...] = jnp.zeros_like(cnt_ref)

    targets = tgt_ref[0]
    n_tgt = sum_ref.shape[1]
    rows = lax.broadcasted_iota(jnp.int32, (n_tgt, targets.shape[1]), 0)
    hot = (rows == targets).astype(jnp.bfloat16)
    dims = (((1,), (1,)), ((), ()))
    sum_ref[...] += lax.dot_general(rec_ref[0], hot, dims, preferred_element_type=jnp.float32)
    ones = jnp.ones((cnt_ref.shape[0], targets.shape[1]), jnp.bfloat16)
    cnt_ref[...] += lax.dot_general(ones, hot, dims, preferred_element_type=jnp.float32)


def aggregate(targets, received_t, n_tgt):
    n_src, width, cap = received_t.shape
    targets = targets.reshape(n_src, 1, cap)
    return pl.pallas_call(
        _aggregate_kernel,
        grid=(n_src,),
        in_specs=[
            pl.BlockSpec((1, 1, cap), lambda s: (s, 0, 0)),
            pl.BlockSpec((1, width, cap), lambda s: (s, 0, 0)),
        ],
        out_specs=[
            pl.BlockSpec((width, n_tgt), lambda s: (0, 0)),
            pl.BlockSpec((8, n_tgt), lambda s: (0, 0)),
        ],
        out_shape=[
            jax.ShapeDtypeStruct((width, n_tgt), jnp.float32),
            jax.ShapeDtypeStruct((8, n_tgt), jnp.float32),
        ],
        cost_estimate=pl.CostEstimate(
            flops=2 * n_src * n_tgt * cap * (width + 8),
            transcendentals=0,
            bytes_accessed=n_src * cap * (width * 2 + 4) + n_tgt * (width + 8) * 4,
        ),
    )(targets, received_t)


def _xor_pairs(n, bit):
    return [(i, i ^ bit) for i in range(n)]


def _is_pow2(n):
    return n & (n - 1) == 0


def reduce_scatter_blocks(x, axis, n, send_dtype):
    if not _is_pow2(n):
        got = lax.all_to_all(x.astype(send_dtype), axis, 0, 0, tiled=True)
        return jnp.sum(got.astype(x.dtype), axis=0)
    me = lax.axis_index(axis)
    k = n.bit_length() - 1
    cur = x.reshape((2,) * k + x.shape[1:])
    for b in range(k):
        ax = k - 1 - b
        mine = (me >> b) & 1
        keep = lax.dynamic_index_in_dim(cur, mine, axis=ax, keepdims=False)
        send = lax.dynamic_index_in_dim(cur, 1 - mine, axis=ax, keepdims=False)
        got = lax.ppermute(send.astype(send_dtype), axis, _xor_pairs(n, 1 << b))
        cur = keep + got.astype(keep.dtype)
    return cur


def all_gather_blocks(x, axis, n):
    if not _is_pow2(n):
        return lax.all_gather(x, axis, axis=0, tiled=False)
    me = lax.axis_index(axis)
    k = n.bit_length() - 1
    cur = x
    for b in reversed(range(k)):
        mine = (me >> b) & 1
        got = lax.ppermute(cur, axis, _xor_pairs(n, 1 << b))
        low = jnp.where(mine == 0, cur, got)
        high = jnp.where(mine == 0, got, cur)
        cur = jnp.stack([low, high], axis=k - 1 - b)
    return cur.reshape((n,) + x.shape)


def local(
    features,
    edge_source,
    edge_target,
    neigh_weight,
    self_weight,
    bias_one,
    upper_weight,
    bias_two,
    upper_neighbours,
    out_cotangent,
):
    n_dom = lax.axis_size("dom")
    n_cols = lax.axis_size("cols")
    capacity = edge_source.shape[2]
    width = features.shape[1]
    hidden = upper_weight.shape[1]
    tgt_loc = upper_neighbours.shape[0]
    tgt_dev = tgt_loc * n_cols
    w_rows = neigh_weight.shape[0]
    up_rows = upper_weight.shape[0]

    packed = jnp.concatenate([neigh_weight, self_weight, upper_weight], axis=0)
    gathered = lax.all_gather(packed, "cols", axis=0, tiled=False)
    neigh_full = gathered[:, :w_rows]
    self_full = gathered[:, w_rows : 2 * w_rows]
    full_upper = gathered[:, 2 * w_rows :].reshape(n_cols * up_rows, hidden)

    outgoing = features.at[edge_source[0].reshape(-1)].get(mode="promise_in_bounds")
    received = lax.all_to_all(outgoing, "dom", split_axis=0, concat_axis=0, tiled=True)
    received_t = jnp.swapaxes(received.reshape(n_dom, capacity, width), 1, 2)
    summed_t, counts = aggregate(edge_target[0], received_t, tgt_dev)
    mean_t = (summed_t / jnp.maximum(counts[:1], 1.0)).astype(jnp.bfloat16)
    own_t = features[:tgt_dev].T
    both_t = jnp.concatenate([mean_t, own_t], axis=0)

    got = lax.all_to_all(both_t, "cols", split_axis=1, concat_axis=0, tiled=True).reshape(
        n_cols, 2 * width, tgt_loc
    )
    pre_one = (
        jnp.einsum(
            "cft,cfh->th", got[:, :width], neigh_full, preferred_element_type=jnp.float32
        )
        + jnp.einsum(
            "cft,cfh->th", got[:, width:], self_full, preferred_element_type=jnp.float32
        )
        + bias_one
    )
    hidden_one = jax.nn.silu(pre_one).astype(jnp.bfloat16)
    mix_matrix = mixing(upper_neighbours, tgt_loc)
    upper_input = jnp.dot(
        mix_matrix, hidden_one.astype(jnp.float32), precision=lax.Precision.HIGHEST
    ).astype(jnp.bfloat16)
    pre_two = jnp.dot(upper_input, full_upper, preferred_element_type=jnp.float32) + bias_two
    hidden_two = jax.nn.silu(pre_two).astype(jnp.bfloat16)
    slope_two = (out_cotangent.astype(jnp.float32) * swish_slope(pre_two)).astype(jnp.bfloat16)

    local_grad = contract_rows(upper_input, slope_two)
    col_sum = reduce_scatter_blocks(
        local_grad.reshape(n_cols, up_rows, hidden), "cols", n_cols, jnp.bfloat16
    )
    dom_rows = up_rows // n_dom
    dom_sum = reduce_scatter_blocks(
        col_sum.reshape(n_dom, dom_rows, hidden), "dom", n_dom, jnp.bfloat16
    )
    grad_upper = lax.all_to_all(
        jnp.broadcast_to(dom_sum.astype(jnp.bfloat16)[None], (n_dom, dom_rows, hidden)),
        "dom",
        split_axis=0,
        concat_axis=0,
        tiled=True,
    ).reshape(up_rows, hidden).astype(jnp.float32)

    back_mixed = lax.dot_general(
        slope_two, full_upper, (((1,), (1,)), ((), ())), preferred_element_type=jnp.float32
    )
    back_one = jnp.dot(mix_matrix.T, back_mixed, precision=lax.Precision.HIGHEST)
    slope_one = (back_one * swish_slope(pre_one)).astype(jnp.bfloat16)
    slab_rows = all_gather_blocks(slope_one, "cols", n_cols).reshape(tgt_dev, hidden)
    stacked = jnp.dot(both_t, slab_rows, preferred_element_type=jnp.float32)
    dom_cols = hidden // n_dom
    grad_layer = reduce_scatter_blocks(
        jnp.swapaxes(stacked.reshape(2 * width, n_dom, dom_cols), 0, 1),
        "dom",
        n_dom,
        jnp.bfloat16,
    )
    grad_neigh = grad_layer[:w_rows]
    grad_self = grad_layer[w_rows:]
    return (hidden_two, grad_neigh, grad_self, grad_upper)


def solution(mesh):
    in_specs = (
        P(("groups", "dom"), "cols"),
        P(("groups", "dom"), None, None),
        P(("groups", "dom"), None, None),
        P("cols", None),
        P("cols", None),
        P(),
        P("cols", None),
        P(),
        P(("groups", "dom", "cols"), None),
        P(("groups", "dom", "cols"), None),
    )
    out_specs = (
        P(("groups", "dom", "cols"), None),
        P(("groups", "cols"), "dom"),
        P(("groups", "cols"), "dom"),
        P(("groups", "cols"), None),
    )
    return jax.shard_map(local, mesh=mesh, in_specs=in_specs, out_specs=out_specs, check_vma=False)
```

time: 258 us -> 202 us (0.78)
  waiting for transfers between devices: 141 us -> 96.9 us
  matrix products: 15.7 us -> 10.9 us
  local copies, waits for them, and re-layouts: 42.9 us -> 38.6 us
    all_to_all x4 -> x2, waiting for transfers between devices: 74 us -> 8.93 us  [the longest x1 8.92 us: local(): lax.all_to_all(both_t, 'cols', split_axis=1, concat_axis=0, tiled=True)]
    ppermute x0 -> x8, waiting for transfers between devices: none -> 52.7 us  [the longest x6 43.5 us: reduce_scatter_blocks(): got = lax.ppermute(send.astype(send_dtype), axis, _xor_pairs(n, 1 << b))]
    psum x1 -> x0, waiting for transfers between devices: 30.3 us -> none  [local(): grad_upper = lax.psum(col_sum, 'dom')]
    ppermute x0 -> x8, starting transfers between devices: none -> 6.22 us  [the longest x6 5.8 us: reduce_scatter_blocks(): got = lax.ppermute(send.astype(send_dtype), axis, _xor_pairs(n, 1 << b))]
    all_to_all x4 -> x2, starting transfers between devices: 15.2 us -> 9.02 us  [the longest x1 4.65 us: local(): lax.all_to_all(jnp.broadcast_to(dom_sum.astype(jnp.bfloat16)[None], (n_do...]
    dot_general x3 -> x1, matrix products: 6.86 us -> 0.9 us  [contract_rows(): lax.dot_general(left_mat, right_mat, (((0,), (0,)), ((), ())), preferred_...]
    gather x2 -> x1, local copies, waits for them, and re-layouts: 20.9 us -> 16.9 us  [local(): features.at[edge_source[0].reshape(-1)].get(mode='promise_in_bounds')]
    add x0 -> x5, other arithmetic: none -> 3.91 us  [reduce_scatter_blocks(): cur = keep + got.astype(keep.dtype)]
  transfers between devices with their start and end apart: 7 -> 12, of which waited for: 6 -> 7; matrix products, arithmetic and copies ran while one was open for 22% -> 21% of each run, Pallas kernels for 3% -> 4%
where the time goes in v2:
time: 202 us
  waiting for transfers between devices  96.9 us (48%)
  local copies, waits for them, and re-layouts  38.6 us (19%)
  starting transfers between devices  21.7 us (11%)
  between operations  14.4 us (7%)
  other arithmetic  11.8 us (6%)
  matrix products  10.9 us (5%)
  Pallas kernels  7.22 us (4%)
    ppermute x6, waiting for transfers between devices, reduce_scatter_blocks(): got = lax.ppermute(send.astype(send_dtype), axis, _xor_pairs(n, 1 << b))  43.5 us
    all_to_all x1, waiting for transfers between devices, local(): lax.all_to_all(outgoing, 'dom', split_axis=0, concat_axis=0, tiled=True)  35.3 us
    gather x1, local copies, waits for them, and re-layouts, local(): features.at[edge_source[0].reshape(-1)].get(mode='promise_in_bounds')  16.9 us
    ppermute x2, waiting for transfers between devices, all_gather_blocks(): got = lax.ppermute(cur, axis, _xor_pairs(n, 1 << b))  9.11 us
    all_to_all x1, waiting for transfers between devices, local(): lax.all_to_all(both_t, 'cols', split_axis=1, concat_axis=0, tiled=True)  8.92 us
    unnamed x22, local copies, waits for them, and re-layouts  7.65 us
    pallas_call x1, Pallas kernels, aggregate(): pl.pallas_call(_aggregate_kernel, grid=(n_src,), in_specs=[pl.BlockSpec((...  7.22 us
    all_to_all x1, starting transfers between devices, local(): lax.all_to_all(outgoing, 'dom', split_axis=0, concat_axis=0, tiled=True)  6.45 us
  transfers between devices with their start and end apart: 12, of which 7 were waited for; matrix products, arithmetic and copies ran while one was open for 21% of the time, Pallas kernels for 4%

profile of v2, /device:TPU:0, one launch (start us, length us, event | category | flops | bytes accessed | tf_op | source)
XLA Modules:
  0.0 201.5 jit_solution(1828607572693114858)
XLA Ops:
  7.2 2.4 %pad_maximum_fusion.1 = bf16[640,1024]{1,0:T(8,128)(2,1)} fusion(bf16[256,1024]{1,0:T(8,128)(2,1)} %param.16, bf16[192,1024]{1,0:T(8,128)(2,1)} %param.14, bf16[192,1024]{1,0:T(8,128)(2,1)} %param.13), kind=kLoop, calls=%fused_computation.14 | loop fusion | flops 3932160 | bytes 2621440 | tf_op jit(solution)/shard_map/concatenate | solution.py:134
  9.7 3.2 %copy.26 = bf16[4096,192]{1,0:T(8,128)(2,1)S(1)} copy(bf16[4096,192]{0,1:T(8,128)(2,1)} %param.10) | data formatting | bytes 3145728 | tf_op args[0]
  12.9 16.9 %gather_fusion = bf16[4096,192]{1,0:T(8,128)(2,1)} fusion(bf16[4096,192]{1,0:T(8,128)(2,1)S(1)} %copy.26, s32[4096]{0:T(1024)S(1)} %broadcast_clamp_fusion), kind=kCustom, calls=%fused_computation | custom fusion | bytes 3162112 | tf_op jit(solution)/shard_map/gather | solution.py:140
  29.8 3.9 %copy.28 = bf16[4,1024,192]{1,2,0:T(8,128)(2,1)} copy(bf16[4,1024,192]{2,1,0:T(8,128)(2,1)} %bitcast.86) | data formatting | bytes 3145728 | tf_op jit(solution)/shard_map/all_to_all | solution.py:141
  33.8 6.4 %all-to-all-start = ((bf16[4,1024,192]{1,2,0:T(8,128)(2,1)}), bf16[4,1024,192]{1,2,0:T(8,128)(2,1)S(1)}, u32[]{:S(2)}, u32[]{:S(2)}) async-start(bf16[4,1024,192]{1,2,0:T(8,128)(2,1)} %copy.28), calls=%async_computation | async-start | bytes 3145728 | tf_op jit(solution)/shard_map/all_to_all | solution.py:141
  41.9 35.3 %all-to-all-done = bf16[4,1024,192]{1,2,0:T(8,128)(2,1)S(1)} async-done(((bf16[4,1024,192]{1,2,0:T(8,128)(2,1)}), bf16[4,1024,192]{1,2,0:T(8,128)(2,1)S(1)}, u32[]{:S(2)}, u32[]{:S(2)}) %all-to-all-start) | async-done | bytes 1572896 | tf_op jit(solution)/shard_map/all_to_all | solution.py:141
  77.2 1.2 copy-done.3
  78.4 7.2 %shard_map.129 = (f32[192,1024]{1,0:T(8,128)}, f32[8,1024]{1,0:T(8,128)}) custom-call(s32[4,1,1024]{2,1,0:T(1,128)} %reshape_squeeze.6.tgt_ref, bf16[4,192,1024]{2,1,0:T(8,128)(2,1)} %bitcast.93), custom_call_target="tpu_custom_call" | custom-call | flops 1677721600 | bytes 2408448 | tf_op jit(solution)/shard_map/pallas_call | solution.py:49
  86.3 1.2 divide_convert_fusion
  88.6 4.4 %all-to-all-start.1 = ((bf16[384,4,256]{2,0,1:T(8,128)(2,1)}), bf16[384,4,256]{2,0,1:T(8,128)(2,1)}, u32[]{:S(2)}, u32[]{:S(2)}) async-start(bf16[384,4,256]{2,0,1:T(8,128)(2,1)} %bitcast.82), calls=%async_computation.1 | async-start | bytes 1572864 | tf_op jit(solution)/shard_map/all_to_all | solution.py:148
  93.8 1.8 slice.42
  95.5 8.9 %all-to-all-done.1 = bf16[384,4,256]{2,0,1:T(8,128)(2,1)} async-done(((bf16[384,4,256]{2,0,1:T(8,128)(2,1)}), bf16[384,4,256]{2,0,1:T(8,128)(2,1)}, u32[]{:S(2)}, u32[]{:S(2)}) %all-to-all-start.1) | async-done | bytes 786464 | tf_op jit(solution)/shard_map/all_to_all | solution.py:148
  104.5 2.1 %fusion.4 = f32[256,1024]{1,0:T(8,128)S(1)} fusion(bf16[4,640,1024]{2,1,0:T(8,128)(2,1)} %bitcast.97, bf16[4,384,256]{2,1,0:T(8,128)(2,1)} %bitcast.5), kind=kOutput, calls=%fused_computation.10 | convolution fusion | flops 402653184 | bytes 3014656 | tf_op jit(solution)/shard_map/cft,cfh->th/dot_general | solution.py:152
  106.6 2.2 %fusion.13 = f32[256,1024]{1,0:T(8,128)S(1)} fusion(f32[256,1024]{1,0:T(8,128)S(1)} %fusion.4, bf16[4,640,1024]{2,1,0:T(8,128)(2,1)} %bitcast.98, f32[1024]{0:T(1024)S(1)} %copy-done.8, bf16[4,384,256]{2,1,0:T(8,128)(2,1)} %bitcast.5), kind=kOutput, calls=%fused_computation.16 | convolution fusion | flops 403177472 | bytes 4067328 | tf_op jit(solution)/shard_map/cft,cfh->th/dot_general | solution.py:155
  109.6 1.7 multiply_convert_fusion.1
  112.2 1.3 fusion.16
  114.9 1.9 copy-done
  116.9 1.1 fusion.17
  118.0 9.1 %collective-permute-done = bf16[256,1024]{1,0:T(8,128)(2,1)S(1)} collective-permute-done((bf16[256,1024]{1,0:T(8,128)(2,1)S(1)}, bf16[256,1024]{1,0:T(8,128)(2,1)S(1)}, u32[]{:S(2)}, u32[]{:S(2)}) %collective-permute-start) | collective-permute-done | bytes 524320 | tf_op jit(solution)/shard_map/ppermute | solution.py:105
  127.2 1.1 pad_maximum_fusion.2
  128.3 2.2 %bitcast_add_fusion = f32[2,256,1024]{2,1,0:T(8,128)S(1)} fusion(bf16[2,256,1024]{2,1,0:T(8,128)(2,1)} %collective-permute-done.4, f32[2,2,256,1024]{3,2,1,0:T(8,128)} %bitcast.84, s32[]{:T(128)S(6)} %select_n.79), kind=kLoop, calls=%fused_computation.4 | loop fusion | flops 1048576 | bytes 5242884 | tf_op jit(solution)/shard_map/add | solution.py:93
  130.5 1.3 copy-done.1
  133.0 2.6 %copy.31 = bf16[1024,1024]{1,0:T(8,128)(2,1)} copy(bf16[1024,1024]{0,1:T(8,128)(2,1)S(1)} %bitcast.85) | data formatting | bytes 4194304 | tf_op jit(solution)/shard_map/dot_general | solution.py:191
  135.6 10.8 %collective-permute-done.5 = bf16[256,1024]{1,0:T(8,128)(2,1)} collective-permute-done((bf16[256,1024]{1,0:T(8,128)(2,1)S(1)}, bf16[256,1024]{1,0:T(8,128)(2,1)}, u32[]{:S(2)}, u32[]{:S(2)}) %collective-permute-start.5) | collective-permute-done | bytes 524320 | tf_op jit(solution)/shard_map/ppermute | solution.py:92
  146.4 1.5 bitcast_add_fusion.1
  149.1 2.1 %collective-permute-start.2 = (bf16[2,384,256]{2,1,0:T(8,128)(2,1)S(1)}, bf16[2,384,256]{2,1,0:T(8,128)(2,1)S(1)}, u32[]{:S(2)}, u32[]{:S(2)}) collective-permute-start(bf16[2,384,256]{2,1,0:T(8,128)(2,1)S(1)} %fusion.21), channel_id=1, source_target_pairs={{0,4},{4,0},{8,12},{12,8},{1,5},{5,1},{9,13},{13,9},{2,6},{6,2},{1... | collective-permute-start | bytes 1179656 | tf_op jit(solution)/shard_map/ppermute | solution.py:92
  151.2 6.0 %collective-permute-done.6 = bf16[2,64,1024]{2,1,0:T(8,128)(2,1)S(1)} collective-permute-done((bf16[2,64,1024]{2,1,0:T(8,128)(2,1)S(1)}, bf16[2,64,1024]{2,1,0:T(8,128)(2,1)S(1)}, u32[]{:S(2)}, u32[]{:S(2)}) %collective-permute-start.6) | collective-permute-done | bytes 262176 | tf_op jit(solution)/shard_map/ppermute | solution.py:92
  157.4 7.6 %collective-permute-done.7 = bf16[64,1024]{1,0:T(8,128)(2,1)S(1)} collective-permute-done((bf16[64,1024]{1,0:T(8,128)(2,1)S(1)}, bf16[64,1024]{1,0:T(8,128)(2,1)S(1)}, u32[]{:S(2)}, u32[]{:S(2)}) %collective-permute-start.7) | collective-permute-done | bytes 131104 | tf_op jit(solution)/shard_map/ppermute | solution.py:92
  165.9 4.6 %all-to-all-start.2 = ((bf16[4,64,1024]{2,1,0:T(8,128)(2,1)}), bf16[4,64,1024]{2,1,0:T(8,128)(2,1)S(1)}, u32[]{:S(2)}, u32[]{:S(2)}) async-start(bf16[4,64,1024]{2,1,0:T(8,128)(2,1)} %broadcast_in_dim.2), calls=%async_computation.2 | async-start | bytes 1048576 | tf_op jit(solution)/shard_map/all_to_all | solution.py:177
  170.6 3.0 %collective-permute-start.3 = (bf16[384,256]{1,0:T(8,128)(2,1)S(1)}, bf16[384,256]{1,0:T(8,128)(2,1)S(1)}, u32[]{:S(2)}, u32[]{:S(2)}) collective-permute-start(bf16[384,256]{1,0:T(8,128)(2,1)S(1)} %fusion.26), channel_id=1, source_target_pairs={{0,8},{4,12},{8,0},{12,4},{1,9},{5,13},{9,1},{13,5},{2,10},{6,14},... | collective-permute-start | bytes 589832 | tf_op jit(solution)/shard_map/ppermute | solution.py:92
  173.6 19.1 %collective-permute-done.3 = bf16[384,256]{1,0:T(8,128)(2,1)S(1)} collective-permute-done((bf16[384,256]{1,0:T(8,128)(2,1)S(1)}, bf16[384,256]{1,0:T(8,128)(2,1)S(1)}, u32[]{:S(2)}, u32[]{:S(2)}) %collective-permute-start.3) | collective-permute-done | bytes 196640 | tf_op jit(solution)/shard_map/ppermute | solution.py:92
  193.6 1.1 bitcast_convert_fusion.1
  (58 shorter events, 11.8 us)
Async XLA Ops:
  7.2 86.6 %all-gather.3.cloned.1.call-start = ((), (), s32[]{:S(2)}) async-start(), calls=%async_computation.3 | async-start | bytes 6553600 | tf_op jit(solution)/shard_map/all_gather | solution.py:135
  9.6 3.2 %copy-start.6 = (s32[1,4,1024]{2,1,0:T(4,128)S(1)}, s32[1,4,1024]{2,1,0:T(4,128)}, u32[]{:S(2)}) copy-start(s32[1,4,1024]{2,1,0:T(4,128)} %param.11) | copy-start | bytes 49156
  33.8 6.5 %copy-start.7 = (s32[1,4,1024]{2,1,0:T(4,128)S(1)}, s32[1,4,1024]{2,1,0:T(4,128)}, u32[]{:S(2)}) copy-start(s32[1,4,1024]{2,1,0:T(4,128)} %param.12) | copy-start | bytes 49156
  33.8 43.4 %all-to-all-start = ((bf16[4,1024,192]{1,2,0:T(8,128)(2,1)}), bf16[4,1024,192]{1,2,0:T(8,128)(2,1)S(1)}, u32[]{:S(2)}, u32[]{:S(2)}) async-start(bf16[4,1024,192]{1,2,0:T(8,128)(2,1)} %copy.28), calls=%async_computation | async-start | bytes 3145728 | tf_op jit(solution)/shard_map/all_to_all | solution.py:141
  77.2 1.2 copy-start.3
  87.5 5.4 %copy-start.5 = (s32[256,15]{0,1:T(8,128)S(1)}, s32[256,15]{0,1:T(8,128)}, u32[]{:S(2)}) copy-start(s32[256,15]{0,1:T(8,128)} %param.18) | copy-start | bytes 46084
  88.6 15.9 %all-to-all-start.1 = ((bf16[384,4,256]{2,0,1:T(8,128)(2,1)}), bf16[384,4,256]{2,0,1:T(8,128)(2,1)}, u32[]{:S(2)}, u32[]{:S(2)}) async-start(bf16[384,4,256]{2,0,1:T(8,128)(2,1)} %bitcast.82), calls=%async_computation.1 | async-start | bytes 1572864 | tf_op jit(solution)/shard_map/all_to_all | solution.py:148
  95.5 11.1 %copy-start.8 = (f32[1024]{0:T(1024)S(1)}, f32[1024]{0:T(1024)}, u32[]{:S(2)}) copy-start(f32[1024]{0:T(1024)} %param.15) | copy-start | bytes 12292
  108.8 0.8 copy-start.9
  109.6 1.7 copy-start.4
  113.6 13.5 %collective-permute-start = (bf16[256,1024]{1,0:T(8,128)(2,1)S(1)}, bf16[256,1024]{1,0:T(8,128)(2,1)S(1)}, u32[]{:S(2)}, u32[]{:S(2)}) collective-permute-start(bf16[256,1024]{1,0:T(8,128)(2,1)S(1)} %fusion.16), channel_id=1, source_target_pairs={{0,2},{1,3},{2,0},{3,1},{4,6},{5,7},{6,4},{7,5},{8,10},{9,11},{10,... | collective-permute-start | bytes 1572872 | tf_op jit(solution)/shard_map/ppermute | solution.py:105
  114.9 2.0 copy-start
  118.0 10.3 %collective-permute-start.4 = (bf16[2,256,1024]{2,1,0:T(8,128)(2,1)}, bf16[2,256,1024]{2,1,0:T(8,128)(2,1)}, u32[]{:S(2)}, u32[]{:S(2)}) collective-permute-start(bf16[2,256,1024]{2,1,0:T(8,128)(2,1)} %fusion.17), channel_id=1, source_target_pairs={{0,1},{1,0},{2,3},{3,2},{4,5},{5,4},{6,7},{7,6},{8,9},{9,8},{10,11... | collective-permute-start | bytes 3145736 | tf_op jit(solution)/shard_map/ppermute | solution.py:92
  128.2 4.2 %collective-permute-start.1 = (bf16[2,256,1024]{2,1,0:T(8,128)(2,1)}, bf16[2,256,1024]{2,1,0:T(8,128)(2,1)S(1)}, u32[]{:S(2)}, u32[]{:S(2)}) collective-permute-start(bf16[2,256,1024]{2,1,0:T(8,128)(2,1)} %pad_maximum_fusion.2), channel_id=1, source_target_pairs={{0,1},{1,0},{2,3},{3,2},{4,5},{5,4},{6,7},{7,6},{8,9},{9,8},{10,11... | collective-permute-start | bytes 3145736 | tf_op jit(solution)/shard_map/ppermute | solution.py:105
  130.5 1.3 copy-start.1
  131.9 14.5 %collective-permute-start.5 = (bf16[256,1024]{1,0:T(8,128)(2,1)S(1)}, bf16[256,1024]{1,0:T(8,128)(2,1)}, u32[]{:S(2)}, u32[]{:S(2)}) collective-permute-start(bf16[256,1024]{1,0:T(8,128)(2,1)S(1)} %fusion.20), channel_id=1, source_target_pairs={{0,2},{1,3},{2,0},{3,1},{4,6},{5,7},{6,4},{7,5},{8,10},{9,11},{10,... | collective-permute-start | bytes 1572872 | tf_op jit(solution)/shard_map/ppermute | solution.py:92
  135.6 12.5 %copy-start.2 = (bf16[1024,1024]{1,0:T(8,128)(2,1)S(1)}, bf16[1024,1024]{1,0:T(8,128)(2,1)}, u32[]{:S(2)}) copy-start(bf16[1024,1024]{1,0:T(8,128)(2,1)} %copy.31) | copy-start | bytes 6291460
  147.9 9.3 %collective-permute-start.6 = (bf16[2,64,1024]{2,1,0:T(8,128)(2,1)S(1)}, bf16[2,64,1024]{2,1,0:T(8,128)(2,1)S(1)}, u32[]{:S(2)}, u32[]{:S(2)}) collective-permute-start(bf16[2,64,1024]{2,1,0:T(8,128)(2,1)S(1)} %fusion.24), channel_id=1, source_target_pairs={{0,4},{4,0},{8,12},{12,8},{1,5},{5,1},{9,13},{13,9},{2,6},{6,2},{1... | collective-permute-start | bytes 786440 | tf_op jit(solution)/shard_map/ppermute | solution.py:92
  149.1 21.4 %collective-permute-start.2 = (bf16[2,384,256]{2,1,0:T(8,128)(2,1)S(1)}, bf16[2,384,256]{2,1,0:T(8,128)(2,1)S(1)}, u32[]{:S(2)}, u32[]{:S(2)}) collective-permute-start(bf16[2,384,256]{2,1,0:T(8,128)(2,1)S(1)} %fusion.21), channel_id=1, source_target_pairs={{0,4},{4,0},{8,12},{12,8},{1,5},{5,1},{9,13},{13,9},{2,6},{6,2},{1... | collective-permute-start | bytes 1179656 | tf_op jit(solution)/shard_map/ppermute | solution.py:92
  157.3 7.7 %collective-permute-start.7 = (bf16[64,1024]{1,0:T(8,128)(2,1)S(1)}, bf16[64,1024]{1,0:T(8,128)(2,1)S(1)}, u32[]{:S(2)}, u32[]{:S(2)}) collective-permute-start(bf16[64,1024]{1,0:T(8,128)(2,1)S(1)} %fusion.27), channel_id=1, source_target_pairs={{0,8},{4,12},{8,0},{12,4},{1,9},{5,13},{9,1},{13,5},{2,10},{6,14},... | collective-permute-start | bytes 393224 | tf_op jit(solution)/shard_map/ppermute | solution.py:92
  165.9 27.7 %all-to-all-start.2 = ((bf16[4,64,1024]{2,1,0:T(8,128)(2,1)}), bf16[4,64,1024]{2,1,0:T(8,128)(2,1)S(1)}, u32[]{:S(2)}, u32[]{:S(2)}) async-start(bf16[4,64,1024]{2,1,0:T(8,128)(2,1)} %broadcast_in_dim.2), calls=%async_computation.2 | async-start | bytes 1048576 | tf_op jit(solution)/shard_map/all_to_all | solution.py:177
  170.6 22.1 %collective-permute-start.3 = (bf16[384,256]{1,0:T(8,128)(2,1)S(1)}, bf16[384,256]{1,0:T(8,128)(2,1)S(1)}, u32[]{:S(2)}, u32[]{:S(2)}) collective-permute-start(bf16[384,256]{1,0:T(8,128)(2,1)S(1)} %fusion.26), channel_id=1, source_target_pairs={{0,8},{4,12},{8,0},{12,4},{1,9},{5,13},{9,1},{13,5},{2,10},{6,14},... | collective-permute-start | bytes 589832 | tf_op jit(solution)/shard_map/ppermute | solution.py:92
Sparse Core Ops, SparseCore 0:
  9.8 43.1 all-gather.2

commit v3 on v2

--- a/solution.py
+++ b/solution.py
@@ -25,48 +25,41 @@
     )
 
 
-def _aggregate_kernel(tgt_ref, rec_ref, sum_ref, cnt_ref):
-    step = pl.program_id(0)
-
-    @pl.when(step == 0)
-    def _():
-        sum_ref[...] = jnp.zeros_like(sum_ref)
-        cnt_ref[...] = jnp.zeros_like(cnt_ref)
-
-    targets = tgt_ref[0]
+def _accumulate_kernel(tgt_ref, rec_ref, sum_in, cnt_in, sum_ref, cnt_ref):
+    targets = tgt_ref[...]
     n_tgt = sum_ref.shape[1]
     rows = lax.broadcasted_iota(jnp.int32, (n_tgt, targets.shape[1]), 0)
     hot = (rows == targets).astype(jnp.bfloat16)
     dims = (((1,), (1,)), ((), ()))
-    sum_ref[...] += lax.dot_general(rec_ref[0], hot, dims, preferred_element_type=jnp.float32)
+    sum_ref[...] = sum_in[...] + lax.dot_general(
+        rec_ref[...], hot, dims, preferred_element_type=jnp.float32
+    )
     ones = jnp.ones((cnt_ref.shape[0], targets.shape[1]), jnp.bfloat16)
-    cnt_ref[...] += lax.dot_general(ones, hot, dims, preferred_element_type=jnp.float32)
-
-
-def aggregate(targets, received_t, n_tgt):
-    n_src, width, cap = received_t.shape
-    targets = targets.reshape(n_src, 1, cap)
+    cnt_ref[...] = cnt_in[...] + lax.dot_general(
+        ones, hot, dims, preferred_element_type=jnp.float32
+    )
+
+
+def accumulate(targets, rec_t, acc_sum, acc_cnt):
+    width, cap = rec_t.shape
+    n_tgt = acc_sum.shape[1]
     return pl.pallas_call(
-        _aggregate_kernel,
-        grid=(n_src,),
-        in_specs=[
-            pl.BlockSpec((1, 1, cap), lambda s: (s, 0, 0)),
-            pl.BlockSpec((1, width, cap), lambda s: (s, 0, 0)),
+        _accumulate_kernel,
+        out_shape=[
+            jax.ShapeDtypeStruct(acc_sum.shape, jnp.float32),
+            jax.ShapeDtypeStruct(acc_cnt.shape, jnp.float32),
         ],
-        out_specs=[
-            pl.BlockSpec((width, n_tgt), lambda s: (0, 0)),
-            pl.BlockSpec((8, n_tgt), lambda s: (0, 0)),
-        ],
-        out_shape=[
-            jax.ShapeDtypeStruct((width, n_tgt), jnp.float32),
-            jax.ShapeDtypeStruct((8, n_tgt), jnp.float32),
-        ],
+        input_output_aliases={2: 0, 3: 1},
         cost_estimate=pl.CostEstimate(
-            flops=2 * n_src * n_tgt * cap * (width + 8),
+            flops=2 * n_tgt * cap * (width + acc_cnt.shape[0]),
             transcendentals=0,
-            bytes_accessed=n_src * cap * (width * 2 + 4) + n_tgt * (width + 8) * 4,
+            bytes_accessed=cap * (width * 2 + 4) + 2 * n_tgt * (width + acc_cnt.shape[0]) * 4,
         ),
-    )(targets, received_t)
+    )(targets, rec_t, acc_sum, acc_cnt)
+
+
+def _shift_pairs(n, shift):
+    return [(i, (i + shift) % n) for i in range(n)]
 
 
 def _xor_pairs(n, bit):
@@ -137,26 +130,42 @@
     self_full = gathered[:, w_rows : 2 * w_rows]
     full_upper = gathered[:, 2 * w_rows :].reshape(n_cols * up_rows, hidden)
 
-    outgoing = features.at[edge_source[0].reshape(-1)].get(mode="promise_in_bounds")
-    received = lax.all_to_all(outgoing, "dom", split_axis=0, concat_axis=0, tiled=True)
-    received_t = jnp.swapaxes(received.reshape(n_dom, capacity, width), 1, 2)
-    summed_t, counts = aggregate(edge_target[0], received_t, tgt_dev)
+    me_dom = lax.axis_index("dom")
+    me_col = lax.axis_index("cols")
+    own_t = features[:tgt_dev].T
+    own_pre = bias_one
+    for shift in range(n_cols):
+        dest = (me_col + shift) % n_cols
+        src = (me_col - shift) % n_cols
+        chunk = lax.dynamic_slice_in_dim(own_t, dest * tgt_loc, tgt_loc, axis=1)
+        if shift:
+            chunk = lax.ppermute(chunk, "cols", _shift_pairs(n_cols, shift))
+        weight = lax.dynamic_index_in_dim(self_full, src, 0, keepdims=False)
+        own_pre = own_pre + contract_rows(chunk, weight)
+
+    summed_t = jnp.zeros((width, tgt_dev), jnp.float32)
+    counts = jnp.zeros((8, tgt_dev), jnp.float32)
+    for shift in range(n_dom):
+        dest = (me_dom + shift) % n_dom
+        src = (me_dom - shift) % n_dom
+        slots = lax.dynamic_index_in_dim(edge_source[0], dest, 0, keepdims=False)
+        rows_t = features.at[slots].get(mode="promise_in_bounds").T
+        if shift:
+            rows_t = lax.ppermute(rows_t, "dom", _shift_pairs(n_dom, shift))
+        targets = lax.dynamic_index_in_dim(edge_target[0], src, 0, keepdims=True)
+        summed_t, counts = accumulate(targets, rows_t, summed_t, counts)
     mean_t = (summed_t / jnp.maximum(counts[:1], 1.0)).astype(jnp.bfloat16)
-    own_t = features[:tgt_dev].T
     both_t = jnp.concatenate([mean_t, own_t], axis=0)
 
-    got = lax.all_to_all(both_t, "cols", split_axis=1, concat_axis=0, tiled=True).reshape(
-        n_cols, 2 * width, tgt_loc
-    )
-    pre_one = (
-        jnp.einsum(
-            "cft,cfh->th", got[:, :width], neigh_full, preferred_element_type=jnp.float32
-        )
-        + jnp.einsum(
-            "cft,cfh->th", got[:, width:], self_full, preferred_element_type=jnp.float32
-        )
-        + bias_one
-    )
+    pre_one = own_pre
+    for shift in range(n_cols):
+        dest = (me_col + shift) % n_cols
+        src = (me_col - shift) % n_cols
+        chunk = lax.dynamic_slice_in_dim(mean_t, dest * tgt_loc, tgt_loc, axis=1)
+        if shift:
+            chunk = lax.ppermute(chunk, "cols", _shift_pairs(n_cols, shift))
+        weight = lax.dynamic_index_in_dim(neigh_full, src, 0, keepdims=False)
+        pre_one = pre_one + contract_rows(chunk, weight)
     hidden_one = jax.nn.silu(pre_one).astype(jnp.bfloat16)
     mix_matrix = mixing(upper_neighbours, tgt_loc)
     upper_input = jnp.dot(
@@ -170,32 +179,35 @@
     col_sum = reduce_scatter_blocks(
         local_grad.reshape(n_cols, up_rows, hidden), "cols", n_cols, jnp.bfloat16
     )
+    back_mixed = lax.dot_general(
+        slope_two, full_upper, (((1,), (1,)), ((), ())), preferred_element_type=jnp.float32
+    )
+    back_one = jnp.dot(mix_matrix.T, back_mixed, precision=lax.Precision.HIGHEST)
+    slope_one = (back_one * swish_slope(pre_one)).astype(jnp.bfloat16)
+    slab_rows = all_gather_blocks(slope_one, "cols", n_cols).reshape(tgt_dev, hidden)
+    stacked = jnp.dot(both_t, slab_rows, preferred_element_type=jnp.float32)
+    dom_cols = hidden // n_dom
     dom_rows = up_rows // n_dom
-    dom_sum = reduce_scatter_blocks(
-        col_sum.reshape(n_dom, dom_rows, hidden), "dom", n_dom, jnp.bfloat16
-    )
+    upper_len = dom_rows * hidden
+    payload = jnp.concatenate(
+        [
+            col_sum.reshape(n_dom, upper_len),
+            jnp.swapaxes(stacked.reshape(2 * width, n_dom, dom_cols), 0, 1).reshape(n_dom, -1),
+        ],
+        axis=1,
+    )
+    reduced = reduce_scatter_blocks(payload, "dom", n_dom, jnp.bfloat16)
+    grad_layer = reduced[upper_len:].reshape(2 * width, dom_cols)
     grad_upper = lax.all_to_all(
-        jnp.broadcast_to(dom_sum.astype(jnp.bfloat16)[None], (n_dom, dom_rows, hidden)),
+        jnp.broadcast_to(
+            reduced[:upper_len].astype(jnp.bfloat16).reshape(1, dom_rows, hidden),
+            (n_dom, dom_rows, hidden),
+        ),
         "dom",
         split_axis=0,
         concat_axis=0,
         tiled=True,
     ).reshape(up_rows, hidden).astype(jnp.float32)
-
-    back_mixed = lax.dot_general(
-        slope_two, full_upper, (((1,), (1,)), ((), ())), preferred_element_type=jnp.float32
-    )
-    back_one = jnp.dot(mix_matrix.T, back_mixed, precision=lax.Precision.HIGHEST)
-    slope_one = (back_one * swish_slope(pre_one)).astype(jnp.bfloat16)
-    slab_rows = all_gather_blocks(slope_one, "cols", n_cols).reshape(tgt_dev, hidden)
-    stacked = jnp.dot(both_t, slab_rows, preferred_element_type=jnp.float32)
-    dom_cols = hidden // n_dom
-    grad_layer = reduce_scatter_blocks(
-        jnp.swapaxes(stacked.reshape(2 * width, n_dom, dom_cols), 0, 1),
-        "dom",
-        n_dom,
-        jnp.bfloat16,
-    )
     grad_neigh = grad_layer[:w_rows]
     grad_self = grad_layer[w_rows:]
     return (hidden_two, grad_neigh, grad_self, grad_upper)

time: 202 us -> 190 us (0.941)
  waiting for transfers between devices: 96.9 us -> 54 us
  local copies, waits for them, and re-layouts: 38.6 us -> 56.4 us
  Pallas kernels: 7.22 us -> 13 us
  starting transfers between devices: 21.7 us -> 25 us
  matrix products: 10.9 us -> 13 us
    all_to_all x3 -> x1, waiting for transfers between devices: 44.2 us -> 13.1 us  [local(): lax.all_to_all(jnp.broadcast_to(reduced[:upper_len].astype(jnp.bfloat16)....]
    ppermute x0 -> x9, starting transfers between devices: none -> 12.8 us  [the longest x3 7.03 us: local(): rows_t = lax.ppermute(rows_t, 'dom', _shift_pairs(n_dom, shift))]
    ppermute x6 -> x4, waiting for transfers between devices: 43.5 us -> 31.1 us  [reduce_scatter_blocks(): got = lax.ppermute(send.astype(send_dtype), axis, _xor_pairs(n, 1 << b))]
    all_to_all x3 -> x1, starting transfers between devices: 15.5 us -> 4.77 us  [local(): lax.all_to_all(jnp.broadcast_to(reduced[:upper_len].astype(jnp.bfloat16)....]
    concatenate x0 -> x3, local copies, waits for them, and re-layouts: none -> 6.28 us  [local(): jnp.concatenate([col_sum.reshape(n_dom, upper_len), jnp.swapaxes(stacked....]
    convert_element_type x6 -> x4, local copies, waits for them, and re-layouts: 1.35 us -> 7.5 us  [reduce_scatter_blocks(): got = lax.ppermute(send.astype(send_dtype), axis, _xor_pairs(n, 1 << b))]
    pallas_call x1 -> x4, Pallas kernels: 7.22 us -> 13 us  [accumulate(): pl.pallas_call(_accumulate_kernel, out_shape=[jax.ShapeDtypeStruct(acc_su...]
    all_to_all x2 -> x0, local copies, waits for them, and re-layouts: 4.85 us -> none  [the longest x1 3.92 us: local(): lax.all_to_all(outgoing, 'dom', split_axis=0, concat_axis=0, tiled=True)]
  transfers between devices with their start and end apart: 12 -> 17, of which waited for: 7 -> 6; matrix products, arithmetic and copies ran while one was open for 21% -> 28% of each run, Pallas kernels for 4% -> 7%
where the time goes in v3:
time: 190 us; the launch traced here: 189 us
  local copies, waits for them, and re-layouts  56.4 us (30%)
  waiting for transfers between devices  54 us (28%)
  starting transfers between devices  25 us (13%)
  between operations  14.6 us (8%)
  other arithmetic  13.1 us (7%)
  Pallas kernels  13 us (7%)
  matrix products  13 us (7%)
    ppermute x4, waiting for transfers between devices, reduce_scatter_blocks(): got = lax.ppermute(send.astype(send_dtype), axis, _xor_pairs(n, 1 << b))  31.1 us
    gather x8, local copies, waits for them, and re-layouts, local(): rows_t = features.at[slots].get(mode='promise_in_bounds').T  18.8 us
    all_to_all x1, waiting for transfers between devices, local(): lax.all_to_all(jnp.broadcast_to(reduced[:upper_len].astype(jnp.bfloat16)....  13.1 us
    pallas_call x4, Pallas kernels, accumulate(): pl.pallas_call(_accumulate_kernel, out_shape=[jax.ShapeDtypeStruct(acc_su...  13 us
    unnamed x28, local copies, waits for them, and re-layouts  8.98 us
    ppermute x2, waiting for transfers between devices, all_gather_blocks(): got = lax.ppermute(cur, axis, _xor_pairs(n, 1 << b))  8.64 us
    convert_element_type x4, local copies, waits for them, and re-layouts, reduce_scatter_blocks(): got = lax.ppermute(send.astype(send_dtype), axis, _xor_pairs(n, 1 << b))  7.5 us
    ppermute x3, starting transfers between devices, local(): rows_t = lax.ppermute(rows_t, 'dom', _shift_pairs(n_dom, shift))  7.03 us
  transfers between devices with their start and end apart: 17, of which 6 were waited for; matrix products, arithmetic and copies ran while one was open for 28% of the time, Pallas kernels for 7%

profile of v3, /device:TPU:0, one launch (start us, length us, event | category | flops | bytes accessed | tf_op | source)
XLA Modules:
  0.0 189.0 jit_solution(2116539125891999306)
XLA Ops:
  7.2 2.5 %pad_maximum_fusion.1 = bf16[640,1024]{1,0:T(8,128)(2,1)} fusion(bf16[256,1024]{1,0:T(8,128)(2,1)} %param.16, bf16[192,1024]{1,0:T(8,128)(2,1)} %param.14, bf16[192,1024]{1,0:T(8,128)(2,1)} %param.13), kind=kLoop, calls=%fused_computation.20 | loop fusion | flops 3932160 | bytes 2621440 | tf_op jit(solution)/shard_map/concatenate | solution.py:127
  9.8 3.2 %copy.57 = bf16[4096,192]{1,0:T(8,128)(2,1)S(1)} copy(bf16[4096,192]{0,1:T(8,128)(2,1)} %param.10) | data formatting | bytes 3145728 | tf_op args[0]
  13.0 3.9 %gather_fusion.2 = bf16[1024,192]{1,0:T(8,128)(2,1)S(1)} fusion(bf16[4096,192]{1,0:T(8,128)(2,1)S(1)} %copy.57, s32[1024]{0:T(1024)S(1)} %get-tuple-element.47), kind=kCustom, calls=%fused_computation.2 | custom fusion | bytes 790528 | tf_op jit(solution)/shard_map/gather | solution.py:152
  18.0 3.0 %collective-permute-start.5 = (bf16[192,1024]{1,0:T(8,128)(2,1)}, bf16[192,1024]{1,0:T(8,128)(2,1)}, u32[]{:S(2)}, u32[]{:S(2)}) collective-permute-start(bf16[192,1024]{1,0:T(8,128)(2,1)} %bitcast.19), channel_id=1, source_target_pairs={{0,4},{4,8},{8,12},{12,0},{1,5},{5,9},{9,13},{13,1},{2,6},{6,10},{... | collective-permute-start | bytes 1179656 | tf_op jit(solution)/shard_map/ppermute | solution.py:154
  21.0 3.9 %gather_fusion.1 = bf16[1024,192]{1,0:T(8,128)(2,1)S(1)} fusion(bf16[4096,192]{1,0:T(8,128)(2,1)S(1)} %copy.57, s32[1024]{0:T(1024)S(1)} %get-tuple-element.48), kind=kCustom, calls=%fused_computation.1 | custom fusion | bytes 790528 | tf_op jit(solution)/shard_map/gather | solution.py:152
  25.1 2.7 %collective-permute-start.4 = (bf16[192,1024]{1,0:T(8,128)(2,1)S(1)}, bf16[192,1024]{1,0:T(8,128)(2,1)}, u32[]{:S(2)}, u32[]{:S(2)}) collective-permute-start(bf16[192,1024]{1,0:T(8,128)(2,1)S(1)} %bitcast.126), channel_id=1, source_target_pairs={{0,8},{4,12},{8,0},{12,4},{1,9},{5,13},{9,1},{13,5},{2,10},{6,14},... | collective-permute-start | bytes 1179656 | tf_op jit(solution)/shard_map/ppermute | solution.py:154
  27.8 1.8 slice_bitcast_fusion
  30.3 1.7 collective-permute-start.2
  32.1 3.9 %gather_fusion = bf16[1024,192]{1,0:T(8,128)(2,1)S(1)} fusion(bf16[4096,192]{1,0:T(8,128)(2,1)S(1)} %copy.57, s32[1024]{0:T(1024)S(1)} %get-tuple-element.49), kind=kCustom, calls=%fused_computation | custom fusion | bytes 790528 | tf_op jit(solution)/shard_map/gather | solution.py:152
  38.3 3.9 %gather_fusion.3 = bf16[1024,192]{1,0:T(8,128)(2,1)S(1)} fusion(bf16[4096,192]{1,0:T(8,128)(2,1)S(1)} %copy.57, s32[1024]{0:T(1024)S(1)} %get-tuple-element.46), kind=kCustom, calls=%fused_computation.3 | custom fusion | bytes 790528 | tf_op jit(solution)/shard_map/gather | solution.py:152
  45.4 3.3 %shard_map.129 = (f32[192,1024]{1,0:T(8,128)}, f32[8,1024]{1,0:T(8,128)}) custom-call(s32[1,1024]{1,0:T(1,128)} %get-tuple-element.40.tgt_ref, bf16[192,1024]{1,0:T(8,128)(2,1)} %bitcast.128, f32[192,1024]{1,0:T(8,128)} %broadcast_in_dim.6.sum_in, f32[8,1024]{1,0:T(8,128)} %broadcast_in_dim.7.cnt_in), custom_call_target="tpu_custom_call", output_to_operand_aliasing={{0}: (2, {}), {1}: (3, {})} | custom-call | flops 419430400 | bytes 2035712 | tf_op jit(solution)/shard_map/pallas_call | solution.py:46
  51.1 3.3 %shard_map.130 = (f32[192,1024]{1,0:T(8,128)}, f32[8,1024]{1,0:T(8,128)}) custom-call(s32[1,1024]{1,0:T(1,128)} %get-tuple-element.43.tgt_ref, bf16[192,1024]{1,0:T(8,128)(2,1)} %collective-permute-done.5.rec_ref, f32[192,1024]{1,0:T(8,128)} %get-tuple-element.12.sum_in, ...), custom_call_target="tpu_custom_call", output_to_operand_aliasing={{0}: (2, {}), {1}: (3, {})} | custom-call | flops 419430400 | bytes 2035712 | tf_op jit(solution)/shard_map/pallas_call | solution.py:46
  54.4 3.3 %shard_map.131 = (f32[192,1024]{1,0:T(8,128)}, f32[8,1024]{1,0:T(8,128)}) custom-call(s32[1,1024]{1,0:T(1,128)} %get-tuple-element.41.tgt_ref, bf16[192,1024]{1,0:T(8,128)(2,1)} %collective-permute-done.4.rec_ref, f32[192,1024]{1,0:T(8,128)} %get-tuple-element.14.sum_in, ...), custom_call_target="tpu_custom_call", output_to_operand_aliasing={{0}: (2, {}), {1}: (3, {})} | custom-call | flops 419430400 | bytes 2035712 | tf_op jit(solution)/shard_map/pallas_call | solution.py:46
  57.6 3.3 %shard_map.132 = (f32[192,1024]{1,0:T(8,128)}, f32[8,1024]{1,0:T(8,128)}) custom-call(s32[1,1024]{1,0:T(1,128)} %get-tuple-element.42.tgt_ref, bf16[192,1024]{1,0:T(8,128)(2,1)} %collective-permute-done.3.rec_ref, f32[192,1024]{1,0:T(8,128)} %get-tuple-element.16.sum_in, ...), custom_call_target="tpu_custom_call", output_to_operand_aliasing={{0}: (2, {}), {1}: (3, {})} | custom-call | flops 419430400 | bytes 2035712 | tf_op jit(solution)/shard_map/pallas_call | solution.py:46
  64.7 2.2 %fusion.58 = (bf16[4,192,1024]{2,1,0:T(8,128)(2,1)S(1)}, bf16[4,192,1024]{2,1,0:T(8,128)(2,1)S(1)}) fusion(bf16[4,640,1024]{2,1,0:T(8,128)(2,1)} %bitcast.120), kind=kLoop, calls=%fused_computation.124 | loop fusion | bytes 6291456 | tf_op jit(solution)/shard_map/slice | solution.py:130
  71.9 1.8 slice.80
  80.4 2.0 %copy-done = f32[1024,1024]{1,0:T(8,128)} copy-done((f32[1024,1024]{1,0:T(8,128)}, f32[1024,1024]{1,0:T(8,128)S(1)}, u32[]{:S(2)}) %copy-start) | copy-done | bytes 4194328
  82.6 8.6 %collective-permute-done.11 = bf16[256,1024]{1,0:T(8,128)(2,1)S(1)} collective-permute-done((bf16[256,1024]{1,0:T(8,128)(2,1)S(1)}, bf16[256,1024]{1,0:T(8,128)(2,1)S(1)}, u32[]{:S(2)}, u32[]{:S(2)}) %collective-permute-start.11) | collective-permute-done | bytes 524320 | tf_op jit(solution)/shard_map/ppermute | solution.py:98
  92.4 2.2 %bitcast_add_fusion = f32[2,256,1024]{2,1,0:T(8,128)S(1)} fusion(bf16[2,256,1024]{2,1,0:T(8,128)(2,1)} %collective-permute-done.9, f32[2,2,256,1024]{3,2,1,0:T(8,128)} %bitcast.118, s32[]{:T(128)S(6)} %select_n.261), kind=kLoop, calls=%fused_computation.8 | loop fusion | flops 1048576 | bytes 5242884 | tf_op jit(solution)/shard_map/add | solution.py:86
  96.4 2.8 %copy.67 = bf16[1024,1024]{1,0:T(8,128)(2,1)} copy(bf16[1024,1024]{0,1:T(8,128)(2,1)S(1)} %bitcast.119) | data formatting | bytes 4194304 | tf_op jit(solution)/shard_map/dot_general | solution.py:188
  99.2 3.8 %convolution_bitcast_fusion = f32[4,384,256]{2,1,0:T(8,128)} fusion(bf16[4,256,1024]{2,1,0:T(8,128)(2,1)} %bitcast.125, bf16[192,1024]{1,0:T(8,128)(2,1)S(1)} %copy-done.6, bf16[192,1024]{1,0:T(8,128)(2,1)S(1)} %divide_convert_fusion), kind=kOutput, calls=%fused_computation.10 | convolution fusion | flops 806879232 | bytes 4456448 | tf_op jit(solution)/shard_map/dot_general | solution.py:188
  103.0 3.3 %concatenate.17 = f32[2,2,98304]{2,1,0:T(2,128)} reshape(f32[4,384,256]{2,1,0:T(8,128)} %convolution_bitcast_fusion) | data formatting | bytes 3145728 | tf_op jit(solution)/shard_map/concatenate | solution.py:192
  106.2 3.0 %collective-permute-done.10 = bf16[256,1024]{1,0:T(8,128)(2,1)} collective-permute-done((bf16[256,1024]{1,0:T(8,128)(2,1)S(1)}, bf16[256,1024]{1,0:T(8,128)(2,1)}, u32[]{:S(2)}, u32[]{:S(2)}) %collective-permute-start.10) | collective-permute-done | bytes 524320 | tf_op jit(solution)/shard_map/ppermute | solution.py:85
  112.2 2.0 %copy_dynamic-update-slice_fusion.1 = f32[2,2,163840]{2,0,1:T(2,128)S(1)} fusion(f32[2,2,65536]{2,1,0:T(2,128)} %concatenate.15), kind=kLoop, calls=%fused_computation.27 | loop fusion | bytes 2097152
  117.5 2.3 %collective-permute-start.13 = (bf16[2,163840]{1,0:T(2,128)(2,1)S(1)}, bf16[2,163840]{1,0:T(2,128)(2,1)S(1)}, u32[]{:S(2)}, u32[]{:S(2)}) collective-permute-start(bf16[2,163840]{1,0:T(2,128)(2,1)S(1)} %fusion.8), channel_id=1, source_target_pairs={{0,4},{4,0},{8,12},{12,8},{1,5},{5,1},{9,13},{13,9},{2,6},{6,2},{1... | collective-permute-start | bytes 1966088 | tf_op jit(solution)/shard_map/ppermute | solution.py:85
  119.8 14.6 %collective-permute-done.13 = bf16[2,163840]{1,0:T(2,128)(2,1)S(1)} collective-permute-done((bf16[2,163840]{1,0:T(2,128)(2,1)S(1)}, bf16[2,163840]{1,0:T(2,128)(2,1)S(1)}, u32[]{:S(2)}, u32[]{:S(2)}) %collective-permute-start.13) | collective-permute-done | bytes 655392 | tf_op jit(solution)/shard_map/ppermute | solution.py:85
  134.5 1.8 bitcast_add_fusion.1
  136.3 6.8 %convert_reduce_fusion.1 = bf16[163840]{0:T(1024)(128)(2,1)S(1)} fusion(f32[2,163840]{1,0:T(2,128)S(1)} %bitcast_add_fusion.1, s32[]{:T(128)S(6)} %select_n.274), kind=kLoop, calls=%fused_computation.43 | loop fusion | bytes 655364 | tf_op jit(solution)/shard_map/convert_element_type | solution.py:85
  143.1 3.6 %collective-permute-start.14 = (bf16[163840]{0:T(1024)(128)(2,1)S(1)}, bf16[163840]{0:T(1024)(128)(2,1)S(1)}, u32[]{:S(2)}, u32[]{:S(2)}) collective-permute-start(bf16[163840]{0:T(1024)(128)(2,1)S(1)} %convert_reduce_fusion.1), channel_id=1, source_target_pairs={{0,8},{4,12},{8,0},{12,4},{1,9},{5,13},{9,1},{13,5},{2,10},{6,14},... | collective-permute-start | bytes 983048 | tf_op jit(solution)/shard_map/ppermute | solution.py:85
  147.2 13.5 %collective-permute-done.14 = bf16[163840]{0:T(1024)(128)(2,1)S(1)} collective-permute-done((bf16[163840]{0:T(1024)(128)(2,1)S(1)}, bf16[163840]{0:T(1024)(128)(2,1)S(1)}, u32[]{:S(2)}, u32[]{:S(2)}) %collective-permute-start.14) | collective-permute-done | bytes 327712 | tf_op jit(solution)/shard_map/ppermute | solution.py:85
  161.7 4.8 %all-to-all-start = ((bf16[4,64,1024]{2,1,0:T(8,128)(2,1)}), bf16[4,64,1024]{2,1,0:T(8,128)(2,1)S(1)}, u32[]{:S(2)}, u32[]{:S(2)}) async-start(bf16[4,64,1024]{2,1,0:T(8,128)(2,1)} %broadcast_in_dim.8), calls=%async_computation | async-start | bytes 1048576 | tf_op jit(solution)/shard_map/all_to_all | solution.py:201
  167.9 13.1 %all-to-all-done = bf16[4,64,1024]{2,1,0:T(8,128)(2,1)S(1)} async-done(((bf16[4,64,1024]{2,1,0:T(8,128)(2,1)}), bf16[4,64,1024]{2,1,0:T(8,128)(2,1)S(1)}, u32[]{:S(2)}, u32[]{:S(2)}) %all-to-all-start) | async-done | bytes 524320 | tf_op jit(solution)/shard_map/all_to_all | solution.py:201
  (97 shorter events, 38.6 us)
Async XLA Ops:
  7.2 57.5 %all-gather.3.cloned.1.call-start = ((), (), s32[]{:S(2)}) async-start(), calls=%async_computation.1 | async-start | bytes 6553600 | tf_op jit(solution)/shard_map/all_gather | solution.py:128
  9.7 3.3 %copy-start.9 = (s32[1,4,1024]{2,1,0:T(4,128)S(1)}, s32[1,4,1024]{2,1,0:T(4,128)}, u32[]{:S(2)}) copy-start(s32[1,4,1024]{2,1,0:T(4,128)} %param.11) | copy-start | bytes 49156
  18.0 31.5 %collective-permute-start.5 = (bf16[192,1024]{1,0:T(8,128)(2,1)}, bf16[192,1024]{1,0:T(8,128)(2,1)}, u32[]{:S(2)}, u32[]{:S(2)}) collective-permute-start(bf16[192,1024]{1,0:T(8,128)(2,1)} %bitcast.19), channel_id=1, source_target_pairs={{0,4},{4,8},{8,12},{12,0},{1,5},{5,9},{9,13},{13,1},{2,6},{6,10},{... | collective-permute-start | bytes 1179656 | tf_op jit(solution)/shard_map/ppermute | solution.py:154
  25.1 29.2 %collective-permute-start.4 = (bf16[192,1024]{1,0:T(8,128)(2,1)S(1)}, bf16[192,1024]{1,0:T(8,128)(2,1)}, u32[]{:S(2)}, u32[]{:S(2)}) collective-permute-start(bf16[192,1024]{1,0:T(8,128)(2,1)S(1)} %bitcast.126), channel_id=1, source_target_pairs={{0,8},{4,12},{8,0},{12,4},{1,9},{5,13},{9,1},{13,5},{2,10},{6,14},... | collective-permute-start | bytes 1179656 | tf_op jit(solution)/shard_map/ppermute | solution.py:154
  30.3 38.5 %collective-permute-start = (bf16[192,256]{1,0:T(8,128)(2,1)}, bf16[192,256]{1,0:T(8,128)(2,1)}, u32[]{:S(2)}, u32[]{:S(2)}) collective-permute-start(bf16[192,256]{1,0:T(8,128)(2,1)} %get-tuple-element.33), channel_id=1, source_target_pairs={{0,1},{1,2},{2,3},{3,0},{4,5},{5,6},{6,7},{7,4},{8,9},{9,10},{10,1... | collective-permute-start | bytes 294920 | tf_op jit(solution)/shard_map/ppermute | solution.py:142
  30.3 36.6 %collective-permute-start.2 = (bf16[192,256]{1,0:T(8,128)(2,1)}, bf16[192,256]{1,0:T(8,128)(2,1)S(1)}, u32[]{:S(2)}, u32[]{:S(2)}) collective-permute-start(bf16[192,256]{1,0:T(8,128)(2,1)} %get-tuple-element.34), channel_id=1, source_target_pairs={{0,3},{1,0},{2,1},{3,2},{4,7},{5,4},{6,5},{7,6},{8,11},{9,8},{10,9... | collective-permute-start | bytes 294920 | tf_op jit(solution)/shard_map/ppermute | solution.py:142
  37.0 20.7 %collective-permute-start.3 = (bf16[192,1024]{1,0:T(8,128)(2,1)}, bf16[192,1024]{1,0:T(8,128)(2,1)}, u32[]{:S(2)}, u32[]{:S(2)}) collective-permute-start(bf16[192,1024]{1,0:T(8,128)(2,1)} %bitcast.127), channel_id=1, source_target_pairs={{0,12},{4,0},{8,4},{12,8},{1,13},{5,1},{9,5},{13,9},{2,14},{6,2},{... | collective-permute-start | bytes 1179656 | tf_op jit(solution)/shard_map/ppermute | solution.py:154
  38.3 4.9 %copy-start.10 = (s32[1,4,1024]{2,1,0:T(4,128)S(1)}, s32[1,4,1024]{2,1,0:T(4,128)}, u32[]{:S(2)}) copy-start(s32[1,4,1024]{2,1,0:T(4,128)} %param.12) | copy-start | bytes 49156
  42.2 6.5 %copy-start.8 = (s32[256,15]{0,1:T(8,128)S(1)}, s32[256,15]{0,1:T(8,128)}, u32[]{:S(2)}) copy-start(s32[256,15]{0,1:T(8,128)} %param.18) | copy-start | bytes 46084
  42.3 7.2 %copy-start.7 = (bf16[192,256]{1,0:T(8,128)(2,1)S(1)}, bf16[192,256]{1,0:T(8,128)(2,1)}, u32[]{:S(2)}) copy-start(bf16[192,256]{1,0:T(8,128)(2,1)} %get-tuple-element.35) | copy-start | bytes 294916
  49.5 18.7 %collective-permute-start.1 = (bf16[192,256]{1,0:T(8,128)(2,1)S(1)}, bf16[192,256]{1,0:T(8,128)(2,1)S(1)}, u32[]{:S(2)}, u32[]{:S(2)}) collective-permute-start(bf16[192,256]{1,0:T(8,128)(2,1)S(1)} %copy-done.7), channel_id=1, source_target_pairs={{0,2},{1,3},{2,0},{3,1},{4,6},{5,7},{6,4},{7,5},{8,10},{9,11},{10,... | collective-permute-start | bytes 294920 | tf_op jit(solution)/shard_map/ppermute | solution.py:142
  62.9 10.8 %collective-permute-start.6 = (bf16[192,256]{1,0:T(8,128)(2,1)S(1)}, bf16[192,256]{1,0:T(8,128)(2,1)S(1)}, u32[]{:S(2)}, u32[]{:S(2)}) collective-permute-start(bf16[192,256]{1,0:T(8,128)(2,1)S(1)} %get-tuple-element.30), channel_id=1, source_target_pairs={{0,1},{1,2},{2,3},{3,0},{4,5},{5,6},{6,7},{7,4},{8,9},{9,10},{10,1... | collective-permute-start | bytes 294920 | tf_op jit(solution)/shard_map/ppermute | solution.py:166
  63.0 7.2 %collective-permute-start.8 = (bf16[192,256]{1,0:T(8,128)(2,1)S(1)}, bf16[192,256]{1,0:T(8,128)(2,1)S(1)}, u32[]{:S(2)}, u32[]{:S(2)}) collective-permute-start(bf16[192,256]{1,0:T(8,128)(2,1)S(1)} %get-tuple-element.31), channel_id=1, source_target_pairs={{0,3},{1,0},{2,1},{3,2},{4,7},{5,4},{6,5},{7,6},{8,11},{9,8},{10,9... | collective-permute-start | bytes 294920 | tf_op jit(solution)/shard_map/ppermute | solution.py:166
  64.7 3.2 %copy-start.11 = (f32[1024]{0:T(1024)S(1)}, f32[1024]{0:T(1024)}, u32[]{:S(2)}) copy-start(f32[1024]{0:T(1024)} %param.15) | copy-start | bytes 12292
  66.9 4.7 %collective-permute-start.7 = (bf16[192,256]{1,0:T(8,128)(2,1)S(1)}, bf16[192,256]{1,0:T(8,128)(2,1)S(1)}, u32[]{:S(2)}, u32[]{:S(2)}) collective-permute-start(bf16[192,256]{1,0:T(8,128)(2,1)S(1)} %get-tuple-element.32), channel_id=1, source_target_pairs={{0,2},{1,3},{2,0},{3,1},{4,6},{5,7},{6,4},{7,5},{8,10},{9,11},{10,... | collective-permute-start | bytes 294920 | tf_op jit(solution)/shard_map/ppermute | solution.py:166
  74.1 0.8 copy-start.12
  74.9 1.7 copy-start.5
  78.9 12.4 %collective-permute-start.11 = (bf16[256,1024]{1,0:T(8,128)(2,1)S(1)}, bf16[256,1024]{1,0:T(8,128)(2,1)S(1)}, u32[]{:S(2)}, u32[]{:S(2)}) collective-permute-start(bf16[256,1024]{1,0:T(8,128)(2,1)S(1)} %multiply_convert_fusion), channel_id=1, source_target_pairs={{0,2},{1,3},{2,0},{3,1},{4,6},{5,7},{6,4},{7,5},{8,10},{9,11},{10,... | collective-permute-start | bytes 1572872 | tf_op jit(solution)/shard_map/ppermute | solution.py:98
  80.4 2.0 %copy-start = (f32[1024,1024]{1,0:T(8,128)}, f32[1024,1024]{1,0:T(8,128)S(1)}, u32[]{:S(2)}) copy-start(f32[1024,1024]{1,0:T(8,128)S(1)} %fusion.57) | copy-start | bytes 12582916
  82.5 9.9 %collective-permute-start.9 = (bf16[2,256,1024]{2,1,0:T(8,128)(2,1)S(1)}, bf16[2,256,1024]{2,1,0:T(8,128)(2,1)}, u32[]{:S(2)}, u32[]{:S(2)}) collective-permute-start(bf16[2,256,1024]{2,1,0:T(8,128)(2,1)S(1)} %fusion.5), channel_id=1, source_target_pairs={{0,1},{1,0},{2,3},{3,2},{4,5},{5,4},{6,7},{7,6},{8,9},{9,8},{10,11... | collective-permute-start | bytes 3145736 | tf_op jit(solution)/shard_map/ppermute | solution.py:85
  92.4 3.1 %collective-permute-start.12 = (bf16[2,256,1024]{2,1,0:T(8,128)(2,1)}, bf16[2,256,1024]{2,1,0:T(8,128)(2,1)S(1)}, u32[]{:S(2)}, u32[]{:S(2)}) collective-permute-start(bf16[2,256,1024]{2,1,0:T(8,128)(2,1)} %pad_maximum_fusion.2), channel_id=1, source_target_pairs={{0,1},{1,0},{2,3},{3,2},{4,5},{5,4},{6,7},{7,6},{8,9},{9,8},{10,11... | collective-permute-start | bytes 3145736 | tf_op jit(solution)/shard_map/ppermute | solution.py:98
  94.6 1.4 copy-start.1
  94.7 14.5 %collective-permute-start.10 = (bf16[256,1024]{1,0:T(8,128)(2,1)S(1)}, bf16[256,1024]{1,0:T(8,128)(2,1)}, u32[]{:S(2)}, u32[]{:S(2)}) collective-permute-start(bf16[256,1024]{1,0:T(8,128)(2,1)S(1)} %fusion.9), channel_id=1, source_target_pairs={{0,2},{1,3},{2,0},{3,1},{4,6},{5,7},{6,4},{7,5},{8,10},{9,11},{10,... | collective-permute-start | bytes 1572872 | tf_op jit(solution)/shard_map/ppermute | solution.py:85
  96.4 2.8 %copy-start.6 = (bf16[192,1024]{1,0:T(8,128)(2,1)S(1)}, bf16[192,1024]{1,0:T(8,128)(2,1)}, u32[]{:S(2)}) copy-start(bf16[192,1024]{1,0:T(8,128)(2,1)} %get-tuple-element.24) | copy-start | bytes 1179652
  103.0 6.3 %copy-start.2 = (f32[2,256,1024]{2,1,0:T(8,128)S(1)}, f32[2,256,1024]{2,1,0:T(8,128)}, u32[]{:S(2)}) copy-start(f32[2,256,1024]{2,1,0:T(8,128)} %copy-done.1) | copy-start | bytes 6291460
  110.4 3.8 %copy-start.3 = (f32[2,2,98304]{2,1,0:T(2,128)S(1)}, f32[2,2,98304]{2,1,0:T(2,128)}, u32[]{:S(2)}) copy-start(f32[2,2,98304]{2,1,0:T(2,128)} %concatenate.17) | copy-start | bytes 4718596
  115.5 1.5 copy-start.4
  117.5 17.0 %collective-permute-start.13 = (bf16[2,163840]{1,0:T(2,128)(2,1)S(1)}, bf16[2,163840]{1,0:T(2,128)(2,1)S(1)}, u32[]{:S(2)}, u32[]{:S(2)}) collective-permute-start(bf16[2,163840]{1,0:T(2,128)(2,1)S(1)} %fusion.8), channel_id=1, source_target_pairs={{0,4},{4,0},{8,12},{12,8},{1,5},{5,1},{9,13},{13,9},{2,6},{6,2},{1... | collective-permute-start | bytes 1966088 | tf_op jit(solution)/shard_map/ppermute | solution.py:85
  143.1 17.6 %collective-permute-start.14 = (bf16[163840]{0:T(1024)(128)(2,1)S(1)}, bf16[163840]{0:T(1024)(128)(2,1)S(1)}, u32[]{:S(2)}, u32[]{:S(2)}) collective-permute-start(bf16[163840]{0:T(1024)(128)(2,1)S(1)} %convert_reduce_fusion.1), channel_id=1, source_target_pairs={{0,8},{4,12},{8,0},{12,4},{1,9},{5,13},{9,1},{13,5},{2,10},{6,14},... | collective-permute-start | bytes 983048 | tf_op jit(solution)/shard_map/ppermute | solution.py:85
  161.7 19.4 %all-to-all-start = ((bf16[4,64,1024]{2,1,0:T(8,128)(2,1)}), bf16[4,64,1024]{2,1,0:T(8,128)(2,1)S(1)}, u32[]{:S(2)}, u32[]{:S(2)}) async-start(bf16[4,64,1024]{2,1,0:T(8,128)(2,1)} %broadcast_in_dim.8), calls=%async_computation | async-start | bytes 1048576 | tf_op jit(solution)/shard_map/all_to_all | solution.py:201
Sparse Core Ops, SparseCore 0:
  9.8 46.7 all-gather.2

commit v4 on v3

--- a/solution.py
+++ b/solution.py
@@ -70,15 +70,17 @@
     return n & (n - 1) == 0
 
 
-def reduce_scatter_blocks(x, axis, n, send_dtype):
+def reduce_scatter_blocks(x, axis, n, send_dtype, high_first=False):
     if not _is_pow2(n):
         got = lax.all_to_all(x.astype(send_dtype), axis, 0, 0, tiled=True)
         return jnp.sum(got.astype(x.dtype), axis=0)
     me = lax.axis_index(axis)
     k = n.bit_length() - 1
     cur = x.reshape((2,) * k + x.shape[1:])
-    for b in range(k):
-        ax = k - 1 - b
+    axis_bits = list(reversed(range(k)))
+    for b in (axis_bits[:] if high_first else list(range(k))):
+        ax = axis_bits.index(b)
+        axis_bits.remove(b)
         mine = (me >> b) & 1
         keep = lax.dynamic_index_in_dim(cur, mine, axis=ax, keepdims=False)
         send = lax.dynamic_index_in_dim(cur, 1 - mine, axis=ax, keepdims=False)
@@ -188,26 +190,17 @@
     stacked = jnp.dot(both_t, slab_rows, preferred_element_type=jnp.float32)
     dom_cols = hidden // n_dom
     dom_rows = up_rows // n_dom
-    upper_len = dom_rows * hidden
-    payload = jnp.concatenate(
-        [
-            col_sum.reshape(n_dom, upper_len),
-            jnp.swapaxes(stacked.reshape(2 * width, n_dom, dom_cols), 0, 1).reshape(n_dom, -1),
-        ],
-        axis=1,
-    )
-    reduced = reduce_scatter_blocks(payload, "dom", n_dom, jnp.bfloat16)
-    grad_layer = reduced[upper_len:].reshape(2 * width, dom_cols)
-    grad_upper = lax.all_to_all(
-        jnp.broadcast_to(
-            reduced[:upper_len].astype(jnp.bfloat16).reshape(1, dom_rows, hidden),
-            (n_dom, dom_rows, hidden),
-        ),
+    upper_part = reduce_scatter_blocks(
+        col_sum.reshape(n_dom, dom_rows, hidden), "dom", n_dom, jnp.bfloat16, high_first=True
+    )
+    grad_upper = all_gather_blocks(upper_part.astype(jnp.bfloat16), "dom", n_dom)
+    grad_upper = grad_upper.reshape(up_rows, hidden).astype(jnp.float32)
+    grad_layer = reduce_scatter_blocks(
+        jnp.swapaxes(stacked.reshape(2 * width, n_dom, dom_cols), 0, 1),
         "dom",
-        split_axis=0,
-        concat_axis=0,
-        tiled=True,
-    ).reshape(up_rows, hidden).astype(jnp.float32)
+        n_dom,
+        jnp.bfloat16,
+    )
     grad_neigh = grad_layer[:w_rows]
     grad_self = grad_layer[w_rows:]
     return (hidden_two, grad_neigh, grad_self, grad_upper)

time: 190 us -> 170 us (0.89)
  local copies, waits for them, and re-layouts: 56.4 us -> 38 us
  waiting for transfers between devices: 54 us -> 63.3 us
  starting transfers between devices: 25 us -> 18.8 us
  matrix products: 13 us -> 10.2 us
    ppermute x2 -> x4, waiting for transfers between devices: 8.64 us -> 22.5 us  [all_gather_blocks(): got = lax.ppermute(cur, axis, _xor_pairs(n, 1 << b))]
    all_to_all x1 -> x0, waiting for transfers between devices: 13.1 us -> none  [local(): lax.all_to_all(jnp.broadcast_to(reduced[:upper_len].astype(jnp.bfloat16)....]
    ppermute x3, waiting for transfers between devices: 0.01 us -> 8.62 us  [local(): rows_t = lax.ppermute(rows_t, 'dom', _shift_pairs(n_dom, shift))]
    convert_element_type x4 -> x6, local copies, waits for them, and re-layouts: 7.5 us -> 0.36 us  [reduce_scatter_blocks(): got = lax.ppermute(send.astype(send_dtype), axis, _xor_pairs(n, 1 << b))]
    concatenate x3 -> x0, local copies, waits for them, and re-layouts: 6.28 us -> none  [local(): jnp.concatenate([col_sum.reshape(n_dom, upper_len), jnp.swapaxes(stacked....]
    all_to_all x1 -> x0, starting transfers between devices: 4.77 us -> none  [local(): lax.all_to_all(jnp.broadcast_to(reduced[:upper_len].astype(jnp.bfloat16)....]
    dot_general x1, matrix products: 3.77 us -> 1.01 us  [local(): stacked = jnp.dot(both_t, slab_rows, preferred_element_type=jnp.float32)]
    unnamed x28 -> x23, local copies, waits for them, and re-layouts: 8.98 us -> 6.46 us
  transfers between devices with their start and end apart: 17 -> 20, of which waited for: 6 -> 9; matrix products, arithmetic and copies ran while one was open for 28% -> 27% of each run, Pallas kernels for 7% -> 8%
where the time goes in v4:
time: 170 us
  waiting for transfers between devices  63.3 us (37%)
  local copies, waits for them, and re-layouts  38 us (22%)
  starting transfers between devices  18.8 us (11%)
  between operations  14.6 us (9%)
  Pallas kernels  13 us (8%)
  other arithmetic  11.8 us (7%)
  matrix products  10.2 us (6%)
    ppermute x6, waiting for transfers between devices, reduce_scatter_blocks(): got = lax.ppermute(send.astype(send_dtype), axis, _xor_pairs(n, 1 << b))  31.1 us
    ppermute x4, waiting for transfers between devices, all_gather_blocks(): got = lax.ppermute(cur, axis, _xor_pairs(n, 1 << b))  22.5 us
    gather x8, local copies, waits for them, and re-layouts, local(): rows_t = features.at[slots].get(mode='promise_in_bounds').T  18.8 us
    pallas_call x4, Pallas kernels, accumulate(): pl.pallas_call(_accumulate_kernel, out_shape=[jax.ShapeDtypeStruct(acc_su...  13 us
    ppermute x3, waiting for transfers between devices, local(): rows_t = lax.ppermute(rows_t, 'dom', _shift_pairs(n_dom, shift))  8.62 us
    unnamed x23, local copies, waits for them, and re-layouts  6.46 us
    ppermute x6, starting transfers between devices, local(): chunk = lax.ppermute(chunk, 'cols', _shift_pairs(n_cols, shift))  6.33 us
    ppermute x6, starting transfers between devices, reduce_scatter_blocks(): got = lax.ppermute(send.astype(send_dtype), axis, _xor_pairs(n, 1 << b))  5.95 us
  transfers between devices with their start and end apart: 20, of which 9 were waited for; matrix products, arithmetic and copies ran while one was open for 27% of the time, Pallas kernels for 8%

profile of v4, /device:TPU:0, one launch (start us, length us, event | category | flops | bytes accessed | tf_op | source)
XLA Modules:
  0.0 169.7 jit_solution(2154789754678605567)
XLA Ops:
  7.2 2.5 %pad_maximum_fusion.1 = bf16[640,1024]{1,0:T(8,128)(2,1)} fusion(bf16[256,1024]{1,0:T(8,128)(2,1)} %param.16, bf16[192,1024]{1,0:T(8,128)(2,1)} %param.14, bf16[192,1024]{1,0:T(8,128)(2,1)} %param.13), kind=kLoop, calls=%fused_computation.18 | loop fusion | flops 3932160 | bytes 2621440 | tf_op jit(solution)/shard_map/concatenate | solution.py:129
  9.8 1.8 %slice_bitcast_fusion = (bf16[192,1024]{1,0:T(8,128)(2,1)}, bf16[1024,192]{0,1:T(8,128)(2,1)S(1)}) fusion(bf16[4096,192]{0,1:T(8,128)(2,1)} %param.10), kind=kLoop, calls=%fused_computation.131 | loop fusion | bytes 1179648 | tf_op jit(solution)/shard_map/transpose | solution.py:137
  12.8 1.9 %collective-permute-start.2 = (bf16[192,256]{1,0:T(8,128)(2,1)}, bf16[192,256]{1,0:T(8,128)(2,1)S(1)}, u32[]{:S(2)}, u32[]{:S(2)}) collective-permute-start(bf16[192,256]{1,0:T(8,128)(2,1)} %get-tuple-element.36), channel_id=1, source_target_pairs={{0,3},{1,0},{2,1},{3,2},{4,7},{5,4},{6,5},{7,6},{8,11},{9,8},{10,9... | collective-permute-start | bytes 294920 | tf_op jit(solution)/shard_map/ppermute | solution.py:144
  14.7 3.1 %copy.46 = bf16[4096,192]{1,0:T(8,128)(2,1)S(1)} copy(bf16[4096,192]{0,1:T(8,128)(2,1)} %param.10) | data formatting | bytes 3145728 | tf_op args[0]
  17.9 3.9 %gather_fusion.2 = bf16[1024,192]{1,0:T(8,128)(2,1)S(1)} fusion(bf16[4096,192]{1,0:T(8,128)(2,1)S(1)} %copy.46, s32[1024]{0:T(1024)S(1)} %broadcast_clamp_fusion.1), kind=kCustom, calls=%fused_computation.2 | custom fusion | bytes 790528 | tf_op jit(solution)/shard_map/gather | solution.py:154
  22.9 2.4 %collective-permute-start.5 = (bf16[192,1024]{1,0:T(8,128)(2,1)}, bf16[192,1024]{1,0:T(8,128)(2,1)}, u32[]{:S(2)}, u32[]{:S(2)}) collective-permute-start(bf16[192,1024]{1,0:T(8,128)(2,1)} %bitcast.19), channel_id=1, source_target_pairs={{0,4},{4,8},{8,12},{12,0},{1,5},{5,9},{9,13},{13,1},{2,6},{6,10},{... | collective-permute-start | bytes 1179656 | tf_op jit(solution)/shard_map/ppermute | solution.py:156
  25.3 3.9 %gather_fusion = bf16[1024,192]{1,0:T(8,128)(2,1)S(1)} fusion(bf16[4096,192]{1,0:T(8,128)(2,1)S(1)} %copy.46, s32[1024]{0:T(1024)S(1)} %broadcast_clamp_fusion.3), kind=kCustom, calls=%fused_computation | custom fusion | bytes 790528 | tf_op jit(solution)/shard_map/gather | solution.py:154
  29.4 2.1 %collective-permute-start.3 = (bf16[192,1024]{1,0:T(8,128)(2,1)S(1)}, bf16[192,1024]{1,0:T(8,128)(2,1)}, u32[]{:S(2)}, u32[]{:S(2)}) collective-permute-start(bf16[192,1024]{1,0:T(8,128)(2,1)S(1)} %bitcast.154), channel_id=1, source_target_pairs={{0,12},{4,0},{8,4},{12,8},{1,13},{5,1},{9,5},{13,9},{2,14},{6,2},{... | collective-permute-start | bytes 1179656 | tf_op jit(solution)/shard_map/ppermute | solution.py:156
  31.5 3.9 %gather_fusion.1 = bf16[1024,192]{1,0:T(8,128)(2,1)S(1)} fusion(bf16[4096,192]{1,0:T(8,128)(2,1)S(1)} %copy.46, s32[1024]{0:T(1024)S(1)} %broadcast_clamp_fusion.2), kind=kCustom, calls=%fused_computation.1 | custom fusion | bytes 790528 | tf_op jit(solution)/shard_map/gather | solution.py:154
  37.4 3.9 %gather_fusion.3 = bf16[1024,192]{1,0:T(8,128)(2,1)S(1)} fusion(bf16[4096,192]{1,0:T(8,128)(2,1)S(1)} %copy.46, s32[1024]{0:T(1024)S(1)} %broadcast_clamp_fusion), kind=kCustom, calls=%fused_computation.3 | custom fusion | bytes 790528 | tf_op jit(solution)/shard_map/gather | solution.py:154
  44.5 3.3 %shard_map.129 = (f32[192,1024]{1,0:T(8,128)}, f32[8,1024]{1,0:T(8,128)}) custom-call(s32[1,1024]{1,0:T(1,128)} %get-tuple-element.44.tgt_ref, bf16[192,1024]{1,0:T(8,128)(2,1)} %bitcast.156, f32[192,1024]{1,0:T(8,128)} %broadcast_in_dim.4.sum_in, f32[8,1024]{1,0:T(8,128)} %broadcast_in_dim.5.cnt_in), custom_call_target="tpu_custom_call", output_to_operand_aliasing={{0}: (2, {}), {1}: (3, {})} | custom-call | flops 419430400 | bytes 2035712 | tf_op jit(solution)/shard_map/pallas_call | solution.py:46
  48.6 1.6 collective-permute-start.1
  50.2 3.3 %shard_map.130 = (f32[192,1024]{1,0:T(8,128)}, f32[8,1024]{1,0:T(8,128)}) custom-call(s32[1,1024]{1,0:T(1,128)} %get-tuple-element.47.tgt_ref, bf16[192,1024]{1,0:T(8,128)(2,1)} %collective-permute-done.5.rec_ref, f32[192,1024]{1,0:T(8,128)} %get-tuple-element.12.sum_in, ...), custom_call_target="tpu_custom_call", output_to_operand_aliasing={{0}: (2, {}), {1}: (3, {})} | custom-call | flops 419430400 | bytes 2035712 | tf_op jit(solution)/shard_map/pallas_call | solution.py:46
  53.4 8.6 %collective-permute-done.4.rec_ref = bf16[192,1024]{1,0:T(8,128)(2,1)} collective-permute-done((bf16[192,1024]{1,0:T(8,128)(2,1)}, bf16[192,1024]{1,0:T(8,128)(2,1)}, u32[]{:S(2)}, u32[]{:S(2)}) %collective-permute-start.4) | collective-permute-done | bytes 393248 | tf_op jit(solution)/shard_map/ppermute | solution.py:156
  62.0 3.3 %shard_map.131 = (f32[192,1024]{1,0:T(8,128)}, f32[8,1024]{1,0:T(8,128)}) custom-call(s32[1,1024]{1,0:T(1,128)} %get-tuple-element.45.tgt_ref, bf16[192,1024]{1,0:T(8,128)(2,1)} %collective-permute-done.4.rec_ref, f32[192,1024]{1,0:T(8,128)} %get-tuple-element.14.sum_in, ...), custom_call_target="tpu_custom_call", output_to_operand_aliasing={{0}: (2, {}), {1}: (3, {})} | custom-call | flops 419430400 | bytes 2035712 | tf_op jit(solution)/shard_map/pallas_call | solution.py:46
  65.3 3.3 %shard_map.132 = (f32[192,1024]{1,0:T(8,128)}, f32[8,1024]{1,0:T(8,128)}) custom-call(s32[1,1024]{1,0:T(1,128)} %get-tuple-element.46.tgt_ref, bf16[192,1024]{1,0:T(8,128)(2,1)} %collective-permute-done.3.rec_ref, f32[192,1024]{1,0:T(8,128)} %get-tuple-element.16.sum_in, ...), custom_call_target="tpu_custom_call", output_to_operand_aliasing={{0}: (2, {}), {1}: (3, {})} | custom-call | flops 419430400 | bytes 2035712 | tf_op jit(solution)/shard_map/pallas_call | solution.py:46
  70.7 1.7 %collective-permute-start.8 = (bf16[192,256]{1,0:T(8,128)(2,1)S(1)}, bf16[192,256]{1,0:T(8,128)(2,1)S(1)}, u32[]{:S(2)}, u32[]{:S(2)}) collective-permute-start(bf16[192,256]{1,0:T(8,128)(2,1)S(1)} %get-tuple-element.33), channel_id=1, source_target_pairs={{0,3},{1,0},{2,1},{3,2},{4,7},{5,4},{6,5},{7,6},{8,11},{9,8},{10,9... | collective-permute-start | bytes 294920 | tf_op jit(solution)/shard_map/ppermute | solution.py:168
  72.4 2.2 %fusion.63 = (bf16[4,192,1024]{2,1,0:T(8,128)(2,1)S(1)}, bf16[4,192,1024]{2,1,0:T(8,128)(2,1)S(1)}) fusion(bf16[4,640,1024]{2,1,0:T(8,128)(2,1)} %bitcast.145), kind=kLoop, calls=%fused_computation.134 | loop fusion | bytes 6291456 | tf_op jit(solution)/shard_map/slice | solution.py:132
  79.6 1.8 %slice.38 = bf16[4,256,1024]{2,1,0:T(8,128)(2,1)S(1)} slice(bf16[4,640,1024]{2,1,0:T(8,128)(2,1)} %bitcast.146), slice={[0:4], [384:640], [0:1024]} | slice | bytes 4194304 | tf_op jit(solution)/shard_map/slice | solution.py:133
  82.6 1.7 multiply_convert_fusion.2
  88.1 1.9 %copy-done = f32[1024,1024]{1,0:T(8,128)} copy-done((f32[1024,1024]{1,0:T(8,128)}, f32[1024,1024]{1,0:T(8,128)S(1)}, u32[]{:S(2)}) %copy-start) | copy-done | bytes 4194328
  90.2 8.7 %collective-permute-done.9 = bf16[256,1024]{1,0:T(8,128)(2,1)S(1)} collective-permute-done((bf16[256,1024]{1,0:T(8,128)(2,1)S(1)}, bf16[256,1024]{1,0:T(8,128)(2,1)S(1)}, u32[]{:S(2)}, u32[]{:S(2)}) %collective-permute-start.9) | collective-permute-done | bytes 524320 | tf_op jit(solution)/shard_map/ppermute | solution.py:100
  100.1 2.2 %bitcast_add_fusion = f32[2,256,1024]{2,1,0:T(8,128)S(1)} fusion(bf16[2,256,1024]{2,1,0:T(8,128)(2,1)} %collective-permute-done.13, f32[2,2,256,1024]{3,2,1,0:T(8,128)} %bitcast.143, s32[]{:T(128)S(6)} %select_n.303), kind=kLoop, calls=%fused_computation.7 | loop fusion | flops 1048576 | bytes 5242884 | tf_op jit(solution)/shard_map/add | solution.py:88
  105.1 2.6 %copy.55 = bf16[1024,1024]{1,0:T(8,128)(2,1)} copy(bf16[1024,1024]{0,1:T(8,128)(2,1)S(1)} %bitcast.144) | data formatting | bytes 4194304 | tf_op jit(solution)/shard_map/dot_general | solution.py:190
  107.6 10.5 %collective-permute-done.14 = bf16[256,1024]{1,0:T(8,128)(2,1)S(1)} collective-permute-done((bf16[256,1024]{1,0:T(8,128)(2,1)S(1)}, bf16[256,1024]{1,0:T(8,128)(2,1)S(1)}, u32[]{:S(2)}, u32[]{:S(2)}) %collective-permute-start.14) | collective-permute-done | bytes 524320 | tf_op jit(solution)/shard_map/ppermute | solution.py:87
  120.7 2.2 %collective-permute-start.11 = (bf16[2,384,256]{2,1,0:T(8,128)(2,1)S(1)}, bf16[2,384,256]{2,1,0:T(8,128)(2,1)S(1)}, u32[]{:S(2)}, u32[]{:S(2)}) collective-permute-start(bf16[2,384,256]{2,1,0:T(8,128)(2,1)S(1)} %fusion.10), channel_id=1, source_target_pairs={{0,4},{4,0},{8,12},{12,8},{1,5},{5,1},{9,13},{13,9},{2,6},{6,2},{1... | collective-permute-start | bytes 1179656 | tf_op jit(solution)/shard_map/ppermute | solution.py:87
  122.9 10.2 %collective-permute-done.15 = bf16[2,64,1024]{2,1,0:T(8,128)(2,1)S(1)} collective-permute-done((bf16[2,64,1024]{2,1,0:T(8,128)(2,1)S(1)}, bf16[2,64,1024]{2,1,0:T(8,128)(2,1)S(1)}, u32[]{:S(2)}, u32[]{:S(2)}) %collective-permute-start.15) | collective-permute-done | bytes 262176 | tf_op jit(solution)/shard_map/ppermute | solution.py:87
  133.3 6.7 %collective-permute-done.16 = bf16[64,1024]{1,0:T(8,128)(2,1)S(1)} collective-permute-done((bf16[64,1024]{1,0:T(8,128)(2,1)S(1)}, bf16[64,1024]{1,0:T(8,128)(2,1)S(1)}, u32[]{:S(2)}, u32[]{:S(2)}) %collective-permute-start.16) | collective-permute-done | bytes 131104 | tf_op jit(solution)/shard_map/ppermute | solution.py:87
  140.5 2.7 %collective-permute-start.12 = (bf16[384,256]{1,0:T(8,128)(2,1)S(1)}, bf16[384,256]{1,0:T(8,128)(2,1)S(1)}, u32[]{:S(2)}, u32[]{:S(2)}) collective-permute-start(bf16[384,256]{1,0:T(8,128)(2,1)S(1)} %fusion.35), channel_id=1, source_target_pairs={{0,8},{4,12},{8,0},{12,4},{1,9},{5,13},{9,1},{13,5},{2,10},{6,14},... | collective-permute-start | bytes 589832 | tf_op jit(solution)/shard_map/ppermute | solution.py:87
  143.2 9.1 %collective-permute-done.17 = bf16[64,1024]{1,0:T(8,128)(2,1)S(1)} collective-permute-done((bf16[64,1024]{1,0:T(8,128)(2,1)S(1)}, bf16[64,1024]{1,0:T(8,128)(2,1)S(1)}, u32[]{:S(2)}, u32[]{:S(2)}) %collective-permute-start.17) | collective-permute-done | bytes 131104 | tf_op jit(solution)/shard_map/ppermute | solution.py:100
  152.4 3.7 %collective-permute-done.12 = bf16[384,256]{1,0:T(8,128)(2,1)S(1)} collective-permute-done((bf16[384,256]{1,0:T(8,128)(2,1)S(1)}, bf16[384,256]{1,0:T(8,128)(2,1)S(1)}, u32[]{:S(2)}, u32[]{:S(2)}) %collective-permute-start.12) | collective-permute-done | bytes 196640 | tf_op jit(solution)/shard_map/ppermute | solution.py:87
  156.9 4.7 %collective-permute-done.18 = bf16[2,64,1024]{2,1,0:T(8,128)(2,1)S(1)} collective-permute-done((bf16[2,64,1024]{2,1,0:T(8,128)(2,1)S(1)}, bf16[2,64,1024]{2,1,0:T(8,128)(2,1)S(1)}, u32[]{:S(2)}, u32[]{:S(2)}) %collective-permute-start.18) | collective-permute-done | bytes 262176 | tf_op jit(solution)/shard_map/ppermute | solution.py:100
  (99 shorter events, 29.7 us)
Async XLA Ops:
  7.2 65.2 %all-gather.3.cloned.1.call-start = ((), (), s32[]{:S(2)}) async-start(), calls=%async_computation | async-start | bytes 6553600 | tf_op jit(solution)/shard_map/all_gather | solution.py:130
  11.6 6.3 %copy-start.7 = (s32[1,4,1024]{2,1,0:T(4,128)S(1)}, s32[1,4,1024]{2,1,0:T(4,128)}, u32[]{:S(2)}) copy-start(s32[1,4,1024]{2,1,0:T(4,128)} %param.11) | copy-start | bytes 49156
  12.3 64.2 %collective-permute-start = (bf16[192,256]{1,0:T(8,128)(2,1)}, bf16[192,256]{1,0:T(8,128)(2,1)}, u32[]{:S(2)}, u32[]{:S(2)}) collective-permute-start(bf16[192,256]{1,0:T(8,128)(2,1)} %get-tuple-element.35), channel_id=1, source_target_pairs={{0,1},{1,2},{2,3},{3,0},{4,5},{5,6},{6,7},{7,4},{8,9},{9,10},{10,1... | collective-permute-start | bytes 294920 | tf_op jit(solution)/shard_map/ppermute | solution.py:144
  12.8 61.8 %collective-permute-start.2 = (bf16[192,256]{1,0:T(8,128)(2,1)}, bf16[192,256]{1,0:T(8,128)(2,1)S(1)}, u32[]{:S(2)}, u32[]{:S(2)}) collective-permute-start(bf16[192,256]{1,0:T(8,128)(2,1)} %get-tuple-element.36), channel_id=1, source_target_pairs={{0,3},{1,0},{2,1},{3,2},{4,7},{5,4},{6,5},{7,6},{8,11},{9,8},{10,9... | collective-permute-start | bytes 294920 | tf_op jit(solution)/shard_map/ppermute | solution.py:144
  22.9 25.7 %collective-permute-start.5 = (bf16[192,1024]{1,0:T(8,128)(2,1)}, bf16[192,1024]{1,0:T(8,128)(2,1)}, u32[]{:S(2)}, u32[]{:S(2)}) collective-permute-start(bf16[192,1024]{1,0:T(8,128)(2,1)} %bitcast.19), channel_id=1, source_target_pairs={{0,4},{4,8},{8,12},{12,0},{1,5},{5,9},{9,13},{13,1},{2,6},{6,10},{... | collective-permute-start | bytes 1179656 | tf_op jit(solution)/shard_map/ppermute | solution.py:156
  29.4 35.9 %collective-permute-start.3 = (bf16[192,1024]{1,0:T(8,128)(2,1)S(1)}, bf16[192,1024]{1,0:T(8,128)(2,1)}, u32[]{:S(2)}, u32[]{:S(2)}) collective-permute-start(bf16[192,1024]{1,0:T(8,128)(2,1)S(1)} %bitcast.154), channel_id=1, source_target_pairs={{0,12},{4,0},{8,4},{12,8},{1,13},{5,1},{9,5},{13,9},{2,14},{6,2},{... | collective-permute-start | bytes 1179656 | tf_op jit(solution)/shard_map/ppermute | solution.py:156
  36.4 25.7 %collective-permute-start.4 = (bf16[192,1024]{1,0:T(8,128)(2,1)}, bf16[192,1024]{1,0:T(8,128)(2,1)}, u32[]{:S(2)}, u32[]{:S(2)}) collective-permute-start(bf16[192,1024]{1,0:T(8,128)(2,1)} %bitcast.155), channel_id=1, source_target_pairs={{0,8},{4,12},{8,0},{12,4},{1,9},{5,13},{9,1},{13,5},{2,10},{6,14},... | collective-permute-start | bytes 1179656 | tf_op jit(solution)/shard_map/ppermute | solution.py:156
  37.4 4.9 %copy-start.8 = (s32[1,4,1024]{2,1,0:T(4,128)S(1)}, s32[1,4,1024]{2,1,0:T(4,128)}, u32[]{:S(2)}) copy-start(s32[1,4,1024]{2,1,0:T(4,128)} %param.12) | copy-start | bytes 49156
  41.3 6.5 %copy-start.6 = (s32[256,15]{0,1:T(8,128)S(1)}, s32[256,15]{0,1:T(8,128)}, u32[]{:S(2)}) copy-start(s32[256,15]{0,1:T(8,128)} %param.18) | copy-start | bytes 46084
  41.4 7.2 %copy-start.5 = (bf16[192,256]{1,0:T(8,128)(2,1)S(1)}, bf16[192,256]{1,0:T(8,128)(2,1)}, u32[]{:S(2)}) copy-start(bf16[192,256]{1,0:T(8,128)(2,1)} %get-tuple-element.37) | copy-start | bytes 294916
  48.6 27.3 %collective-permute-start.1 = (bf16[192,256]{1,0:T(8,128)(2,1)S(1)}, bf16[192,256]{1,0:T(8,128)(2,1)S(1)}, u32[]{:S(2)}, u32[]{:S(2)}) collective-permute-start(bf16[192,256]{1,0:T(8,128)(2,1)S(1)} %copy-done.5), channel_id=1, source_target_pairs={{0,2},{1,3},{2,0},{3,1},{4,6},{5,7},{6,4},{7,5},{8,10},{9,11},{10,... | collective-permute-start | bytes 294920 | tf_op jit(solution)/shard_map/ppermute | solution.py:144
  70.6 10.8 %collective-permute-start.6 = (bf16[192,256]{1,0:T(8,128)(2,1)S(1)}, bf16[192,256]{1,0:T(8,128)(2,1)S(1)}, u32[]{:S(2)}, u32[]{:S(2)}) collective-permute-start(bf16[192,256]{1,0:T(8,128)(2,1)S(1)} %get-tuple-element.32), channel_id=1, source_target_pairs={{0,1},{1,2},{2,3},{3,0},{4,5},{5,6},{6,7},{7,4},{8,9},{9,10},{10,1... | collective-permute-start | bytes 294920 | tf_op jit(solution)/shard_map/ppermute | solution.py:168
  70.7 7.2 %collective-permute-start.8 = (bf16[192,256]{1,0:T(8,128)(2,1)S(1)}, bf16[192,256]{1,0:T(8,128)(2,1)S(1)}, u32[]{:S(2)}, u32[]{:S(2)}) collective-permute-start(bf16[192,256]{1,0:T(8,128)(2,1)S(1)} %get-tuple-element.33), channel_id=1, source_target_pairs={{0,3},{1,0},{2,1},{3,2},{4,7},{5,4},{6,5},{7,6},{8,11},{9,8},{10,9... | collective-permute-start | bytes 294920 | tf_op jit(solution)/shard_map/ppermute | solution.py:168
  72.4 3.1 %copy-start.9 = (f32[1024]{0:T(1024)S(1)}, f32[1024]{0:T(1024)}, u32[]{:S(2)}) copy-start(f32[1024]{0:T(1024)} %param.15) | copy-start | bytes 12292
  74.6 4.7 %collective-permute-start.7 = (bf16[192,256]{1,0:T(8,128)(2,1)S(1)}, bf16[192,256]{1,0:T(8,128)(2,1)S(1)}, u32[]{:S(2)}, u32[]{:S(2)}) collective-permute-start(bf16[192,256]{1,0:T(8,128)(2,1)S(1)} %get-tuple-element.34), channel_id=1, source_target_pairs={{0,2},{1,3},{2,0},{3,1},{4,6},{5,7},{6,4},{7,5},{8,10},{9,11},{10,... | collective-permute-start | bytes 294920 | tf_op jit(solution)/shard_map/ppermute | solution.py:168
  81.7 0.8 copy-start.10
  82.6 1.7 copy-start.3
  86.5 12.4 %collective-permute-start.9 = (bf16[256,1024]{1,0:T(8,128)(2,1)S(1)}, bf16[256,1024]{1,0:T(8,128)(2,1)S(1)}, u32[]{:S(2)}, u32[]{:S(2)}) collective-permute-start(bf16[256,1024]{1,0:T(8,128)(2,1)S(1)} %multiply_convert_fusion), channel_id=1, source_target_pairs={{0,2},{1,3},{2,0},{3,1},{4,6},{5,7},{6,4},{7,5},{8,10},{9,11},{10,... | collective-permute-start | bytes 1572872 | tf_op jit(solution)/shard_map/ppermute | solution.py:100
  88.0 2.0 %copy-start = (f32[1024,1024]{1,0:T(8,128)}, f32[1024,1024]{1,0:T(8,128)S(1)}, u32[]{:S(2)}) copy-start(f32[1024,1024]{1,0:T(8,128)S(1)} %fusion.61) | copy-start | bytes 12582916
  90.2 9.9 %collective-permute-start.13 = (bf16[2,256,1024]{2,1,0:T(8,128)(2,1)S(1)}, bf16[2,256,1024]{2,1,0:T(8,128)(2,1)}, u32[]{:S(2)}, u32[]{:S(2)}) collective-permute-start(bf16[2,256,1024]{2,1,0:T(8,128)(2,1)S(1)} %fusion.5), channel_id=1, source_target_pairs={{0,1},{1,0},{2,3},{3,2},{4,5},{5,4},{6,7},{7,6},{8,9},{9,8},{10,11... | collective-permute-start | bytes 3145736 | tf_op jit(solution)/shard_map/ppermute | solution.py:87
  100.1 4.5 %collective-permute-start.10 = (bf16[2,256,1024]{2,1,0:T(8,128)(2,1)}, bf16[2,256,1024]{2,1,0:T(8,128)(2,1)S(1)}, u32[]{:S(2)}, u32[]{:S(2)}) collective-permute-start(bf16[2,256,1024]{2,1,0:T(8,128)(2,1)} %pad_maximum_fusion.2), channel_id=1, source_target_pairs={{0,1},{1,0},{2,3},{3,2},{4,5},{5,4},{6,7},{7,6},{8,9},{9,8},{10,11... | collective-permute-start | bytes 3145736 | tf_op jit(solution)/shard_map/ppermute | solution.py:100
  102.3 1.3 copy-start.1
  103.7 14.4 %collective-permute-start.14 = (bf16[256,1024]{1,0:T(8,128)(2,1)S(1)}, bf16[256,1024]{1,0:T(8,128)(2,1)S(1)}, u32[]{:S(2)}, u32[]{:S(2)}) collective-permute-start(bf16[256,1024]{1,0:T(8,128)(2,1)S(1)} %fusion.9), channel_id=1, source_target_pairs={{0,2},{1,3},{2,0},{3,1},{4,6},{5,7},{6,4},{7,5},{8,10},{9,11},{10,... | collective-permute-start | bytes 1572872 | tf_op jit(solution)/shard_map/ppermute | solution.py:87
  107.6 12.0 %copy-start.2 = (bf16[1024,1024]{1,0:T(8,128)(2,1)S(1)}, bf16[1024,1024]{1,0:T(8,128)(2,1)}, u32[]{:S(2)}) copy-start(bf16[1024,1024]{1,0:T(8,128)(2,1)} %copy.55) | copy-start | bytes 6291460
  107.6 12.0 %copy-start.4 = (bf16[192,1024]{1,0:T(8,128)(2,1)S(1)}, bf16[192,1024]{1,0:T(8,128)(2,1)}, u32[]{:S(2)}) copy-start(bf16[192,1024]{1,0:T(8,128)(2,1)} %get-tuple-element.24) | copy-start | bytes 1179652
  119.5 13.6 %collective-permute-start.15 = (bf16[2,64,1024]{2,1,0:T(8,128)(2,1)S(1)}, bf16[2,64,1024]{2,1,0:T(8,128)(2,1)S(1)}, u32[]{:S(2)}, u32[]{:S(2)}) collective-permute-start(bf16[2,64,1024]{2,1,0:T(8,128)(2,1)S(1)} %fusion.32), channel_id=1, source_target_pairs={{0,8},{4,12},{8,0},{12,4},{1,9},{5,13},{9,1},{13,5},{2,10},{6,14},... | collective-permute-start | bytes 786440 | tf_op jit(solution)/shard_map/ppermute | solution.py:87
  120.7 19.7 %collective-permute-start.11 = (bf16[2,384,256]{2,1,0:T(8,128)(2,1)S(1)}, bf16[2,384,256]{2,1,0:T(8,128)(2,1)S(1)}, u32[]{:S(2)}, u32[]{:S(2)}) collective-permute-start(bf16[2,384,256]{2,1,0:T(8,128)(2,1)S(1)} %fusion.10), channel_id=1, source_target_pairs={{0,4},{4,0},{8,12},{12,8},{1,5},{5,1},{9,13},{13,9},{2,6},{6,2},{1... | collective-permute-start | bytes 1179656 | tf_op jit(solution)/shard_map/ppermute | solution.py:87
  133.2 6.8 %collective-permute-start.16 = (bf16[64,1024]{1,0:T(8,128)(2,1)S(1)}, bf16[64,1024]{1,0:T(8,128)(2,1)S(1)}, u32[]{:S(2)}, u32[]{:S(2)}) collective-permute-start(bf16[64,1024]{1,0:T(8,128)(2,1)S(1)} %fusion.36), channel_id=1, source_target_pairs={{0,4},{4,0},{8,12},{12,8},{1,5},{5,1},{9,13},{13,9},{2,6},{6,2},{1... | collective-permute-start | bytes 393224 | tf_op jit(solution)/shard_map/ppermute | solution.py:87
  140.0 12.3 %collective-permute-start.17 = (bf16[64,1024]{1,0:T(8,128)(2,1)S(1)}, bf16[64,1024]{1,0:T(8,128)(2,1)S(1)}, u32[]{:S(2)}, u32[]{:S(2)}) collective-permute-start(bf16[64,1024]{1,0:T(8,128)(2,1)S(1)} %fusion.33), channel_id=1, source_target_pairs={{0,8},{4,12},{8,0},{12,4},{1,9},{5,13},{9,1},{13,5},{2,10},{6,14},... | collective-permute-start | bytes 393224 | tf_op jit(solution)/shard_map/ppermute | solution.py:100
  140.5 15.6 %collective-permute-start.12 = (bf16[384,256]{1,0:T(8,128)(2,1)S(1)}, bf16[384,256]{1,0:T(8,128)(2,1)S(1)}, u32[]{:S(2)}, u32[]{:S(2)}) collective-permute-start(bf16[384,256]{1,0:T(8,128)(2,1)S(1)} %fusion.35), channel_id=1, source_target_pairs={{0,8},{4,12},{8,0},{12,4},{1,9},{5,13},{9,1},{13,5},{2,10},{6,14},... | collective-permute-start | bytes 589832 | tf_op jit(solution)/shard_map/ppermute | solution.py:87
  152.4 9.3 %collective-permute-start.18 = (bf16[2,64,1024]{2,1,0:T(8,128)(2,1)S(1)}, bf16[2,64,1024]{2,1,0:T(8,128)(2,1)S(1)}, u32[]{:S(2)}, u32[]{:S(2)}) collective-permute-start(bf16[2,64,1024]{2,1,0:T(8,128)(2,1)S(1)} %pad_maximum_fusion.4), channel_id=1, source_target_pairs={{0,4},{4,0},{8,12},{12,8},{1,5},{5,1},{9,13},{13,9},{2,6},{6,2},{1... | collective-permute-start | bytes 786440 | tf_op jit(solution)/shard_map/ppermute | solution.py:100
Sparse Core Ops, SparseCore 0:
  9.8 43.7 all-gather.2

commit v5 on v4

--- a/solution.py
+++ b/solution.py
@@ -74,11 +74,18 @@
     if not _is_pow2(n):
         got = lax.all_to_all(x.astype(send_dtype), axis, 0, 0, tiled=True)
         return jnp.sum(got.astype(x.dtype), axis=0)
+    k = n.bit_length() - 1
+    axis_bits = list(reversed(range(k)))
+    order = axis_bits[:] if high_first else list(range(k))
+    return _butterfly_reduce(
+        x.reshape((2,) * k + x.shape[1:]), axis, n, axis_bits, order, send_dtype
+    )
+
+
+def _butterfly_reduce(cur, axis, n, axis_bits, order, send_dtype):
     me = lax.axis_index(axis)
-    k = n.bit_length() - 1
-    cur = x.reshape((2,) * k + x.shape[1:])
-    axis_bits = list(reversed(range(k)))
-    for b in (axis_bits[:] if high_first else list(range(k))):
+    axis_bits = list(axis_bits)
+    for b in order:
         ax = axis_bits.index(b)
         axis_bits.remove(b)
         mine = (me >> b) & 1
@@ -87,6 +94,20 @@
         got = lax.ppermute(send.astype(send_dtype), axis, _xor_pairs(n, 1 << b))
         cur = keep + got.astype(keep.dtype)
     return cur
+
+
+def reduce_scatter_grid(x, n_dom, n_cols, send_dtype):
+    if not (_is_pow2(n_dom) and _is_pow2(n_cols)):
+        part = reduce_scatter_blocks(x, "cols", n_cols, send_dtype)
+        return reduce_scatter_blocks(part, "dom", n_dom, send_dtype)
+    kc = n_cols.bit_length() - 1
+    kd = n_dom.bit_length() - 1
+    axis_bits = [kc - 1 - i for i in range(kc)] + [kc + kd - 1 - i for i in range(kd)]
+    order = list(range(min(kc, 1))) + list(range(kc, kc + kd)) + list(range(1, kc))
+    cur = x.reshape((2,) * (kc + kd) + x.shape[2:])
+    return _butterfly_reduce(
+        cur, ("dom", "cols"), n_dom * n_cols, axis_bits, order, send_dtype
+    )
 
 
 def all_gather_blocks(x, axis, n):
@@ -126,11 +147,11 @@
     w_rows = neigh_weight.shape[0]
     up_rows = upper_weight.shape[0]
 
-    packed = jnp.concatenate([neigh_weight, self_weight, upper_weight], axis=0)
+    packed = jnp.concatenate([neigh_weight, self_weight], axis=0)
     gathered = lax.all_gather(packed, "cols", axis=0, tiled=False)
     neigh_full = gathered[:, :w_rows]
-    self_full = gathered[:, w_rows : 2 * w_rows]
-    full_upper = gathered[:, 2 * w_rows :].reshape(n_cols * up_rows, hidden)
+    self_full = gathered[:, w_rows:]
+    full_upper = lax.all_gather(upper_weight, "cols", axis=0, tiled=True)
 
     me_dom = lax.axis_index("dom")
     me_col = lax.axis_index("cols")
@@ -178,8 +199,9 @@
     slope_two = (out_cotangent.astype(jnp.float32) * swish_slope(pre_two)).astype(jnp.bfloat16)
 
     local_grad = contract_rows(upper_input, slope_two)
-    col_sum = reduce_scatter_blocks(
-        local_grad.reshape(n_cols, up_rows, hidden), "cols", n_cols, jnp.bfloat16
+    dom_rows = up_rows // n_dom
+    upper_part = reduce_scatter_grid(
+        local_grad.reshape(n_cols, n_dom, dom_rows, hidden), n_dom, n_cols, jnp.bfloat16
     )
     back_mixed = lax.dot_general(
         slope_two, full_upper, (((1,), (1,)), ((), ())), preferred_element_type=jnp.float32
@@ -189,10 +211,6 @@
     slab_rows = all_gather_blocks(slope_one, "cols", n_cols).reshape(tgt_dev, hidden)
     stacked = jnp.dot(both_t, slab_rows, preferred_element_type=jnp.float32)
     dom_cols = hidden // n_dom
-    dom_rows = up_rows // n_dom
-    upper_part = reduce_scatter_blocks(
-        col_sum.reshape(n_dom, dom_rows, hidden), "dom", n_dom, jnp.bfloat16, high_first=True
-    )
     grad_upper = all_gather_blocks(upper_part.astype(jnp.bfloat16), "dom", n_dom)
     grad_upper = grad_upper.reshape(up_rows, hidden).astype(jnp.float32)
     grad_layer = reduce_scatter_blocks(

time: 170 us -> 171 us (level)
  waiting for transfers between devices: 63.3 us -> 55 us
  starting transfers between devices: 18.8 us -> 26 us
  matrix products: 10.2 us -> 12.7 us
    ppermute x6, starting transfers between devices: 5.95 us -> 14.8 us  [_butterfly_reduce(): got = lax.ppermute(send.astype(send_dtype), axis, _xor_pairs(n, 1 << b))]
    ppermute x3, waiting for transfers between devices: 8.62 us -> 3.77 us  [local(): rows_t = lax.ppermute(rows_t, 'dom', _shift_pairs(n_dom, shift))]
    ppermute x6, waiting for transfers between devices: 31.1 us -> 26.5 us  [_butterfly_reduce(): got = lax.ppermute(send.astype(send_dtype), axis, _xor_pairs(n, 1 << b))]
    ppermute x6, starting transfers between devices: 6.33 us -> 3.79 us  [local(): chunk = lax.ppermute(chunk, 'cols', _shift_pairs(n_cols, shift))]
    slice x2 -> x1, local copies, waits for them, and re-layouts: 3.99 us -> 2.2 us  [local(): self_full = gathered[:, w_rows:]]
    dot_general x1, matrix products: 1.67 us -> 3.4 us  [local(): jnp.dot(upper_input, full_upper, preferred_element_type=jnp.float32)]
    unnamed x23 -> x29, local copies, waits for them, and re-layouts: 6.46 us -> 6.5 us
  transfers between devices with their start and end apart: 20 -> 21, of which waited for: 9 -> 9; matrix products, arithmetic and copies ran while one was open for 27% -> 28% of each run, Pallas kernels for 8% -> 8%
where the time goes in v5:
time: 171 us; the launch traced here: 170 us
  waiting for transfers between devices  55 us (32%)
  local copies, waits for them, and re-layouts  37.4 us (22%)
  starting transfers between devices  26 us (15%)
  between operations  14.8 us (9%)
  Pallas kernels  13.1 us (8%)
  matrix products  12.7 us (7%)
  other arithmetic  11.3 us (7%)
    ppermute x6, waiting for transfers between devices, _butterfly_reduce(): got = lax.ppermute(send.astype(send_dtype), axis, _xor_pairs(n, 1 << b))  26.5 us
    ppermute x4, waiting for transfers between devices, all_gather_blocks(): got = lax.ppermute(cur, axis, _xor_pairs(n, 1 << b))  24 us
    gather x8, local copies, waits for them, and re-layouts, local(): rows_t = features.at[slots].get(mode='promise_in_bounds').T  18.9 us
    ppermute x6, starting transfers between devices, _butterfly_reduce(): got = lax.ppermute(send.astype(send_dtype), axis, _xor_pairs(n, 1 << b))  14.8 us
    pallas_call x4, Pallas kernels, accumulate(): pl.pallas_call(_accumulate_kernel, out_shape=[jax.ShapeDtypeStruct(acc_su...  13.1 us
    unnamed x29, local copies, waits for them, and re-layouts  6.5 us
    ppermute x3, starting transfers between devices, local(): rows_t = lax.ppermute(rows_t, 'dom', _shift_pairs(n_dom, shift))  6.11 us
    dot_general x9, matrix products, contract_rows(): lax.dot_general(left_mat, right_mat, (((0,), (0,)), ((), ())), preferred_...  4.41 us
  transfers between devices with their start and end apart: 21, of which 9 were waited for; matrix products, arithmetic and copies ran while one was open for 28% of the time, Pallas kernels for 8%

profile of v5, /device:TPU:0, one launch (start us, length us, event | category | flops | bytes accessed | tf_op | source)
XLA Modules:
  0.0 170.1 jit_solution(13176584123570074502)
XLA Ops:
  7.2 2.1 %pad_maximum_fusion.2 = bf16[384,1024]{1,0:T(8,128)(2,1)} fusion(bf16[192,1024]{1,0:T(8,128)(2,1)} %param.14, bf16[192,1024]{1,0:T(8,128)(2,1)} %param.13), kind=kLoop, calls=%fused_computation.31 | loop fusion | flops 1572864 | bytes 1572864 | tf_op jit(solution)/shard_map/concatenate | solution.py:150
  9.4 3.2 %copy.46 = bf16[4096,192]{1,0:T(8,128)(2,1)S(1)} copy(bf16[4096,192]{0,1:T(8,128)(2,1)} %param.10) | data formatting | bytes 3145728 | tf_op args[0]
  12.7 3.9 %gather_fusion = bf16[1024,192]{1,0:T(8,128)(2,1)S(1)} fusion(bf16[4096,192]{1,0:T(8,128)(2,1)S(1)} %copy.46, s32[1024]{0:T(1024)S(1)} %broadcast_clamp_fusion.3), kind=kCustom, calls=%fused_computation | custom fusion | bytes 790528 | tf_op jit(solution)/shard_map/gather | solution.py:175
  16.8 5.1 %collective-permute-start.3 = (bf16[192,1024]{1,0:T(8,128)(2,1)S(1)}, bf16[192,1024]{1,0:T(8,128)(2,1)}, u32[]{:S(2)}, u32[]{:S(2)}) collective-permute-start(bf16[192,1024]{1,0:T(8,128)(2,1)S(1)} %bitcast.144), channel_id=1, source_target_pairs={{0,12},{4,0},{8,4},{12,8},{1,13},{5,1},{9,5},{13,9},{2,14},{6,2},{... | collective-permute-start | bytes 1179656 | tf_op jit(solution)/shard_map/ppermute | solution.py:177
  21.9 3.9 %gather_fusion.1 = bf16[1024,192]{1,0:T(8,128)(2,1)S(1)} fusion(bf16[4096,192]{1,0:T(8,128)(2,1)S(1)} %copy.46, s32[1024]{0:T(1024)S(1)} %broadcast_clamp_fusion.2), kind=kCustom, calls=%fused_computation.1 | custom fusion | bytes 790528 | tf_op jit(solution)/shard_map/gather | solution.py:175
  26.8 3.9 %gather_fusion.2 = bf16[1024,192]{1,0:T(8,128)(2,1)S(1)} fusion(bf16[4096,192]{1,0:T(8,128)(2,1)S(1)} %copy.46, s32[1024]{0:T(1024)S(1)} %broadcast_clamp_fusion.1), kind=kCustom, calls=%fused_computation.2 | custom fusion | bytes 790528 | tf_op jit(solution)/shard_map/gather | solution.py:175
  32.8 1.8 %slice_bitcast_fusion = (bf16[192,1024]{1,0:T(8,128)(2,1)}, bf16[1024,192]{0,1:T(8,128)(2,1)S(1)}) fusion(bf16[4096,192]{0,1:T(8,128)(2,1)} %param.10), kind=kLoop, calls=%fused_computation.130 | loop fusion | bytes 1179648 | tf_op jit(solution)/shard_map/transpose | solution.py:158
  35.4 1.4 collective-permute-start.1
  37.0 3.9 %gather_fusion.3 = bf16[1024,192]{1,0:T(8,128)(2,1)S(1)} fusion(bf16[4096,192]{1,0:T(8,128)(2,1)S(1)} %copy.46, s32[1024]{0:T(1024)S(1)} %broadcast_clamp_fusion), kind=kCustom, calls=%fused_computation.3 | custom fusion | bytes 790528 | tf_op jit(solution)/shard_map/gather | solution.py:175
  44.2 3.3 %shard_map.129 = (f32[192,1024]{1,0:T(8,128)}, f32[8,1024]{1,0:T(8,128)}) custom-call(s32[1,1024]{1,0:T(1,128)} %get-tuple-element.44.tgt_ref, bf16[192,1024]{1,0:T(8,128)(2,1)} %bitcast.145, f32[192,1024]{1,0:T(8,128)} %broadcast_in_dim.4.sum_in, f32[8,1024]{1,0:T(8,128)} %broadcast_in_dim.5.cnt_in), custom_call_target="tpu_custom_call", output_to_operand_aliasing={{0}: (2, {}), {1}: (3, {})} | custom-call | flops 419430400 | bytes 2035712 | tf_op jit(solution)/shard_map/pallas_call | solution.py:46
  48.5 3.3 %shard_map.130 = (f32[192,1024]{1,0:T(8,128)}, f32[8,1024]{1,0:T(8,128)}) custom-call(s32[1,1024]{1,0:T(1,128)} %get-tuple-element.47.tgt_ref, bf16[192,1024]{1,0:T(8,128)(2,1)} %collective-permute-done.5.rec_ref, f32[192,1024]{1,0:T(8,128)} %get-tuple-element.12.sum_in, ...), custom_call_target="tpu_custom_call", output_to_operand_aliasing={{0}: (2, {}), {1}: (3, {})} | custom-call | flops 419430400 | bytes 2035712 | tf_op jit(solution)/shard_map/pallas_call | solution.py:46
  51.8 3.7 %collective-permute-done.4.rec_ref = bf16[192,1024]{1,0:T(8,128)(2,1)} collective-permute-done((bf16[192,1024]{1,0:T(8,128)(2,1)}, bf16[192,1024]{1,0:T(8,128)(2,1)}, u32[]{:S(2)}, u32[]{:S(2)}) %collective-permute-start.4) | collective-permute-done | bytes 393248 | tf_op jit(solution)/shard_map/ppermute | solution.py:177
  55.6 3.3 %shard_map.131 = (f32[192,1024]{1,0:T(8,128)}, f32[8,1024]{1,0:T(8,128)}) custom-call(s32[1,1024]{1,0:T(1,128)} %get-tuple-element.45.tgt_ref, bf16[192,1024]{1,0:T(8,128)(2,1)} %collective-permute-done.4.rec_ref, f32[192,1024]{1,0:T(8,128)} %get-tuple-element.14.sum_in, ...), custom_call_target="tpu_custom_call", output_to_operand_aliasing={{0}: (2, {}), {1}: (3, {})} | custom-call | flops 419430400 | bytes 2035712 | tf_op jit(solution)/shard_map/pallas_call | solution.py:46
  58.8 3.3 %shard_map.132 = (f32[192,1024]{1,0:T(8,128)}, f32[8,1024]{1,0:T(8,128)}) custom-call(s32[1,1024]{1,0:T(1,128)} %get-tuple-element.46.tgt_ref, bf16[192,1024]{1,0:T(8,128)(2,1)} %collective-permute-done.3.rec_ref, f32[192,1024]{1,0:T(8,128)} %get-tuple-element.16.sum_in, ...), custom_call_target="tpu_custom_call", output_to_operand_aliasing={{0}: (2, {}), {1}: (3, {})} | custom-call | flops 419430400 | bytes 2035712 | tf_op jit(solution)/shard_map/pallas_call | solution.py:46
  65.8 2.2 %fusion.63 = (bf16[4,192,1024]{2,1,0:T(8,128)(2,1)S(1)}, bf16[4,192,1024]{2,1,0:T(8,128)(2,1)S(1)}) fusion(bf16[4,384,1024]{2,1,0:T(8,128)(2,1)} %bitcast.139), kind=kLoop, calls=%fused_computation.133 | loop fusion | bytes 6291456 | tf_op jit(solution)/shard_map/slice | solution.py:153
  73.5 3.4 %multiply_convert_fusion.2 = (bf16[256,1024]{1,0:T(8,128)(2,1)}, f32[256,1024]{1,0:T(8,128)S(1)}) fusion(f32[1024]{0:T(1024)S(1)} %copy-done.13, bf16[256,1024]{1,0:T(8,128)(2,1)S(1)} %convolution_convert_fusion, bf16[1024,1024]{1,0:T(8,128)(2,1)} %all-gather.4.cloned.1.call-done), kind=kOutput, calls=%fused_computation.27 | convolution fusion | flops 538443776 | bytes 4198400 | tf_op jit(solution)/shard_map/dot_general | solution.py:197
  77.8 2.1 %multiply_convert_fusion = bf16[256,1024]{1,0:T(8,128)(2,1)} fusion(f32[256,1024]{1,0:T(8,128)S(1)} %fusion.4, f32[256,1024]{1,0:T(8,128)S(1)} %fusion.62, f32[256,256]{1,0:T(8,128)S(1)} %copy-done.6), kind=kOutput, calls=%fused_computation.25 | convolution fusion | flops 807927808 | bytes 2883584 | tf_op jit(solution)/shard_map/dot_general | solution.py:209
  81.9 2.0 %copy-done = f32[1024,1024]{1,0:T(8,128)} copy-done((f32[1024,1024]{1,0:T(8,128)}, f32[1024,1024]{1,0:T(8,128)S(1)}, u32[]{:S(2)}) %copy-start) | copy-done | bytes 4194328
  84.1 10.2 %collective-permute-done.9 = bf16[256,1024]{1,0:T(8,128)(2,1)S(1)} collective-permute-done((bf16[256,1024]{1,0:T(8,128)(2,1)}, bf16[256,1024]{1,0:T(8,128)(2,1)S(1)}, u32[]{:S(2)}, u32[]{:S(2)}) %collective-permute-start.9) | collective-permute-done | bytes 524320 | tf_op jit(solution)/shard_map/ppermute | solution.py:121
  96.5 2.2 %bitcast_add_fusion = f32[2,2,2,64,1024]{4,3,2,1,0:T(8,128)S(1)} fusion(bf16[2,2,2,64,1024]{4,3,2,1,0:T(8,128)(2,1)} %collective-permute-done.13, f32[2,2,2,2,64,1024]{5,4,3,2,1,0:T(8,128)} %bitcast.137, s32[]{:T(128)S(6)} %select_n.311), kind=kLoop, calls=%fused_computation.7 | loop fusion | flops 1048576 | bytes 5242884 | tf_op jit(solution)/shard_map/add | solution.py:95
  100.2 6.1 %collective-permute-start.14 = (bf16[2,2,64,1024]{3,2,1,0:T(8,128)(2,1)S(1)}, bf16[2,2,64,1024]{3,2,1,0:T(8,128)(2,1)S(1)}, u32[]{:S(2)}, u32[]{:S(2)}) collective-permute-start(bf16[2,2,64,1024]{3,2,1,0:T(8,128)(2,1)S(1)} %fusion.9), channel_id=1, source_target_pairs={{0,4},{1,5},{2,6},{3,7},{4,0},{5,1},{6,2},{7,3},{8,12},{9,13},{10,... | collective-permute-start | bytes 1572872 | tf_op jit(solution)/shard_map/ppermute | solution.py:94
  106.8 2.6 %copy.55 = bf16[1024,1024]{1,0:T(8,128)(2,1)} copy(bf16[1024,1024]{0,1:T(8,128)(2,1)S(1)} %bitcast.138) | data formatting | bytes 4194304 | tf_op jit(solution)/shard_map/dot_general | solution.py:212
  109.4 9.5 %collective-permute-done.14 = bf16[2,2,64,1024]{3,2,1,0:T(8,128)(2,1)S(1)} collective-permute-done((bf16[2,2,64,1024]{3,2,1,0:T(8,128)(2,1)S(1)}, bf16[2,2,64,1024]{3,2,1,0:T(8,128)(2,1)S(1)}, u32[]{:S(2)}, u32[]{:S(2)}) %collective-permute-start.14) | collective-permute-done | bytes 524320 | tf_op jit(solution)/shard_map/ppermute | solution.py:94
  118.9 1.4 bitcast_add_fusion.1
  120.3 3.7 %collective-permute-start.15 = (bf16[2,64,1024]{2,1,0:T(8,128)(2,1)S(1)}, bf16[2,64,1024]{2,1,0:T(8,128)(2,1)S(1)}, u32[]{:S(2)}, u32[]{:S(2)}) collective-permute-start(bf16[2,64,1024]{2,1,0:T(8,128)(2,1)S(1)} %fusion.32), channel_id=1, source_target_pairs={{0,8},{1,9},{2,10},{3,11},{4,12},{5,13},{6,14},{7,15},{8,0},{9,1},... | collective-permute-start | bytes 786440 | tf_op jit(solution)/shard_map/ppermute | solution.py:94
  125.4 10.5 %collective-permute-done.15 = bf16[2,64,1024]{2,1,0:T(8,128)(2,1)S(1)} collective-permute-done((bf16[2,64,1024]{2,1,0:T(8,128)(2,1)S(1)}, bf16[2,64,1024]{2,1,0:T(8,128)(2,1)S(1)}, u32[]{:S(2)}, u32[]{:S(2)}) %collective-permute-start.15) | collective-permute-done | bytes 262176 | tf_op jit(solution)/shard_map/ppermute | solution.py:94
  136.0 1.6 collective-permute-start.16
  137.6 3.7 %collective-permute-done.16 = bf16[64,1024]{1,0:T(8,128)(2,1)S(1)} collective-permute-done((bf16[64,1024]{1,0:T(8,128)(2,1)S(1)}, bf16[64,1024]{1,0:T(8,128)(2,1)S(1)}, u32[]{:S(2)}, u32[]{:S(2)}) %collective-permute-start.16) | collective-permute-done | bytes 131104 | tf_op jit(solution)/shard_map/ppermute | solution.py:94
  141.5 3.0 %collective-permute-start.12 = (bf16[384,256]{1,0:T(8,128)(2,1)S(1)}, bf16[384,256]{1,0:T(8,128)(2,1)S(1)}, u32[]{:S(2)}, u32[]{:S(2)}) collective-permute-start(bf16[384,256]{1,0:T(8,128)(2,1)S(1)} %fusion.35), channel_id=1, source_target_pairs={{0,8},{4,12},{8,0},{12,4},{1,9},{5,13},{9,1},{13,5},{2,10},{6,14},... | collective-permute-start | bytes 589832 | tf_op jit(solution)/shard_map/ppermute | solution.py:94
  144.5 9.1 %collective-permute-done.17 = bf16[64,1024]{1,0:T(8,128)(2,1)S(1)} collective-permute-done((bf16[64,1024]{1,0:T(8,128)(2,1)S(1)}, bf16[64,1024]{1,0:T(8,128)(2,1)S(1)}, u32[]{:S(2)}, u32[]{:S(2)}) %collective-permute-start.17) | collective-permute-done | bytes 131104 | tf_op jit(solution)/shard_map/ppermute | solution.py:121
  153.7 2.9 %collective-permute-done.12 = bf16[384,256]{1,0:T(8,128)(2,1)S(1)} collective-permute-done((bf16[384,256]{1,0:T(8,128)(2,1)S(1)}, bf16[384,256]{1,0:T(8,128)(2,1)S(1)}, u32[]{:S(2)}, u32[]{:S(2)}) %collective-permute-start.12) | collective-permute-done | bytes 196640 | tf_op jit(solution)/shard_map/ppermute | solution.py:94
  157.4 4.7 %collective-permute-done.18 = bf16[2,64,1024]{2,1,0:T(8,128)(2,1)S(1)} collective-permute-done((bf16[2,64,1024]{2,1,0:T(8,128)(2,1)S(1)}, bf16[2,64,1024]{2,1,0:T(8,128)(2,1)S(1)}, u32[]{:S(2)}, u32[]{:S(2)}) %collective-permute-start.18) | collective-permute-done | bytes 262176 | tf_op jit(solution)/shard_map/ppermute | solution.py:121
  (107 shorter events, 28.5 us)
Async XLA Ops:
  7.2 58.6 %all-gather.6.cloned.1.call-start = ((), (), s32[]{:S(2)}) async-start(), calls=%async_computation.1 | async-start | bytes 3932160 | tf_op jit(solution)/shard_map/all_gather | solution.py:151
  9.3 3.3 %copy-start.9 = (s32[1,4,1024]{2,1,0:T(4,128)S(1)}, s32[1,4,1024]{2,1,0:T(4,128)}, u32[]{:S(2)}) copy-start(s32[1,4,1024]{2,1,0:T(4,128)} %param.11) | copy-start | bytes 49156
  9.3 64.1 %all-gather.4.cloned.1.call-start = ((), (), s32[]{:S(2)}) async-start(), calls=%async_computation | async-start | bytes 2621440 | tf_op jit(solution)/shard_map/all_gather | solution.py:154
  16.8 42.0 %collective-permute-start.3 = (bf16[192,1024]{1,0:T(8,128)(2,1)S(1)}, bf16[192,1024]{1,0:T(8,128)(2,1)}, u32[]{:S(2)}, u32[]{:S(2)}) collective-permute-start(bf16[192,1024]{1,0:T(8,128)(2,1)S(1)} %bitcast.144), channel_id=1, source_target_pairs={{0,12},{4,0},{8,4},{12,8},{1,13},{5,1},{9,5},{13,9},{2,14},{6,2},{... | collective-permute-start | bytes 1179656 | tf_op jit(solution)/shard_map/ppermute | solution.py:177
  26.8 28.8 %collective-permute-start.4 = (bf16[192,1024]{1,0:T(8,128)(2,1)}, bf16[192,1024]{1,0:T(8,128)(2,1)}, u32[]{:S(2)}, u32[]{:S(2)}) collective-permute-start(bf16[192,1024]{1,0:T(8,128)(2,1)} %bitcast.15), channel_id=1, source_target_pairs={{0,8},{4,12},{8,0},{12,4},{1,9},{5,13},{9,1},{13,5},{2,10},{6,14},... | collective-permute-start | bytes 1179656 | tf_op jit(solution)/shard_map/ppermute | solution.py:177
  31.8 16.5 %collective-permute-start.5 = (bf16[192,1024]{1,0:T(8,128)(2,1)}, bf16[192,1024]{1,0:T(8,128)(2,1)}, u32[]{:S(2)}, u32[]{:S(2)}) collective-permute-start(bf16[192,1024]{1,0:T(8,128)(2,1)} %bitcast.19), channel_id=1, source_target_pairs={{0,4},{4,8},{8,12},{12,0},{1,5},{5,9},{9,13},{13,1},{2,6},{6,10},{... | collective-permute-start | bytes 1179656 | tf_op jit(solution)/shard_map/ppermute | solution.py:177
  35.3 32.6 %collective-permute-start.2 = (bf16[192,256]{1,0:T(8,128)(2,1)}, bf16[192,256]{1,0:T(8,128)(2,1)}, u32[]{:S(2)}, u32[]{:S(2)}) collective-permute-start(bf16[192,256]{1,0:T(8,128)(2,1)} %get-tuple-element.36), channel_id=1, source_target_pairs={{0,3},{1,0},{2,1},{3,2},{4,7},{5,4},{6,5},{7,6},{8,11},{9,8},{10,9... | collective-permute-start | bytes 294920 | tf_op jit(solution)/shard_map/ppermute | solution.py:165
  35.4 34.5 %collective-permute-start.1 = (bf16[192,256]{1,0:T(8,128)(2,1)}, bf16[192,256]{1,0:T(8,128)(2,1)S(1)}, u32[]{:S(2)}, u32[]{:S(2)}) collective-permute-start(bf16[192,256]{1,0:T(8,128)(2,1)} %get-tuple-element.37), channel_id=1, source_target_pairs={{0,2},{1,3},{2,0},{3,1},{4,6},{5,7},{6,4},{7,5},{8,10},{9,11},{10,... | collective-permute-start | bytes 294920 | tf_op jit(solution)/shard_map/ppermute | solution.py:165
  37.0 5.0 %copy-start.10 = (s32[1,4,1024]{2,1,0:T(4,128)S(1)}, s32[1,4,1024]{2,1,0:T(4,128)}, u32[]{:S(2)}) copy-start(s32[1,4,1024]{2,1,0:T(4,128)} %param.12) | copy-start | bytes 49156
  41.0 6.5 %copy-start.8 = (s32[256,15]{0,1:T(8,128)S(1)}, s32[256,15]{0,1:T(8,128)}, u32[]{:S(2)}) copy-start(s32[256,15]{0,1:T(8,128)} %param.18) | copy-start | bytes 46084
  41.0 7.3 %copy-start.7 = (bf16[192,256]{1,0:T(8,128)(2,1)S(1)}, bf16[192,256]{1,0:T(8,128)(2,1)}, u32[]{:S(2)}) copy-start(bf16[192,256]{1,0:T(8,128)(2,1)} %get-tuple-element.35) | copy-start | bytes 294916
  48.2 24.4 %copy-start.5 = (f32[256,256]{1,0:T(8,128)}, f32[256,256]{1,0:T(8,128)S(1)}, u32[]{:S(2)}) copy-start(f32[256,256]{1,0:T(8,128)S(1)} %convert_reduce_fusion) | copy-start | bytes 786436
  48.3 22.3 %collective-permute-start = (bf16[192,256]{1,0:T(8,128)(2,1)S(1)}, bf16[192,256]{1,0:T(8,128)(2,1)S(1)}, u32[]{:S(2)}, u32[]{:S(2)}) collective-permute-start(bf16[192,256]{1,0:T(8,128)(2,1)S(1)} %copy-done.7), channel_id=1, source_target_pairs={{0,1},{1,2},{2,3},{3,0},{4,5},{5,6},{6,7},{7,4},{8,9},{9,10},{10,1... | collective-permute-start | bytes 294920 | tf_op jit(solution)/shard_map/ppermute | solution.py:165
  64.1 6.8 %collective-permute-start.8 = (bf16[192,256]{1,0:T(8,128)(2,1)S(1)}, bf16[192,256]{1,0:T(8,128)(2,1)S(1)}, u32[]{:S(2)}, u32[]{:S(2)}) collective-permute-start(bf16[192,256]{1,0:T(8,128)(2,1)S(1)} %get-tuple-element.33), channel_id=1, source_target_pairs={{0,3},{1,0},{2,1},{3,2},{4,7},{5,4},{6,5},{7,6},{8,11},{9,8},{10,9... | collective-permute-start | bytes 294920 | tf_op jit(solution)/shard_map/ppermute | solution.py:189
  64.8 6.5 %collective-permute-start.7 = (bf16[192,256]{1,0:T(8,128)(2,1)S(1)}, bf16[192,256]{1,0:T(8,128)(2,1)S(1)}, u32[]{:S(2)}, u32[]{:S(2)}) collective-permute-start(bf16[192,256]{1,0:T(8,128)(2,1)S(1)} %get-tuple-element.34), channel_id=1, source_target_pairs={{0,2},{1,3},{2,0},{3,1},{4,6},{5,7},{6,4},{7,5},{8,10},{9,11},{10,... | collective-permute-start | bytes 294920 | tf_op jit(solution)/shard_map/ppermute | solution.py:189
  65.8 3.8 %copy-start.11 = (f32[1024]{0:T(1024)S(1)}, f32[1024]{0:T(1024)}, u32[]{:S(2)}) copy-start(f32[1024]{0:T(1024)} %param.15) | copy-start | bytes 12292
  68.0 4.3 %collective-permute-start.6 = (bf16[192,256]{1,0:T(8,128)(2,1)S(1)}, bf16[192,256]{1,0:T(8,128)(2,1)S(1)}, u32[]{:S(2)}, u32[]{:S(2)}) collective-permute-start(bf16[192,256]{1,0:T(8,128)(2,1)S(1)} %get-tuple-element.32), channel_id=1, source_target_pairs={{0,1},{1,2},{2,3},{3,0},{4,5},{5,6},{6,7},{7,4},{8,9},{9,10},{10,1... | collective-permute-start | bytes 294920 | tf_op jit(solution)/shard_map/ppermute | solution.py:189
  73.4 3.5 %copy-start.3 = (bf16[256,1024]{1,0:T(8,128)(2,1)S(1)}, bf16[256,1024]{1,0:T(8,128)(2,1)}, u32[]{:S(2)}) copy-start(bf16[256,1024]{1,0:T(8,128)(2,1)} %param.19) | copy-start | bytes 1572868
  73.5 3.4 %copy-start.12 = (bf16[1024,1024]{1,0:T(8,128)(2,1)S(1)}, bf16[1024,1024]{1,0:T(8,128)(2,1)}, u32[]{:S(2)}) copy-start(bf16[1024,1024]{1,0:T(8,128)(2,1)} %all-gather.4.cloned.1.call-done) | copy-start | bytes 6291460
  79.9 14.4 %collective-permute-start.9 = (bf16[256,1024]{1,0:T(8,128)(2,1)}, bf16[256,1024]{1,0:T(8,128)(2,1)S(1)}, u32[]{:S(2)}, u32[]{:S(2)}) collective-permute-start(bf16[256,1024]{1,0:T(8,128)(2,1)} %multiply_convert_fusion), channel_id=1, source_target_pairs={{0,2},{1,3},{2,0},{3,1},{4,6},{5,7},{6,4},{7,5},{8,10},{9,11},{10,... | collective-permute-start | bytes 1572872 | tf_op jit(solution)/shard_map/ppermute | solution.py:121
  81.9 2.0 %copy-start = (f32[1024,1024]{1,0:T(8,128)}, f32[1024,1024]{1,0:T(8,128)S(1)}, u32[]{:S(2)}) copy-start(f32[1024,1024]{1,0:T(8,128)S(1)} %fusion.61) | copy-start | bytes 12582916
  84.0 12.5 %collective-permute-start.13 = (bf16[2,2,2,64,1024]{4,3,2,1,0:T(8,128)(2,1)S(1)}, bf16[2,2,2,64,1024]{4,3,2,1,0:T(8,128)(2,1)}, u32[]{:S(2)}, u32[]{:S(2)}) collective-permute-start(bf16[2,2,2,64,1024]{4,3,2,1,0:T(8,128)(2,1)S(1)} %fusion.5), channel_id=1, source_target_pairs={{0,1},{1,0},{2,3},{3,2},{4,5},{5,4},{6,7},{7,6},{8,9},{9,8},{10,11... | collective-permute-start | bytes 3145736 | tf_op jit(solution)/shard_map/ppermute | solution.py:94
  96.5 9.7 %collective-permute-start.10 = (bf16[2,256,1024]{2,1,0:T(8,128)(2,1)}, bf16[2,256,1024]{2,1,0:T(8,128)(2,1)S(1)}, u32[]{:S(2)}, u32[]{:S(2)}) collective-permute-start(bf16[2,256,1024]{2,1,0:T(8,128)(2,1)} %pad_maximum_fusion.1), channel_id=1, source_target_pairs={{0,1},{1,0},{2,3},{3,2},{4,5},{5,4},{6,7},{7,6},{8,9},{9,8},{10,11... | collective-permute-start | bytes 3145736 | tf_op jit(solution)/shard_map/ppermute | solution.py:121
  100.2 18.7 %collective-permute-start.14 = (bf16[2,2,64,1024]{3,2,1,0:T(8,128)(2,1)S(1)}, bf16[2,2,64,1024]{3,2,1,0:T(8,128)(2,1)S(1)}, u32[]{:S(2)}, u32[]{:S(2)}) collective-permute-start(bf16[2,2,64,1024]{3,2,1,0:T(8,128)(2,1)S(1)} %fusion.9), channel_id=1, source_target_pairs={{0,4},{1,5},{2,6},{3,7},{4,0},{5,1},{6,2},{7,3},{8,12},{9,13},{10,... | collective-permute-start | bytes 1572872 | tf_op jit(solution)/shard_map/ppermute | solution.py:94
  109.4 14.6 %copy-start.2 = (bf16[1024,1024]{1,0:T(8,128)(2,1)S(1)}, bf16[1024,1024]{1,0:T(8,128)(2,1)}, u32[]{:S(2)}) copy-start(bf16[1024,1024]{1,0:T(8,128)(2,1)} %copy.55) | copy-start | bytes 6291460
  109.4 14.6 %copy-start.4 = (bf16[192,1024]{1,0:T(8,128)(2,1)S(1)}, bf16[192,1024]{1,0:T(8,128)(2,1)}, u32[]{:S(2)}) copy-start(bf16[192,1024]{1,0:T(8,128)(2,1)} %get-tuple-element.24) | copy-start | bytes 1179652
  120.3 15.6 %collective-permute-start.15 = (bf16[2,64,1024]{2,1,0:T(8,128)(2,1)S(1)}, bf16[2,64,1024]{2,1,0:T(8,128)(2,1)S(1)}, u32[]{:S(2)}, u32[]{:S(2)}) collective-permute-start(bf16[2,64,1024]{2,1,0:T(8,128)(2,1)S(1)} %fusion.32), channel_id=1, source_target_pairs={{0,8},{1,9},{2,10},{3,11},{4,12},{5,13},{6,14},{7,15},{8,0},{9,1},... | collective-permute-start | bytes 786440 | tf_op jit(solution)/shard_map/ppermute | solution.py:94
  125.1 16.3 %collective-permute-start.11 = (bf16[2,384,256]{2,1,0:T(8,128)(2,1)S(1)}, bf16[2,384,256]{2,1,0:T(8,128)(2,1)S(1)}, u32[]{:S(2)}, u32[]{:S(2)}) collective-permute-start(bf16[2,384,256]{2,1,0:T(8,128)(2,1)S(1)} %fusion.10), channel_id=1, source_target_pairs={{0,4},{4,0},{8,12},{12,8},{1,5},{5,1},{9,13},{13,9},{2,6},{6,2},{1... | collective-permute-start | bytes 1179656 | tf_op jit(solution)/shard_map/ppermute | solution.py:94
  136.0 5.3 %collective-permute-start.16 = (bf16[64,1024]{1,0:T(8,128)(2,1)S(1)}, bf16[64,1024]{1,0:T(8,128)(2,1)S(1)}, u32[]{:S(2)}, u32[]{:S(2)}) collective-permute-start(bf16[64,1024]{1,0:T(8,128)(2,1)S(1)} %fusion.36), channel_id=1, source_target_pairs={{0,2},{1,3},{2,0},{3,1},{4,6},{5,7},{6,4},{7,5},{8,10},{9,11},{10,... | collective-permute-start | bytes 393224 | tf_op jit(solution)/shard_map/ppermute | solution.py:94
  141.3 12.3 %collective-permute-start.17 = (bf16[64,1024]{1,0:T(8,128)(2,1)S(1)}, bf16[64,1024]{1,0:T(8,128)(2,1)S(1)}, u32[]{:S(2)}, u32[]{:S(2)}) collective-permute-start(bf16[64,1024]{1,0:T(8,128)(2,1)S(1)} %fusion.33), channel_id=1, source_target_pairs={{0,8},{4,12},{8,0},{12,4},{1,9},{5,13},{9,1},{13,5},{2,10},{6,14},... | collective-permute-start | bytes 393224 | tf_op jit(solution)/shard_map/ppermute | solution.py:121
  141.5 15.1 %collective-permute-start.12 = (bf16[384,256]{1,0:T(8,128)(2,1)S(1)}, bf16[384,256]{1,0:T(8,128)(2,1)S(1)}, u32[]{:S(2)}, u32[]{:S(2)}) collective-permute-start(bf16[384,256]{1,0:T(8,128)(2,1)S(1)} %fusion.35), channel_id=1, source_target_pairs={{0,8},{4,12},{8,0},{12,4},{1,9},{5,13},{9,1},{13,5},{2,10},{6,14},... | collective-permute-start | bytes 589832 | tf_op jit(solution)/shard_map/ppermute | solution.py:94
  153.6 8.5 %collective-permute-start.18 = (bf16[2,64,1024]{2,1,0:T(8,128)(2,1)S(1)}, bf16[2,64,1024]{2,1,0:T(8,128)(2,1)S(1)}, u32[]{:S(2)}, u32[]{:S(2)}) collective-permute-start(bf16[2,64,1024]{2,1,0:T(8,128)(2,1)S(1)} %pad_maximum_fusion.3), channel_id=1, source_target_pairs={{0,4},{4,0},{8,12},{12,8},{1,5},{5,1},{9,13},{13,9},{2,6},{6,2},{1... | collective-permute-start | bytes 786440 | tf_op jit(solution)/shard_map/ppermute | solution.py:121
  (3 other events, 3.2 us)
Sparse Core Ops, SparseCore 0:
  9.6 32.1 all-gather.5
  43.3 23.0 all-gather.3

commit v6 on v5

--- a/solution.py
+++ b/solution.py
@@ -213,12 +213,9 @@
     dom_cols = hidden // n_dom
     grad_upper = all_gather_blocks(upper_part.astype(jnp.bfloat16), "dom", n_dom)
     grad_upper = grad_upper.reshape(up_rows, hidden).astype(jnp.float32)
-    grad_layer = reduce_scatter_blocks(
-        jnp.swapaxes(stacked.reshape(2 * width, n_dom, dom_cols), 0, 1),
-        "dom",
-        n_dom,
-        jnp.bfloat16,
-    )
+    grad_layer = lax.psum_scatter(
+        stacked.astype(jnp.bfloat16), "dom", scatter_dimension=1, tiled=True
+    ).astype(jnp.float32)
     grad_neigh = grad_layer[:w_rows]
     grad_self = grad_layer[w_rows:]
     return (hidden_two, grad_neigh, grad_self, grad_upper)

time: 171 us -> 173 us (1.012)
  waiting for transfers between devices: 55 us -> 58.5 us
  local copies, waits for them, and re-layouts: 37.4 us -> 35 us
    ppermute x6 -> x4, waiting for transfers between devices: 26.5 us -> 34.2 us  [_butterfly_reduce(): got = lax.ppermute(send.astype(send_dtype), axis, _xor_pairs(n, 1 << b))]
    ppermute x6 -> x4, starting transfers between devices: 14.8 us -> 10.5 us  [_butterfly_reduce(): got = lax.ppermute(send.astype(send_dtype), axis, _xor_pairs(n, 1 << b))]
    ppermute x4, waiting for transfers between devices: 24 us -> 20.4 us  [all_gather_blocks(): got = lax.ppermute(cur, axis, _xor_pairs(n, 1 << b))]
    ppermute x4, starting transfers between devices: 1.18 us -> 4.01 us  [all_gather_blocks(): got = lax.ppermute(cur, axis, _xor_pairs(n, 1 << b))]
    dot_general x1 -> x0, local copies, waits for them, and re-layouts: 2.58 us -> none  [local(): stacked = jnp.dot(both_t, slab_rows, preferred_element_type=jnp.float32)]
    unnamed x29 -> x23, local copies, waits for them, and re-layouts: 6.5 us -> 5.17 us
    add x5 -> x3, other arithmetic: 3.76 us -> 3.48 us  [_butterfly_reduce(): cur = keep + got.astype(keep.dtype)]
  transfers between devices with their start and end apart: 21 -> 20, of which waited for: 9 -> 8; matrix products, arithmetic and copies ran while one was open for 28% -> 28% of each run, Pallas kernels for 8% -> 8%
where the time goes in v6:
time: 173 us; the launch traced here: 172 us
  waiting for transfers between devices  58.5 us (34%)
  local copies, waits for them, and re-layouts  35 us (20%)
  starting transfers between devices  24.5 us (14%)
  between operations  14.4 us (8%)
  matrix products  13.6 us (8%)
  Pallas kernels  13.1 us (8%)
  other arithmetic  13 us (8%)
    ppermute x4, waiting for transfers between devices, _butterfly_reduce(): got = lax.ppermute(send.astype(send_dtype), axis, _xor_pairs(n, 1 << b))  34.2 us
    ppermute x4, waiting for transfers between devices, all_gather_blocks(): got = lax.ppermute(cur, axis, _xor_pairs(n, 1 << b))  20.4 us
    gather x8, local copies, waits for them, and re-layouts, local(): rows_t = features.at[slots].get(mode='promise_in_bounds').T  18.8 us
    pallas_call x4, Pallas kernels, accumulate(): pl.pallas_call(_accumulate_kernel, out_shape=[jax.ShapeDtypeStruct(acc_su...  13.1 us
    ppermute x4, starting transfers between devices, _butterfly_reduce(): got = lax.ppermute(send.astype(send_dtype), axis, _xor_pairs(n, 1 << b))  10.5 us
    ppermute x3, starting transfers between devices, local(): rows_t = lax.ppermute(rows_t, 'dom', _shift_pairs(n_dom, shift))  6.11 us
    unnamed x23, local copies, waits for them, and re-layouts  5.17 us
    dot_general x9, matrix products, contract_rows(): lax.dot_general(left_mat, right_mat, (((0,), (0,)), ((), ())), preferred_...  4.41 us
  transfers between devices with their start and end apart: 20, of which 8 were waited for; matrix products, arithmetic and copies ran while one was open for 28% of the time, Pallas kernels for 8%

profile of v6, /device:TPU:0, one launch (start us, length us, event | category | flops | bytes accessed | tf_op | source)
XLA Modules:
  0.0 172.0 jit_solution(7549761352417174156)
XLA Ops:
  7.2 2.1 %pad_maximum_fusion.2 = bf16[384,1024]{1,0:T(8,128)(2,1)} fusion(bf16[192,1024]{1,0:T(8,128)(2,1)} %param.14, bf16[192,1024]{1,0:T(8,128)(2,1)} %param.13), kind=kLoop, calls=%fused_computation.32 | loop fusion | flops 1572864 | bytes 1572864 | tf_op jit(solution)/shard_map/concatenate | solution.py:150
  9.4 3.2 %copy.43 = bf16[4096,192]{1,0:T(8,128)(2,1)S(1)} copy(bf16[4096,192]{0,1:T(8,128)(2,1)} %param.10) | data formatting | bytes 3145728 | tf_op args[0]
  12.7 3.9 %gather_fusion = bf16[1024,192]{1,0:T(8,128)(2,1)S(1)} fusion(bf16[4096,192]{1,0:T(8,128)(2,1)S(1)} %copy.43, s32[1024]{0:T(1024)S(1)} %broadcast_clamp_fusion.3), kind=kCustom, calls=%fused_computation | custom fusion | bytes 790528 | tf_op jit(solution)/shard_map/gather | solution.py:175
  16.8 5.1 %collective-permute-start.3 = (bf16[192,1024]{1,0:T(8,128)(2,1)S(1)}, bf16[192,1024]{1,0:T(8,128)(2,1)}, u32[]{:S(2)}, u32[]{:S(2)}) collective-permute-start(bf16[192,1024]{1,0:T(8,128)(2,1)S(1)} %bitcast.120), channel_id=1, source_target_pairs={{0,12},{4,0},{8,4},{12,8},{1,13},{5,1},{9,5},{13,9},{2,14},{6,2},{... | collective-permute-start | bytes 1179656 | tf_op jit(solution)/shard_map/ppermute | solution.py:177
  21.9 3.9 %gather_fusion.1 = bf16[1024,192]{1,0:T(8,128)(2,1)S(1)} fusion(bf16[4096,192]{1,0:T(8,128)(2,1)S(1)} %copy.43, s32[1024]{0:T(1024)S(1)} %broadcast_clamp_fusion.2), kind=kCustom, calls=%fused_computation.1 | custom fusion | bytes 790528 | tf_op jit(solution)/shard_map/gather | solution.py:175
  26.8 3.9 %gather_fusion.2 = bf16[1024,192]{1,0:T(8,128)(2,1)S(1)} fusion(bf16[4096,192]{1,0:T(8,128)(2,1)S(1)} %copy.43, s32[1024]{0:T(1024)S(1)} %broadcast_clamp_fusion.1), kind=kCustom, calls=%fused_computation.2 | custom fusion | bytes 790528 | tf_op jit(solution)/shard_map/gather | solution.py:175
  32.7 1.8 %slice_bitcast_fusion = (bf16[192,1024]{1,0:T(8,128)(2,1)}, bf16[1024,192]{0,1:T(8,128)(2,1)S(1)}) fusion(bf16[4096,192]{0,1:T(8,128)(2,1)} %param.10), kind=kLoop, calls=%fused_computation.124 | loop fusion | bytes 1179648 | tf_op jit(solution)/shard_map/transpose | solution.py:158
  35.3 1.4 collective-permute-start.1
  37.0 3.9 %gather_fusion.3 = bf16[1024,192]{1,0:T(8,128)(2,1)S(1)} fusion(bf16[4096,192]{1,0:T(8,128)(2,1)S(1)} %copy.43, s32[1024]{0:T(1024)S(1)} %broadcast_clamp_fusion), kind=kCustom, calls=%fused_computation.3 | custom fusion | bytes 790528 | tf_op jit(solution)/shard_map/gather | solution.py:175
  44.1 3.2 %shard_map.129 = (f32[192,1024]{1,0:T(8,128)}, f32[8,1024]{1,0:T(8,128)}) custom-call(s32[1,1024]{1,0:T(1,128)} %get-tuple-element.44.tgt_ref, bf16[192,1024]{1,0:T(8,128)(2,1)} %bitcast.121, f32[192,1024]{1,0:T(8,128)} %broadcast_in_dim.4.sum_in, f32[8,1024]{1,0:T(8,128)} %broadcast_in_dim.5.cnt_in), custom_call_target="tpu_custom_call", output_to_operand_aliasing={{0}: (2, {}), {1}: (3, {})} | custom-call | flops 419430400 | bytes 2035712 | tf_op jit(solution)/shard_map/pallas_call | solution.py:46
  47.4 1.5 convert_reduce_fusion
  49.1 3.3 %shard_map.130 = (f32[192,1024]{1,0:T(8,128)}, f32[8,1024]{1,0:T(8,128)}) custom-call(s32[1,1024]{1,0:T(1,128)} %get-tuple-element.47.tgt_ref, bf16[192,1024]{1,0:T(8,128)(2,1)} %collective-permute-done.5.rec_ref, f32[192,1024]{1,0:T(8,128)} %get-tuple-element.12.sum_in, ...), custom_call_target="tpu_custom_call", output_to_operand_aliasing={{0}: (2, {}), {1}: (3, {})} | custom-call | flops 419430400 | bytes 2035712 | tf_op jit(solution)/shard_map/pallas_call | solution.py:46
  52.4 3.2 %collective-permute-done.4.rec_ref = bf16[192,1024]{1,0:T(8,128)(2,1)} collective-permute-done((bf16[192,1024]{1,0:T(8,128)(2,1)}, bf16[192,1024]{1,0:T(8,128)(2,1)}, u32[]{:S(2)}, u32[]{:S(2)}) %collective-permute-start.4) | collective-permute-done | bytes 393248 | tf_op jit(solution)/shard_map/ppermute | solution.py:177
  55.5 3.3 %shard_map.131 = (f32[192,1024]{1,0:T(8,128)}, f32[8,1024]{1,0:T(8,128)}) custom-call(s32[1,1024]{1,0:T(1,128)} %get-tuple-element.45.tgt_ref, bf16[192,1024]{1,0:T(8,128)(2,1)} %collective-permute-done.4.rec_ref, f32[192,1024]{1,0:T(8,128)} %get-tuple-element.14.sum_in, ...), custom_call_target="tpu_custom_call", output_to_operand_aliasing={{0}: (2, {}), {1}: (3, {})} | custom-call | flops 419430400 | bytes 2035712 | tf_op jit(solution)/shard_map/pallas_call | solution.py:46
  58.8 3.2 %shard_map.132 = (f32[192,1024]{1,0:T(8,128)}, f32[8,1024]{1,0:T(8,128)}) custom-call(s32[1,1024]{1,0:T(1,128)} %get-tuple-element.46.tgt_ref, bf16[192,1024]{1,0:T(8,128)(2,1)} %collective-permute-done.3.rec_ref, f32[192,1024]{1,0:T(8,128)} %get-tuple-element.16.sum_in, ...), custom_call_target="tpu_custom_call", output_to_operand_aliasing={{0}: (2, {}), {1}: (3, {})} | custom-call | flops 419430400 | bytes 2035712 | tf_op jit(solution)/shard_map/pallas_call | solution.py:46
  65.7 2.2 %fusion.61 = (bf16[4,192,1024]{2,1,0:T(8,128)(2,1)S(1)}, bf16[4,192,1024]{2,1,0:T(8,128)(2,1)S(1)}) fusion(bf16[4,384,1024]{2,1,0:T(8,128)(2,1)} %bitcast.117), kind=kLoop, calls=%fused_computation.127 | loop fusion | bytes 6291456 | tf_op jit(solution)/shard_map/slice | solution.py:153
  73.4 3.4 %multiply_convert_fusion.2 = (bf16[256,1024]{1,0:T(8,128)(2,1)}, f32[256,1024]{1,0:T(8,128)S(1)}) fusion(f32[1024]{0:T(1024)S(1)} %copy-done.10, bf16[256,1024]{1,0:T(8,128)(2,1)S(1)} %convolution_convert_fusion.1, bf16[1024,1024]{1,0:T(8,128)(2,1)} %all-gather.4.cloned.1.call-done), kind=kOutput, calls=%fused_computation.28 | convolution fusion | flops 538443776 | bytes 4198400 | tf_op jit(solution)/shard_map/dot_general | solution.py:197
  77.8 2.1 %multiply_convert_fusion = bf16[256,1024]{1,0:T(8,128)(2,1)} fusion(f32[256,1024]{1,0:T(8,128)S(1)} %fusion.4, f32[256,1024]{1,0:T(8,128)S(1)} %fusion.60, f32[256,256]{1,0:T(8,128)S(1)} %copy-done.4), kind=kOutput, calls=%fused_computation.26 | convolution fusion | flops 807927808 | bytes 2883584 | tf_op jit(solution)/shard_map/dot_general | solution.py:209
  81.9 2.0 %copy-done = f32[1024,1024]{1,0:T(8,128)} copy-done((f32[1024,1024]{1,0:T(8,128)}, f32[1024,1024]{1,0:T(8,128)S(1)}, u32[]{:S(2)}) %copy-start) | copy-done | bytes 4194328
  84.7 10.2 %collective-permute-done.9 = bf16[256,1024]{1,0:T(8,128)(2,1)S(1)} collective-permute-done((bf16[256,1024]{1,0:T(8,128)(2,1)}, bf16[256,1024]{1,0:T(8,128)(2,1)S(1)}, u32[]{:S(2)}, u32[]{:S(2)}) %collective-permute-start.9) | collective-permute-done | bytes 524320 | tf_op jit(solution)/shard_map/ppermute | solution.py:121
  97.1 2.2 %bitcast_add_fusion = f32[2,2,2,64,1024]{4,3,2,1,0:T(8,128)S(1)} fusion(bf16[2,2,2,64,1024]{4,3,2,1,0:T(8,128)(2,1)} %collective-permute-done.11, f32[2,2,2,2,64,1024]{5,4,3,2,1,0:T(8,128)} %bitcast.116, s32[]{:T(128)S(6)} %select_n.293), kind=kLoop, calls=%fused_computation.7 | loop fusion | flops 1048576 | bytes 5242884 | tf_op jit(solution)/shard_map/add | solution.py:95
  100.2 6.0 %collective-permute-start.12 = (bf16[2,2,64,1024]{3,2,1,0:T(8,128)(2,1)}, bf16[2,2,64,1024]{3,2,1,0:T(8,128)(2,1)}, u32[]{:S(2)}, u32[]{:S(2)}) collective-permute-start(bf16[2,2,64,1024]{3,2,1,0:T(8,128)(2,1)} %fusion.9), channel_id=1, source_target_pairs={{0,4},{1,5},{2,6},{3,7},{4,0},{5,1},{6,2},{7,3},{8,12},{9,13},{10,... | collective-permute-start | bytes 1572872 | tf_op jit(solution)/shard_map/ppermute | solution.py:94
  106.2 1.4 select_bitcast_fusion.1
  108.0 11.1 %collective-permute-done.12 = bf16[2,2,64,1024]{3,2,1,0:T(8,128)(2,1)} collective-permute-done((bf16[2,2,64,1024]{3,2,1,0:T(8,128)(2,1)}, bf16[2,2,64,1024]{3,2,1,0:T(8,128)(2,1)}, u32[]{:S(2)}, u32[]{:S(2)}) %collective-permute-start.12) | collective-permute-done | bytes 524320 | tf_op jit(solution)/shard_map/ppermute | solution.py:94
  120.4 3.7 %collective-permute-start.13 = (bf16[2,64,1024]{2,1,0:T(8,128)(2,1)S(1)}, bf16[2,64,1024]{2,1,0:T(8,128)(2,1)S(1)}, u32[]{:S(2)}, u32[]{:S(2)}) collective-permute-start(bf16[2,64,1024]{2,1,0:T(8,128)(2,1)S(1)} %fusion.31), channel_id=1, source_target_pairs={{0,8},{1,9},{2,10},{3,11},{4,12},{5,13},{6,14},{7,15},{8,0},{9,1},... | collective-permute-start | bytes 786440 | tf_op jit(solution)/shard_map/ppermute | solution.py:94
  124.1 1.9 %convolution_convert_fusion = bf16[384,1024]{1,0:T(8,128)(2,1)} fusion(bf16[1024,1024]{1,0:T(8,128)(2,1)S(1)} %bitcast.118, bf16[192,1024]{1,0:T(8,128)(2,1)S(1)} %copy-done.2, bf16[192,1024]{1,0:T(8,128)(2,1)S(1)} %divide_convert_fusion), kind=kOutput, calls=%fused_computation.9 | convolution fusion | flops 807272448 | bytes 3670016 | tf_op jit(solution)/shard_map/dot_general | solution.py:212
  126.0 18.1 %collective-permute-done.13 = bf16[2,64,1024]{2,1,0:T(8,128)(2,1)S(1)} collective-permute-done((bf16[2,64,1024]{2,1,0:T(8,128)(2,1)S(1)}, bf16[2,64,1024]{2,1,0:T(8,128)(2,1)S(1)}, u32[]{:S(2)}, u32[]{:S(2)}) %collective-permute-start.13) | collective-permute-done | bytes 262176 | tf_op jit(solution)/shard_map/ppermute | solution.py:94
  144.4 5.0 %collective-permute-done.14 = bf16[64,1024]{1,0:T(8,128)(2,1)S(1)} collective-permute-done((bf16[64,1024]{1,0:T(8,128)(2,1)S(1)}, bf16[64,1024]{1,0:T(8,128)(2,1)S(1)}, u32[]{:S(2)}, u32[]{:S(2)}) %collective-permute-start.14) | collective-permute-done | bytes 131104 | tf_op jit(solution)/shard_map/ppermute | solution.py:94
  149.4 5.8 %collective-permute-done.15 = bf16[64,1024]{1,0:T(8,128)(2,1)S(1)} collective-permute-done((bf16[64,1024]{1,0:T(8,128)(2,1)S(1)}, bf16[64,1024]{1,0:T(8,128)(2,1)S(1)}, u32[]{:S(2)}, u32[]{:S(2)}) %collective-permute-start.15) | collective-permute-done | bytes 131104 | tf_op jit(solution)/shard_map/ppermute | solution.py:121
  155.3 2.9 %collective-permute-start.16 = (bf16[2,64,1024]{2,1,0:T(8,128)(2,1)S(1)}, bf16[2,64,1024]{2,1,0:T(8,128)(2,1)S(1)}, u32[]{:S(2)}, u32[]{:S(2)}) collective-permute-start(bf16[2,64,1024]{2,1,0:T(8,128)(2,1)S(1)} %pad_maximum_fusion.3), channel_id=1, source_target_pairs={{0,4},{4,0},{8,12},{12,8},{1,5},{5,1},{9,13},{13,9},{2,6},{6,2},{1... | collective-permute-start | bytes 786440 | tf_op jit(solution)/shard_map/ppermute | solution.py:121
  158.2 4.4 %collective-permute-done.16 = bf16[2,64,1024]{2,1,0:T(8,128)(2,1)S(1)} collective-permute-done((bf16[2,64,1024]{2,1,0:T(8,128)(2,1)S(1)}, bf16[2,64,1024]{2,1,0:T(8,128)(2,1)S(1)}, u32[]{:S(2)}, u32[]{:S(2)}) %collective-permute-start.16) | collective-permute-done | bytes 262176 | tf_op jit(solution)/shard_map/ppermute | solution.py:121
  163.8 1.7 fusion.62
  (95 shorter events, 26.5 us)
Async XLA Ops:
  7.2 58.6 %all-gather.6.cloned.1.call-start = ((), (), s32[]{:S(2)}) async-start(), calls=%async_computation.3 | async-start | bytes 3932160 | tf_op jit(solution)/shard_map/all_gather | solution.py:151
  9.3 3.3 %copy-start.6 = (s32[1,4,1024]{2,1,0:T(4,128)S(1)}, s32[1,4,1024]{2,1,0:T(4,128)}, u32[]{:S(2)}) copy-start(s32[1,4,1024]{2,1,0:T(4,128)} %param.11) | copy-start | bytes 49156
  9.3 64.1 %all-gather.4.cloned.1.call-start = ((), (), s32[]{:S(2)}) async-start(), calls=%async_computation.1 | async-start | bytes 2621440 | tf_op jit(solution)/shard_map/all_gather | solution.py:154
  16.8 42.0 %collective-permute-start.3 = (bf16[192,1024]{1,0:T(8,128)(2,1)S(1)}, bf16[192,1024]{1,0:T(8,128)(2,1)}, u32[]{:S(2)}, u32[]{:S(2)}) collective-permute-start(bf16[192,1024]{1,0:T(8,128)(2,1)S(1)} %bitcast.120), channel_id=1, source_target_pairs={{0,12},{4,0},{8,4},{12,8},{1,13},{5,1},{9,5},{13,9},{2,14},{6,2},{... | collective-permute-start | bytes 1179656 | tf_op jit(solution)/shard_map/ppermute | solution.py:177
  26.8 28.8 %collective-permute-start.4 = (bf16[192,1024]{1,0:T(8,128)(2,1)}, bf16[192,1024]{1,0:T(8,128)(2,1)}, u32[]{:S(2)}, u32[]{:S(2)}) collective-permute-start(bf16[192,1024]{1,0:T(8,128)(2,1)} %bitcast.15), channel_id=1, source_target_pairs={{0,8},{4,12},{8,0},{12,4},{1,9},{5,13},{9,1},{13,5},{2,10},{6,14},... | collective-permute-start | bytes 1179656 | tf_op jit(solution)/shard_map/ppermute | solution.py:177
  31.7 17.2 %collective-permute-start.5 = (bf16[192,1024]{1,0:T(8,128)(2,1)}, bf16[192,1024]{1,0:T(8,128)(2,1)}, u32[]{:S(2)}, u32[]{:S(2)}) collective-permute-start(bf16[192,1024]{1,0:T(8,128)(2,1)} %bitcast.19), channel_id=1, source_target_pairs={{0,4},{4,8},{8,12},{12,0},{1,5},{5,9},{9,13},{13,1},{2,6},{6,10},{... | collective-permute-start | bytes 1179656 | tf_op jit(solution)/shard_map/ppermute | solution.py:177
  35.3 32.7 %collective-permute-start.2 = (bf16[192,256]{1,0:T(8,128)(2,1)}, bf16[192,256]{1,0:T(8,128)(2,1)}, u32[]{:S(2)}, u32[]{:S(2)}) collective-permute-start(bf16[192,256]{1,0:T(8,128)(2,1)} %get-tuple-element.34), channel_id=1, source_target_pairs={{0,3},{1,0},{2,1},{3,2},{4,7},{5,4},{6,5},{7,6},{8,11},{9,8},{10,9... | collective-permute-start | bytes 294920 | tf_op jit(solution)/shard_map/ppermute | solution.py:165
  35.3 34.6 %collective-permute-start.1 = (bf16[192,256]{1,0:T(8,128)(2,1)}, bf16[192,256]{1,0:T(8,128)(2,1)S(1)}, u32[]{:S(2)}, u32[]{:S(2)}) collective-permute-start(bf16[192,256]{1,0:T(8,128)(2,1)} %get-tuple-element.35), channel_id=1, source_target_pairs={{0,2},{1,3},{2,0},{3,1},{4,6},{5,7},{6,4},{7,5},{8,10},{9,11},{10,... | collective-permute-start | bytes 294920 | tf_op jit(solution)/shard_map/ppermute | solution.py:165
  36.8 127.0 %reduce-scatter.2.cloned.1.call-start = ((), (), s32[]{:S(2)}) async-start(), calls=%async_computation.2 | async-start | bytes 983040 | tf_op jit(solution)/shard_map/reduce_scatter | solution.py:216
  37.0 5.0 %copy-start.7 = (s32[1,4,1024]{2,1,0:T(4,128)S(1)}, s32[1,4,1024]{2,1,0:T(4,128)}, u32[]{:S(2)}) copy-start(s32[1,4,1024]{2,1,0:T(4,128)} %param.12) | copy-start | bytes 49156
  40.9 6.4 %copy-start.5 = (s32[256,15]{0,1:T(8,128)S(1)}, s32[256,15]{0,1:T(8,128)}, u32[]{:S(2)}) copy-start(s32[256,15]{0,1:T(8,128)} %param.18) | copy-start | bytes 46084
  48.9 21.7 %collective-permute-start = (bf16[192,256]{1,0:T(8,128)(2,1)}, bf16[192,256]{1,0:T(8,128)(2,1)S(1)}, u32[]{:S(2)}, u32[]{:S(2)}) collective-permute-start(bf16[192,256]{1,0:T(8,128)(2,1)} %get-tuple-element.33), channel_id=1, source_target_pairs={{0,1},{1,2},{2,3},{3,0},{4,5},{5,6},{6,7},{7,4},{8,9},{9,10},{10,1... | collective-permute-start | bytes 294920 | tf_op jit(solution)/shard_map/ppermute | solution.py:165
  64.1 6.8 %collective-permute-start.8 = (bf16[192,256]{1,0:T(8,128)(2,1)S(1)}, bf16[192,256]{1,0:T(8,128)(2,1)S(1)}, u32[]{:S(2)}, u32[]{:S(2)}) collective-permute-start(bf16[192,256]{1,0:T(8,128)(2,1)S(1)} %get-tuple-element.31), channel_id=1, source_target_pairs={{0,3},{1,0},{2,1},{3,2},{4,7},{5,4},{6,5},{7,6},{8,11},{9,8},{10,9... | collective-permute-start | bytes 294920 | tf_op jit(solution)/shard_map/ppermute | solution.py:189
  64.7 6.5 %collective-permute-start.7 = (bf16[192,256]{1,0:T(8,128)(2,1)S(1)}, bf16[192,256]{1,0:T(8,128)(2,1)S(1)}, u32[]{:S(2)}, u32[]{:S(2)}) collective-permute-start(bf16[192,256]{1,0:T(8,128)(2,1)S(1)} %get-tuple-element.32), channel_id=1, source_target_pairs={{0,2},{1,3},{2,0},{3,1},{4,6},{5,7},{6,4},{7,5},{8,10},{9,11},{10,... | collective-permute-start | bytes 294920 | tf_op jit(solution)/shard_map/ppermute | solution.py:189
  65.7 3.8 %copy-start.8 = (f32[1024]{0:T(1024)S(1)}, f32[1024]{0:T(1024)}, u32[]{:S(2)}) copy-start(f32[1024]{0:T(1024)} %param.15) | copy-start | bytes 12292
  67.9 4.3 %collective-permute-start.6 = (bf16[192,256]{1,0:T(8,128)(2,1)S(1)}, bf16[192,256]{1,0:T(8,128)(2,1)S(1)}, u32[]{:S(2)}, u32[]{:S(2)}) collective-permute-start(bf16[192,256]{1,0:T(8,128)(2,1)S(1)} %get-tuple-element.30), channel_id=1, source_target_pairs={{0,1},{1,2},{2,3},{3,0},{4,5},{5,6},{6,7},{7,4},{8,9},{9,10},{10,1... | collective-permute-start | bytes 294920 | tf_op jit(solution)/shard_map/ppermute | solution.py:189
  71.6 1.0 copy-start.3
  72.6 0.9 copy-start.10
  73.4 3.5 %copy-start.1 = (bf16[256,1024]{1,0:T(8,128)(2,1)S(1)}, bf16[256,1024]{1,0:T(8,128)(2,1)}, u32[]{:S(2)}) copy-start(bf16[256,1024]{1,0:T(8,128)(2,1)} %param.19) | copy-start | bytes 1572868
  73.4 3.4 %copy-start.9 = (bf16[1024,1024]{1,0:T(8,128)(2,1)S(1)}, bf16[1024,1024]{1,0:T(8,128)(2,1)}, u32[]{:S(2)}) copy-start(bf16[1024,1024]{1,0:T(8,128)(2,1)} %all-gather.4.cloned.1.call-done) | copy-start | bytes 6291460
  76.8 1.0 copy-start.4
  79.9 15.0 %collective-permute-start.9 = (bf16[256,1024]{1,0:T(8,128)(2,1)}, bf16[256,1024]{1,0:T(8,128)(2,1)S(1)}, u32[]{:S(2)}, u32[]{:S(2)}) collective-permute-start(bf16[256,1024]{1,0:T(8,128)(2,1)} %multiply_convert_fusion), channel_id=1, source_target_pairs={{0,2},{1,3},{2,0},{3,1},{4,6},{5,7},{6,4},{7,5},{8,10},{9,11},{10,... | collective-permute-start | bytes 1572872 | tf_op jit(solution)/shard_map/ppermute | solution.py:121
  81.9 2.0 %copy-start = (f32[1024,1024]{1,0:T(8,128)}, f32[1024,1024]{1,0:T(8,128)S(1)}, u32[]{:S(2)}) copy-start(f32[1024,1024]{1,0:T(8,128)S(1)} %fusion.59) | copy-start | bytes 12582916
  84.0 13.2 %collective-permute-start.11 = (bf16[2,2,2,64,1024]{4,3,2,1,0:T(8,128)(2,1)S(1)}, bf16[2,2,2,64,1024]{4,3,2,1,0:T(8,128)(2,1)}, u32[]{:S(2)}, u32[]{:S(2)}) collective-permute-start(bf16[2,2,2,64,1024]{4,3,2,1,0:T(8,128)(2,1)S(1)} %fusion.5), channel_id=1, source_target_pairs={{0,1},{1,0},{2,3},{3,2},{4,5},{5,4},{6,7},{7,6},{8,9},{9,8},{10,11... | collective-permute-start | bytes 3145736 | tf_op jit(solution)/shard_map/ppermute | solution.py:94
  97.1 9.1 %collective-permute-start.10 = (bf16[2,256,1024]{2,1,0:T(8,128)(2,1)}, bf16[2,256,1024]{2,1,0:T(8,128)(2,1)}, u32[]{:S(2)}, u32[]{:S(2)}) collective-permute-start(bf16[2,256,1024]{2,1,0:T(8,128)(2,1)} %pad_maximum_fusion.1), channel_id=1, source_target_pairs={{0,1},{1,0},{2,3},{3,2},{4,5},{5,4},{6,7},{7,6},{8,9},{9,8},{10,11... | collective-permute-start | bytes 3145736 | tf_op jit(solution)/shard_map/ppermute | solution.py:121
  100.2 18.9 %collective-permute-start.12 = (bf16[2,2,64,1024]{3,2,1,0:T(8,128)(2,1)}, bf16[2,2,64,1024]{3,2,1,0:T(8,128)(2,1)}, u32[]{:S(2)}, u32[]{:S(2)}) collective-permute-start(bf16[2,2,64,1024]{3,2,1,0:T(8,128)(2,1)} %fusion.9), channel_id=1, source_target_pairs={{0,4},{1,5},{2,6},{3,7},{4,0},{5,1},{6,2},{7,3},{8,12},{9,13},{10,... | collective-permute-start | bytes 1572872 | tf_op jit(solution)/shard_map/ppermute | solution.py:94
  107.9 16.2 %copy-start.2 = (bf16[192,1024]{1,0:T(8,128)(2,1)S(1)}, bf16[192,1024]{1,0:T(8,128)(2,1)}, u32[]{:S(2)}) copy-start(bf16[192,1024]{1,0:T(8,128)(2,1)} %get-tuple-element.24) | copy-start | bytes 1179652
  120.4 23.8 %collective-permute-start.13 = (bf16[2,64,1024]{2,1,0:T(8,128)(2,1)S(1)}, bf16[2,64,1024]{2,1,0:T(8,128)(2,1)S(1)}, u32[]{:S(2)}, u32[]{:S(2)}) collective-permute-start(bf16[2,64,1024]{2,1,0:T(8,128)(2,1)S(1)} %fusion.31), channel_id=1, source_target_pairs={{0,8},{1,9},{2,10},{3,11},{4,12},{5,13},{6,14},{7,15},{8,0},{9,1},... | collective-permute-start | bytes 786440 | tf_op jit(solution)/shard_map/ppermute | solution.py:94
  144.3 5.0 %collective-permute-start.14 = (bf16[64,1024]{1,0:T(8,128)(2,1)S(1)}, bf16[64,1024]{1,0:T(8,128)(2,1)S(1)}, u32[]{:S(2)}, u32[]{:S(2)}) collective-permute-start(bf16[64,1024]{1,0:T(8,128)(2,1)S(1)} %fusion.34), channel_id=1, source_target_pairs={{0,2},{1,3},{2,0},{3,1},{4,6},{5,7},{6,4},{7,5},{8,10},{9,11},{10,... | collective-permute-start | bytes 393224 | tf_op jit(solution)/shard_map/ppermute | solution.py:94
  149.3 5.9 %collective-permute-start.15 = (bf16[64,1024]{1,0:T(8,128)(2,1)S(1)}, bf16[64,1024]{1,0:T(8,128)(2,1)S(1)}, u32[]{:S(2)}, u32[]{:S(2)}) collective-permute-start(bf16[64,1024]{1,0:T(8,128)(2,1)S(1)} %fusion.32), channel_id=1, source_target_pairs={{0,8},{4,12},{8,0},{12,4},{1,9},{5,13},{9,1},{13,5},{2,10},{6,14},... | collective-permute-start | bytes 393224 | tf_op jit(solution)/shard_map/ppermute | solution.py:121
  155.3 7.2 %collective-permute-start.16 = (bf16[2,64,1024]{2,1,0:T(8,128)(2,1)S(1)}, bf16[2,64,1024]{2,1,0:T(8,128)(2,1)S(1)}, u32[]{:S(2)}, u32[]{:S(2)}) collective-permute-start(bf16[2,64,1024]{2,1,0:T(8,128)(2,1)S(1)} %pad_maximum_fusion.3), channel_id=1, source_target_pairs={{0,4},{4,0},{8,12},{12,8},{1,5},{5,1},{9,13},{13,9},{2,6},{6,2},{1... | collective-permute-start | bytes 786440 | tf_op jit(solution)/shard_map/ppermute | solution.py:121
Sparse Core Ops, SparseCore 0:
  9.6 32.1 all-gather.5
  43.4 23.0 all-gather.3
  126.2 23.2 reduce-scatter.1

commit v7 on v6

--- a/solution.py
+++ b/solution.py
@@ -96,18 +96,21 @@
     return cur
 
 
-def reduce_scatter_grid(x, n_dom, n_cols, send_dtype):
+def reduce_scatter_grid(x, n_dom, n_cols, send_dtype, carried):
     if not (_is_pow2(n_dom) and _is_pow2(n_cols)):
         part = reduce_scatter_blocks(x, "cols", n_cols, send_dtype)
-        return reduce_scatter_blocks(part, "dom", n_dom, send_dtype)
+        return reduce_scatter_blocks(part, "dom", n_dom, send_dtype), carried
     kc = n_cols.bit_length() - 1
     kd = n_dom.bit_length() - 1
     axis_bits = [kc - 1 - i for i in range(kc)] + [kc + kd - 1 - i for i in range(kd)]
     order = list(range(min(kc, 1))) + list(range(kc, kc + kd)) + list(range(1, kc))
     cur = x.reshape((2,) * (kc + kd) + x.shape[2:])
-    return _butterfly_reduce(
-        cur, ("dom", "cols"), n_dom * n_cols, axis_bits, order, send_dtype
-    )
+    axes = ("dom", "cols")
+    n = n_dom * n_cols
+    cur = _butterfly_reduce(cur, axes, n, axis_bits, order[:1], send_dtype)
+    cur, carried = lax.optimization_barrier((cur, carried))
+    rest = [b for b in axis_bits if b != order[0]]
+    return _butterfly_reduce(cur, axes, n, rest, order[1:], send_dtype), carried
 
 
 def all_gather_blocks(x, axis, n):
@@ -199,15 +202,19 @@
     slope_two = (out_cotangent.astype(jnp.float32) * swish_slope(pre_two)).astype(jnp.bfloat16)
 
     local_grad = contract_rows(upper_input, slope_two)
-    dom_rows = up_rows // n_dom
-    upper_part = reduce_scatter_grid(
-        local_grad.reshape(n_cols, n_dom, dom_rows, hidden), n_dom, n_cols, jnp.bfloat16
-    )
     back_mixed = lax.dot_general(
         slope_two, full_upper, (((1,), (1,)), ((), ())), preferred_element_type=jnp.float32
     )
     back_one = jnp.dot(mix_matrix.T, back_mixed, precision=lax.Precision.HIGHEST)
     slope_one = (back_one * swish_slope(pre_one)).astype(jnp.bfloat16)
+    dom_rows = up_rows // n_dom
+    upper_part, slope_one = reduce_scatter_grid(
+        local_grad.reshape(n_cols, n_dom, dom_rows, hidden),
+        n_dom,
+        n_cols,
+        jnp.bfloat16,
+        slope_one,
+    )
     slab_rows = all_gather_blocks(slope_one, "cols", n_cols).reshape(tgt_dev, hidden)
     stacked = jnp.dot(both_t, slab_rows, preferred_element_type=jnp.float32)
     dom_cols = hidden // n_dom

time: 173 us -> 166 us (0.960)
  waiting for transfers between devices: 58.5 us -> 51.9 us
  starting transfers between devices: 24.5 us -> 19.5 us
  local copies, waits for them, and re-layouts: 35 us -> 38.8 us
    ppermute x4, waiting for transfers between devices: 34.2 us -> 16.4 us  [_butterfly_reduce(): got = lax.ppermute(send.astype(send_dtype), axis, _xor_pairs(n, 1 << b))]
    ppermute x4, waiting for transfers between devices: 20.4 us -> 34.6 us  [all_gather_blocks(): got = lax.ppermute(cur, axis, _xor_pairs(n, 1 << b))]
    ppermute x4, starting transfers between devices: 4.01 us -> 0.81 us  [all_gather_blocks(): got = lax.ppermute(cur, axis, _xor_pairs(n, 1 << b))]
    ppermute x3, waiting for transfers between devices: 3.17 us -> 0.01 us  [local(): rows_t = lax.ppermute(rows_t, 'dom', _shift_pairs(n_dom, shift))]
    ppermute x4, starting transfers between devices: 10.5 us -> 7.71 us  [_butterfly_reduce(): got = lax.ppermute(send.astype(send_dtype), axis, _xor_pairs(n, 1 << b))]
    unnamed x23 -> x27, local copies, waits for them, and re-layouts: 5.17 us -> 7.8 us
  transfers between devices with their start and end apart: 20 -> 20, of which waited for: 8 -> 6; matrix products, arithmetic and copies ran while one was open for 28% -> 29% of each run, Pallas kernels for 8% -> 8%
where the time goes in v7:
time: 166 us; the launch traced here: 165 us
  waiting for transfers between devices  51.9 us (31%)
  local copies, waits for them, and re-layouts  38.8 us (23%)
  starting transfers between devices  19.5 us (12%)
  between operations  14.5 us (9%)
  matrix products  14.2 us (9%)
  other arithmetic  13.5 us (8%)
  Pallas kernels  13.1 us (8%)
    ppermute x4, waiting for transfers between devices, all_gather_blocks(): got = lax.ppermute(cur, axis, _xor_pairs(n, 1 << b))  34.6 us
    gather x8, local copies, waits for them, and re-layouts, local(): rows_t = features.at[slots].get(mode='promise_in_bounds').T  18.8 us
    ppermute x4, waiting for transfers between devices, _butterfly_reduce(): got = lax.ppermute(send.astype(send_dtype), axis, _xor_pairs(n, 1 << b))  16.4 us
    pallas_call x4, Pallas kernels, accumulate(): pl.pallas_call(_accumulate_kernel, out_shape=[jax.ShapeDtypeStruct(acc_su...  13.1 us
    unnamed x27, local copies, waits for them, and re-layouts  7.8 us
    ppermute x4, starting transfers between devices, _butterfly_reduce(): got = lax.ppermute(send.astype(send_dtype), axis, _xor_pairs(n, 1 << b))  7.71 us
    ppermute x3, starting transfers between devices, local(): rows_t = lax.ppermute(rows_t, 'dom', _shift_pairs(n_dom, shift))  7.01 us
    dot_general x9, matrix products, contract_rows(): lax.dot_general(left_mat, right_mat, (((0,), (0,)), ((), ())), preferred_...  4.4 us
  transfers between devices with their start and end apart: 20, of which 6 were waited for; matrix products, arithmetic and copies ran while one was open for 29% of the time, Pallas kernels for 8%

profile of v7, /device:TPU:0, one launch (start us, length us, event | category | flops | bytes accessed | tf_op | source)
XLA Modules:
  0.0 165.3 jit_solution(10933459308855671637)
XLA Ops:
  7.2 2.0 %pad_maximum_fusion.2 = bf16[384,1024]{1,0:T(8,128)(2,1)} fusion(bf16[192,1024]{1,0:T(8,128)(2,1)} %param.14, bf16[192,1024]{1,0:T(8,128)(2,1)} %param.13), kind=kLoop, calls=%fused_computation.32 | loop fusion | flops 1572864 | bytes 1572864 | tf_op jit(solution)/shard_map/concatenate | solution.py:153
  9.4 3.2 %copy.43 = bf16[4096,192]{1,0:T(8,128)(2,1)S(1)} copy(bf16[4096,192]{0,1:T(8,128)(2,1)} %param.10) | data formatting | bytes 3145728 | tf_op args[0]
  12.6 3.9 %gather_fusion.2 = bf16[1024,192]{1,0:T(8,128)(2,1)S(1)} fusion(bf16[4096,192]{1,0:T(8,128)(2,1)S(1)} %copy.43, s32[1024]{0:T(1024)S(1)} %broadcast_clamp_fusion.1), kind=kCustom, calls=%fused_computation.2 | custom fusion | bytes 790528 | tf_op jit(solution)/shard_map/gather | solution.py:178
  17.6 3.0 %collective-permute-start.5 = (bf16[192,1024]{1,0:T(8,128)(2,1)}, bf16[192,1024]{1,0:T(8,128)(2,1)}, u32[]{:S(2)}, u32[]{:S(2)}) collective-permute-start(bf16[192,1024]{1,0:T(8,128)(2,1)} %bitcast.19), channel_id=1, source_target_pairs={{0,4},{4,8},{8,12},{12,0},{1,5},{5,9},{9,13},{13,1},{2,6},{6,10},{... | collective-permute-start | bytes 1179656 | tf_op jit(solution)/shard_map/ppermute | solution.py:180
  20.6 3.9 %gather_fusion.1 = bf16[1024,192]{1,0:T(8,128)(2,1)S(1)} fusion(bf16[4096,192]{1,0:T(8,128)(2,1)S(1)} %copy.43, s32[1024]{0:T(1024)S(1)} %broadcast_clamp_fusion.2), kind=kCustom, calls=%fused_computation.1 | custom fusion | bytes 790528 | tf_op jit(solution)/shard_map/gather | solution.py:178
  25.5 2.6 %collective-permute-start.4 = (bf16[192,1024]{1,0:T(8,128)(2,1)}, bf16[192,1024]{1,0:T(8,128)(2,1)}, u32[]{:S(2)}, u32[]{:S(2)}) collective-permute-start(bf16[192,1024]{1,0:T(8,128)(2,1)} %bitcast.15), channel_id=1, source_target_pairs={{0,8},{4,12},{8,0},{12,4},{1,9},{5,13},{9,1},{13,5},{2,10},{6,14},... | collective-permute-start | bytes 1179656 | tf_op jit(solution)/shard_map/ppermute | solution.py:180
  28.1 3.9 %gather_fusion = bf16[1024,192]{1,0:T(8,128)(2,1)S(1)} fusion(bf16[4096,192]{1,0:T(8,128)(2,1)S(1)} %copy.43, s32[1024]{0:T(1024)S(1)} %broadcast_clamp_fusion.3), kind=kCustom, calls=%fused_computation | custom fusion | bytes 790528 | tf_op jit(solution)/shard_map/gather | solution.py:178
  32.2 1.4 collective-permute-start.3
  33.6 1.9 %slice_bitcast_fusion = (bf16[192,1024]{1,0:T(8,128)(2,1)}, bf16[1024,192]{0,1:T(8,128)(2,1)S(1)}) fusion(bf16[4096,192]{0,1:T(8,128)(2,1)} %param.10), kind=kLoop, calls=%fused_computation.124 | loop fusion | bytes 1179648 | tf_op jit(solution)/shard_map/transpose | solution.py:161
  36.3 1.4 collective-permute-start.1
  37.9 3.9 %gather_fusion.3 = bf16[1024,192]{1,0:T(8,128)(2,1)S(1)} fusion(bf16[4096,192]{1,0:T(8,128)(2,1)S(1)} %copy.43, s32[1024]{0:T(1024)S(1)} %broadcast_clamp_fusion), kind=kCustom, calls=%fused_computation.3 | custom fusion | bytes 790528 | tf_op jit(solution)/shard_map/gather | solution.py:178
  45.1 3.2 %shard_map.129 = (f32[192,1024]{1,0:T(8,128)}, f32[8,1024]{1,0:T(8,128)}) custom-call(s32[1,1024]{1,0:T(1,128)} %get-tuple-element.48.tgt_ref, bf16[192,1024]{1,0:T(8,128)(2,1)} %bitcast.121, f32[192,1024]{1,0:T(8,128)} %broadcast_in_dim.4.sum_in, f32[8,1024]{1,0:T(8,128)} %broadcast_in_dim.5.cnt_in), custom_call_target="tpu_custom_call", output_to_operand_aliasing={{0}: (2, {}), {1}: (3, {})} | custom-call | flops 419430400 | bytes 2035712 | tf_op jit(solution)/shard_map/pallas_call | solution.py:46
  48.3 1.5 convert_reduce_fusion
  50.0 3.3 %shard_map.130 = (f32[192,1024]{1,0:T(8,128)}, f32[8,1024]{1,0:T(8,128)}) custom-call(s32[1,1024]{1,0:T(1,128)} %get-tuple-element.51.tgt_ref, bf16[192,1024]{1,0:T(8,128)(2,1)} %collective-permute-done.5.rec_ref, f32[192,1024]{1,0:T(8,128)} %get-tuple-element.14.sum_in, ...), custom_call_target="tpu_custom_call", output_to_operand_aliasing={{0}: (2, {}), {1}: (3, {})} | custom-call | flops 419430400 | bytes 2035712 | tf_op jit(solution)/shard_map/pallas_call | solution.py:46
  53.3 3.2 %shard_map.131 = (f32[192,1024]{1,0:T(8,128)}, f32[8,1024]{1,0:T(8,128)}) custom-call(s32[1,1024]{1,0:T(1,128)} %get-tuple-element.49.tgt_ref, bf16[192,1024]{1,0:T(8,128)(2,1)} %collective-permute-done.4.rec_ref, f32[192,1024]{1,0:T(8,128)} %get-tuple-element.16.sum_in, ...), custom_call_target="tpu_custom_call", output_to_operand_aliasing={{0}: (2, {}), {1}: (3, {})} | custom-call | flops 419430400 | bytes 2035712 | tf_op jit(solution)/shard_map/pallas_call | solution.py:46
  56.6 3.3 %shard_map.132 = (f32[192,1024]{1,0:T(8,128)}, f32[8,1024]{1,0:T(8,128)}) custom-call(s32[1,1024]{1,0:T(1,128)} %get-tuple-element.50.tgt_ref, bf16[192,1024]{1,0:T(8,128)(2,1)} %collective-permute-done.3.rec_ref, f32[192,1024]{1,0:T(8,128)} %get-tuple-element.18.sum_in, ...), custom_call_target="tpu_custom_call", output_to_operand_aliasing={{0}: (2, {}), {1}: (3, {})} | custom-call | flops 419430400 | bytes 2035712 | tf_op jit(solution)/shard_map/pallas_call | solution.py:46
  63.8 2.2 %fusion.61 = (bf16[4,192,1024]{2,1,0:T(8,128)(2,1)S(1)}, bf16[4,192,1024]{2,1,0:T(8,128)(2,1)S(1)}) fusion(bf16[4,384,1024]{2,1,0:T(8,128)(2,1)} %bitcast.117), kind=kLoop, calls=%fused_computation.127 | loop fusion | bytes 6291456 | tf_op jit(solution)/shard_map/slice | solution.py:156
  71.5 3.3 %multiply_convert_fusion.2 = (bf16[256,1024]{1,0:T(8,128)(2,1)}, f32[256,1024]{1,0:T(8,128)S(1)}) fusion(f32[1024]{0:T(1024)S(1)} %copy-done.12, bf16[256,1024]{1,0:T(8,128)(2,1)S(1)} %convolution_convert_fusion.1, bf16[1024,1024]{1,0:T(8,128)(2,1)} %all-gather.4.cloned.1.call-done), kind=kOutput, calls=%fused_computation.28 | convolution fusion | flops 538443776 | bytes 4198400 | tf_op jit(solution)/shard_map/dot_general | solution.py:200
  75.7 1.9 %copy-done = f32[1024,1024]{1,0:T(8,128)} copy-done((f32[1024,1024]{1,0:T(8,128)}, f32[1024,1024]{1,0:T(8,128)S(1)}, u32[]{:S(2)}) %copy-start) | copy-done | bytes 4194328
  78.8 1.3 collective-permute-start.9
  80.1 2.5 %fusion.59 = f32[256,1024]{1,0:T(8,128)S(1)} fusion(bf16[1024,1024]{1,0:T(8,128)(2,1)} %all-gather.4.cloned.1.call-done, f32[256,1024]{1,0:T(8,128)S(1)} %get-tuple-element.53, bf16[256,1024]{1,0:T(8,128)(2,1)S(1)} %copy-done.3), kind=kOutput, calls=%fused_computation.125 | convolution fusion | flops 539492352 | bytes 4718592 | tf_op jit(solution)/shard_map/dot_general | solution.py:205
  84.8 1.6 bitcast_add_fusion
  88.0 2.5 %collective-permute-start.12 = (bf16[2,2,64,1024]{3,2,1,0:T(8,128)(2,1)}, bf16[2,2,64,1024]{3,2,1,0:T(8,128)(2,1)}, u32[]{:S(2)}, u32[]{:S(2)}) collective-permute-start(bf16[2,2,64,1024]{3,2,1,0:T(8,128)(2,1)} %fusion.9), channel_id=1, source_target_pairs={{0,4},{1,5},{2,6},{3,7},{4,0},{5,1},{6,2},{7,3},{8,12},{9,13},{10,... | collective-permute-start | bytes 1572872 | tf_op jit(solution)/shard_map/ppermute | solution.py:94
  90.4 10.0 %collective-permute-done.10 = bf16[256,1024]{1,0:T(8,128)(2,1)} collective-permute-done((bf16[256,1024]{1,0:T(8,128)(2,1)S(1)}, bf16[256,1024]{1,0:T(8,128)(2,1)}, u32[]{:S(2)}, u32[]{:S(2)}) %collective-permute-start.10) | collective-permute-done | bytes 524320 | tf_op jit(solution)/shard_map/ppermute | solution.py:124
  105.0 3.3 %collective-permute-start.13 = (bf16[2,64,1024]{2,1,0:T(8,128)(2,1)S(1)}, bf16[2,64,1024]{2,1,0:T(8,128)(2,1)S(1)}, u32[]{:S(2)}, u32[]{:S(2)}) collective-permute-start(bf16[2,64,1024]{2,1,0:T(8,128)(2,1)S(1)} %fusion.31), channel_id=1, source_target_pairs={{0,8},{1,9},{2,10},{3,11},{4,12},{5,13},{6,14},{7,15},{8,0},{9,1},... | collective-permute-start | bytes 786440 | tf_op jit(solution)/shard_map/ppermute | solution.py:94
  108.3 12.0 %collective-permute-done.13 = bf16[2,64,1024]{2,1,0:T(8,128)(2,1)S(1)} collective-permute-done((bf16[2,64,1024]{2,1,0:T(8,128)(2,1)S(1)}, bf16[2,64,1024]{2,1,0:T(8,128)(2,1)S(1)}, u32[]{:S(2)}, u32[]{:S(2)}) %collective-permute-start.13) | collective-permute-done | bytes 262176 | tf_op jit(solution)/shard_map/ppermute | solution.py:94
  121.5 1.4 select_bitcast_fusion.1
  124.0 1.9 %convolution_convert_fusion = bf16[384,1024]{1,0:T(8,128)(2,1)} fusion(bf16[1024,1024]{1,0:T(8,128)(2,1)S(1)} %bitcast.118, bf16[192,1024]{1,0:T(8,128)(2,1)S(1)} %copy-done.5, bf16[192,1024]{1,0:T(8,128)(2,1)S(1)} %divide_convert_fusion), kind=kOutput, calls=%fused_computation.9 | convolution fusion | flops 807272448 | bytes 3670016 | tf_op jit(solution)/shard_map/dot_general | solution.py:219
  126.6 4.4 %collective-permute-done.14 = bf16[64,1024]{1,0:T(8,128)(2,1)S(1)} collective-permute-done((bf16[64,1024]{1,0:T(8,128)(2,1)S(1)}, bf16[64,1024]{1,0:T(8,128)(2,1)S(1)}, u32[]{:S(2)}, u32[]{:S(2)}) %collective-permute-start.14) | collective-permute-done | bytes 131104 | tf_op jit(solution)/shard_map/ppermute | solution.py:94
  131.1 14.5 %collective-permute-done.15 = bf16[64,1024]{1,0:T(8,128)(2,1)S(1)} collective-permute-done((bf16[64,1024]{1,0:T(8,128)(2,1)S(1)}, bf16[64,1024]{1,0:T(8,128)(2,1)S(1)}, u32[]{:S(2)}, u32[]{:S(2)}) %collective-permute-start.15) | collective-permute-done | bytes 131104 | tf_op jit(solution)/shard_map/ppermute | solution.py:124
  145.8 10.1 %collective-permute-done.16 = bf16[2,64,1024]{2,1,0:T(8,128)(2,1)S(1)} collective-permute-done((bf16[2,64,1024]{2,1,0:T(8,128)(2,1)S(1)}, bf16[2,64,1024]{2,1,0:T(8,128)(2,1)S(1)}, u32[]{:S(2)}, u32[]{:S(2)}) %collective-permute-start.16) | collective-permute-done | bytes 262176 | tf_op jit(solution)/shard_map/ppermute | solution.py:124
  157.1 1.7 %fusion.62 = (f32[192,256]{1,0:T(8,128)}, f32[192,256]{1,0:T(8,128)}) fusion(bf16[384,256]{1,0:T(8,128)(2,1)} %reduce-scatter.2.cloned.1.call-done), kind=kLoop, calls=%fused_computation.128 | loop fusion | bytes 786432 | tf_op jit(solution)/shard_map/slice | solution.py:227
  (99 shorter events, 30.5 us)
Async XLA Ops:
  7.2 56.6 %all-gather.6.cloned.1.call-start = ((), (), s32[]{:S(2)}) async-start(), calls=%async_computation.3 | async-start | bytes 3932160 | tf_op jit(solution)/shard_map/all_gather | solution.py:154
  9.3 3.3 %copy-start.9 = (s32[1,4,1024]{2,1,0:T(4,128)S(1)}, s32[1,4,1024]{2,1,0:T(4,128)}, u32[]{:S(2)}) copy-start(s32[1,4,1024]{2,1,0:T(4,128)} %param.11) | copy-start | bytes 49156
  9.3 62.2 %all-gather.4.cloned.1.call-start = ((), (), s32[]{:S(2)}) async-start(), calls=%async_computation.1 | async-start | bytes 2621440 | tf_op jit(solution)/shard_map/all_gather | solution.py:157
  17.6 32.2 %collective-permute-start.5 = (bf16[192,1024]{1,0:T(8,128)(2,1)}, bf16[192,1024]{1,0:T(8,128)(2,1)}, u32[]{:S(2)}, u32[]{:S(2)}) collective-permute-start(bf16[192,1024]{1,0:T(8,128)(2,1)} %bitcast.19), channel_id=1, source_target_pairs={{0,4},{4,8},{8,12},{12,0},{1,5},{5,9},{9,13},{13,1},{2,6},{6,10},{... | collective-permute-start | bytes 1179656 | tf_op jit(solution)/shard_map/ppermute | solution.py:180
  25.5 27.9 %collective-permute-start.4 = (bf16[192,1024]{1,0:T(8,128)(2,1)}, bf16[192,1024]{1,0:T(8,128)(2,1)}, u32[]{:S(2)}, u32[]{:S(2)}) collective-permute-start(bf16[192,1024]{1,0:T(8,128)(2,1)} %bitcast.15), channel_id=1, source_target_pairs={{0,8},{4,12},{8,0},{12,4},{1,9},{5,13},{9,1},{13,5},{2,10},{6,14},... | collective-permute-start | bytes 1179656 | tf_op jit(solution)/shard_map/ppermute | solution.py:180
  32.2 24.4 %collective-permute-start.3 = (bf16[192,1024]{1,0:T(8,128)(2,1)S(1)}, bf16[192,1024]{1,0:T(8,128)(2,1)}, u32[]{:S(2)}, u32[]{:S(2)}) collective-permute-start(bf16[192,1024]{1,0:T(8,128)(2,1)S(1)} %bitcast.120), channel_id=1, source_target_pairs={{0,12},{4,0},{8,4},{12,8},{1,13},{5,1},{9,5},{13,9},{2,14},{6,2},{... | collective-permute-start | bytes 1179656 | tf_op jit(solution)/shard_map/ppermute | solution.py:180
  36.2 29.8 %collective-permute-start.2 = (bf16[192,256]{1,0:T(8,128)(2,1)}, bf16[192,256]{1,0:T(8,128)(2,1)}, u32[]{:S(2)}, u32[]{:S(2)}) collective-permute-start(bf16[192,256]{1,0:T(8,128)(2,1)} %get-tuple-element.38), channel_id=1, source_target_pairs={{0,3},{1,0},{2,1},{3,2},{4,7},{5,4},{6,5},{7,6},{8,11},{9,8},{10,9... | collective-permute-start | bytes 294920 | tf_op jit(solution)/shard_map/ppermute | solution.py:168
  36.3 31.6 %collective-permute-start.1 = (bf16[192,256]{1,0:T(8,128)(2,1)}, bf16[192,256]{1,0:T(8,128)(2,1)S(1)}, u32[]{:S(2)}, u32[]{:S(2)}) collective-permute-start(bf16[192,256]{1,0:T(8,128)(2,1)} %get-tuple-element.39), channel_id=1, source_target_pairs={{0,2},{1,3},{2,0},{3,1},{4,6},{5,7},{6,4},{7,5},{8,10},{9,11},{10,... | collective-permute-start | bytes 294920 | tf_op jit(solution)/shard_map/ppermute | solution.py:168
  37.7 119.4 %reduce-scatter.2.cloned.1.call-start = ((), (), s32[]{:S(2)}) async-start(), calls=%async_computation.2 | async-start | bytes 983040 | tf_op jit(solution)/shard_map/reduce_scatter | solution.py:223
  37.9 4.9 %copy-start.10 = (s32[1,4,1024]{2,1,0:T(4,128)S(1)}, s32[1,4,1024]{2,1,0:T(4,128)}, u32[]{:S(2)}) copy-start(s32[1,4,1024]{2,1,0:T(4,128)} %param.12) | copy-start | bytes 49156
  41.9 6.4 %copy-start.8 = (s32[256,15]{0,1:T(8,128)S(1)}, s32[256,15]{0,1:T(8,128)}, u32[]{:S(2)}) copy-start(s32[256,15]{0,1:T(8,128)} %param.18) | copy-start | bytes 46084
  49.8 18.7 %collective-permute-start = (bf16[192,256]{1,0:T(8,128)(2,1)}, bf16[192,256]{1,0:T(8,128)(2,1)S(1)}, u32[]{:S(2)}, u32[]{:S(2)}) collective-permute-start(bf16[192,256]{1,0:T(8,128)(2,1)} %get-tuple-element.37), channel_id=1, source_target_pairs={{0,1},{1,2},{2,3},{3,0},{4,5},{5,6},{6,7},{7,4},{8,9},{9,10},{10,1... | collective-permute-start | bytes 294920 | tf_op jit(solution)/shard_map/ppermute | solution.py:168
  61.9 7.0 %collective-permute-start.7 = (bf16[192,256]{1,0:T(8,128)(2,1)S(1)}, bf16[192,256]{1,0:T(8,128)(2,1)S(1)}, u32[]{:S(2)}, u32[]{:S(2)}) collective-permute-start(bf16[192,256]{1,0:T(8,128)(2,1)S(1)} %get-tuple-element.36), channel_id=1, source_target_pairs={{0,2},{1,3},{2,0},{3,1},{4,6},{5,7},{6,4},{7,5},{8,10},{9,11},{10,... | collective-permute-start | bytes 294920 | tf_op jit(solution)/shard_map/ppermute | solution.py:192
  62.6 6.6 %collective-permute-start.8 = (bf16[192,256]{1,0:T(8,128)(2,1)S(1)}, bf16[192,256]{1,0:T(8,128)(2,1)S(1)}, u32[]{:S(2)}, u32[]{:S(2)}) collective-permute-start(bf16[192,256]{1,0:T(8,128)(2,1)S(1)} %get-tuple-element.35), channel_id=1, source_target_pairs={{0,3},{1,0},{2,1},{3,2},{4,7},{5,4},{6,5},{7,6},{8,11},{9,8},{10,9... | collective-permute-start | bytes 294920 | tf_op jit(solution)/shard_map/ppermute | solution.py:192
  63.8 3.7 %copy-start.11 = (f32[1024]{0:T(1024)S(1)}, f32[1024]{0:T(1024)}, u32[]{:S(2)}) copy-start(f32[1024]{0:T(1024)} %param.15) | copy-start | bytes 12292
  66.1 4.3 %collective-permute-start.6 = (bf16[192,256]{1,0:T(8,128)(2,1)S(1)}, bf16[192,256]{1,0:T(8,128)(2,1)S(1)}, u32[]{:S(2)}, u32[]{:S(2)}) collective-permute-start(bf16[192,256]{1,0:T(8,128)(2,1)S(1)} %get-tuple-element.34), channel_id=1, source_target_pairs={{0,1},{1,2},{2,3},{3,0},{4,5},{5,6},{6,7},{7,4},{8,9},{9,10},{10,1... | collective-permute-start | bytes 294920 | tf_op jit(solution)/shard_map/ppermute | solution.py:192
  69.6 1.1 copy-start.6
  71.5 3.3 %copy-start.3 = (bf16[256,1024]{1,0:T(8,128)(2,1)S(1)}, bf16[256,1024]{1,0:T(8,128)(2,1)}, u32[]{:S(2)}) copy-start(bf16[256,1024]{1,0:T(8,128)(2,1)} %param.19) | copy-start | bytes 1572868
  75.7 2.0 %copy-start = (f32[1024,1024]{1,0:T(8,128)}, f32[1024,1024]{1,0:T(8,128)S(1)}, u32[]{:S(2)}) copy-start(f32[1024,1024]{1,0:T(8,128)S(1)} %fusion.60) | copy-start | bytes 12582916
  78.8 5.2 %collective-permute-start.9 = (bf16[2,2,2,64,1024]{4,3,2,1,0:T(8,128)(2,1)}, bf16[2,2,2,64,1024]{4,3,2,1,0:T(8,128)(2,1)}, u32[]{:S(2)}, u32[]{:S(2)}) collective-permute-start(bf16[2,2,2,64,1024]{4,3,2,1,0:T(8,128)(2,1)} %fusion.5), channel_id=1, source_target_pairs={{0,1},{1,0},{2,3},{3,2},{4,5},{5,4},{6,7},{7,6},{8,9},{9,8},{10,11... | collective-permute-start | bytes 3145736 | tf_op jit(solution)/shard_map/ppermute | solution.py:94
  80.1 2.5 %copy-start.7 = (f32[256,256]{1,0:T(8,128)S(1)}, f32[256,256]{1,0:T(8,128)}, u32[]{:S(2)}) copy-start(f32[256,256]{1,0:T(8,128)} %convert_reduce_fusion) | copy-start | bytes 786436
  82.7 2.2 %copy-start.1 = (f32[1024,1024]{1,0:T(8,128)S(1)}, f32[1024,1024]{1,0:T(8,128)}, u32[]{:S(2)}) copy-start(f32[1024,1024]{1,0:T(8,128)} %copy-done) | copy-start | bytes 12582916
  84.0 2.4 %copy-start.4 = (bf16[256,1024]{1,0:T(8,128)(2,1)}, bf16[256,1024]{1,0:T(8,128)(2,1)S(1)}, u32[]{:S(2)}) copy-start(bf16[256,1024]{1,0:T(8,128)(2,1)S(1)} %multiply_convert_fusion) | copy-start | bytes 1572868
  86.4 14.0 %collective-permute-start.10 = (bf16[256,1024]{1,0:T(8,128)(2,1)S(1)}, bf16[256,1024]{1,0:T(8,128)(2,1)}, u32[]{:S(2)}, u32[]{:S(2)}) collective-permute-start(bf16[256,1024]{1,0:T(8,128)(2,1)S(1)} %multiply_convert_fusion), channel_id=1, source_target_pairs={{0,2},{1,3},{2,0},{3,1},{4,6},{5,7},{6,4},{7,5},{8,10},{9,11},{10,... | collective-permute-start | bytes 1572872 | tf_op jit(solution)/shard_map/ppermute | solution.py:124
  88.0 14.8 %collective-permute-start.12 = (bf16[2,2,64,1024]{3,2,1,0:T(8,128)(2,1)}, bf16[2,2,64,1024]{3,2,1,0:T(8,128)(2,1)}, u32[]{:S(2)}, u32[]{:S(2)}) collective-permute-start(bf16[2,2,64,1024]{3,2,1,0:T(8,128)(2,1)} %fusion.9), channel_id=1, source_target_pairs={{0,4},{1,5},{2,6},{3,7},{4,0},{5,1},{6,2},{7,3},{8,12},{9,13},{10,... | collective-permute-start | bytes 1572872 | tf_op jit(solution)/shard_map/ppermute | solution.py:94
  102.8 18.7 %collective-permute-start.11 = (bf16[2,256,1024]{2,1,0:T(8,128)(2,1)}, bf16[2,256,1024]{2,1,0:T(8,128)(2,1)}, u32[]{:S(2)}, u32[]{:S(2)}) collective-permute-start(bf16[2,256,1024]{2,1,0:T(8,128)(2,1)} %pad_maximum_fusion.1), channel_id=1, source_target_pairs={{0,1},{1,0},{2,3},{3,2},{4,5},{5,4},{6,7},{7,6},{8,9},{9,8},{10,11... | collective-permute-start | bytes 3145736 | tf_op jit(solution)/shard_map/ppermute | solution.py:124
  104.0 1.0 copy-start.2
  105.0 15.3 %collective-permute-start.13 = (bf16[2,64,1024]{2,1,0:T(8,128)(2,1)S(1)}, bf16[2,64,1024]{2,1,0:T(8,128)(2,1)S(1)}, u32[]{:S(2)}, u32[]{:S(2)}) collective-permute-start(bf16[2,64,1024]{2,1,0:T(8,128)(2,1)S(1)} %fusion.31), channel_id=1, source_target_pairs={{0,8},{1,9},{2,10},{3,11},{4,12},{5,13},{6,14},{7,15},{8,0},{9,1},... | collective-permute-start | bytes 786440 | tf_op jit(solution)/shard_map/ppermute | solution.py:94
  123.0 1.0 copy-start.5
  126.0 5.0 %collective-permute-start.14 = (bf16[64,1024]{1,0:T(8,128)(2,1)S(1)}, bf16[64,1024]{1,0:T(8,128)(2,1)S(1)}, u32[]{:S(2)}, u32[]{:S(2)}) collective-permute-start(bf16[64,1024]{1,0:T(8,128)(2,1)S(1)} %fusion.34), channel_id=1, source_target_pairs={{0,2},{1,3},{2,0},{3,1},{4,6},{5,7},{6,4},{7,5},{8,10},{9,11},{10,... | collective-permute-start | bytes 393224 | tf_op jit(solution)/shard_map/ppermute | solution.py:94
  131.0 14.6 %collective-permute-start.15 = (bf16[64,1024]{1,0:T(8,128)(2,1)S(1)}, bf16[64,1024]{1,0:T(8,128)(2,1)S(1)}, u32[]{:S(2)}, u32[]{:S(2)}) collective-permute-start(bf16[64,1024]{1,0:T(8,128)(2,1)S(1)} %fusion.32), channel_id=1, source_target_pairs={{0,8},{4,12},{8,0},{12,4},{1,9},{5,13},{9,1},{13,5},{2,10},{6,14},... | collective-permute-start | bytes 393224 | tf_op jit(solution)/shard_map/ppermute | solution.py:124
  145.7 10.2 %collective-permute-start.16 = (bf16[2,64,1024]{2,1,0:T(8,128)(2,1)S(1)}, bf16[2,64,1024]{2,1,0:T(8,128)(2,1)S(1)}, u32[]{:S(2)}, u32[]{:S(2)}) collective-permute-start(bf16[2,64,1024]{2,1,0:T(8,128)(2,1)S(1)} %pad_maximum_fusion.3), channel_id=1, source_target_pairs={{0,4},{4,0},{8,12},{12,8},{1,5},{5,1},{9,13},{13,9},{2,6},{6,2},{1... | collective-permute-start | bytes 786440 | tf_op jit(solution)/shard_map/ppermute | solution.py:124
  (1 other events, 0.9 us)
Sparse Core Ops, SparseCore 0:
  9.6 31.2 all-gather.5
  42.4 26.1 all-gather.3
  126.1 27.4 reduce-scatter.1

commit v8 on v7

--- a/solution.py
+++ b/solution.py
@@ -115,17 +115,21 @@
 
 def all_gather_blocks(x, axis, n):
     if not _is_pow2(n):
-        return lax.all_gather(x, axis, axis=0, tiled=False)
+        return jax.tree.map(lambda leaf: lax.all_gather(leaf, axis, axis=0, tiled=False), x)
     me = lax.axis_index(axis)
     k = n.bit_length() - 1
     cur = x
     for b in reversed(range(k)):
         mine = (me >> b) & 1
         got = lax.ppermute(cur, axis, _xor_pairs(n, 1 << b))
-        low = jnp.where(mine == 0, cur, got)
-        high = jnp.where(mine == 0, got, cur)
-        cur = jnp.stack([low, high], axis=k - 1 - b)
-    return cur.reshape((n,) + x.shape)
+
+        def join(held, came, b=b, mine=mine):
+            low = jnp.where(mine == 0, held, came)
+            high = jnp.where(mine == 0, came, held)
+            return jnp.stack([low, high], axis=k - 1 - b)
+
+        cur = jax.tree.map(join, cur, got)
+    return jax.tree.map(lambda leaf, orig: leaf.reshape((n,) + orig.shape), cur, x)
 
 
 def local(
@@ -150,11 +154,10 @@
     w_rows = neigh_weight.shape[0]
     up_rows = upper_weight.shape[0]
 
-    packed = jnp.concatenate([neigh_weight, self_weight], axis=0)
-    gathered = lax.all_gather(packed, "cols", axis=0, tiled=False)
-    neigh_full = gathered[:, :w_rows]
-    self_full = gathered[:, w_rows:]
-    full_upper = lax.all_gather(upper_weight, "cols", axis=0, tiled=True)
+    neigh_full, self_full, full_upper = all_gather_blocks(
+        (neigh_weight, self_weight, upper_weight), "cols", n_cols
+    )
+    full_upper = full_upper.reshape(n_cols * up_rows, hidden)
 
     me_dom = lax.axis_index("dom")
     me_col = lax.axis_index("cols")
@@ -220,9 +223,12 @@
     dom_cols = hidden // n_dom
     grad_upper = all_gather_blocks(upper_part.astype(jnp.bfloat16), "dom", n_dom)
     grad_upper = grad_upper.reshape(up_rows, hidden).astype(jnp.float32)
-    grad_layer = lax.psum_scatter(
-        stacked.astype(jnp.bfloat16), "dom", scatter_dimension=1, tiled=True
-    ).astype(jnp.float32)
+    grad_layer = reduce_scatter_blocks(
+        jnp.swapaxes(stacked.reshape(2 * width, n_dom, dom_cols), 0, 1),
+        "dom",
+        n_dom,
+        jnp.bfloat16,
+    )
     grad_neigh = grad_layer[:w_rows]
     grad_self = grad_layer[w_rows:]
     return (hidden_two, grad_neigh, grad_self, grad_upper)

time: 166 us -> 163 us (0.982)
  between operations: 14.5 us -> 1.42 us
  starting transfers between devices: 19.5 us -> 23.6 us
  other arithmetic: 13.5 us -> 16.3 us
  waiting for transfers between devices: 51.9 us -> 54.1 us
    ppermute x4 -> x10, waiting for transfers between devices: 34.6 us -> 19 us  [all_gather_blocks(): got = lax.ppermute(cur, axis, _xor_pairs(n, 1 << b))]
    ppermute x4 -> x6, waiting for transfers between devices: 16.4 us -> 31.6 us  [_butterfly_reduce(): got = lax.ppermute(send.astype(send_dtype), axis, _xor_pairs(n, 1 << b))]
    ppermute x4 -> x10, starting transfers between devices: 0.81 us -> 7.74 us  [all_gather_blocks(): got = lax.ppermute(cur, axis, _xor_pairs(n, 1 << b))]
    another operation x7 -> x18, other arithmetic: 3.99 us -> 8.7 us  [join(): return jnp.stack([low, high], axis=k - 1 - b)]
    ppermute x3, waiting for transfers between devices: 0.01 us -> 3.49 us  [local(): rows_t = lax.ppermute(rows_t, 'dom', _shift_pairs(n_dom, shift))]
    dot_general x0 -> x1, local copies, waits for them, and re-layouts: none -> 2.6 us  [local(): stacked = jnp.dot(both_t, slab_rows, preferred_element_type=jnp.float32)]
    ppermute x4 -> x6, starting transfers between devices: 7.71 us -> 5.12 us  [_butterfly_reduce(): got = lax.ppermute(send.astype(send_dtype), axis, _xor_pairs(n, 1 << b))]
    slice x1 -> x0, local copies, waits for them, and re-layouts: 2.25 us -> none  [local(): self_full = gathered[:, w_rows:]]
  transfers between devices with their start and end apart: 20 -> 25, of which waited for: 6 -> 8; matrix products, arithmetic and copies ran while one was open for 29% -> 34% of each run, Pallas kernels for 8% -> 8%
where the time goes in v8:
time: 163 us; the launch traced here: 162 us
  waiting for transfers between devices  54.1 us (33%)
  local copies, waits for them, and re-layouts  39.8 us (24%)
  starting transfers between devices  23.6 us (14%)
  other arithmetic  16.3 us (10%)
  matrix products  14 us (9%)
  Pallas kernels  13 us (8%)
    ppermute x6, waiting for transfers between devices, _butterfly_reduce(): got = lax.ppermute(send.astype(send_dtype), axis, _xor_pairs(n, 1 << b))  31.6 us
    ppermute x10, waiting for transfers between devices, all_gather_blocks(): got = lax.ppermute(cur, axis, _xor_pairs(n, 1 << b))  19 us
    gather x8, local copies, waits for them, and re-layouts, local(): rows_t = features.at[slots].get(mode='promise_in_bounds').T  18.8 us
    pallas_call x4, Pallas kernels, accumulate(): pl.pallas_call(_accumulate_kernel, out_shape=[jax.ShapeDtypeStruct(acc_su...  13 us
    unnamed x35, local copies, waits for them, and re-layouts  9.24 us
    another operation x18, other arithmetic, join(): return jnp.stack([low, high], axis=k - 1 - b)  8.7 us
    ppermute x10, starting transfers between devices, all_gather_blocks(): got = lax.ppermute(cur, axis, _xor_pairs(n, 1 << b))  7.74 us
    ppermute x3, starting transfers between devices, local(): rows_t = lax.ppermute(rows_t, 'dom', _shift_pairs(n_dom, shift))  5.81 us
  transfers between devices with their start and end apart: 25, of which 8 were waited for; matrix products, arithmetic and copies ran while one was open for 34% of the time, Pallas kernels for 8%

profile of v8, /device:TPU:0, one launch (start us, length us, event | category | flops | bytes accessed | tf_op | source)
XLA Modules:
  0.0 162.3 jit_solution(11088418830372010691)
XLA Ops:
  0.7 1.8 %slice_bitcast_fusion = (bf16[192,1024]{1,0:T(8,128)(2,1)}, bf16[1024,192]{0,1:T(8,128)(2,1)S(1)}) fusion(bf16[4096,192]{0,1:T(8,128)(2,1)} %param.10), kind=kLoop, calls=%fused_computation.147 | loop fusion | bytes 1179648 | tf_op jit(solution)/shard_map/transpose | solution.py:164
  3.2 2.4 %collective-permute-start.4 = (bf16[192,256]{1,0:T(8,128)(2,1)}, bf16[192,256]{1,0:T(8,128)(2,1)}, u32[]{:S(2)}, u32[]{:S(2)}) collective-permute-start(bf16[192,256]{1,0:T(8,128)(2,1)} %get-tuple-element.50), channel_id=1, source_target_pairs={{0,3},{1,0},{2,1},{3,2},{4,7},{5,4},{6,5},{7,6},{8,11},{9,8},{10,9... | collective-permute-start | bytes 294920 | tf_op jit(solution)/shard_map/ppermute | solution.py:171
  7.6 3.1 %copy.50 = bf16[4096,192]{1,0:T(8,128)(2,1)S(1)} copy(bf16[4096,192]{0,1:T(8,128)(2,1)} %param.10) | data formatting | bytes 3145728 | tf_op args[0]
  10.9 3.9 %gather_fusion.2 = bf16[1024,192]{1,0:T(8,128)(2,1)S(1)} fusion(bf16[4096,192]{1,0:T(8,128)(2,1)S(1)} %copy.50, s32[1024]{0:T(1024)S(1)} %broadcast_clamp_fusion.1), kind=kCustom, calls=%fused_computation.2 | custom fusion | bytes 790528 | tf_op jit(solution)/shard_map/gather | solution.py:181
  15.8 1.6 collective-permute-start.7
  17.3 3.9 %gather_fusion.1 = bf16[1024,192]{1,0:T(8,128)(2,1)S(1)} fusion(bf16[4096,192]{1,0:T(8,128)(2,1)S(1)} %copy.50, s32[1024]{0:T(1024)S(1)} %broadcast_clamp_fusion.2), kind=kCustom, calls=%fused_computation.1 | custom fusion | bytes 790528 | tf_op jit(solution)/shard_map/gather | solution.py:181
  21.5 2.7 %collective-permute-start.6 = (bf16[192,1024]{1,0:T(8,128)(2,1)S(1)}, bf16[192,1024]{1,0:T(8,128)(2,1)}, u32[]{:S(2)}, u32[]{:S(2)}) collective-permute-start(bf16[192,1024]{1,0:T(8,128)(2,1)S(1)} %bitcast.181), channel_id=1, source_target_pairs={{0,8},{4,12},{8,0},{12,4},{1,9},{5,13},{9,1},{13,5},{2,10},{6,14},... | collective-permute-start | bytes 1179656 | tf_op jit(solution)/shard_map/ppermute | solution.py:183
  24.3 3.9 %gather_fusion.3 = bf16[1024,192]{1,0:T(8,128)(2,1)S(1)} fusion(bf16[4096,192]{1,0:T(8,128)(2,1)S(1)} %copy.50, s32[1024]{0:T(1024)S(1)} %broadcast_clamp_fusion), kind=kCustom, calls=%fused_computation.3 | custom fusion | bytes 790528 | tf_op jit(solution)/shard_map/gather | solution.py:181
  29.2 3.9 %gather_fusion = bf16[1024,192]{1,0:T(8,128)(2,1)S(1)} fusion(bf16[4096,192]{1,0:T(8,128)(2,1)S(1)} %copy.50, s32[1024]{0:T(1024)S(1)} %broadcast_clamp_fusion.3), kind=kCustom, calls=%fused_computation | custom fusion | bytes 790528 | tf_op jit(solution)/shard_map/gather | solution.py:181
  36.3 3.3 %shard_map.129 = (f32[192,1024]{1,0:T(8,128)}, f32[8,1024]{1,0:T(8,128)}) custom-call(s32[1,1024]{1,0:T(1,128)} %get-tuple-element.58.tgt_ref, bf16[192,1024]{1,0:T(8,128)(2,1)} %bitcast.182, f32[192,1024]{1,0:T(8,128)} %broadcast_in_dim.4.sum_in, f32[8,1024]{1,0:T(8,128)} %broadcast_in_dim.5.cnt_in), custom_call_target="tpu_custom_call", output_to_operand_aliasing={{0}: (2, {}), {1}: (3, {})} | custom-call | flops 419430400 | bytes 2035712 | tf_op jit(solution)/shard_map/pallas_call | solution.py:46
  41.6 3.2 %shard_map.130 = (f32[192,1024]{1,0:T(8,128)}, f32[8,1024]{1,0:T(8,128)}) custom-call(s32[1,1024]{1,0:T(1,128)} %get-tuple-element.61.tgt_ref, bf16[192,1024]{1,0:T(8,128)(2,1)} %collective-permute-done.7.rec_ref, f32[192,1024]{1,0:T(8,128)} %get-tuple-element.14.sum_in, ...), custom_call_target="tpu_custom_call", output_to_operand_aliasing={{0}: (2, {}), {1}: (3, {})} | custom-call | flops 419430400 | bytes 2035712 | tf_op jit(solution)/shard_map/pallas_call | solution.py:46
  44.9 1.6 collective-permute-start.5
  46.5 3.2 %shard_map.131 = (f32[192,1024]{1,0:T(8,128)}, f32[8,1024]{1,0:T(8,128)}) custom-call(s32[1,1024]{1,0:T(1,128)} %get-tuple-element.59.tgt_ref, bf16[192,1024]{1,0:T(8,128)(2,1)} %collective-permute-done.6.rec_ref, f32[192,1024]{1,0:T(8,128)} %get-tuple-element.16.sum_in, ...), custom_call_target="tpu_custom_call", output_to_operand_aliasing={{0}: (2, {}), {1}: (3, {})} | custom-call | flops 419430400 | bytes 2035712 | tf_op jit(solution)/shard_map/pallas_call | solution.py:46
  49.7 1.6 collective-permute-start.13
  52.6 3.5 %collective-permute-done.5.rec_ref = bf16[192,1024]{1,0:T(8,128)(2,1)S(1)} collective-permute-done((bf16[192,1024]{1,0:T(8,128)(2,1)}, bf16[192,1024]{1,0:T(8,128)(2,1)S(1)}, u32[]{:S(2)}, u32[]{:S(2)}) %collective-permute-start.5) | collective-permute-done | bytes 393248 | tf_op jit(solution)/shard_map/ppermute | solution.py:183
  56.8 3.2 %shard_map.132 = (f32[192,1024]{1,0:T(8,128)}, f32[8,1024]{1,0:T(8,128)}) custom-call(s32[1,1024]{1,0:T(1,128)} %get-tuple-element.60.tgt_ref, bf16[192,1024]{1,0:T(8,128)(2,1)} %copy-done.15, f32[192,1024]{1,0:T(8,128)} %get-tuple-element.18.sum_in, f32[8,1024]{1,0:T(8,128)} %get-tuple-element.19.cnt_in), custom_call_target="tpu_custom_call", output_to_operand_aliasing={{0}: (2, {}), {1}: (3, {})} | custom-call | flops 419430400 | bytes 2035712 | tf_op jit(solution)/shard_map/pallas_call | solution.py:46
  62.2 2.7 %collective-permute-done.13 = bf16[256,1024]{1,0:T(8,128)(2,1)} collective-permute-done((bf16[256,1024]{1,0:T(8,128)(2,1)}, bf16[256,1024]{1,0:T(8,128)(2,1)}, u32[]{:S(2)}, u32[]{:S(2)}) %collective-permute-start.13) | collective-permute-done | bytes 524320 | tf_op jit(solution)/shard_map/ppermute | solution.py:124
  66.5 1.6 collective-permute-start.11
  79.0 1.7 %multiply_convert_fusion.2 = (bf16[256,1024]{1,0:T(8,128)(2,1)}, f32[256,1024]{1,0:T(8,128)S(1)}) fusion(f32[1024]{0:T(1024)S(1)} %copy-done.16, bf16[256,1024]{1,0:T(8,128)(2,1)S(1)} %convolution_convert_fusion, bf16[1024,1024]{1,0:T(8,128)(2,1)S(1)} %bitcast.175), kind=kOutput, calls=%fused_computation.31 | convolution fusion | flops 538443776 | bytes 4198400 | tf_op jit(solution)/shard_map/dot_general | solution.py:203
  81.6 2.0 %copy-done = f32[1024,1024]{1,0:T(8,128)} copy-done((f32[1024,1024]{1,0:T(8,128)}, f32[1024,1024]{1,0:T(8,128)S(1)}, u32[]{:S(2)}) %copy-start) | copy-done | bytes 4194328
  84.7 2.3 %fusion.61 = f32[256,1024]{1,0:T(8,128)S(1)} fusion(bf16[1024,1024]{1,0:T(8,128)(2,1)S(1)} %bitcast.176, f32[256,1024]{1,0:T(8,128)} %copy-done.3, bf16[256,1024]{1,0:T(8,128)(2,1)} %param.19), kind=kOutput, calls=%fused_computation.148 | convolution fusion | flops 539492352 | bytes 4718592 | tf_op jit(solution)/shard_map/dot_general | solution.py:208
  89.2 1.6 bitcast_add_fusion
  93.1 12.2 %collective-permute-done.16 = bf16[256,1024]{1,0:T(8,128)(2,1)} collective-permute-done((bf16[256,1024]{1,0:T(8,128)(2,1)S(1)}, bf16[256,1024]{1,0:T(8,128)(2,1)}, u32[]{:S(2)}, u32[]{:S(2)}) %collective-permute-start.16) | collective-permute-done | bytes 524320 | tf_op jit(solution)/shard_map/ppermute | solution.py:124
  110.0 15.0 %collective-permute-done.21 = bf16[2,64,1024]{2,1,0:T(8,128)(2,1)S(1)} collective-permute-done((bf16[2,64,1024]{2,1,0:T(8,128)(2,1)S(1)}, bf16[2,64,1024]{2,1,0:T(8,128)(2,1)S(1)}, u32[]{:S(2)}, u32[]{:S(2)}) %collective-permute-start.21) | collective-permute-done | bytes 262176 | tf_op jit(solution)/shard_map/ppermute | solution.py:94
  127.1 4.5 %collective-permute-done.22 = bf16[64,1024]{1,0:T(8,128)(2,1)S(1)} collective-permute-done((bf16[64,1024]{1,0:T(8,128)(2,1)S(1)}, bf16[64,1024]{1,0:T(8,128)(2,1)S(1)}, u32[]{:S(2)}, u32[]{:S(2)}) %collective-permute-start.22) | collective-permute-done | bytes 131104 | tf_op jit(solution)/shard_map/ppermute | solution.py:94
  133.6 2.6 %copy.61 = bf16[1024,1024]{1,0:T(8,128)(2,1)} copy(bf16[1024,1024]{0,1:T(8,128)(2,1)S(1)} %bitcast.166) | data formatting | bytes 4194304 | tf_op jit(solution)/shard_map/dot_general | solution.py:222
  136.2 2.6 %fusion.6 = f32[384,4,256]{2,0,1:T(8,128)S(1)} fusion(bf16[4,256,1024]{2,1,0:T(8,128)(2,1)} %bitcast.177, bf16[192,1024]{1,0:T(8,128)(2,1)S(1)} %copy-done.6, bf16[192,1024]{1,0:T(8,128)(2,1)S(1)} %divide_convert_fusion), kind=kOutput, calls=%fused_computation.40 | convolution fusion | flops 806879232 | bytes 4456448 | tf_op jit(solution)/shard_map/dot_general | solution.py:222
  139.5 1.6 collective-permute-start.24
  141.1 9.9 %collective-permute-done.18 = bf16[2,384,256]{2,1,0:T(8,128)(2,1)S(1)} collective-permute-done((bf16[2,384,256]{2,1,0:T(8,128)(2,1)S(1)}, bf16[2,384,256]{2,1,0:T(8,128)(2,1)S(1)}, u32[]{:S(2)}, u32[]{:S(2)}) %collective-permute-start.18) | collective-permute-done | bytes 393248 | tf_op jit(solution)/shard_map/ppermute | solution.py:94
  151.1 3.0 %collective-permute-start.19 = (bf16[384,256]{1,0:T(8,128)(2,1)S(1)}, bf16[384,256]{1,0:T(8,128)(2,1)S(1)}, u32[]{:S(2)}, u32[]{:S(2)}) collective-permute-start(bf16[384,256]{1,0:T(8,128)(2,1)S(1)} %fusion.35), channel_id=1, source_target_pairs={{0,8},{4,12},{8,0},{12,4},{1,9},{5,13},{9,1},{13,5},{2,10},{6,14},... | collective-permute-start | bytes 589832 | tf_op jit(solution)/shard_map/ppermute | solution.py:94
  154.1 4.1 %collective-permute-done.24 = bf16[2,64,1024]{2,1,0:T(8,128)(2,1)S(1)} collective-permute-done((bf16[2,64,1024]{2,1,0:T(8,128)(2,1)S(1)}, bf16[2,64,1024]{2,1,0:T(8,128)(2,1)S(1)}, u32[]{:S(2)}, u32[]{:S(2)}) %collective-permute-start.24) | collective-permute-done | bytes 262176 | tf_op jit(solution)/shard_map/ppermute | solution.py:124
  159.4 2.1 %collective-permute-done.19 = bf16[384,256]{1,0:T(8,128)(2,1)S(1)} collective-permute-done((bf16[384,256]{1,0:T(8,128)(2,1)S(1)}, bf16[384,256]{1,0:T(8,128)(2,1)S(1)}, u32[]{:S(2)}, u32[]{:S(2)}) %collective-permute-start.19) | collective-permute-done | bytes 196640 | tf_op jit(solution)/shard_map/ppermute | solution.py:94
  (130 shorter events, 44.5 us)
Async XLA Ops:
  2.5 8.3 %copy-start.12 = (s32[1,4,1024]{2,1,0:T(4,128)S(1)}, s32[1,4,1024]{2,1,0:T(4,128)}, u32[]{:S(2)}) copy-start(s32[1,4,1024]{2,1,0:T(4,128)} %param.11) | copy-start | bytes 49156
  3.2 67.3 %collective-permute-start.4 = (bf16[192,256]{1,0:T(8,128)(2,1)}, bf16[192,256]{1,0:T(8,128)(2,1)}, u32[]{:S(2)}, u32[]{:S(2)}) collective-permute-start(bf16[192,256]{1,0:T(8,128)(2,1)} %get-tuple-element.50), channel_id=1, source_target_pairs={{0,3},{1,0},{2,1},{3,2},{4,7},{5,4},{6,5},{7,6},{8,11},{9,8},{10,9... | collective-permute-start | bytes 294920 | tf_op jit(solution)/shard_map/ppermute | solution.py:171
  5.6 44.1 %collective-permute-start = (bf16[192,1024]{1,0:T(8,128)(2,1)}, bf16[192,1024]{1,0:T(8,128)(2,1)}, u32[]{:S(2)}, u32[]{:S(2)}) collective-permute-start(bf16[192,1024]{1,0:T(8,128)(2,1)} %param.14), channel_id=1, source_target_pairs={{0,2},{1,3},{2,0},{3,1},{4,6},{5,7},{6,4},{7,5},{8,10},{9,11},{10,... | collective-permute-start | bytes 1179656 | tf_op jit(solution)/shard_map/ppermute | solution.py:124
  6.2 43.5 %collective-permute-start.8 = (bf16[192,1024]{1,0:T(8,128)(2,1)}, bf16[192,1024]{1,0:T(8,128)(2,1)}, u32[]{:S(2)}, u32[]{:S(2)}) collective-permute-start(bf16[192,1024]{1,0:T(8,128)(2,1)} %param.13), channel_id=1, source_target_pairs={{0,2},{1,3},{2,0},{3,1},{4,6},{5,7},{6,4},{7,5},{8,10},{9,11},{10,... | collective-permute-start | bytes 1179656 | tf_op jit(solution)/shard_map/ppermute | solution.py:124
  15.8 25.3 %collective-permute-start.7 = (bf16[192,1024]{1,0:T(8,128)(2,1)}, bf16[192,1024]{1,0:T(8,128)(2,1)}, u32[]{:S(2)}, u32[]{:S(2)}) collective-permute-start(bf16[192,1024]{1,0:T(8,128)(2,1)} %bitcast.24), channel_id=1, source_target_pairs={{0,4},{4,8},{8,12},{12,0},{1,5},{5,9},{9,13},{13,1},{2,6},{6,10},{... | collective-permute-start | bytes 1179656 | tf_op jit(solution)/shard_map/ppermute | solution.py:183
  21.5 23.4 %collective-permute-start.6 = (bf16[192,1024]{1,0:T(8,128)(2,1)S(1)}, bf16[192,1024]{1,0:T(8,128)(2,1)}, u32[]{:S(2)}, u32[]{:S(2)}) collective-permute-start(bf16[192,1024]{1,0:T(8,128)(2,1)S(1)} %bitcast.181), channel_id=1, source_target_pairs={{0,8},{4,12},{8,0},{12,4},{1,9},{5,13},{9,1},{13,5},{2,10},{6,14},... | collective-permute-start | bytes 1179656 | tf_op jit(solution)/shard_map/ppermute | solution.py:183
  29.2 4.9 %copy-start.13 = (s32[1,4,1024]{2,1,0:T(4,128)S(1)}, s32[1,4,1024]{2,1,0:T(4,128)}, u32[]{:S(2)}) copy-start(s32[1,4,1024]{2,1,0:T(4,128)} %param.12) | copy-start | bytes 49156
  33.1 6.5 %copy-start.11 = (s32[256,15]{0,1:T(8,128)S(1)}, s32[256,15]{0,1:T(8,128)}, u32[]{:S(2)}) copy-start(s32[256,15]{0,1:T(8,128)} %param.18) | copy-start | bytes 46084
  36.3 15.0 %copy-start.7 = (bf16[192,1024]{1,0:T(8,128)(2,1)S(1)}, bf16[192,1024]{1,0:T(8,128)(2,1)}, u32[]{:S(2)}) copy-start(bf16[192,1024]{1,0:T(8,128)(2,1)} %param.13) | copy-start | bytes 1179652
  36.3 15.0 %copy-start.8 = (bf16[192,1024]{1,0:T(8,128)(2,1)S(1)}, bf16[192,1024]{1,0:T(8,128)(2,1)}, u32[]{:S(2)}) copy-start(bf16[192,1024]{1,0:T(8,128)(2,1)} %param.14) | copy-start | bytes 1179652
  41.1 31.2 %collective-permute-start.3 = (bf16[192,256]{1,0:T(8,128)(2,1)}, bf16[192,256]{1,0:T(8,128)(2,1)S(1)}, u32[]{:S(2)}, u32[]{:S(2)}) collective-permute-start(bf16[192,256]{1,0:T(8,128)(2,1)} %get-tuple-element.51), channel_id=1, source_target_pairs={{0,2},{1,3},{2,0},{3,1},{4,6},{5,7},{6,4},{7,5},{8,10},{9,11},{10,... | collective-permute-start | bytes 294920 | tf_op jit(solution)/shard_map/ppermute | solution.py:171
  44.9 11.2 %collective-permute-start.5 = (bf16[192,1024]{1,0:T(8,128)(2,1)}, bf16[192,1024]{1,0:T(8,128)(2,1)S(1)}, u32[]{:S(2)}, u32[]{:S(2)}) collective-permute-start(bf16[192,1024]{1,0:T(8,128)(2,1)} %bitcast.16), channel_id=1, source_target_pairs={{0,12},{4,0},{8,4},{12,8},{1,13},{5,1},{9,5},{13,9},{2,14},{6,2},{... | collective-permute-start | bytes 1179656 | tf_op jit(solution)/shard_map/ppermute | solution.py:183
  49.7 24.5 %collective-permute-start.2 = (bf16[192,256]{1,0:T(8,128)(2,1)}, bf16[192,256]{1,0:T(8,128)(2,1)}, u32[]{:S(2)}, u32[]{:S(2)}) collective-permute-start(bf16[192,256]{1,0:T(8,128)(2,1)} %get-tuple-element.49), channel_id=1, source_target_pairs={{0,1},{1,2},{2,3},{3,0},{4,5},{5,6},{6,7},{7,4},{8,9},{9,10},{10,1... | collective-permute-start | bytes 294920 | tf_op jit(solution)/shard_map/ppermute | solution.py:171
  49.7 15.1 %collective-permute-start.13 = (bf16[256,1024]{1,0:T(8,128)(2,1)}, bf16[256,1024]{1,0:T(8,128)(2,1)}, u32[]{:S(2)}, u32[]{:S(2)}) collective-permute-start(bf16[256,1024]{1,0:T(8,128)(2,1)} %param.16), channel_id=1, source_target_pairs={{0,2},{1,3},{2,0},{3,1},{4,6},{5,7},{6,4},{7,5},{8,10},{9,11},{10,... | collective-permute-start | bytes 1572872 | tf_op jit(solution)/shard_map/ppermute | solution.py:124
  56.1 10.4 %collective-permute-start.1 = (bf16[2,192,1024]{2,1,0:T(8,128)(2,1)S(1)}, bf16[2,192,1024]{2,1,0:T(8,128)(2,1)}, u32[]{:S(2)}, u32[]{:S(2)}) collective-permute-start(bf16[2,192,1024]{2,1,0:T(8,128)(2,1)S(1)} %pad_maximum_fusion.6), channel_id=1, source_target_pairs={{0,1},{1,0},{2,3},{3,2},{4,5},{5,4},{6,7},{7,6},{8,9},{9,8},{10,11... | collective-permute-start | bytes 2359304 | tf_op jit(solution)/shard_map/ppermute | solution.py:124
  64.8 4.6 %collective-permute-start.9 = (bf16[2,192,1024]{2,1,0:T(8,128)(2,1)S(1)}, bf16[2,192,1024]{2,1,0:T(8,128)(2,1)S(1)}, u32[]{:S(2)}, u32[]{:S(2)}) collective-permute-start(bf16[2,192,1024]{2,1,0:T(8,128)(2,1)S(1)} %pad_maximum_fusion.7), channel_id=1, source_target_pairs={{0,1},{1,0},{2,3},{3,2},{4,5},{5,4},{6,7},{7,6},{8,9},{9,8},{10,11... | collective-permute-start | bytes 2359304 | tf_op jit(solution)/shard_map/ppermute | solution.py:124
  66.5 9.0 %collective-permute-start.11 = (bf16[192,256]{1,0:T(8,128)(2,1)S(1)}, bf16[192,256]{1,0:T(8,128)(2,1)S(1)}, u32[]{:S(2)}, u32[]{:S(2)}) collective-permute-start(bf16[192,256]{1,0:T(8,128)(2,1)S(1)} %get-tuple-element.48), channel_id=1, source_target_pairs={{0,2},{1,3},{2,0},{3,1},{4,6},{5,7},{6,4},{7,5},{8,10},{9,11},{10,... | collective-permute-start | bytes 294920 | tf_op jit(solution)/shard_map/ppermute | solution.py:195
  69.5 6.3 %collective-permute-start.12 = (bf16[192,256]{1,0:T(8,128)(2,1)S(1)}, bf16[192,256]{1,0:T(8,128)(2,1)S(1)}, u32[]{:S(2)}, u32[]{:S(2)}) collective-permute-start(bf16[192,256]{1,0:T(8,128)(2,1)S(1)} %get-tuple-element.47), channel_id=1, source_target_pairs={{0,3},{1,0},{2,1},{3,2},{4,7},{5,4},{6,5},{7,6},{8,11},{9,8},{10,9... | collective-permute-start | bytes 294920 | tf_op jit(solution)/shard_map/ppermute | solution.py:195
  70.5 5.7 %collective-permute-start.10 = (bf16[192,256]{1,0:T(8,128)(2,1)S(1)}, bf16[192,256]{1,0:T(8,128)(2,1)S(1)}, u32[]{:S(2)}, u32[]{:S(2)}) collective-permute-start(bf16[192,256]{1,0:T(8,128)(2,1)S(1)} %get-tuple-element.46), channel_id=1, source_target_pairs={{0,1},{1,2},{2,3},{3,0},{4,5},{5,6},{6,7},{7,4},{8,9},{9,10},{10,1... | collective-permute-start | bytes 294920 | tf_op jit(solution)/shard_map/ppermute | solution.py:195
  72.3 5.7 %collective-permute-start.14 = (bf16[2,256,1024]{2,1,0:T(8,128)(2,1)S(1)}, bf16[2,256,1024]{2,1,0:T(8,128)(2,1)S(1)}, u32[]{:S(2)}, u32[]{:S(2)}) collective-permute-start(bf16[2,256,1024]{2,1,0:T(8,128)(2,1)S(1)} %pad_maximum_fusion.4), channel_id=1, source_target_pairs={{0,1},{1,0},{2,3},{3,2},{4,5},{5,4},{6,7},{7,6},{8,9},{9,8},{10,11... | collective-permute-start | bytes 3145736 | tf_op jit(solution)/shard_map/ppermute | solution.py:124
  84.7 3.6 %collective-permute-start.15 = (bf16[2,2,2,64,1024]{4,3,2,1,0:T(8,128)(2,1)}, bf16[2,2,2,64,1024]{4,3,2,1,0:T(8,128)(2,1)}, u32[]{:S(2)}, u32[]{:S(2)}) collective-permute-start(bf16[2,2,2,64,1024]{4,3,2,1,0:T(8,128)(2,1)} %fusion.5), channel_id=1, source_target_pairs={{0,1},{1,0},{2,3},{3,2},{4,5},{5,4},{6,7},{7,6},{8,9},{9,8},{10,11... | collective-permute-start | bytes 3145736 | tf_op jit(solution)/shard_map/ppermute | solution.py:94
  88.3 2.4 %copy-start.5 = (bf16[256,1024]{1,0:T(8,128)(2,1)}, bf16[256,1024]{1,0:T(8,128)(2,1)S(1)}, u32[]{:S(2)}) copy-start(bf16[256,1024]{1,0:T(8,128)(2,1)S(1)} %multiply_convert_fusion) | copy-start | bytes 1572868
  90.8 14.5 %collective-permute-start.16 = (bf16[256,1024]{1,0:T(8,128)(2,1)S(1)}, bf16[256,1024]{1,0:T(8,128)(2,1)}, u32[]{:S(2)}, u32[]{:S(2)}) collective-permute-start(bf16[256,1024]{1,0:T(8,128)(2,1)S(1)} %multiply_convert_fusion), channel_id=1, source_target_pairs={{0,2},{1,3},{2,0},{3,1},{4,6},{5,7},{6,4},{7,5},{8,10},{9,11},{10,... | collective-permute-start | bytes 1572872 | tf_op jit(solution)/shard_map/ppermute | solution.py:124
  92.6 15.0 %collective-permute-start.20 = (bf16[2,2,64,1024]{3,2,1,0:T(8,128)(2,1)}, bf16[2,2,64,1024]{3,2,1,0:T(8,128)(2,1)}, u32[]{:S(2)}, u32[]{:S(2)}) collective-permute-start(bf16[2,2,64,1024]{3,2,1,0:T(8,128)(2,1)} %fusion.9), channel_id=1, source_target_pairs={{0,4},{1,5},{2,6},{3,7},{4,0},{5,1},{6,2},{7,3},{8,12},{9,13},{10,... | collective-permute-start | bytes 1572872 | tf_op jit(solution)/shard_map/ppermute | solution.py:94
  107.6 24.2 %collective-permute-start.17 = (bf16[2,256,1024]{2,1,0:T(8,128)(2,1)}, bf16[2,256,1024]{2,1,0:T(8,128)(2,1)}, u32[]{:S(2)}, u32[]{:S(2)}) collective-permute-start(bf16[2,256,1024]{2,1,0:T(8,128)(2,1)} %pad_maximum_fusion.5), channel_id=1, source_target_pairs={{0,1},{1,0},{2,3},{3,2},{4,5},{5,4},{6,7},{7,6},{8,9},{9,8},{10,11... | collective-permute-start | bytes 3145736 | tf_op jit(solution)/shard_map/ppermute | solution.py:124
  109.9 15.2 %collective-permute-start.21 = (bf16[2,64,1024]{2,1,0:T(8,128)(2,1)S(1)}, bf16[2,64,1024]{2,1,0:T(8,128)(2,1)S(1)}, u32[]{:S(2)}, u32[]{:S(2)}) collective-permute-start(bf16[2,64,1024]{2,1,0:T(8,128)(2,1)S(1)} %fusion.32), channel_id=1, source_target_pairs={{0,8},{1,9},{2,10},{3,11},{4,12},{5,13},{6,14},{7,15},{8,0},{9,1},... | collective-permute-start | bytes 786440 | tf_op jit(solution)/shard_map/ppermute | solution.py:94
  126.2 5.5 %collective-permute-start.22 = (bf16[64,1024]{1,0:T(8,128)(2,1)S(1)}, bf16[64,1024]{1,0:T(8,128)(2,1)S(1)}, u32[]{:S(2)}, u32[]{:S(2)}) collective-permute-start(bf16[64,1024]{1,0:T(8,128)(2,1)S(1)} %fusion.36), channel_id=1, source_target_pairs={{0,2},{1,3},{2,0},{3,1},{4,6},{5,7},{6,4},{7,5},{8,10},{9,11},{10,... | collective-permute-start | bytes 393224 | tf_op jit(solution)/shard_map/ppermute | solution.py:94
  131.7 7.7 %collective-permute-start.23 = (bf16[64,1024]{1,0:T(8,128)(2,1)S(1)}, bf16[64,1024]{1,0:T(8,128)(2,1)S(1)}, u32[]{:S(2)}, u32[]{:S(2)}) collective-permute-start(bf16[64,1024]{1,0:T(8,128)(2,1)S(1)} %fusion.33), channel_id=1, source_target_pairs={{0,8},{4,12},{8,0},{12,4},{1,9},{5,13},{9,1},{13,5},{2,10},{6,14},... | collective-permute-start | bytes 393224 | tf_op jit(solution)/shard_map/ppermute | solution.py:124
  133.6 2.6 %copy-start.6 = (bf16[192,1024]{1,0:T(8,128)(2,1)S(1)}, bf16[192,1024]{1,0:T(8,128)(2,1)}, u32[]{:S(2)}) copy-start(bf16[192,1024]{1,0:T(8,128)(2,1)} %get-tuple-element.28) | copy-start | bytes 1179652
  138.8 12.1 %collective-permute-start.18 = (bf16[2,384,256]{2,1,0:T(8,128)(2,1)S(1)}, bf16[2,384,256]{2,1,0:T(8,128)(2,1)S(1)}, u32[]{:S(2)}, u32[]{:S(2)}) collective-permute-start(bf16[2,384,256]{2,1,0:T(8,128)(2,1)S(1)} %fusion.10), channel_id=1, source_target_pairs={{0,4},{4,0},{8,12},{12,8},{1,5},{5,1},{9,13},{13,9},{2,6},{6,2},{1... | collective-permute-start | bytes 1179656 | tf_op jit(solution)/shard_map/ppermute | solution.py:94
  139.5 18.7 %collective-permute-start.24 = (bf16[2,64,1024]{2,1,0:T(8,128)(2,1)S(1)}, bf16[2,64,1024]{2,1,0:T(8,128)(2,1)S(1)}, u32[]{:S(2)}, u32[]{:S(2)}) collective-permute-start(bf16[2,64,1024]{2,1,0:T(8,128)(2,1)S(1)} %pad_maximum_fusion.8), channel_id=1, source_target_pairs={{0,4},{4,0},{8,12},{12,8},{1,5},{5,1},{9,13},{13,9},{2,6},{6,2},{1... | collective-permute-start | bytes 786440 | tf_op jit(solution)/shard_map/ppermute | solution.py:124
  151.1 10.4 %collective-permute-start.19 = (bf16[384,256]{1,0:T(8,128)(2,1)S(1)}, bf16[384,256]{1,0:T(8,128)(2,1)S(1)}, u32[]{:S(2)}, u32[]{:S(2)}) collective-permute-start(bf16[384,256]{1,0:T(8,128)(2,1)S(1)} %fusion.35), channel_id=1, source_target_pairs={{0,8},{4,12},{8,0},{12,4},{1,9},{5,13},{9,1},{13,5},{2,10},{6,14},... | collective-permute-start | bytes 589832 | tf_op jit(solution)/shard_map/ppermute | solution.py:94
  (10 other events, 13.1 us)

commit v9 on v8

--- a/solution.py
+++ b/solution.py
@@ -154,14 +154,21 @@
     w_rows = neigh_weight.shape[0]
     up_rows = upper_weight.shape[0]
 
-    neigh_full, self_full, full_upper = all_gather_blocks(
-        (neigh_weight, self_weight, upper_weight), "cols", n_cols
-    )
-    full_upper = full_upper.reshape(n_cols * up_rows, hidden)
-
     me_dom = lax.axis_index("dom")
     me_col = lax.axis_index("cols")
-    own_t = features[:tgt_dev].T
+    sent = []
+    for shift in range(1, n_dom):
+        dest = (me_dom + shift) % n_dom
+        slots = lax.dynamic_index_in_dim(edge_source[0], dest, 0, keepdims=False)
+        rows_t = features.at[slots].get(mode="promise_in_bounds").T
+        if shift == 1:
+            rows_t, weights, own_rows = lax.optimization_barrier(
+                (rows_t, (neigh_weight, self_weight, upper_weight), features[:tgt_dev])
+            )
+        sent.append(lax.ppermute(rows_t, "dom", _shift_pairs(n_dom, shift)))
+    neigh_full, self_full, full_upper = all_gather_blocks(weights, "cols", n_cols)
+    full_upper = full_upper.reshape(n_cols * up_rows, hidden)
+    own_t = own_rows.T
     own_pre = bias_one
     for shift in range(n_cols):
         dest = (me_col + shift) % n_cols
@@ -175,12 +182,12 @@
     summed_t = jnp.zeros((width, tgt_dev), jnp.float32)
     counts = jnp.zeros((8, tgt_dev), jnp.float32)
     for shift in range(n_dom):
-        dest = (me_dom + shift) % n_dom
         src = (me_dom - shift) % n_dom
-        slots = lax.dynamic_index_in_dim(edge_source[0], dest, 0, keepdims=False)
-        rows_t = features.at[slots].get(mode="promise_in_bounds").T
         if shift:
-            rows_t = lax.ppermute(rows_t, "dom", _shift_pairs(n_dom, shift))
+            rows_t = sent[shift - 1]
+        else:
+            slots = lax.dynamic_index_in_dim(edge_source[0], me_dom, 0, keepdims=False)
+            rows_t = features.at[slots].get(mode="promise_in_bounds").T
         targets = lax.dynamic_index_in_dim(edge_target[0], src, 0, keepdims=True)
         summed_t, counts = accumulate(targets, rows_t, summed_t, counts)
     mean_t = (summed_t / jnp.maximum(counts[:1], 1.0)).astype(jnp.bfloat16)

time: 163 us -> 179 us (1.098)
  waiting for transfers between devices: 54.1 us -> 66.4 us
  starting transfers between devices: 23.6 us -> 34.2 us
  other arithmetic: 16.3 us -> 13 us
  local copies, waits for them, and re-layouts: 39.8 us -> 36.6 us
    ppermute x6, starting transfers between devices: 5.12 us -> 16.1 us  [_butterfly_reduce(): got = lax.ppermute(send.astype(send_dtype), axis, _xor_pairs(n, 1 << b))]
    ppermute x6, waiting for transfers between devices: 31.6 us -> 39.5 us  [_butterfly_reduce(): got = lax.ppermute(send.astype(send_dtype), axis, _xor_pairs(n, 1 << b))]
    ppermute x10, waiting for transfers between devices: 19 us -> 25.8 us  [all_gather_blocks(): got = lax.ppermute(cur, axis, _xor_pairs(n, 1 << b))]
    ppermute x3, waiting for transfers between devices: 3.49 us -> 0.01 us  [local(): sent.append(lax.ppermute(rows_t, 'dom', _shift_pairs(n_dom, shift)))]
    another operation x18 -> x19, other arithmetic: 8.7 us -> 5.26 us  [join(): return jnp.stack([low, high], axis=k - 1 - b)]
    ppermute x10, starting transfers between devices: 7.74 us -> 4.5 us  [all_gather_blocks(): got = lax.ppermute(cur, axis, _xor_pairs(n, 1 << b))]
    unnamed x35 -> x33, local copies, waits for them, and re-layouts: 9.24 us -> 6.77 us
    ppermute x3, starting transfers between devices: 5.81 us -> 7.93 us  [local(): sent.append(lax.ppermute(rows_t, 'dom', _shift_pairs(n_dom, shift)))]
  transfers between devices with their start and end apart: 25 -> 25, of which waited for: 8 -> 12; matrix products, arithmetic and copies ran while one was open for 34% -> 25% of each run, Pallas kernels for 8% -> 7%
where the time goes in v9:
time: 179 us
  waiting for transfers between devices  66.4 us (37%)
  local copies, waits for them, and re-layouts  36.6 us (20%)
  starting transfers between devices  34.2 us (19%)
  matrix products  14 us (8%)
  Pallas kernels  13.1 us (7%)
  other arithmetic  13 us (7%)
    ppermute x6, waiting for transfers between devices, _butterfly_reduce(): got = lax.ppermute(send.astype(send_dtype), axis, _xor_pairs(n, 1 << b))  39.5 us
    ppermute x10, waiting for transfers between devices, all_gather_blocks(): got = lax.ppermute(cur, axis, _xor_pairs(n, 1 << b))  25.8 us
    gather x8, local copies, waits for them, and re-layouts, local(): rows_t = features.at[slots].get(mode='promise_in_bounds').T  18.8 us
    ppermute x6, starting transfers between devices, _butterfly_reduce(): got = lax.ppermute(send.astype(send_dtype), axis, _xor_pairs(n, 1 << b))  16.1 us
    pallas_call x4, Pallas kernels, accumulate(): pl.pallas_call(_accumulate_kernel, out_shape=[jax.ShapeDtypeStruct(acc_su...  13.1 us
    ppermute x3, starting transfers between devices, local(): sent.append(lax.ppermute(rows_t, 'dom', _shift_pairs(n_dom, shift)))  7.93 us
    unnamed x33, local copies, waits for them, and re-layouts  6.77 us
    ppermute x6, starting transfers between devices, local(): chunk = lax.ppermute(chunk, 'cols', _shift_pairs(n_cols, shift))  5.69 us
  transfers between devices with their start and end apart: 25, of which 12 were waited for; matrix products, arithmetic and copies ran while one was open for 25% of the time, Pallas kernels for 7%

profile of v9, /device:TPU:0, one launch (start us, length us, event | category | flops | bytes accessed | tf_op | source)
XLA Modules:
  0.0 178.6 jit_solution(8013779979646618488)
XLA Ops:
  1.6 3.2 %copy.49 = bf16[4096,192]{1,0:T(8,128)(2,1)S(1)} copy(bf16[4096,192]{0,1:T(8,128)(2,1)} %param.10) | data formatting | bytes 3145728 | tf_op args[0]
  4.8 3.9 %gather_fusion.2 = bf16[1024,192]{1,0:T(8,128)(2,1)S(1)} fusion(bf16[4096,192]{1,0:T(8,128)(2,1)S(1)} %copy.49, s32[1024]{0:T(1024)S(1)} %broadcast_clamp_fusion.1), kind=kCustom, calls=%fused_computation.2 | custom fusion | bytes 790528 | tf_op jit(solution)/shard_map/gather | solution.py:163
  8.9 4.1 %collective-permute-start.6 = (bf16[192,1024]{1,0:T(8,128)(2,1)S(1)}, bf16[192,1024]{1,0:T(8,128)(2,1)}, u32[]{:S(2)}, u32[]{:S(2)}) collective-permute-start(bf16[192,1024]{1,0:T(8,128)(2,1)S(1)} %bitcast.181), channel_id=1, source_target_pairs={{0,8},{4,12},{8,0},{12,4},{1,9},{5,13},{9,1},{13,5},{2,10},{6,14},... | collective-permute-start | bytes 1179656 | tf_op jit(solution)/shard_map/ppermute | solution.py:168
  14.0 3.9 %gather_fusion = bf16[1024,192]{1,0:T(8,128)(2,1)S(1)} fusion(bf16[4096,192]{1,0:T(8,128)(2,1)S(1)} %copy.49, s32[1024]{0:T(1024)S(1)} %broadcast_clamp_fusion.3), kind=kCustom, calls=%fused_computation | custom fusion | bytes 790528 | tf_op jit(solution)/shard_map/gather | solution.py:163
  19.6 1.7 collective-permute-start.4
  21.4 1.6 collective-permute-start.7
  23.0 3.9 %gather_fusion.1 = bf16[1024,192]{1,0:T(8,128)(2,1)S(1)} fusion(bf16[4096,192]{1,0:T(8,128)(2,1)S(1)} %copy.49, s32[1024]{0:T(1024)S(1)} %broadcast_clamp_fusion.2), kind=kCustom, calls=%fused_computation.1 | custom fusion | bytes 790528 | tf_op jit(solution)/shard_map/gather | solution.py:163
  27.8 2.2 %collective-permute-start.5 = (bf16[192,1024]{1,0:T(8,128)(2,1)}, bf16[192,1024]{1,0:T(8,128)(2,1)}, u32[]{:S(2)}, u32[]{:S(2)}) collective-permute-start(bf16[192,1024]{1,0:T(8,128)(2,1)} %bitcast.183), channel_id=1, source_target_pairs={{0,12},{4,0},{8,4},{12,8},{1,13},{5,1},{9,5},{13,9},{2,14},{6,2},{... | collective-permute-start | bytes 1179656 | tf_op jit(solution)/shard_map/ppermute | solution.py:168
  30.1 3.9 %gather_fusion.3 = bf16[1024,192]{1,0:T(8,128)(2,1)S(1)} fusion(bf16[4096,192]{1,0:T(8,128)(2,1)S(1)} %copy.49, s32[1024]{0:T(1024)S(1)} %broadcast_clamp_fusion), kind=kCustom, calls=%fused_computation.3 | custom fusion | bytes 790528 | tf_op jit(solution)/shard_map/gather | solution.py:190
  37.2 3.3 %shard_map.129 = (f32[192,1024]{1,0:T(8,128)}, f32[8,1024]{1,0:T(8,128)}) custom-call(s32[1,1024]{1,0:T(1,128)} %get-tuple-element.66.tgt_ref, bf16[192,1024]{1,0:T(8,128)(2,1)} %bitcast.184, f32[192,1024]{1,0:T(8,128)} %broadcast_in_dim.4.sum_in, f32[8,1024]{1,0:T(8,128)} %broadcast_in_dim.5.cnt_in), custom_call_target="tpu_custom_call", output_to_operand_aliasing={{0}: (2, {}), {1}: (3, {})} | custom-call | flops 419430400 | bytes 2035712 | tf_op jit(solution)/shard_map/pallas_call | solution.py:46
  42.9 3.3 %shard_map.130 = (f32[192,1024]{1,0:T(8,128)}, f32[8,1024]{1,0:T(8,128)}) custom-call(s32[1,1024]{1,0:T(1,128)} %get-tuple-element.69.tgt_ref, bf16[192,1024]{1,0:T(8,128)(2,1)} %collective-permute-done.7.rec_ref, f32[192,1024]{1,0:T(8,128)} %get-tuple-element.22.sum_in, ...), custom_call_target="tpu_custom_call", output_to_operand_aliasing={{0}: (2, {}), {1}: (3, {})} | custom-call | flops 419430400 | bytes 2035712 | tf_op jit(solution)/shard_map/pallas_call | solution.py:46
  46.7 3.3 %shard_map.131 = (f32[192,1024]{1,0:T(8,128)}, f32[8,1024]{1,0:T(8,128)}) custom-call(s32[1,1024]{1,0:T(1,128)} %get-tuple-element.67.tgt_ref, bf16[192,1024]{1,0:T(8,128)(2,1)} %collective-permute-done.6.rec_ref, f32[192,1024]{1,0:T(8,128)} %get-tuple-element.24.sum_in, ...), custom_call_target="tpu_custom_call", output_to_operand_aliasing={{0}: (2, {}), {1}: (3, {})} | custom-call | flops 419430400 | bytes 2035712 | tf_op jit(solution)/shard_map/pallas_call | solution.py:46
  51.6 3.3 %shard_map.132 = (f32[192,1024]{1,0:T(8,128)}, f32[8,1024]{1,0:T(8,128)}) custom-call(s32[1,1024]{1,0:T(1,128)} %get-tuple-element.68.tgt_ref, bf16[192,1024]{1,0:T(8,128)(2,1)} %collective-permute-done.5.rec_ref, f32[192,1024]{1,0:T(8,128)} %get-tuple-element.26.sum_in, ...), custom_call_target="tpu_custom_call", output_to_operand_aliasing={{0}: (2, {}), {1}: (3, {})} | custom-call | flops 419430400 | bytes 2035712 | tf_op jit(solution)/shard_map/pallas_call | solution.py:46
  58.9 7.7 %collective-permute-done.8 = bf16[192,1024]{1,0:T(8,128)(2,1)S(1)} collective-permute-done((bf16[192,1024]{1,0:T(8,128)(2,1)S(1)}, bf16[192,1024]{1,0:T(8,128)(2,1)S(1)}, u32[]{:S(2)}, u32[]{:S(2)}) %collective-permute-start.8) | collective-permute-done | bytes 393248 | tf_op jit(solution)/shard_map/ppermute | solution.py:124
  66.8 8.1 %collective-permute-done.13 = bf16[256,1024]{1,0:T(8,128)(2,1)S(1)} collective-permute-done((bf16[256,1024]{1,0:T(8,128)(2,1)S(1)}, bf16[256,1024]{1,0:T(8,128)(2,1)S(1)}, u32[]{:S(2)}, u32[]{:S(2)}) %collective-permute-start.13) | collective-permute-done | bytes 524320 | tf_op jit(solution)/shard_map/ppermute | solution.py:124
  86.3 1.7 multiply_convert_fusion.2
  88.9 2.0 %copy-done = f32[1024,1024]{1,0:T(8,128)} copy-done((f32[1024,1024]{1,0:T(8,128)}, f32[1024,1024]{1,0:T(8,128)S(1)}, u32[]{:S(2)}) %copy-start) | copy-done | bytes 4194328
  92.0 2.3 %fusion.61 = f32[256,1024]{1,0:T(8,128)S(1)} fusion(bf16[1024,1024]{1,0:T(8,128)(2,1)S(1)} %bitcast.175, f32[256,1024]{1,0:T(8,128)} %copy-done.5, bf16[256,1024]{1,0:T(8,128)(2,1)} %param.19), kind=kOutput, calls=%fused_computation.147 | convolution fusion | flops 539492352 | bytes 4718592 | tf_op jit(solution)/shard_map/dot_general | solution.py:215
  94.3 2.1 %multiply_convert_fusion = bf16[256,1024]{1,0:T(8,128)(2,1)} fusion(f32[256,1024]{1,0:T(8,128)S(1)} %fusion.4, f32[256,1024]{1,0:T(8,128)S(1)} %fusion.61, f32[256,256]{1,0:T(8,128)S(1)} %copy-done.11), kind=kOutput, calls=%fused_computation.29 | convolution fusion | flops 807927808 | bytes 2883584 | tf_op jit(solution)/shard_map/dot_general | solution.py:218
  96.5 1.6 bitcast_add_fusion
  100.5 7.6 %collective-permute-start.20 = (bf16[2,2,64,1024]{3,2,1,0:T(8,128)(2,1)}, bf16[2,2,64,1024]{3,2,1,0:T(8,128)(2,1)}, u32[]{:S(2)}, u32[]{:S(2)}) collective-permute-start(bf16[2,2,64,1024]{3,2,1,0:T(8,128)(2,1)} %fusion.9), channel_id=1, source_target_pairs={{0,4},{1,5},{2,6},{3,7},{4,0},{5,1},{6,2},{7,3},{8,12},{9,13},{10,... | collective-permute-start | bytes 1572872 | tf_op jit(solution)/shard_map/ppermute | solution.py:94
  108.1 4.7 %collective-permute-done.16 = bf16[256,1024]{1,0:T(8,128)(2,1)} collective-permute-done((bf16[256,1024]{1,0:T(8,128)(2,1)}, bf16[256,1024]{1,0:T(8,128)(2,1)}, u32[]{:S(2)}, u32[]{:S(2)}) %collective-permute-start.16) | collective-permute-done | bytes 524320 | tf_op jit(solution)/shard_map/ppermute | solution.py:124
  115.1 5.6 %collective-permute-done.20 = bf16[2,2,64,1024]{3,2,1,0:T(8,128)(2,1)} collective-permute-done((bf16[2,2,64,1024]{3,2,1,0:T(8,128)(2,1)}, bf16[2,2,64,1024]{3,2,1,0:T(8,128)(2,1)}, u32[]{:S(2)}, u32[]{:S(2)}) %collective-permute-start.20) | collective-permute-done | bytes 524320 | tf_op jit(solution)/shard_map/ppermute | solution.py:94
  123.0 4.9 %collective-permute-start.21 = (bf16[2,64,1024]{2,1,0:T(8,128)(2,1)S(1)}, bf16[2,64,1024]{2,1,0:T(8,128)(2,1)S(1)}, u32[]{:S(2)}, u32[]{:S(2)}) collective-permute-start(bf16[2,64,1024]{2,1,0:T(8,128)(2,1)S(1)} %fusion.32), channel_id=1, source_target_pairs={{0,8},{1,9},{2,10},{3,11},{4,12},{5,13},{6,14},{7,15},{8,0},{9,1},... | collective-permute-start | bytes 786440 | tf_op jit(solution)/shard_map/ppermute | solution.py:94
  127.9 12.6 %collective-permute-done.21 = bf16[2,64,1024]{2,1,0:T(8,128)(2,1)S(1)} collective-permute-done((bf16[2,64,1024]{2,1,0:T(8,128)(2,1)S(1)}, bf16[2,64,1024]{2,1,0:T(8,128)(2,1)S(1)}, u32[]{:S(2)}, u32[]{:S(2)}) %collective-permute-start.21) | collective-permute-done | bytes 262176 | tf_op jit(solution)/shard_map/ppermute | solution.py:94
  142.2 4.8 %collective-permute-done.22 = bf16[64,1024]{1,0:T(8,128)(2,1)S(1)} collective-permute-done((bf16[64,1024]{1,0:T(8,128)(2,1)S(1)}, bf16[64,1024]{1,0:T(8,128)(2,1)S(1)}, u32[]{:S(2)}, u32[]{:S(2)}) %collective-permute-start.22) | collective-permute-done | bytes 131104 | tf_op jit(solution)/shard_map/ppermute | solution.py:94
  148.9 2.6 %copy.61 = bf16[1024,1024]{1,0:T(8,128)(2,1)} copy(bf16[1024,1024]{0,1:T(8,128)(2,1)S(1)} %bitcast.165) | data formatting | bytes 4194304 | tf_op jit(solution)/shard_map/dot_general | solution.py:229
  151.5 2.6 %fusion.6 = f32[384,4,256]{2,0,1:T(8,128)S(1)} fusion(bf16[4,256,1024]{2,1,0:T(8,128)(2,1)} %bitcast.176, bf16[192,1024]{1,0:T(8,128)(2,1)S(1)} %bitcast.177, bf16[192,1024]{1,0:T(8,128)(2,1)S(1)} %copy-done.4), kind=kOutput, calls=%fused_computation.40 | convolution fusion | flops 806879232 | bytes 4456448 | tf_op jit(solution)/shard_map/dot_general | solution.py:229
  154.2 2.2 %collective-permute-start.18 = (bf16[2,384,256]{2,1,0:T(8,128)(2,1)S(1)}, bf16[2,384,256]{2,1,0:T(8,128)(2,1)S(1)}, u32[]{:S(2)}, u32[]{:S(2)}) collective-permute-start(bf16[2,384,256]{2,1,0:T(8,128)(2,1)S(1)} %fusion.10), channel_id=1, source_target_pairs={{0,4},{4,0},{8,12},{12,8},{1,5},{5,1},{9,13},{13,9},{2,6},{6,2},{1... | collective-permute-start | bytes 1179656 | tf_op jit(solution)/shard_map/ppermute | solution.py:94
  156.5 12.0 %collective-permute-done.18 = bf16[2,384,256]{2,1,0:T(8,128)(2,1)S(1)} collective-permute-done((bf16[2,384,256]{2,1,0:T(8,128)(2,1)S(1)}, bf16[2,384,256]{2,1,0:T(8,128)(2,1)S(1)}, u32[]{:S(2)}, u32[]{:S(2)}) %collective-permute-start.18) | collective-permute-done | bytes 393248 | tf_op jit(solution)/shard_map/ppermute | solution.py:94
  169.4 2.7 %collective-permute-done.24 = bf16[2,64,1024]{2,1,0:T(8,128)(2,1)S(1)} collective-permute-done((bf16[2,64,1024]{2,1,0:T(8,128)(2,1)S(1)}, bf16[2,64,1024]{2,1,0:T(8,128)(2,1)S(1)}, u32[]{:S(2)}, u32[]{:S(2)}) %collective-permute-start.24) | collective-permute-done | bytes 262176 | tf_op jit(solution)/shard_map/ppermute | solution.py:124
  173.3 4.5 %collective-permute-done.19 = bf16[384,256]{1,0:T(8,128)(2,1)S(1)} collective-permute-done((bf16[384,256]{1,0:T(8,128)(2,1)S(1)}, bf16[384,256]{1,0:T(8,128)(2,1)S(1)}, u32[]{:S(2)}, u32[]{:S(2)}) %collective-permute-start.19) | collective-permute-done | bytes 196640 | tf_op jit(solution)/shard_map/ppermute | solution.py:94
  (129 shorter events, 43.4 us)
Async XLA Ops:
  8.9 37.2 %collective-permute-start.6 = (bf16[192,1024]{1,0:T(8,128)(2,1)S(1)}, bf16[192,1024]{1,0:T(8,128)(2,1)}, u32[]{:S(2)}, u32[]{:S(2)}) collective-permute-start(bf16[192,1024]{1,0:T(8,128)(2,1)S(1)} %bitcast.181), channel_id=1, source_target_pairs={{0,8},{4,12},{8,0},{12,4},{1,9},{5,13},{9,1},{13,5},{2,10},{6,14},... | collective-permute-start | bytes 1179656 | tf_op jit(solution)/shard_map/ppermute | solution.py:168
  19.6 61.3 %collective-permute-start.2 = (bf16[192,256]{1,0:T(8,128)(2,1)}, bf16[192,256]{1,0:T(8,128)(2,1)}, u32[]{:S(2)}, u32[]{:S(2)}) collective-permute-start(bf16[192,256]{1,0:T(8,128)(2,1)} %get-tuple-element.57), channel_id=1, source_target_pairs={{0,1},{1,2},{2,3},{3,0},{4,5},{5,6},{6,7},{7,4},{8,9},{9,10},{10,1... | collective-permute-start | bytes 294920 | tf_op jit(solution)/shard_map/ppermute | solution.py:178
  19.6 59.3 %collective-permute-start.4 = (bf16[192,256]{1,0:T(8,128)(2,1)}, bf16[192,256]{1,0:T(8,128)(2,1)S(1)}, u32[]{:S(2)}, u32[]{:S(2)}) collective-permute-start(bf16[192,256]{1,0:T(8,128)(2,1)} %get-tuple-element.58), channel_id=1, source_target_pairs={{0,3},{1,0},{2,1},{3,2},{4,7},{5,4},{6,5},{7,6},{8,11},{9,8},{10,9... | collective-permute-start | bytes 294920 | tf_op jit(solution)/shard_map/ppermute | solution.py:178
  21.4 19.9 %collective-permute-start.7 = (bf16[192,1024]{1,0:T(8,128)(2,1)}, bf16[192,1024]{1,0:T(8,128)(2,1)}, u32[]{:S(2)}, u32[]{:S(2)}) collective-permute-start(bf16[192,1024]{1,0:T(8,128)(2,1)} %bitcast.182), channel_id=1, source_target_pairs={{0,4},{4,8},{8,12},{12,0},{1,5},{5,9},{9,13},{13,1},{2,6},{6,10},{... | collective-permute-start | bytes 1179656 | tf_op jit(solution)/shard_map/ppermute | solution.py:168
  27.8 22.2 %collective-permute-start.5 = (bf16[192,1024]{1,0:T(8,128)(2,1)}, bf16[192,1024]{1,0:T(8,128)(2,1)}, u32[]{:S(2)}, u32[]{:S(2)}) collective-permute-start(bf16[192,1024]{1,0:T(8,128)(2,1)} %bitcast.183), channel_id=1, source_target_pairs={{0,12},{4,0},{8,4},{12,8},{1,13},{5,1},{9,5},{13,9},{2,14},{6,2},{... | collective-permute-start | bytes 1179656 | tf_op jit(solution)/shard_map/ppermute | solution.py:168
  30.1 4.9 %copy-start.13 = (s32[1,4,1024]{2,1,0:T(4,128)S(1)}, s32[1,4,1024]{2,1,0:T(4,128)}, u32[]{:S(2)}) copy-start(s32[1,4,1024]{2,1,0:T(4,128)} %param.12) | copy-start | bytes 49156
  34.0 6.5 %copy-start.12 = (s32[256,15]{0,1:T(8,128)S(1)}, s32[256,15]{0,1:T(8,128)}, u32[]{:S(2)}) copy-start(s32[256,15]{0,1:T(8,128)} %param.18) | copy-start | bytes 46084
  36.2 9.9 %copy-start.8 = (bf16[192,1024]{1,0:T(8,128)(2,1)S(1)}, bf16[192,1024]{1,0:T(8,128)(2,1)}, u32[]{:S(2)}) copy-start(bf16[192,1024]{1,0:T(8,128)(2,1)} %param.14) | copy-start | bytes 1179652
  37.2 12.8 %copy-start.9 = (bf16[192,1024]{1,0:T(8,128)(2,1)S(1)}, bf16[192,1024]{1,0:T(8,128)(2,1)}, u32[]{:S(2)}) copy-start(bf16[192,1024]{1,0:T(8,128)(2,1)} %param.13) | copy-start | bytes 1179652
  41.3 43.1 %copy-start.10 = (f32[256,256]{1,0:T(8,128)}, f32[256,256]{1,0:T(8,128)S(1)}, u32[]{:S(2)}) copy-start(f32[256,256]{1,0:T(8,128)S(1)} %convert_reduce_fusion) | copy-start | bytes 786436
  41.3 38.8 %collective-permute-start.3 = (bf16[192,256]{1,0:T(8,128)(2,1)}, bf16[192,256]{1,0:T(8,128)(2,1)S(1)}, u32[]{:S(2)}, u32[]{:S(2)}) collective-permute-start(bf16[192,256]{1,0:T(8,128)(2,1)} %get-tuple-element.59), channel_id=1, source_target_pairs={{0,2},{1,3},{2,0},{3,1},{4,6},{5,7},{6,4},{7,5},{8,10},{9,11},{10,... | collective-permute-start | bytes 294920 | tf_op jit(solution)/shard_map/ppermute | solution.py:178
  46.1 12.1 %collective-permute-start = (bf16[192,1024]{1,0:T(8,128)(2,1)S(1)}, bf16[192,1024]{1,0:T(8,128)(2,1)S(1)}, u32[]{:S(2)}, u32[]{:S(2)}) collective-permute-start(bf16[192,1024]{1,0:T(8,128)(2,1)S(1)} %copy-done.8), channel_id=1, source_target_pairs={{0,2},{1,3},{2,0},{3,1},{4,6},{5,7},{6,4},{7,5},{8,10},{9,11},{10,... | collective-permute-start | bytes 1179656 | tf_op jit(solution)/shard_map/ppermute | solution.py:124
  46.7 11.5 %copy-start.6 = (bf16[256,1024]{1,0:T(8,128)(2,1)S(1)}, bf16[256,1024]{1,0:T(8,128)(2,1)}, u32[]{:S(2)}) copy-start(bf16[256,1024]{1,0:T(8,128)(2,1)} %param.16) | copy-start | bytes 1572868
  50.0 16.6 %collective-permute-start.8 = (bf16[192,1024]{1,0:T(8,128)(2,1)S(1)}, bf16[192,1024]{1,0:T(8,128)(2,1)S(1)}, u32[]{:S(2)}, u32[]{:S(2)}) collective-permute-start(bf16[192,1024]{1,0:T(8,128)(2,1)S(1)} %copy-done.9), channel_id=1, source_target_pairs={{0,2},{1,3},{2,0},{3,1},{4,6},{5,7},{6,4},{7,5},{8,10},{9,11},{10,... | collective-permute-start | bytes 1179656 | tf_op jit(solution)/shard_map/ppermute | solution.py:124
  56.8 23.7 %copy-start.3 = (bf16[192,1024]{1,0:T(8,128)(2,1)}, bf16[192,1024]{1,0:T(8,128)(2,1)S(1)}, u32[]{:S(2)}) copy-start(bf16[192,1024]{1,0:T(8,128)(2,1)S(1)} %divide_convert_fusion) | copy-start | bytes 1179652
  58.2 16.7 %collective-permute-start.13 = (bf16[256,1024]{1,0:T(8,128)(2,1)S(1)}, bf16[256,1024]{1,0:T(8,128)(2,1)S(1)}, u32[]{:S(2)}, u32[]{:S(2)}) collective-permute-start(bf16[256,1024]{1,0:T(8,128)(2,1)S(1)} %copy-done.6), channel_id=1, source_target_pairs={{0,2},{1,3},{2,0},{3,1},{4,6},{5,7},{6,4},{7,5},{8,10},{9,11},{10,... | collective-permute-start | bytes 1572872 | tf_op jit(solution)/shard_map/ppermute | solution.py:124
  66.7 8.5 %collective-permute-start.1 = (bf16[2,192,1024]{2,1,0:T(8,128)(2,1)S(1)}, bf16[2,192,1024]{2,1,0:T(8,128)(2,1)S(1)}, u32[]{:S(2)}, u32[]{:S(2)}) collective-permute-start(bf16[2,192,1024]{2,1,0:T(8,128)(2,1)S(1)} %pad_maximum_fusion.6), channel_id=1, source_target_pairs={{0,1},{1,0},{2,3},{3,2},{4,5},{5,4},{6,7},{7,6},{8,9},{9,8},{10,11... | collective-permute-start | bytes 2359304 | tf_op jit(solution)/shard_map/ppermute | solution.py:124
  74.9 2.3 %collective-permute-start.9 = (bf16[2,192,1024]{2,1,0:T(8,128)(2,1)S(1)}, bf16[2,192,1024]{2,1,0:T(8,128)(2,1)S(1)}, u32[]{:S(2)}, u32[]{:S(2)}) collective-permute-start(bf16[2,192,1024]{2,1,0:T(8,128)(2,1)S(1)} %pad_maximum_fusion.7), channel_id=1, source_target_pairs={{0,1},{1,0},{2,3},{3,2},{4,5},{5,4},{6,7},{7,6},{8,9},{9,8},{10,11... | collective-permute-start | bytes 2359304 | tf_op jit(solution)/shard_map/ppermute | solution.py:124
  75.1 8.9 %collective-permute-start.10 = (bf16[192,256]{1,0:T(8,128)(2,1)S(1)}, bf16[192,256]{1,0:T(8,128)(2,1)S(1)}, u32[]{:S(2)}, u32[]{:S(2)}) collective-permute-start(bf16[192,256]{1,0:T(8,128)(2,1)S(1)} %get-tuple-element.54), channel_id=1, source_target_pairs={{0,1},{1,2},{2,3},{3,0},{4,5},{5,6},{6,7},{7,4},{8,9},{9,10},{10,1... | collective-permute-start | bytes 294920 | tf_op jit(solution)/shard_map/ppermute | solution.py:202
  77.2 5.0 %collective-permute-start.12 = (bf16[192,256]{1,0:T(8,128)(2,1)S(1)}, bf16[192,256]{1,0:T(8,128)(2,1)S(1)}, u32[]{:S(2)}, u32[]{:S(2)}) collective-permute-start(bf16[192,256]{1,0:T(8,128)(2,1)S(1)} %get-tuple-element.55), channel_id=1, source_target_pairs={{0,3},{1,0},{2,1},{3,2},{4,7},{5,4},{6,5},{7,6},{8,11},{9,8},{10,9... | collective-permute-start | bytes 294920 | tf_op jit(solution)/shard_map/ppermute | solution.py:202
  78.9 4.8 %collective-permute-start.11 = (bf16[192,256]{1,0:T(8,128)(2,1)S(1)}, bf16[192,256]{1,0:T(8,128)(2,1)S(1)}, u32[]{:S(2)}, u32[]{:S(2)}) collective-permute-start(bf16[192,256]{1,0:T(8,128)(2,1)S(1)} %get-tuple-element.56), channel_id=1, source_target_pairs={{0,2},{1,3},{2,0},{3,1},{4,6},{5,7},{6,4},{7,5},{8,10},{9,11},{10,... | collective-permute-start | bytes 294920 | tf_op jit(solution)/shard_map/ppermute | solution.py:202
  80.1 5.1 %collective-permute-start.14 = (bf16[2,256,1024]{2,1,0:T(8,128)(2,1)S(1)}, bf16[2,256,1024]{2,1,0:T(8,128)(2,1)S(1)}, u32[]{:S(2)}, u32[]{:S(2)}) collective-permute-start(bf16[2,256,1024]{2,1,0:T(8,128)(2,1)S(1)} %pad_maximum_fusion.4), channel_id=1, source_target_pairs={{0,1},{1,0},{2,3},{3,2},{4,5},{5,4},{6,7},{7,6},{8,9},{9,8},{10,11... | collective-permute-start | bytes 3145736 | tf_op jit(solution)/shard_map/ppermute | solution.py:124
  92.0 4.4 %collective-permute-start.15 = (bf16[2,2,2,64,1024]{4,3,2,1,0:T(8,128)(2,1)}, bf16[2,2,2,64,1024]{4,3,2,1,0:T(8,128)(2,1)}, u32[]{:S(2)}, u32[]{:S(2)}) collective-permute-start(bf16[2,2,2,64,1024]{4,3,2,1,0:T(8,128)(2,1)} %fusion.5), channel_id=1, source_target_pairs={{0,1},{1,0},{2,3},{3,2},{4,5},{5,4},{6,7},{7,6},{8,9},{9,8},{10,11... | collective-permute-start | bytes 3145736 | tf_op jit(solution)/shard_map/ppermute | solution.py:94
  98.1 14.7 %collective-permute-start.16 = (bf16[256,1024]{1,0:T(8,128)(2,1)}, bf16[256,1024]{1,0:T(8,128)(2,1)}, u32[]{:S(2)}, u32[]{:S(2)}) collective-permute-start(bf16[256,1024]{1,0:T(8,128)(2,1)} %multiply_convert_fusion), channel_id=1, source_target_pairs={{0,2},{1,3},{2,0},{3,1},{4,6},{5,7},{6,4},{7,5},{8,10},{9,11},{10,... | collective-permute-start | bytes 1572872 | tf_op jit(solution)/shard_map/ppermute | solution.py:124
  100.5 20.3 %collective-permute-start.20 = (bf16[2,2,64,1024]{3,2,1,0:T(8,128)(2,1)}, bf16[2,2,64,1024]{3,2,1,0:T(8,128)(2,1)}, u32[]{:S(2)}, u32[]{:S(2)}) collective-permute-start(bf16[2,2,64,1024]{3,2,1,0:T(8,128)(2,1)} %fusion.9), channel_id=1, source_target_pairs={{0,4},{1,5},{2,6},{3,7},{4,0},{5,1},{6,2},{7,3},{8,12},{9,13},{10,... | collective-permute-start | bytes 1572872 | tf_op jit(solution)/shard_map/ppermute | solution.py:94
  115.1 32.0 %collective-permute-start.17 = (bf16[2,256,1024]{2,1,0:T(8,128)(2,1)}, bf16[2,256,1024]{2,1,0:T(8,128)(2,1)}, u32[]{:S(2)}, u32[]{:S(2)}) collective-permute-start(bf16[2,256,1024]{2,1,0:T(8,128)(2,1)} %pad_maximum_fusion.5), channel_id=1, source_target_pairs={{0,1},{1,0},{2,3},{3,2},{4,5},{5,4},{6,7},{7,6},{8,9},{9,8},{10,11... | collective-permute-start | bytes 3145736 | tf_op jit(solution)/shard_map/ppermute | solution.py:124
  123.0 17.5 %collective-permute-start.21 = (bf16[2,64,1024]{2,1,0:T(8,128)(2,1)S(1)}, bf16[2,64,1024]{2,1,0:T(8,128)(2,1)S(1)}, u32[]{:S(2)}, u32[]{:S(2)}) collective-permute-start(bf16[2,64,1024]{2,1,0:T(8,128)(2,1)S(1)} %fusion.32), channel_id=1, source_target_pairs={{0,8},{1,9},{2,10},{3,11},{4,12},{5,13},{6,14},{7,15},{8,0},{9,1},... | collective-permute-start | bytes 786440 | tf_op jit(solution)/shard_map/ppermute | solution.py:94
  141.6 5.4 %collective-permute-start.22 = (bf16[64,1024]{1,0:T(8,128)(2,1)S(1)}, bf16[64,1024]{1,0:T(8,128)(2,1)S(1)}, u32[]{:S(2)}, u32[]{:S(2)}) collective-permute-start(bf16[64,1024]{1,0:T(8,128)(2,1)S(1)} %fusion.36), channel_id=1, source_target_pairs={{0,2},{1,3},{2,0},{3,1},{4,6},{5,7},{6,4},{7,5},{8,10},{9,11},{10,... | collective-permute-start | bytes 393224 | tf_op jit(solution)/shard_map/ppermute | solution.py:94
  147.1 9.3 %collective-permute-start.23 = (bf16[64,1024]{1,0:T(8,128)(2,1)S(1)}, bf16[64,1024]{1,0:T(8,128)(2,1)S(1)}, u32[]{:S(2)}, u32[]{:S(2)}) collective-permute-start(bf16[64,1024]{1,0:T(8,128)(2,1)S(1)} %fusion.33), channel_id=1, source_target_pairs={{0,8},{4,12},{8,0},{12,4},{1,9},{5,13},{9,1},{13,5},{2,10},{6,14},... | collective-permute-start | bytes 393224 | tf_op jit(solution)/shard_map/ppermute | solution.py:124
  154.2 14.3 %collective-permute-start.18 = (bf16[2,384,256]{2,1,0:T(8,128)(2,1)S(1)}, bf16[2,384,256]{2,1,0:T(8,128)(2,1)S(1)}, u32[]{:S(2)}, u32[]{:S(2)}) collective-permute-start(bf16[2,384,256]{2,1,0:T(8,128)(2,1)S(1)} %fusion.10), channel_id=1, source_target_pairs={{0,4},{4,0},{8,12},{12,8},{1,5},{5,1},{9,13},{13,9},{2,6},{6,2},{1... | collective-permute-start | bytes 1179656 | tf_op jit(solution)/shard_map/ppermute | solution.py:94
  156.4 15.7 %collective-permute-start.24 = (bf16[2,64,1024]{2,1,0:T(8,128)(2,1)S(1)}, bf16[2,64,1024]{2,1,0:T(8,128)(2,1)S(1)}, u32[]{:S(2)}, u32[]{:S(2)}) collective-permute-start(bf16[2,64,1024]{2,1,0:T(8,128)(2,1)S(1)} %pad_maximum_fusion.8), channel_id=1, source_target_pairs={{0,4},{4,0},{8,12},{12,8},{1,5},{5,1},{9,13},{13,9},{2,6},{6,2},{1... | collective-permute-start | bytes 786440 | tf_op jit(solution)/shard_map/ppermute | solution.py:124
  168.6 9.2 %collective-permute-start.19 = (bf16[384,256]{1,0:T(8,128)(2,1)S(1)}, bf16[384,256]{1,0:T(8,128)(2,1)S(1)}, u32[]{:S(2)}, u32[]{:S(2)}) collective-permute-start(bf16[384,256]{1,0:T(8,128)(2,1)S(1)} %fusion.35), channel_id=1, source_target_pairs={{0,8},{4,12},{8,0},{12,4},{1,9},{5,13},{9,1},{13,5},{2,10},{6,14},... | collective-permute-start | bytes 589832 | tf_op jit(solution)/shard_map/ppermute | solution.py:94
  (9 other events, 16.0 us)

commit v10 on v8

--- a/solution.py
+++ b/solution.py
@@ -183,6 +183,10 @@
             rows_t = lax.ppermute(rows_t, "dom", _shift_pairs(n_dom, shift))
         targets = lax.dynamic_index_in_dim(edge_target[0], src, 0, keepdims=True)
         summed_t, counts = accumulate(targets, rows_t, summed_t, counts)
+        if shift == min(1, n_dom - 1):
+            summed_t, counts, neigh_full, full_upper = lax.optimization_barrier(
+                (summed_t, counts, neigh_full, full_upper)
+            )
     mean_t = (summed_t / jnp.maximum(counts[:1], 1.0)).astype(jnp.bfloat16)
     both_t = jnp.concatenate([mean_t, own_t], axis=0)
 

time: 163 us -> 165 us (1.012)
  matrix products: 14 us -> 17 us
  waiting for transfers between devices: 54.1 us -> 51.8 us
  local copies, waits for them, and re-layouts: 39.8 us -> 41.8 us
    ppermute x10, waiting for transfers between devices: 19 us -> 13.6 us  [all_gather_blocks(): got = lax.ppermute(cur, axis, _xor_pairs(n, 1 << b))]
    ppermute x6, waiting for transfers between devices: 31.6 us -> 35.2 us  [_butterfly_reduce(): got = lax.ppermute(send.astype(send_dtype), axis, _xor_pairs(n, 1 << b))]
    ppermute x3, waiting for transfers between devices: 3.49 us -> 0.01 us  [local(): rows_t = lax.ppermute(rows_t, 'dom', _shift_pairs(n_dom, shift))]
    ppermute x6, waiting for transfers between devices: 0.02 us -> 2.96 us  [local(): chunk = lax.ppermute(chunk, 'cols', _shift_pairs(n_cols, shift))]
    dot_general x9, matrix products: 5.42 us -> 8.36 us  [contract_rows(): lax.dot_general(left_mat, right_mat, (((0,), (0,)), ((), ())), preferred_...]
    unnamed x35 -> x47, local copies, waits for them, and re-layouts: 9.24 us -> 8.97 us
  transfers between devices with their start and end apart: 25 -> 25, of which waited for: 8 -> 10; matrix products, arithmetic and copies ran while one was open for 34% -> 32% of each run, Pallas kernels for 8% -> 8%
where the time goes in v10:
time: 165 us; the launch traced here: 164 us
  waiting for transfers between devices  51.8 us (31%)
  local copies, waits for them, and re-layouts  41.8 us (25%)
  starting transfers between devices  23.4 us (14%)
  matrix products  17 us (10%)
  other arithmetic  15.3 us (9%)
  Pallas kernels  13.1 us (8%)
    ppermute x6, waiting for transfers between devices, _butterfly_reduce(): got = lax.ppermute(send.astype(send_dtype), axis, _xor_pairs(n, 1 << b))  35.2 us
    gather x8, local copies, waits for them, and re-layouts, local(): rows_t = features.at[slots].get(mode='promise_in_bounds').T  19.5 us
    ppermute x10, waiting for transfers between devices, all_gather_blocks(): got = lax.ppermute(cur, axis, _xor_pairs(n, 1 << b))  13.6 us
    pallas_call x4, Pallas kernels, accumulate(): pl.pallas_call(_accumulate_kernel, out_shape=[jax.ShapeDtypeStruct(acc_su...  13.1 us
    unnamed x47, local copies, waits for them, and re-layouts  8.97 us
    dot_general x9, matrix products, contract_rows(): lax.dot_general(left_mat, right_mat, (((0,), (0,)), ((), ())), preferred_...  8.36 us
    another operation x18, other arithmetic, join(): return jnp.stack([low, high], axis=k - 1 - b)  7.57 us
    ppermute x10, starting transfers between devices, all_gather_blocks(): got = lax.ppermute(cur, axis, _xor_pairs(n, 1 << b))  7.08 us
  transfers between devices with their start and end apart: 25, of which 10 were waited for; matrix products, arithmetic and copies ran while one was open for 32% of the time, Pallas kernels for 8%

profile of v10, /device:TPU:0, one launch (start us, length us, event | category | flops | bytes accessed | tf_op | source)
XLA Modules:
  0.0 163.7 jit_solution(15474906243925178049)
XLA Ops:
  0.7 3.2 %copy.50 = bf16[4096,192]{1,0:T(8,128)(2,1)S(1)} copy(bf16[4096,192]{0,1:T(8,128)(2,1)} %param.10) | data formatting | bytes 3145728 | tf_op args[0]
  4.0 3.9 %gather_fusion.2 = bf16[1024,192]{1,0:T(8,128)(2,1)S(1)} fusion(bf16[4096,192]{1,0:T(8,128)(2,1)S(1)} %copy.50, s32[1024]{0:T(1024)S(1)} %broadcast_clamp_fusion.1), kind=kCustom, calls=%fused_computation.2 | custom fusion | bytes 790528 | tf_op jit(solution)/shard_map/gather | solution.py:181
  8.9 3.0 %collective-permute-start.7 = (bf16[192,1024]{1,0:T(8,128)(2,1)}, bf16[192,1024]{1,0:T(8,128)(2,1)}, u32[]{:S(2)}, u32[]{:S(2)}) collective-permute-start(bf16[192,1024]{1,0:T(8,128)(2,1)} %bitcast.24), channel_id=1, source_target_pairs={{0,4},{4,8},{8,12},{12,0},{1,5},{5,9},{9,13},{13,1},{2,6},{6,10},{... | collective-permute-start | bytes 1179656 | tf_op jit(solution)/shard_map/ppermute | solution.py:183
  11.9 1.5 collective-permute-start
  13.9 1.5 collective-permute-start.10
  15.4 3.9 %gather_fusion.1 = bf16[1024,192]{1,0:T(8,128)(2,1)S(1)} fusion(bf16[4096,192]{1,0:T(8,128)(2,1)S(1)} %copy.50, s32[1024]{0:T(1024)S(1)} %broadcast_clamp_fusion.2), kind=kCustom, calls=%fused_computation.1 | custom fusion | bytes 790528 | tf_op jit(solution)/shard_map/gather | solution.py:181
  20.3 2.6 %collective-permute-start.6 = (bf16[192,1024]{1,0:T(8,128)(2,1)}, bf16[192,1024]{1,0:T(8,128)(2,1)}, u32[]{:S(2)}, u32[]{:S(2)}) collective-permute-start(bf16[192,1024]{1,0:T(8,128)(2,1)} %bitcast.20), channel_id=1, source_target_pairs={{0,8},{4,12},{8,0},{12,4},{1,9},{5,13},{9,1},{13,5},{2,10},{6,14},... | collective-permute-start | bytes 1179656 | tf_op jit(solution)/shard_map/ppermute | solution.py:183
  23.5 3.9 %gather_fusion.3 = bf16[1024,192]{1,0:T(8,128)(2,1)S(1)} fusion(bf16[4096,192]{1,0:T(8,128)(2,1)S(1)} %copy.50, s32[1024]{0:T(1024)S(1)} %broadcast_clamp_fusion), kind=kCustom, calls=%fused_computation.3 | custom fusion | bytes 790528 | tf_op jit(solution)/shard_map/gather | solution.py:181
  28.4 3.9 %gather_fusion = bf16[1024,192]{1,0:T(8,128)(2,1)S(1)} fusion(bf16[4096,192]{1,0:T(8,128)(2,1)S(1)} %copy.50, s32[1024]{0:T(1024)S(1)} %broadcast_clamp_fusion.3), kind=kCustom, calls=%fused_computation | custom fusion | bytes 790528 | tf_op jit(solution)/shard_map/gather | solution.py:181
  33.3 1.8 %slice_bitcast_fusion = (bf16[192,1024]{1,0:T(8,128)(2,1)}, bf16[1024,192]{0,1:T(8,128)(2,1)S(1)}) fusion(bf16[4096,192]{0,1:T(8,128)(2,1)} %param.10), kind=kLoop, calls=%fused_computation.147 | loop fusion | bytes 1179648 | tf_op jit(solution)/shard_map/transpose | solution.py:164
  40.2 3.3 %shard_map.129 = (f32[192,1024]{1,0:T(8,128)}, f32[8,1024]{1,0:T(8,128)}) custom-call(s32[1,1024]{1,0:T(1,128)} %get-tuple-element.66.tgt_ref, bf16[192,1024]{1,0:T(8,128)(2,1)} %bitcast.181, f32[192,1024]{1,0:T(8,128)} %broadcast_in_dim.4.sum_in, f32[8,1024]{1,0:T(8,128)} %broadcast_in_dim.5.cnt_in), custom_call_target="tpu_custom_call", output_to_operand_aliasing={{0}: (2, {}), {1}: (3, {})} | custom-call | flops 419430400 | bytes 2035712 | tf_op jit(solution)/shard_map/pallas_call | solution.py:46
  45.6 3.3 %shard_map.130 = (f32[192,1024]{1,0:T(8,128)}, f32[8,1024]{1,0:T(8,128)}) custom-call(s32[1,1024]{1,0:T(1,128)} %get-tuple-element.69.tgt_ref, bf16[192,1024]{1,0:T(8,128)(2,1)} %collective-permute-done.7.rec_ref, f32[192,1024]{1,0:T(8,128)} %get-tuple-element.18.sum_in, ...), custom_call_target="tpu_custom_call", output_to_operand_aliasing={{0}: (2, {}), {1}: (3, {})} | custom-call | flops 419430400 | bytes 2035712 | tf_op jit(solution)/shard_map/pallas_call | solution.py:46
  53.1 1.5 collective-permute-start.3
  54.6 2.2 %fusion.18 = f32[256,1024]{1,0:T(8,128)} fusion(bf16[192,256]{1,0:T(8,128)(2,1)} %collective-permute-done.4, bf16[4,192,1024]{2,1,0:T(8,128)(2,1)S(1)} %bitcast.168, s32[]{:T(128)S(6)} %select_n.342), kind=kOutput, calls=%fused_computation.67 | convolution fusion | flops 100663296 | bytes 1540100 | tf_op jit(solution)/shard_map/dot_general | solution.py:23
  59.6 1.5 copy.59
  61.1 3.3 %shard_map.131 = (f32[192,1024]{1,0:T(8,128)}, f32[8,1024]{1,0:T(8,128)}) custom-call(s32[1,1024]{1,0:T(1,128)} %get-tuple-element.67.tgt_ref, bf16[192,1024]{1,0:T(8,128)(2,1)} %collective-permute-done.6.rec_ref, f32[192,1024]{1,0:T(8,128)} %get-tuple-element.22.sum_in, ...), custom_call_target="tpu_custom_call", output_to_operand_aliasing={{0}: (2, {}), {1}: (3, {})} | custom-call | flops 419430400 | bytes 2035712 | tf_op jit(solution)/shard_map/pallas_call | solution.py:46
  64.4 3.3 %shard_map.132 = (f32[192,1024]{1,0:T(8,128)}, f32[8,1024]{1,0:T(8,128)}) custom-call(s32[1,1024]{1,0:T(1,128)} %get-tuple-element.68.tgt_ref, bf16[192,1024]{1,0:T(8,128)(2,1)} %collective-permute-done.5.rec_ref, f32[192,1024]{1,0:T(8,128)} %get-tuple-element.24.sum_in, ...), custom_call_target="tpu_custom_call", output_to_operand_aliasing={{0}: (2, {}), {1}: (3, {})} | custom-call | flops 419430400 | bytes 2035712 | tf_op jit(solution)/shard_map/pallas_call | solution.py:46
  69.9 1.6 collective-permute-start.13
  79.0 1.6 %multiply_convert_fusion.2 = (bf16[256,1024]{1,0:T(8,128)(2,1)}, f32[256,1024]{1,0:T(8,128)S(1)}) fusion(f32[1024]{0:T(1024)S(1)} %copy-done.22, bf16[256,1024]{1,0:T(8,128)(2,1)S(1)} %convolution_convert_fusion, bf16[1024,1024]{1,0:T(8,128)(2,1)S(1)} %bitcast.175), kind=kOutput, calls=%fused_computation.31 | convolution fusion | flops 538443776 | bytes 4198400 | tf_op jit(solution)/shard_map/dot_general | solution.py:207
  81.6 2.0 %copy-done = f32[1024,1024]{1,0:T(8,128)} copy-done((f32[1024,1024]{1,0:T(8,128)}, f32[1024,1024]{1,0:T(8,128)S(1)}, u32[]{:S(2)}) %copy-start) | copy-done | bytes 4194328
  85.7 2.3 %fusion.61 = f32[256,1024]{1,0:T(8,128)S(1)} fusion(bf16[1024,1024]{1,0:T(8,128)(2,1)S(1)} %bitcast.176, f32[256,1024]{1,0:T(8,128)} %copy-done.9, bf16[256,1024]{1,0:T(8,128)(2,1)} %param.19), kind=kOutput, calls=%fused_computation.148 | convolution fusion | flops 539492352 | bytes 4718592 | tf_op jit(solution)/shard_map/dot_general | solution.py:212
  90.3 1.6 bitcast_add_fusion
  91.8 1.5 collective-permute-start.16
  94.9 11.0 %collective-permute-done.16 = bf16[256,1024]{1,0:T(8,128)(2,1)} collective-permute-done((bf16[256,1024]{1,0:T(8,128)(2,1)S(1)}, bf16[256,1024]{1,0:T(8,128)(2,1)}, u32[]{:S(2)}, u32[]{:S(2)}) %collective-permute-start.16) | collective-permute-done | bytes 524320 | tf_op jit(solution)/shard_map/ppermute | solution.py:124
  110.9 14.9 %collective-permute-done.21 = bf16[2,64,1024]{2,1,0:T(8,128)(2,1)S(1)} collective-permute-done((bf16[2,64,1024]{2,1,0:T(8,128)(2,1)S(1)}, bf16[2,64,1024]{2,1,0:T(8,128)(2,1)S(1)}, u32[]{:S(2)}, u32[]{:S(2)}) %collective-permute-start.21) | collective-permute-done | bytes 262176 | tf_op jit(solution)/shard_map/ppermute | solution.py:94
  126.9 1.5 collective-permute-start.22
  128.4 3.9 %collective-permute-done.22 = bf16[64,1024]{1,0:T(8,128)(2,1)S(1)} collective-permute-done((bf16[64,1024]{1,0:T(8,128)(2,1)S(1)}, bf16[64,1024]{1,0:T(8,128)(2,1)S(1)}, u32[]{:S(2)}, u32[]{:S(2)}) %collective-permute-start.22) | collective-permute-done | bytes 131104 | tf_op jit(solution)/shard_map/ppermute | solution.py:94
  134.1 2.6 %copy.61 = bf16[1024,1024]{1,0:T(8,128)(2,1)} copy(bf16[1024,1024]{0,1:T(8,128)(2,1)S(1)} %bitcast.166) | data formatting | bytes 4194304 | tf_op jit(solution)/shard_map/dot_general | solution.py:226
  136.7 2.6 %fusion.6 = f32[384,4,256]{2,0,1:T(8,128)S(1)} fusion(bf16[4,256,1024]{2,1,0:T(8,128)(2,1)} %bitcast.177, bf16[192,1024]{1,0:T(8,128)(2,1)S(1)} %copy-done.12, bf16[192,1024]{1,0:T(8,128)(2,1)S(1)} %divide_convert_fusion), kind=kOutput, calls=%fused_computation.40 | convolution fusion | flops 806879232 | bytes 4456448 | tf_op jit(solution)/shard_map/dot_general | solution.py:226
  141.6 12.0 %collective-permute-done.18 = bf16[2,384,256]{2,1,0:T(8,128)(2,1)S(1)} collective-permute-done((bf16[2,384,256]{2,1,0:T(8,128)(2,1)S(1)}, bf16[2,384,256]{2,1,0:T(8,128)(2,1)S(1)}, u32[]{:S(2)}, u32[]{:S(2)}) %collective-permute-start.18) | collective-permute-done | bytes 393248 | tf_op jit(solution)/shard_map/ppermute | solution.py:94
  154.6 2.6 %collective-permute-done.24 = bf16[2,64,1024]{2,1,0:T(8,128)(2,1)S(1)} collective-permute-done((bf16[2,64,1024]{2,1,0:T(8,128)(2,1)S(1)}, bf16[2,64,1024]{2,1,0:T(8,128)(2,1)S(1)}, u32[]{:S(2)}, u32[]{:S(2)}) %collective-permute-start.24) | collective-permute-done | bytes 262176 | tf_op jit(solution)/shard_map/ppermute | solution.py:124
  158.4 4.5 %collective-permute-done.19 = bf16[384,256]{1,0:T(8,128)(2,1)S(1)} collective-permute-done((bf16[384,256]{1,0:T(8,128)(2,1)S(1)}, bf16[384,256]{1,0:T(8,128)(2,1)S(1)}, u32[]{:S(2)}, u32[]{:S(2)}) %collective-permute-start.19) | collective-permute-done | bytes 196640 | tf_op jit(solution)/shard_map/ppermute | solution.py:94
  (142 shorter events, 48.8 us)
Async XLA Ops:
  3.9 7.9 %copy-start.14 = (bf16[192,1024]{1,0:T(8,128)(2,1)S(1)}, bf16[192,1024]{1,0:T(8,128)(2,1)}, u32[]{:S(2)}) copy-start(bf16[192,1024]{1,0:T(8,128)(2,1)} %param.14) | copy-start | bytes 1179652
  4.0 9.4 %copy-start.13 = (bf16[192,1024]{1,0:T(8,128)(2,1)S(1)}, bf16[192,1024]{1,0:T(8,128)(2,1)}, u32[]{:S(2)}) copy-start(bf16[192,1024]{1,0:T(8,128)(2,1)} %param.13) | copy-start | bytes 1179652
  8.9 36.1 %collective-permute-start.7 = (bf16[192,1024]{1,0:T(8,128)(2,1)}, bf16[192,1024]{1,0:T(8,128)(2,1)}, u32[]{:S(2)}, u32[]{:S(2)}) collective-permute-start(bf16[192,1024]{1,0:T(8,128)(2,1)} %bitcast.24), channel_id=1, source_target_pairs={{0,4},{4,8},{8,12},{12,0},{1,5},{5,9},{9,13},{13,1},{2,6},{6,10},{... | collective-permute-start | bytes 1179656 | tf_op jit(solution)/shard_map/ppermute | solution.py:183
  11.9 24.0 %collective-permute-start = (bf16[192,1024]{1,0:T(8,128)(2,1)S(1)}, bf16[192,1024]{1,0:T(8,128)(2,1)}, u32[]{:S(2)}, u32[]{:S(2)}) collective-permute-start(bf16[192,1024]{1,0:T(8,128)(2,1)S(1)} %copy-done.14), channel_id=1, source_target_pairs={{0,2},{1,3},{2,0},{3,1},{4,6},{5,7},{6,4},{7,5},{8,10},{9,11},{10,... | collective-permute-start | bytes 1179656 | tf_op jit(solution)/shard_map/ppermute | solution.py:124
  13.4 23.9 %collective-permute-start.8 = (bf16[192,1024]{1,0:T(8,128)(2,1)S(1)}, bf16[192,1024]{1,0:T(8,128)(2,1)}, u32[]{:S(2)}, u32[]{:S(2)}) collective-permute-start(bf16[192,1024]{1,0:T(8,128)(2,1)S(1)} %copy-done.13), channel_id=1, source_target_pairs={{0,2},{1,3},{2,0},{3,1},{4,6},{5,7},{6,4},{7,5},{8,10},{9,11},{10,... | collective-permute-start | bytes 1179656 | tf_op jit(solution)/shard_map/ppermute | solution.py:124
  13.9 35.0 %collective-permute-start.10 = (bf16[256,1024]{1,0:T(8,128)(2,1)}, bf16[256,1024]{1,0:T(8,128)(2,1)}, u32[]{:S(2)}, u32[]{:S(2)}) collective-permute-start(bf16[256,1024]{1,0:T(8,128)(2,1)} %param.16), channel_id=1, source_target_pairs={{0,2},{1,3},{2,0},{3,1},{4,6},{5,7},{6,4},{7,5},{8,10},{9,11},{10,... | collective-permute-start | bytes 1572872 | tf_op jit(solution)/shard_map/ppermute | solution.py:124
  15.4 7.5 %copy-start.20 = (s32[1,4,1024]{2,1,0:T(4,128)S(1)}, s32[1,4,1024]{2,1,0:T(4,128)}, u32[]{:S(2)}) copy-start(s32[1,4,1024]{2,1,0:T(4,128)} %param.12) | copy-start | bytes 49156
  20.3 40.8 %collective-permute-start.6 = (bf16[192,1024]{1,0:T(8,128)(2,1)}, bf16[192,1024]{1,0:T(8,128)(2,1)}, u32[]{:S(2)}, u32[]{:S(2)}) collective-permute-start(bf16[192,1024]{1,0:T(8,128)(2,1)} %bitcast.20), channel_id=1, source_target_pairs={{0,8},{4,12},{8,0},{12,4},{1,9},{5,13},{9,1},{13,5},{2,10},{6,14},... | collective-permute-start | bytes 1179656 | tf_op jit(solution)/shard_map/ppermute | solution.py:183
  35.9 28.5 %collective-permute-start.5 = (bf16[192,1024]{1,0:T(8,128)(2,1)}, bf16[192,1024]{1,0:T(8,128)(2,1)}, u32[]{:S(2)}, u32[]{:S(2)}) collective-permute-start(bf16[192,1024]{1,0:T(8,128)(2,1)} %bitcast.16), channel_id=1, source_target_pairs={{0,12},{4,0},{8,4},{12,8},{1,13},{5,1},{9,5},{13,9},{2,14},{6,2},{... | collective-permute-start | bytes 1179656 | tf_op jit(solution)/shard_map/ppermute | solution.py:183
  38.5 5.0 %copy-start.18 = (s32[256,15]{0,1:T(8,128)S(1)}, s32[256,15]{0,1:T(8,128)}, u32[]{:S(2)}) copy-start(s32[256,15]{0,1:T(8,128)} %param.18) | copy-start | bytes 46084
  38.6 11.9 %collective-permute-start.1 = (bf16[2,192,1024]{2,1,0:T(8,128)(2,1)S(1)}, bf16[2,192,1024]{2,1,0:T(8,128)(2,1)S(1)}, u32[]{:S(2)}, u32[]{:S(2)}) collective-permute-start(bf16[2,192,1024]{2,1,0:T(8,128)(2,1)S(1)} %pad_maximum_fusion.6), channel_id=1, source_target_pairs={{0,1},{1,0},{2,3},{3,2},{4,5},{5,4},{6,7},{7,6},{8,9},{9,8},{10,11... | collective-permute-start | bytes 2359304 | tf_op jit(solution)/shard_map/ppermute | solution.py:124
  45.0 8.2 %collective-permute-start.4 = (bf16[192,256]{1,0:T(8,128)(2,1)}, bf16[192,256]{1,0:T(8,128)(2,1)}, u32[]{:S(2)}, u32[]{:S(2)}) collective-permute-start(bf16[192,256]{1,0:T(8,128)(2,1)} %get-tuple-element.58), channel_id=1, source_target_pairs={{0,3},{1,0},{2,1},{3,2},{4,7},{5,4},{6,5},{7,6},{8,11},{9,8},{10,9... | collective-permute-start | bytes 294920 | tf_op jit(solution)/shard_map/ppermute | solution.py:171
  48.9 7.9 %collective-permute-start.9 = (bf16[2,192,1024]{2,1,0:T(8,128)(2,1)S(1)}, bf16[2,192,1024]{2,1,0:T(8,128)(2,1)S(1)}, u32[]{:S(2)}, u32[]{:S(2)}) collective-permute-start(bf16[2,192,1024]{2,1,0:T(8,128)(2,1)S(1)} %pad_maximum_fusion.7), channel_id=1, source_target_pairs={{0,1},{1,0},{2,3},{3,2},{4,5},{5,4},{6,7},{7,6},{8,9},{9,8},{10,11... | collective-permute-start | bytes 2359304 | tf_op jit(solution)/shard_map/ppermute | solution.py:124
  50.4 8.8 %collective-permute-start.11 = (bf16[2,256,1024]{2,1,0:T(8,128)(2,1)S(1)}, bf16[2,256,1024]{2,1,0:T(8,128)(2,1)S(1)}, u32[]{:S(2)}, u32[]{:S(2)}) collective-permute-start(bf16[2,256,1024]{2,1,0:T(8,128)(2,1)S(1)} %pad_maximum_fusion.4), channel_id=1, source_target_pairs={{0,1},{1,0},{2,3},{3,2},{4,5},{5,4},{6,7},{7,6},{8,9},{9,8},{10,11... | collective-permute-start | bytes 3145736 | tf_op jit(solution)/shard_map/ppermute | solution.py:124
  53.1 4.7 %collective-permute-start.3 = (bf16[192,256]{1,0:T(8,128)(2,1)S(1)}, bf16[192,256]{1,0:T(8,128)(2,1)S(1)}, u32[]{:S(2)}, u32[]{:S(2)}) collective-permute-start(bf16[192,256]{1,0:T(8,128)(2,1)S(1)} %copy-done.17), channel_id=1, source_target_pairs={{0,2},{1,3},{2,0},{3,1},{4,6},{5,7},{6,4},{7,5},{8,10},{9,11},{10,... | collective-permute-start | bytes 294920 | tf_op jit(solution)/shard_map/ppermute | solution.py:171
  56.8 15.4 %collective-permute-start.2 = (bf16[192,256]{1,0:T(8,128)(2,1)}, bf16[192,256]{1,0:T(8,128)(2,1)}, u32[]{:S(2)}, u32[]{:S(2)}) collective-permute-start(bf16[192,256]{1,0:T(8,128)(2,1)} %get-tuple-element.57), channel_id=1, source_target_pairs={{0,1},{1,2},{2,3},{3,0},{4,5},{5,6},{6,7},{7,4},{8,9},{9,10},{10,1... | collective-permute-start | bytes 294920 | tf_op jit(solution)/shard_map/ppermute | solution.py:171
  67.6 4.6 %copy-start.2 = (f32[256,1024]{1,0:T(8,128)S(1)}, f32[256,1024]{1,0:T(8,128)}, u32[]{:S(2)}) copy-start(f32[256,1024]{1,0:T(8,128)} %convolution_add_fusion.2) | copy-start | bytes 3145732
  67.6 4.6 %copy-start.3 = (f32[256,1024]{1,0:T(8,128)S(1)}, f32[256,1024]{1,0:T(8,128)}, u32[]{:S(2)}) copy-start(f32[256,1024]{1,0:T(8,128)} %fusion.18) | copy-start | bytes 3145732
  67.6 4.6 %copy-start.4 = (f32[256,1024]{1,0:T(8,128)S(1)}, f32[256,1024]{1,0:T(8,128)}, u32[]{:S(2)}) copy-start(f32[256,1024]{1,0:T(8,128)} %fusion.20) | copy-start | bytes 3145732
  69.9 5.0 %collective-permute-start.13 = (bf16[192,256]{1,0:T(8,128)(2,1)S(1)}, bf16[192,256]{1,0:T(8,128)(2,1)S(1)}, u32[]{:S(2)}, u32[]{:S(2)}) collective-permute-start(bf16[192,256]{1,0:T(8,128)(2,1)S(1)} %get-tuple-element.56), channel_id=1, source_target_pairs={{0,2},{1,3},{2,0},{3,1},{4,6},{5,7},{6,4},{7,5},{8,10},{9,11},{10,... | collective-permute-start | bytes 294920 | tf_op jit(solution)/shard_map/ppermute | solution.py:199
  71.4 4.3 %collective-permute-start.14 = (bf16[192,256]{1,0:T(8,128)(2,1)S(1)}, bf16[192,256]{1,0:T(8,128)(2,1)S(1)}, u32[]{:S(2)}, u32[]{:S(2)}) collective-permute-start(bf16[192,256]{1,0:T(8,128)(2,1)S(1)} %get-tuple-element.55), channel_id=1, source_target_pairs={{0,3},{1,0},{2,1},{3,2},{4,7},{5,4},{6,5},{7,6},{8,11},{9,8},{10,9... | collective-permute-start | bytes 294920 | tf_op jit(solution)/shard_map/ppermute | solution.py:199
  71.4 5.1 %collective-permute-start.12 = (bf16[192,256]{1,0:T(8,128)(2,1)S(1)}, bf16[192,256]{1,0:T(8,128)(2,1)S(1)}, u32[]{:S(2)}, u32[]{:S(2)}) collective-permute-start(bf16[192,256]{1,0:T(8,128)(2,1)S(1)} %get-tuple-element.54), channel_id=1, source_target_pairs={{0,1},{1,2},{2,3},{3,0},{4,5},{5,6},{6,7},{7,4},{8,9},{9,10},{10,1... | collective-permute-start | bytes 294920 | tf_op jit(solution)/shard_map/ppermute | solution.py:199
  84.9 4.6 %collective-permute-start.15 = (bf16[2,2,2,64,1024]{4,3,2,1,0:T(8,128)(2,1)}, bf16[2,2,2,64,1024]{4,3,2,1,0:T(8,128)(2,1)}, u32[]{:S(2)}, u32[]{:S(2)}) collective-permute-start(bf16[2,2,2,64,1024]{4,3,2,1,0:T(8,128)(2,1)} %fusion.5), channel_id=1, source_target_pairs={{0,1},{1,0},{2,3},{3,2},{4,5},{5,4},{6,7},{7,6},{8,9},{9,8},{10,11... | collective-permute-start | bytes 3145736 | tf_op jit(solution)/shard_map/ppermute | solution.py:94
  91.8 14.0 %collective-permute-start.16 = (bf16[256,1024]{1,0:T(8,128)(2,1)S(1)}, bf16[256,1024]{1,0:T(8,128)(2,1)}, u32[]{:S(2)}, u32[]{:S(2)}) collective-permute-start(bf16[256,1024]{1,0:T(8,128)(2,1)S(1)} %multiply_convert_fusion), channel_id=1, source_target_pairs={{0,2},{1,3},{2,0},{3,1},{4,6},{5,7},{6,4},{7,5},{8,10},{9,11},{10,... | collective-permute-start | bytes 1572872 | tf_op jit(solution)/shard_map/ppermute | solution.py:124
  94.2 14.0 %collective-permute-start.20 = (bf16[2,2,64,1024]{3,2,1,0:T(8,128)(2,1)}, bf16[2,2,64,1024]{3,2,1,0:T(8,128)(2,1)}, u32[]{:S(2)}, u32[]{:S(2)}) collective-permute-start(bf16[2,2,64,1024]{3,2,1,0:T(8,128)(2,1)} %fusion.9), channel_id=1, source_target_pairs={{0,4},{1,5},{2,6},{3,7},{4,0},{5,1},{6,2},{7,3},{8,12},{9,13},{10,... | collective-permute-start | bytes 1572872 | tf_op jit(solution)/shard_map/ppermute | solution.py:94
  108.2 24.2 %collective-permute-start.17 = (bf16[2,256,1024]{2,1,0:T(8,128)(2,1)}, bf16[2,256,1024]{2,1,0:T(8,128)(2,1)}, u32[]{:S(2)}, u32[]{:S(2)}) collective-permute-start(bf16[2,256,1024]{2,1,0:T(8,128)(2,1)} %pad_maximum_fusion.5), channel_id=1, source_target_pairs={{0,1},{1,0},{2,3},{3,2},{4,5},{5,4},{6,7},{7,6},{8,9},{9,8},{10,11... | collective-permute-start | bytes 3145736 | tf_op jit(solution)/shard_map/ppermute | solution.py:124
  110.5 15.3 %collective-permute-start.21 = (bf16[2,64,1024]{2,1,0:T(8,128)(2,1)S(1)}, bf16[2,64,1024]{2,1,0:T(8,128)(2,1)S(1)}, u32[]{:S(2)}, u32[]{:S(2)}) collective-permute-start(bf16[2,64,1024]{2,1,0:T(8,128)(2,1)S(1)} %fusion.32), channel_id=1, source_target_pairs={{0,8},{1,9},{2,10},{3,11},{4,12},{5,13},{6,14},{7,15},{8,0},{9,1},... | collective-permute-start | bytes 786440 | tf_op jit(solution)/shard_map/ppermute | solution.py:94
  126.9 5.4 %collective-permute-start.22 = (bf16[64,1024]{1,0:T(8,128)(2,1)S(1)}, bf16[64,1024]{1,0:T(8,128)(2,1)S(1)}, u32[]{:S(2)}, u32[]{:S(2)}) collective-permute-start(bf16[64,1024]{1,0:T(8,128)(2,1)S(1)} %fusion.36), channel_id=1, source_target_pairs={{0,2},{1,3},{2,0},{3,1},{4,6},{5,7},{6,4},{7,5},{8,10},{9,11},{10,... | collective-permute-start | bytes 393224 | tf_op jit(solution)/shard_map/ppermute | solution.py:94
  132.3 8.0 %collective-permute-start.23 = (bf16[64,1024]{1,0:T(8,128)(2,1)S(1)}, bf16[64,1024]{1,0:T(8,128)(2,1)S(1)}, u32[]{:S(2)}, u32[]{:S(2)}) collective-permute-start(bf16[64,1024]{1,0:T(8,128)(2,1)S(1)} %fusion.33), channel_id=1, source_target_pairs={{0,8},{4,12},{8,0},{12,4},{1,9},{5,13},{9,1},{13,5},{2,10},{6,14},... | collective-permute-start | bytes 393224 | tf_op jit(solution)/shard_map/ppermute | solution.py:124
  139.4 14.2 %collective-permute-start.18 = (bf16[2,384,256]{2,1,0:T(8,128)(2,1)S(1)}, bf16[2,384,256]{2,1,0:T(8,128)(2,1)S(1)}, u32[]{:S(2)}, u32[]{:S(2)}) collective-permute-start(bf16[2,384,256]{2,1,0:T(8,128)(2,1)S(1)} %fusion.10), channel_id=1, source_target_pairs={{0,4},{4,0},{8,12},{12,8},{1,5},{5,1},{9,13},{13,9},{2,6},{6,2},{1... | collective-permute-start | bytes 1179656 | tf_op jit(solution)/shard_map/ppermute | solution.py:94
  140.3 16.9 %collective-permute-start.24 = (bf16[2,64,1024]{2,1,0:T(8,128)(2,1)S(1)}, bf16[2,64,1024]{2,1,0:T(8,128)(2,1)S(1)}, u32[]{:S(2)}, u32[]{:S(2)}) collective-permute-start(bf16[2,64,1024]{2,1,0:T(8,128)(2,1)S(1)} %pad_maximum_fusion.8), channel_id=1, source_target_pairs={{0,4},{4,0},{8,12},{12,8},{1,5},{5,1},{9,13},{13,9},{2,6},{6,2},{1... | collective-permute-start | bytes 786440 | tf_op jit(solution)/shard_map/ppermute | solution.py:124
  153.7 9.2 %collective-permute-start.19 = (bf16[384,256]{1,0:T(8,128)(2,1)S(1)}, bf16[384,256]{1,0:T(8,128)(2,1)S(1)}, u32[]{:S(2)}, u32[]{:S(2)}) collective-permute-start(bf16[384,256]{1,0:T(8,128)(2,1)S(1)} %fusion.35), channel_id=1, source_target_pairs={{0,8},{4,12},{8,0},{12,4},{1,9},{5,13},{9,1},{13,5},{2,10},{6,14},... | collective-permute-start | bytes 589832 | tf_op jit(solution)/shard_map/ppermute | solution.py:94
  (16 other events, 29.4 us)

commit v11 on v10

--- a/solution.py
+++ b/solution.py
@@ -28,20 +28,18 @@
 def _accumulate_kernel(tgt_ref, rec_ref, sum_in, cnt_in, sum_ref, cnt_ref):
     targets = tgt_ref[...]
     n_tgt = sum_ref.shape[1]
-    rows = lax.broadcasted_iota(jnp.int32, (n_tgt, targets.shape[1]), 0)
-    hot = (rows == targets).astype(jnp.bfloat16)
-    dims = (((1,), (1,)), ((), ()))
-    sum_ref[...] = sum_in[...] + lax.dot_general(
-        rec_ref[...], hot, dims, preferred_element_type=jnp.float32
-    )
-    ones = jnp.ones((cnt_ref.shape[0], targets.shape[1]), jnp.bfloat16)
-    cnt_ref[...] = cnt_in[...] + lax.dot_general(
-        ones, hot, dims, preferred_element_type=jnp.float32
-    )
+    cols = lax.broadcasted_iota(jnp.int32, (targets.shape[0], n_tgt), 1)
+    hot = (cols == targets).astype(jnp.bfloat16)
+    sum_ref[...] = sum_in[...] + jnp.dot(
+        rec_ref[...], hot, preferred_element_type=jnp.float32
+    )
+    ones = jnp.ones((cnt_ref.shape[0], targets.shape[0]), jnp.bfloat16)
+    cnt_ref[...] = cnt_in[...] + jnp.dot(ones, hot, preferred_element_type=jnp.float32)
 
 
 def accumulate(targets, rec_t, acc_sum, acc_cnt):
     width, cap = rec_t.shape
+    assert targets.shape == (cap, 1)
     n_tgt = acc_sum.shape[1]
     return pl.pallas_call(
         _accumulate_kernel,
@@ -172,6 +170,7 @@
         weight = lax.dynamic_index_in_dim(self_full, src, 0, keepdims=False)
         own_pre = own_pre + contract_rows(chunk, weight)
 
+    target_cols = edge_target[0].reshape(n_dom, capacity, 1)
     summed_t = jnp.zeros((width, tgt_dev), jnp.float32)
     counts = jnp.zeros((8, tgt_dev), jnp.float32)
     for shift in range(n_dom):
@@ -181,7 +180,7 @@
         rows_t = features.at[slots].get(mode="promise_in_bounds").T
         if shift:
             rows_t = lax.ppermute(rows_t, "dom", _shift_pairs(n_dom, shift))
-        targets = lax.dynamic_index_in_dim(edge_target[0], src, 0, keepdims=True)
+        targets = lax.dynamic_index_in_dim(target_cols, src, 0, keepdims=False)
         summed_t, counts = accumulate(targets, rows_t, summed_t, counts)
         if shift == min(1, n_dom - 1):
             summed_t, counts, neigh_full, full_upper = lax.optimization_barrier(

time: 165 us -> 168 us (1.018)
  local copies, waits for them, and re-layouts: 41.8 us -> 45.3 us
    squeeze x0 -> x5, local copies, waits for them, and re-layouts: none -> 4.16 us  [local(): targets = lax.dynamic_index_in_dim(target_cols, src, 0, keepdims=False)]
    unnamed x47 -> x45, local copies, waits for them, and re-layouts: 8.97 us -> 8.91 us
  transfers between devices with their start and end apart: 25 -> 25, of which waited for: 10 -> 10; matrix products, arithmetic and copies ran while one was open for 32% -> 34% of each run, Pallas kernels for 8% -> 8%
where the time goes in v11:
time: 168 us; the launch traced here: 167 us
  waiting for transfers between devices  51.8 us (31%)
  local copies, waits for them, and re-layouts  45.3 us (27%)
  starting transfers between devices  23.4 us (14%)
  matrix products  16.6 us (10%)
  other arithmetic  15.3 us (9%)
  Pallas kernels  13 us (8%)
    ppermute x6, waiting for transfers between devices, _butterfly_reduce(): got = lax.ppermute(send.astype(send_dtype), axis, _xor_pairs(n, 1 << b))  35.2 us
    gather x8, local copies, waits for them, and re-layouts, local(): rows_t = features.at[slots].get(mode='promise_in_bounds').T  19.6 us
    ppermute x10, waiting for transfers between devices, all_gather_blocks(): got = lax.ppermute(cur, axis, _xor_pairs(n, 1 << b))  13.6 us
    pallas_call x4, Pallas kernels, accumulate(): pl.pallas_call(_accumulate_kernel, out_shape=[jax.ShapeDtypeStruct(acc_su...  13 us
    unnamed x45, local copies, waits for them, and re-layouts  8.91 us
    dot_general x9, matrix products, contract_rows(): lax.dot_general(left_mat, right_mat, (((0,), (0,)), ((), ())), preferred_...  8.22 us
    another operation x18, other arithmetic, join(): return jnp.stack([low, high], axis=k - 1 - b)  7.57 us
    ppermute x10, starting transfers between devices, all_gather_blocks(): got = lax.ppermute(cur, axis, _xor_pairs(n, 1 << b))  7.08 us
  transfers between devices with their start and end apart: 25, of which 10 were waited for; matrix products, arithmetic and copies ran while one was open for 34% of the time, Pallas kernels for 8%

profile of v11, /device:TPU:0, one launch (start us, length us, event | category | flops | bytes accessed | tf_op | source)
XLA Modules:
  0.0 166.9 jit_solution(15271822083652782646)
XLA Ops:
  0.7 3.2 %copy.54 = bf16[4096,192]{1,0:T(8,128)(2,1)S(1)} copy(bf16[4096,192]{0,1:T(8,128)(2,1)} %param.10) | data formatting | bytes 3145728 | tf_op args[0]
  4.0 3.9 %gather_fusion.2 = bf16[1024,192]{1,0:T(8,128)(2,1)S(1)} fusion(bf16[4096,192]{1,0:T(8,128)(2,1)S(1)} %copy.54, s32[1024]{0:T(1024)S(1)} %broadcast_clamp_fusion.1), kind=kCustom, calls=%fused_computation.2 | custom fusion | bytes 790528 | tf_op jit(solution)/shard_map/gather | solution.py:180
  8.9 3.0 %collective-permute-start.7 = (bf16[192,1024]{1,0:T(8,128)(2,1)}, bf16[192,1024]{1,0:T(8,128)(2,1)}, u32[]{:S(2)}, u32[]{:S(2)}) collective-permute-start(bf16[192,1024]{1,0:T(8,128)(2,1)} %bitcast.24), channel_id=1, source_target_pairs={{0,4},{4,8},{8,12},{12,0},{1,5},{5,9},{9,13},{13,1},{2,6},{6,10},{... | collective-permute-start | bytes 1179656 | tf_op jit(solution)/shard_map/ppermute | solution.py:182
  11.9 1.5 collective-permute-start
  13.9 1.5 collective-permute-start.10
  15.4 3.9 %gather_fusion.1 = bf16[1024,192]{1,0:T(8,128)(2,1)S(1)} fusion(bf16[4096,192]{1,0:T(8,128)(2,1)S(1)} %copy.54, s32[1024]{0:T(1024)S(1)} %broadcast_clamp_fusion.2), kind=kCustom, calls=%fused_computation.1 | custom fusion | bytes 790528 | tf_op jit(solution)/shard_map/gather | solution.py:180
  20.3 2.6 %collective-permute-start.6 = (bf16[192,1024]{1,0:T(8,128)(2,1)}, bf16[192,1024]{1,0:T(8,128)(2,1)}, u32[]{:S(2)}, u32[]{:S(2)}) collective-permute-start(bf16[192,1024]{1,0:T(8,128)(2,1)} %bitcast.20), channel_id=1, source_target_pairs={{0,8},{4,12},{8,0},{12,4},{1,9},{5,13},{9,1},{13,5},{2,10},{6,14},... | collective-permute-start | bytes 1179656 | tf_op jit(solution)/shard_map/ppermute | solution.py:182
  23.1 3.9 %gather_fusion.3 = bf16[1024,192]{1,0:T(8,128)(2,1)S(1)} fusion(bf16[4096,192]{1,0:T(8,128)(2,1)S(1)} %copy.54, s32[1024]{0:T(1024)S(1)} %broadcast_clamp_fusion), kind=kCustom, calls=%fused_computation.3 | custom fusion | bytes 790528 | tf_op jit(solution)/shard_map/gather | solution.py:180
  31.1 3.9 %gather_fusion = bf16[1024,192]{1,0:T(8,128)(2,1)S(1)} fusion(bf16[4096,192]{1,0:T(8,128)(2,1)S(1)} %copy.54, s32[1024]{0:T(1024)S(1)} %broadcast_clamp_fusion.3), kind=kCustom, calls=%fused_computation | custom fusion | bytes 790528 | tf_op jit(solution)/shard_map/gather | solution.py:180
  37.1 1.8 %slice_bitcast_fusion = (bf16[192,1024]{1,0:T(8,128)(2,1)}, bf16[1024,192]{0,1:T(8,128)(2,1)S(1)}) fusion(bf16[4096,192]{0,1:T(8,128)(2,1)} %param.10), kind=kLoop, calls=%fused_computation.147 | loop fusion | bytes 1179648 | tf_op jit(solution)/shard_map/transpose | solution.py:162
  44.0 3.3 %shard_map.129 = (f32[192,1024]{1,0:T(8,128)}, f32[8,1024]{1,0:T(8,128)}) custom-call(s32[1024,1]{1,0:T(8,128)} %copy.62.tgt_ref, bf16[192,1024]{1,0:T(8,128)(2,1)} %bitcast.178, f32[192,1024]{1,0:T(8,128)} %broadcast_in_dim.4.sum_in, f32[8,1024]{1,0:T(8,128)} %broadcast_in_dim.5.cnt_in), custom_call_target="tpu_custom_call", output_to_operand_aliasing={{0}: (2, {}), {1}: (3, {})} | custom-call | flops 419430400 | bytes 2035712 | tf_op jit(solution)/shard_map/pallas_call | solution.py:44
  47.2 1.5 convert_reduce_fusion
  49.4 3.3 %shard_map.130 = (f32[192,1024]{1,0:T(8,128)}, f32[8,1024]{1,0:T(8,128)}) custom-call(s32[1024,1]{1,0:T(8,128)} %copy.63.tgt_ref, bf16[192,1024]{1,0:T(8,128)(2,1)} %collective-permute-done.7.rec_ref, f32[192,1024]{1,0:T(8,128)} %get-tuple-element.18.sum_in, f32[8,1024]{1,0:T(8,128)} %get-tuple-element.19.cnt_in), custom_call_target="tpu_custom_call", output_to_operand_aliasing={{0}: (2, {}), {1}: (3, {})} | custom-call | flops 419430400 | bytes 2035712 | tf_op jit(solution)/shard_map/pallas_call | solution.py:44
  58.3 2.2 %fusion.18 = f32[256,1024]{1,0:T(8,128)} fusion(bf16[192,256]{1,0:T(8,128)(2,1)} %collective-permute-done.4, bf16[4,192,1024]{2,1,0:T(8,128)(2,1)S(1)} %bitcast.168, s32[]{:T(128)S(6)} %select_n.342), kind=kOutput, calls=%fused_computation.67 | convolution fusion | flops 100663296 | bytes 1540100 | tf_op jit(solution)/shard_map/dot_general | solution.py:23
  63.2 1.5 copy.65
  64.8 3.3 %shard_map.131 = (f32[192,1024]{1,0:T(8,128)}, f32[8,1024]{1,0:T(8,128)}) custom-call(s32[1024,1]{1,0:T(8,128)} %copy.66.tgt_ref, bf16[192,1024]{1,0:T(8,128)(2,1)} %collective-permute-done.6.rec_ref, f32[192,1024]{1,0:T(8,128)} %get-tuple-element.22.sum_in, f32[8,1024]{1,0:T(8,128)} %get-tuple-element.23.cnt_in), custom_call_target="tpu_custom_call", output_to_operand_aliasing={{0}: (2, {}), {1}: (3, {})} | custom-call | flops 419430400 | bytes 2035712 | tf_op jit(solution)/shard_map/pallas_call | solution.py:44
  68.0 3.3 %shard_map.132 = (f32[192,1024]{1,0:T(8,128)}, f32[8,1024]{1,0:T(8,128)}) custom-call(s32[1024,1]{1,0:T(8,128)} %copy.67.tgt_ref, bf16[192,1024]{1,0:T(8,128)(2,1)} %collective-permute-done.5.rec_ref, f32[192,1024]{1,0:T(8,128)} %get-tuple-element.24.sum_in, f32[8,1024]{1,0:T(8,128)} %get-tuple-element.25.cnt_in), custom_call_target="tpu_custom_call", output_to_operand_aliasing={{0}: (2, {}), {1}: (3, {})} | custom-call | flops 419430400 | bytes 2035712 | tf_op jit(solution)/shard_map/pallas_call | solution.py:44
  73.5 1.5 collective-permute-start.13
  82.6 1.6 multiply_convert_fusion.2
  85.2 2.0 %copy-done = f32[1024,1024]{1,0:T(8,128)} copy-done((f32[1024,1024]{1,0:T(8,128)}, f32[1024,1024]{1,0:T(8,128)S(1)}, u32[]{:S(2)}) %copy-start) | copy-done | bytes 4194328
  89.2 2.0 %fusion.61 = f32[256,1024]{1,0:T(8,128)S(1)} fusion(bf16[1024,1024]{1,0:T(8,128)(2,1)S(1)} %bitcast.176, f32[256,1024]{1,0:T(8,128)S(1)} %get-tuple-element.71, bf16[256,1024]{1,0:T(8,128)(2,1)} %param.19), kind=kOutput, calls=%fused_computation.148 | convolution fusion | flops 539492352 | bytes 4718592 | tf_op jit(solution)/shard_map/dot_general | solution.py:211
  93.4 1.6 bitcast_add_fusion
  95.0 1.5 collective-permute-start.16
  98.1 10.9 %collective-permute-done.16 = bf16[256,1024]{1,0:T(8,128)(2,1)} collective-permute-done((bf16[256,1024]{1,0:T(8,128)(2,1)S(1)}, bf16[256,1024]{1,0:T(8,128)(2,1)}, u32[]{:S(2)}, u32[]{:S(2)}) %collective-permute-start.16) | collective-permute-done | bytes 524320 | tf_op jit(solution)/shard_map/ppermute | solution.py:122
  114.1 14.9 %collective-permute-done.21 = bf16[2,64,1024]{2,1,0:T(8,128)(2,1)S(1)} collective-permute-done((bf16[2,64,1024]{2,1,0:T(8,128)(2,1)S(1)}, bf16[2,64,1024]{2,1,0:T(8,128)(2,1)S(1)}, u32[]{:S(2)}, u32[]{:S(2)}) %collective-permute-start.21) | collective-permute-done | bytes 262176 | tf_op jit(solution)/shard_map/ppermute | solution.py:92
  130.1 1.5 collective-permute-start.22
  131.6 3.8 %collective-permute-done.22 = bf16[64,1024]{1,0:T(8,128)(2,1)S(1)} collective-permute-done((bf16[64,1024]{1,0:T(8,128)(2,1)S(1)}, bf16[64,1024]{1,0:T(8,128)(2,1)S(1)}, u32[]{:S(2)}, u32[]{:S(2)}) %collective-permute-start.22) | collective-permute-done | bytes 131104 | tf_op jit(solution)/shard_map/ppermute | solution.py:92
  137.3 2.6 %copy.69 = bf16[1024,1024]{1,0:T(8,128)(2,1)} copy(bf16[1024,1024]{0,1:T(8,128)(2,1)S(1)} %bitcast.166) | data formatting | bytes 4194304 | tf_op jit(solution)/shard_map/dot_general | solution.py:225
  139.9 2.6 %fusion.6 = f32[384,4,256]{2,0,1:T(8,128)S(1)} fusion(bf16[4,256,1024]{2,1,0:T(8,128)(2,1)} %bitcast.177, bf16[192,1024]{1,0:T(8,128)(2,1)S(1)} %copy-done.11, bf16[192,1024]{1,0:T(8,128)(2,1)S(1)} %divide_convert_fusion), kind=kOutput, calls=%fused_computation.40 | convolution fusion | flops 806879232 | bytes 4456448 | tf_op jit(solution)/shard_map/dot_general | solution.py:225
  144.8 12.0 %collective-permute-done.18 = bf16[2,384,256]{2,1,0:T(8,128)(2,1)S(1)} collective-permute-done((bf16[2,384,256]{2,1,0:T(8,128)(2,1)S(1)}, bf16[2,384,256]{2,1,0:T(8,128)(2,1)S(1)}, u32[]{:S(2)}, u32[]{:S(2)}) %collective-permute-start.18) | collective-permute-done | bytes 393248 | tf_op jit(solution)/shard_map/ppermute | solution.py:92
  157.8 2.6 %collective-permute-done.24 = bf16[2,64,1024]{2,1,0:T(8,128)(2,1)S(1)} collective-permute-done((bf16[2,64,1024]{2,1,0:T(8,128)(2,1)S(1)}, bf16[2,64,1024]{2,1,0:T(8,128)(2,1)S(1)}, u32[]{:S(2)}, u32[]{:S(2)}) %collective-permute-start.24) | collective-permute-done | bytes 262176 | tf_op jit(solution)/shard_map/ppermute | solution.py:122
  161.7 4.5 %collective-permute-done.19 = bf16[384,256]{1,0:T(8,128)(2,1)S(1)} collective-permute-done((bf16[384,256]{1,0:T(8,128)(2,1)S(1)}, bf16[384,256]{1,0:T(8,128)(2,1)S(1)}, u32[]{:S(2)}, u32[]{:S(2)}) %collective-permute-start.19) | collective-permute-done | bytes 196640 | tf_op jit(solution)/shard_map/ppermute | solution.py:92
  (144 shorter events, 52.1 us)
Async XLA Ops:
  3.9 7.9 %copy-start.13 = (bf16[192,1024]{1,0:T(8,128)(2,1)S(1)}, bf16[192,1024]{1,0:T(8,128)(2,1)}, u32[]{:S(2)}) copy-start(bf16[192,1024]{1,0:T(8,128)(2,1)} %param.14) | copy-start | bytes 1179652
  4.0 9.4 %copy-start.12 = (bf16[192,1024]{1,0:T(8,128)(2,1)S(1)}, bf16[192,1024]{1,0:T(8,128)(2,1)}, u32[]{:S(2)}) copy-start(bf16[192,1024]{1,0:T(8,128)(2,1)} %param.13) | copy-start | bytes 1179652
  8.9 39.9 %collective-permute-start.7 = (bf16[192,1024]{1,0:T(8,128)(2,1)}, bf16[192,1024]{1,0:T(8,128)(2,1)}, u32[]{:S(2)}, u32[]{:S(2)}) collective-permute-start(bf16[192,1024]{1,0:T(8,128)(2,1)} %bitcast.24), channel_id=1, source_target_pairs={{0,4},{4,8},{8,12},{12,0},{1,5},{5,9},{9,13},{13,1},{2,6},{6,10},{... | collective-permute-start | bytes 1179656 | tf_op jit(solution)/shard_map/ppermute | solution.py:182
  11.9 27.7 %collective-permute-start = (bf16[192,1024]{1,0:T(8,128)(2,1)S(1)}, bf16[192,1024]{1,0:T(8,128)(2,1)}, u32[]{:S(2)}, u32[]{:S(2)}) collective-permute-start(bf16[192,1024]{1,0:T(8,128)(2,1)S(1)} %copy-done.13), channel_id=1, source_target_pairs={{0,2},{1,3},{2,0},{3,1},{4,6},{5,7},{6,4},{7,5},{8,10},{9,11},{10,... | collective-permute-start | bytes 1179656 | tf_op jit(solution)/shard_map/ppermute | solution.py:122
  13.4 27.6 %collective-permute-start.8 = (bf16[192,1024]{1,0:T(8,128)(2,1)S(1)}, bf16[192,1024]{1,0:T(8,128)(2,1)}, u32[]{:S(2)}, u32[]{:S(2)}) collective-permute-start(bf16[192,1024]{1,0:T(8,128)(2,1)S(1)} %copy-done.12), channel_id=1, source_target_pairs={{0,2},{1,3},{2,0},{3,1},{4,6},{5,7},{6,4},{7,5},{8,10},{9,11},{10,... | collective-permute-start | bytes 1179656 | tf_op jit(solution)/shard_map/ppermute | solution.py:122
  13.9 38.8 %collective-permute-start.10 = (bf16[256,1024]{1,0:T(8,128)(2,1)}, bf16[256,1024]{1,0:T(8,128)(2,1)}, u32[]{:S(2)}, u32[]{:S(2)}) collective-permute-start(bf16[256,1024]{1,0:T(8,128)(2,1)} %param.16), channel_id=1, source_target_pairs={{0,2},{1,3},{2,0},{3,1},{4,6},{5,7},{6,4},{7,5},{8,10},{9,11},{10,... | collective-permute-start | bytes 1572872 | tf_op jit(solution)/shard_map/ppermute | solution.py:122
  15.4 7.6 %copy-start.19 = (s32[1,4,1024]{2,1,0:T(4,128)S(1)}, s32[1,4,1024]{2,1,0:T(4,128)}, u32[]{:S(2)}) copy-start(s32[1,4,1024]{2,1,0:T(4,128)} %param.12) | copy-start | bytes 49156
  20.3 44.4 %collective-permute-start.6 = (bf16[192,1024]{1,0:T(8,128)(2,1)}, bf16[192,1024]{1,0:T(8,128)(2,1)}, u32[]{:S(2)}, u32[]{:S(2)}) collective-permute-start(bf16[192,1024]{1,0:T(8,128)(2,1)} %bitcast.20), channel_id=1, source_target_pairs={{0,8},{4,12},{8,0},{12,4},{1,9},{5,13},{9,1},{13,5},{2,10},{6,14},... | collective-permute-start | bytes 1179656 | tf_op jit(solution)/shard_map/ppermute | solution.py:182
  39.6 28.4 %collective-permute-start.5 = (bf16[192,1024]{1,0:T(8,128)(2,1)}, bf16[192,1024]{1,0:T(8,128)(2,1)}, u32[]{:S(2)}, u32[]{:S(2)}) collective-permute-start(bf16[192,1024]{1,0:T(8,128)(2,1)} %bitcast.16), channel_id=1, source_target_pairs={{0,12},{4,0},{8,4},{12,8},{1,13},{5,1},{9,5},{13,9},{2,14},{6,2},{... | collective-permute-start | bytes 1179656 | tf_op jit(solution)/shard_map/ppermute | solution.py:182
  42.2 5.0 %copy-start.17 = (s32[256,15]{0,1:T(8,128)S(1)}, s32[256,15]{0,1:T(8,128)}, u32[]{:S(2)}) copy-start(s32[256,15]{0,1:T(8,128)} %param.18) | copy-start | bytes 46084
  42.3 11.9 %collective-permute-start.1 = (bf16[2,192,1024]{2,1,0:T(8,128)(2,1)S(1)}, bf16[2,192,1024]{2,1,0:T(8,128)(2,1)S(1)}, u32[]{:S(2)}, u32[]{:S(2)}) collective-permute-start(bf16[2,192,1024]{2,1,0:T(8,128)(2,1)S(1)} %pad_maximum_fusion.6), channel_id=1, source_target_pairs={{0,1},{1,0},{2,3},{3,2},{4,5},{5,4},{6,7},{7,6},{8,9},{9,8},{10,11... | collective-permute-start | bytes 2359304 | tf_op jit(solution)/shard_map/ppermute | solution.py:122
  48.7 8.1 %collective-permute-start.4 = (bf16[192,256]{1,0:T(8,128)(2,1)}, bf16[192,256]{1,0:T(8,128)(2,1)}, u32[]{:S(2)}, u32[]{:S(2)}) collective-permute-start(bf16[192,256]{1,0:T(8,128)(2,1)} %get-tuple-element.58), channel_id=1, source_target_pairs={{0,3},{1,0},{2,1},{3,2},{4,7},{5,4},{6,5},{7,6},{8,11},{9,8},{10,9... | collective-permute-start | bytes 294920 | tf_op jit(solution)/shard_map/ppermute | solution.py:169
  52.7 7.8 %collective-permute-start.9 = (bf16[2,192,1024]{2,1,0:T(8,128)(2,1)S(1)}, bf16[2,192,1024]{2,1,0:T(8,128)(2,1)S(1)}, u32[]{:S(2)}, u32[]{:S(2)}) collective-permute-start(bf16[2,192,1024]{2,1,0:T(8,128)(2,1)S(1)} %pad_maximum_fusion.7), channel_id=1, source_target_pairs={{0,1},{1,0},{2,3},{3,2},{4,5},{5,4},{6,7},{7,6},{8,9},{9,8},{10,11... | collective-permute-start | bytes 2359304 | tf_op jit(solution)/shard_map/ppermute | solution.py:122
  54.2 8.7 %collective-permute-start.11 = (bf16[2,256,1024]{2,1,0:T(8,128)(2,1)S(1)}, bf16[2,256,1024]{2,1,0:T(8,128)(2,1)S(1)}, u32[]{:S(2)}, u32[]{:S(2)}) collective-permute-start(bf16[2,256,1024]{2,1,0:T(8,128)(2,1)S(1)} %pad_maximum_fusion.4), channel_id=1, source_target_pairs={{0,1},{1,0},{2,3},{3,2},{4,5},{5,4},{6,7},{7,6},{8,9},{9,8},{10,11... | collective-permute-start | bytes 3145736 | tf_op jit(solution)/shard_map/ppermute | solution.py:122
  56.9 4.7 %collective-permute-start.3 = (bf16[192,256]{1,0:T(8,128)(2,1)S(1)}, bf16[192,256]{1,0:T(8,128)(2,1)S(1)}, u32[]{:S(2)}, u32[]{:S(2)}) collective-permute-start(bf16[192,256]{1,0:T(8,128)(2,1)S(1)} %copy-done.16), channel_id=1, source_target_pairs={{0,2},{1,3},{2,0},{3,1},{4,6},{5,7},{6,4},{7,5},{8,10},{9,11},{10,... | collective-permute-start | bytes 294920 | tf_op jit(solution)/shard_map/ppermute | solution.py:169
  60.5 15.3 %collective-permute-start.2 = (bf16[192,256]{1,0:T(8,128)(2,1)}, bf16[192,256]{1,0:T(8,128)(2,1)}, u32[]{:S(2)}, u32[]{:S(2)}) collective-permute-start(bf16[192,256]{1,0:T(8,128)(2,1)} %get-tuple-element.57), channel_id=1, source_target_pairs={{0,1},{1,2},{2,3},{3,0},{4,5},{5,6},{6,7},{7,4},{8,9},{9,10},{10,1... | collective-permute-start | bytes 294920 | tf_op jit(solution)/shard_map/ppermute | solution.py:169
  71.3 4.6 %copy-start.2 = (f32[256,1024]{1,0:T(8,128)S(1)}, f32[256,1024]{1,0:T(8,128)}, u32[]{:S(2)}) copy-start(f32[256,1024]{1,0:T(8,128)} %convolution_add_fusion.2) | copy-start | bytes 3145732
  71.3 4.6 %copy-start.3 = (f32[256,1024]{1,0:T(8,128)S(1)}, f32[256,1024]{1,0:T(8,128)}, u32[]{:S(2)}) copy-start(f32[256,1024]{1,0:T(8,128)} %fusion.18) | copy-start | bytes 3145732
  71.3 4.6 %copy-start.4 = (f32[256,1024]{1,0:T(8,128)S(1)}, f32[256,1024]{1,0:T(8,128)}, u32[]{:S(2)}) copy-start(f32[256,1024]{1,0:T(8,128)} %fusion.20) | copy-start | bytes 3145732
  73.5 5.0 %collective-permute-start.13 = (bf16[192,256]{1,0:T(8,128)(2,1)S(1)}, bf16[192,256]{1,0:T(8,128)(2,1)S(1)}, u32[]{:S(2)}, u32[]{:S(2)}) collective-permute-start(bf16[192,256]{1,0:T(8,128)(2,1)S(1)} %get-tuple-element.56), channel_id=1, source_target_pairs={{0,2},{1,3},{2,0},{3,1},{4,6},{5,7},{6,4},{7,5},{8,10},{9,11},{10,... | collective-permute-start | bytes 294920 | tf_op jit(solution)/shard_map/ppermute | solution.py:198
  75.0 4.4 %collective-permute-start.14 = (bf16[192,256]{1,0:T(8,128)(2,1)S(1)}, bf16[192,256]{1,0:T(8,128)(2,1)S(1)}, u32[]{:S(2)}, u32[]{:S(2)}) collective-permute-start(bf16[192,256]{1,0:T(8,128)(2,1)S(1)} %get-tuple-element.55), channel_id=1, source_target_pairs={{0,3},{1,0},{2,1},{3,2},{4,7},{5,4},{6,5},{7,6},{8,11},{9,8},{10,9... | collective-permute-start | bytes 294920 | tf_op jit(solution)/shard_map/ppermute | solution.py:198
  75.0 5.1 %collective-permute-start.12 = (bf16[192,256]{1,0:T(8,128)(2,1)S(1)}, bf16[192,256]{1,0:T(8,128)(2,1)S(1)}, u32[]{:S(2)}, u32[]{:S(2)}) collective-permute-start(bf16[192,256]{1,0:T(8,128)(2,1)S(1)} %get-tuple-element.54), channel_id=1, source_target_pairs={{0,1},{1,2},{2,3},{3,0},{4,5},{5,6},{6,7},{7,4},{8,9},{9,10},{10,1... | collective-permute-start | bytes 294920 | tf_op jit(solution)/shard_map/ppermute | solution.py:198
  88.4 4.3 %collective-permute-start.15 = (bf16[2,2,2,64,1024]{4,3,2,1,0:T(8,128)(2,1)}, bf16[2,2,2,64,1024]{4,3,2,1,0:T(8,128)(2,1)}, u32[]{:S(2)}, u32[]{:S(2)}) collective-permute-start(bf16[2,2,2,64,1024]{4,3,2,1,0:T(8,128)(2,1)} %fusion.5), channel_id=1, source_target_pairs={{0,1},{1,0},{2,3},{3,2},{4,5},{5,4},{6,7},{7,6},{8,9},{9,8},{10,11... | collective-permute-start | bytes 3145736 | tf_op jit(solution)/shard_map/ppermute | solution.py:92
  95.0 14.0 %collective-permute-start.16 = (bf16[256,1024]{1,0:T(8,128)(2,1)S(1)}, bf16[256,1024]{1,0:T(8,128)(2,1)}, u32[]{:S(2)}, u32[]{:S(2)}) collective-permute-start(bf16[256,1024]{1,0:T(8,128)(2,1)S(1)} %multiply_convert_fusion), channel_id=1, source_target_pairs={{0,2},{1,3},{2,0},{3,1},{4,6},{5,7},{6,4},{7,5},{8,10},{9,11},{10,... | collective-permute-start | bytes 1572872 | tf_op jit(solution)/shard_map/ppermute | solution.py:122
  97.4 13.9 %collective-permute-start.20 = (bf16[2,2,64,1024]{3,2,1,0:T(8,128)(2,1)}, bf16[2,2,64,1024]{3,2,1,0:T(8,128)(2,1)}, u32[]{:S(2)}, u32[]{:S(2)}) collective-permute-start(bf16[2,2,64,1024]{3,2,1,0:T(8,128)(2,1)} %fusion.9), channel_id=1, source_target_pairs={{0,4},{1,5},{2,6},{3,7},{4,0},{5,1},{6,2},{7,3},{8,12},{9,13},{10,... | collective-permute-start | bytes 1572872 | tf_op jit(solution)/shard_map/ppermute | solution.py:92
  111.4 24.2 %collective-permute-start.17 = (bf16[2,256,1024]{2,1,0:T(8,128)(2,1)}, bf16[2,256,1024]{2,1,0:T(8,128)(2,1)}, u32[]{:S(2)}, u32[]{:S(2)}) collective-permute-start(bf16[2,256,1024]{2,1,0:T(8,128)(2,1)} %pad_maximum_fusion.5), channel_id=1, source_target_pairs={{0,1},{1,0},{2,3},{3,2},{4,5},{5,4},{6,7},{7,6},{8,9},{9,8},{10,11... | collective-permute-start | bytes 3145736 | tf_op jit(solution)/shard_map/ppermute | solution.py:122
  113.6 15.3 %collective-permute-start.21 = (bf16[2,64,1024]{2,1,0:T(8,128)(2,1)S(1)}, bf16[2,64,1024]{2,1,0:T(8,128)(2,1)S(1)}, u32[]{:S(2)}, u32[]{:S(2)}) collective-permute-start(bf16[2,64,1024]{2,1,0:T(8,128)(2,1)S(1)} %fusion.32), channel_id=1, source_target_pairs={{0,8},{1,9},{2,10},{3,11},{4,12},{5,13},{6,14},{7,15},{8,0},{9,1},... | collective-permute-start | bytes 786440 | tf_op jit(solution)/shard_map/ppermute | solution.py:92
  130.1 5.4 %collective-permute-start.22 = (bf16[64,1024]{1,0:T(8,128)(2,1)S(1)}, bf16[64,1024]{1,0:T(8,128)(2,1)S(1)}, u32[]{:S(2)}, u32[]{:S(2)}) collective-permute-start(bf16[64,1024]{1,0:T(8,128)(2,1)S(1)} %fusion.36), channel_id=1, source_target_pairs={{0,2},{1,3},{2,0},{3,1},{4,6},{5,7},{6,4},{7,5},{8,10},{9,11},{10,... | collective-permute-start | bytes 393224 | tf_op jit(solution)/shard_map/ppermute | solution.py:92
  135.5 8.0 %collective-permute-start.23 = (bf16[64,1024]{1,0:T(8,128)(2,1)S(1)}, bf16[64,1024]{1,0:T(8,128)(2,1)S(1)}, u32[]{:S(2)}, u32[]{:S(2)}) collective-permute-start(bf16[64,1024]{1,0:T(8,128)(2,1)S(1)} %fusion.33), channel_id=1, source_target_pairs={{0,8},{4,12},{8,0},{12,4},{1,9},{5,13},{9,1},{13,5},{2,10},{6,14},... | collective-permute-start | bytes 393224 | tf_op jit(solution)/shard_map/ppermute | solution.py:122
  142.6 14.2 %collective-permute-start.18 = (bf16[2,384,256]{2,1,0:T(8,128)(2,1)S(1)}, bf16[2,384,256]{2,1,0:T(8,128)(2,1)S(1)}, u32[]{:S(2)}, u32[]{:S(2)}) collective-permute-start(bf16[2,384,256]{2,1,0:T(8,128)(2,1)S(1)} %fusion.10), channel_id=1, source_target_pairs={{0,4},{4,0},{8,12},{12,8},{1,5},{5,1},{9,13},{13,9},{2,6},{6,2},{1... | collective-permute-start | bytes 1179656 | tf_op jit(solution)/shard_map/ppermute | solution.py:92
  143.6 16.9 %collective-permute-start.24 = (bf16[2,64,1024]{2,1,0:T(8,128)(2,1)S(1)}, bf16[2,64,1024]{2,1,0:T(8,128)(2,1)S(1)}, u32[]{:S(2)}, u32[]{:S(2)}) collective-permute-start(bf16[2,64,1024]{2,1,0:T(8,128)(2,1)S(1)} %pad_maximum_fusion.8), channel_id=1, source_target_pairs={{0,4},{4,0},{8,12},{12,8},{1,5},{5,1},{9,13},{13,9},{2,6},{6,2},{1... | collective-permute-start | bytes 786440 | tf_op jit(solution)/shard_map/ppermute | solution.py:122
  157.0 9.2 %collective-permute-start.19 = (bf16[384,256]{1,0:T(8,128)(2,1)S(1)}, bf16[384,256]{1,0:T(8,128)(2,1)S(1)}, u32[]{:S(2)}, u32[]{:S(2)}) collective-permute-start(bf16[384,256]{1,0:T(8,128)(2,1)S(1)} %fusion.35), channel_id=1, source_target_pairs={{0,8},{4,12},{8,0},{12,4},{1,9},{5,13},{9,1},{13,5},{2,10},{6,14},... | collective-permute-start | bytes 589832 | tf_op jit(solution)/shard_map/ppermute | solution.py:92
  (15 other events, 27.7 us)

commit v12 on v8

--- a/solution.py
+++ b/solution.py
@@ -130,6 +130,16 @@
 
         cur = jax.tree.map(join, cur, got)
     return jax.tree.map(lambda leaf, orig: leaf.reshape((n,) + orig.shape), cur, x)
+
+
+def gather_block_list(x, axis, n):
+    held = {0: x}
+    for b in reversed(range(n.bit_length() - 1)):
+        keys = sorted(held)
+        came = lax.ppermute(tuple(held[q] for q in keys), axis, _xor_pairs(n, 1 << b))
+        for q, blocks in zip(keys, came):
+            held[q | (1 << b)] = blocks
+    return [held[q] for q in range(n)]
 
 
 def local(
@@ -154,23 +164,36 @@
     w_rows = neigh_weight.shape[0]
     up_rows = upper_weight.shape[0]
 
-    neigh_full, self_full, full_upper = all_gather_blocks(
-        (neigh_weight, self_weight, upper_weight), "cols", n_cols
-    )
-    full_upper = full_upper.reshape(n_cols * up_rows, hidden)
-
     me_dom = lax.axis_index("dom")
     me_col = lax.axis_index("cols")
+    if _is_pow2(n_cols):
+        layer_weights = gather_block_list((neigh_weight, self_weight), "cols", n_cols)
+        full_upper = all_gather_blocks(upper_weight, "cols", n_cols)
+        partners = [(me_col ^ j, me_col ^ j, _xor_pairs(n_cols, j)) for j in range(n_cols)]
+    else:
+        neigh_full, self_full, full_upper = all_gather_blocks(
+            (neigh_weight, self_weight, upper_weight), "cols", n_cols
+        )
+        partners = [
+            ((me_col + j) % n_cols, (me_col - j) % n_cols, _shift_pairs(n_cols, j))
+            for j in range(n_cols)
+        ]
+        layer_weights = [
+            tuple(
+                lax.dynamic_index_in_dim(full, partners[j][1], 0, keepdims=False)
+                for full in (neigh_full, self_full)
+            )
+            for j in range(n_cols)
+        ]
+    full_upper = full_upper.reshape(n_cols * up_rows, hidden)
+
     own_t = features[:tgt_dev].T
     own_pre = bias_one
-    for shift in range(n_cols):
-        dest = (me_col + shift) % n_cols
-        src = (me_col - shift) % n_cols
+    for j, (dest, src, pairs) in enumerate(partners):
         chunk = lax.dynamic_slice_in_dim(own_t, dest * tgt_loc, tgt_loc, axis=1)
-        if shift:
-            chunk = lax.ppermute(chunk, "cols", _shift_pairs(n_cols, shift))
-        weight = lax.dynamic_index_in_dim(self_full, src, 0, keepdims=False)
-        own_pre = own_pre + contract_rows(chunk, weight)
+        if j:
+            chunk = lax.ppermute(chunk, "cols", pairs)
+        own_pre = own_pre + contract_rows(chunk, layer_weights[j][1])
 
     summed_t = jnp.zeros((width, tgt_dev), jnp.float32)
     counts = jnp.zeros((8, tgt_dev), jnp.float32)
@@ -187,14 +210,11 @@
     both_t = jnp.concatenate([mean_t, own_t], axis=0)
 
     pre_one = own_pre
-    for shift in range(n_cols):
-        dest = (me_col + shift) % n_cols
-        src = (me_col - shift) % n_cols
+    for j, (dest, src, pairs) in enumerate(partners):
         chunk = lax.dynamic_slice_in_dim(mean_t, dest * tgt_loc, tgt_loc, axis=1)
-        if shift:
-            chunk = lax.ppermute(chunk, "cols", _shift_pairs(n_cols, shift))
-        weight = lax.dynamic_index_in_dim(neigh_full, src, 0, keepdims=False)
-        pre_one = pre_one + contract_rows(chunk, weight)
+        if j:
+            chunk = lax.ppermute(chunk, "cols", pairs)
+        pre_one = pre_one + contract_rows(chunk, layer_weights[j][0])
     hidden_one = jax.nn.silu(pre_one).astype(jnp.bfloat16)
     mix_matrix = mixing(upper_neighbours, tgt_loc)
     upper_input = jnp.dot(

time: 163 us -> 169 us (1.037)
  starting transfers between devices: 23.6 us -> 29.4 us
  waiting for transfers between devices: 54.1 us -> 58.5 us
  other arithmetic: 16.3 us -> 12 us
    ppermute x6 -> x12, waiting for transfers between devices: 0.02 us -> 15.1 us  [the longest x6 13.8 us: local(): chunk = lax.ppermute(chunk, 'cols', pairs)]
    ppermute x6, starting transfers between devices: 5.12 us -> 12.9 us  [_butterfly_reduce(): got = lax.ppermute(send.astype(send_dtype), axis, _xor_pairs(n, 1 << b))]
    ppermute x10 -> x6, starting transfers between devices: 7.74 us -> 3.11 us  [all_gather_blocks(): got = lax.ppermute(cur, axis, _xor_pairs(n, 1 << b))]
    another operation x18 -> x11, other arithmetic: 8.7 us -> 4.49 us  [join(): return jnp.stack([low, high], axis=k - 1 - b)]
    ppermute x10 -> x6, waiting for transfers between devices: 19 us -> 15.4 us  [all_gather_blocks(): got = lax.ppermute(cur, axis, _xor_pairs(n, 1 << b))]
    ppermute x6, waiting for transfers between devices: 31.6 us -> 28 us  [_butterfly_reduce(): got = lax.ppermute(send.astype(send_dtype), axis, _xor_pairs(n, 1 << b))]
    ppermute x3, waiting for transfers between devices: 3.49 us -> 0.01 us  [local(): rows_t = lax.ppermute(rows_t, 'dom', _shift_pairs(n_dom, shift))]
    ppermute x6 -> x12, starting transfers between devices: 4.9 us -> 7.79 us  [the longest x6 4.9 us: gather_block_list(): lax.ppermute(tuple((held[q] for q in keys)), axis, _xor_pairs(n, 1 << b))]
  transfers between devices with their start and end apart: 25 -> 27, of which waited for: 8 -> 9; matrix products, arithmetic and copies ran while one was open for 34% -> 32% of each run, Pallas kernels for 8% -> 8%
where the time goes in v12:
time: 169 us; the launch traced here: 168 us
  waiting for transfers between devices  58.5 us (35%)
  local copies, waits for them, and re-layouts  39.5 us (23%)
  starting transfers between devices  29.4 us (17%)
  matrix products  14.1 us (8%)
  Pallas kernels  13.1 us (8%)
  other arithmetic  12 us (7%)
    ppermute x6, waiting for transfers between devices, _butterfly_reduce(): got = lax.ppermute(send.astype(send_dtype), axis, _xor_pairs(n, 1 << b))  28 us
    gather x8, local copies, waits for them, and re-layouts, local(): rows_t = features.at[slots].get(mode='promise_in_bounds').T  19.7 us
    ppermute x6, waiting for transfers between devices, all_gather_blocks(): got = lax.ppermute(cur, axis, _xor_pairs(n, 1 << b))  15.4 us
    ppermute x6, waiting for transfers between devices, local(): chunk = lax.ppermute(chunk, 'cols', pairs)  13.8 us
    pallas_call x4, Pallas kernels, accumulate(): pl.pallas_call(_accumulate_kernel, out_shape=[jax.ShapeDtypeStruct(acc_su...  13.1 us
    ppermute x6, starting transfers between devices, _butterfly_reduce(): got = lax.ppermute(send.astype(send_dtype), axis, _xor_pairs(n, 1 << b))  12.9 us
    unnamed x39, local copies, waits for them, and re-layouts  8.02 us
    ppermute x3, starting transfers between devices, local(): rows_t = lax.ppermute(rows_t, 'dom', _shift_pairs(n_dom, shift))  5.51 us
  transfers between devices with their start and end apart: 27, of which 9 were waited for; matrix products, arithmetic and copies ran while one was open for 32% of the time, Pallas kernels for 8%

profile of v12, /device:TPU:0, one launch (start us, length us, event | category | flops | bytes accessed | tf_op | source)
XLA Modules:
  0.0 167.8 jit_solution(18309615220996626224)
XLA Ops:
  0.6 3.0 %collective-permute-start.3 = (bf16[192,1024]{1,0:T(8,128)(2,1)}, bf16[192,1024]{1,0:T(8,128)(2,1)}, u32[]{:S(2)}, u32[]{:S(2)}) collective-permute-start(bf16[192,1024]{1,0:T(8,128)(2,1)} %param.14), channel_id=1, source_target_pairs={{0,2},{1,3},{2,0},{3,1},{4,6},{5,7},{6,4},{7,5},{8,10},{9,11},{10,... | collective-permute-start | bytes 1179656 | tf_op jit(solution)/shard_map/ppermute | solution.py:139
  3.6 3.1 %copy.47 = bf16[4096,192]{1,0:T(8,128)(2,1)S(1)} copy(bf16[4096,192]{0,1:T(8,128)(2,1)} %param.10) | data formatting | bytes 3145728 | tf_op args[0]
  6.9 3.9 %gather_fusion.2 = bf16[1024,192]{1,0:T(8,128)(2,1)S(1)} fusion(bf16[4096,192]{1,0:T(8,128)(2,1)S(1)} %copy.47, s32[1024]{0:T(1024)S(1)} %broadcast_clamp_fusion.1), kind=kCustom, calls=%fused_computation.2 | custom fusion | bytes 790528 | tf_op jit(solution)/shard_map/gather | solution.py:204
  11.8 1.6 collective-permute-start.8
  13.4 3.9 %gather_fusion.1 = bf16[1024,192]{1,0:T(8,128)(2,1)S(1)} fusion(bf16[4096,192]{1,0:T(8,128)(2,1)S(1)} %copy.47, s32[1024]{0:T(1024)S(1)} %broadcast_clamp_fusion.2), kind=kCustom, calls=%fused_computation.1 | custom fusion | bytes 790528 | tf_op jit(solution)/shard_map/gather | solution.py:204
  18.3 2.6 %collective-permute-start.7 = (bf16[192,1024]{1,0:T(8,128)(2,1)}, bf16[192,1024]{1,0:T(8,128)(2,1)}, u32[]{:S(2)}, u32[]{:S(2)}) collective-permute-start(bf16[192,1024]{1,0:T(8,128)(2,1)} %bitcast.10), channel_id=1, source_target_pairs={{0,8},{4,12},{8,0},{12,4},{1,9},{5,13},{9,1},{13,5},{2,10},{6,14},... | collective-permute-start | bytes 1179656 | tf_op jit(solution)/shard_map/ppermute | solution.py:206
  20.8 3.9 %gather_fusion = bf16[1024,192]{1,0:T(8,128)(2,1)S(1)} fusion(bf16[4096,192]{1,0:T(8,128)(2,1)S(1)} %copy.47, s32[1024]{0:T(1024)S(1)} %broadcast_clamp_fusion.3), kind=kCustom, calls=%fused_computation | custom fusion | bytes 790528 | tf_op jit(solution)/shard_map/gather | solution.py:204
  27.1 1.9 %slice_bitcast_fusion = (bf16[192,1024]{1,0:T(8,128)(2,1)}, bf16[1024,192]{0,1:T(8,128)(2,1)S(1)}) fusion(bf16[4096,192]{0,1:T(8,128)(2,1)} %param.10), kind=kLoop, calls=%fused_computation.109 | loop fusion | bytes 1179648 | tf_op jit(solution)/shard_map/transpose | solution.py:190
  31.8 4.1 %gather_fusion.3 = bf16[1024,192]{1,0:T(8,128)(2,1)S(1)} fusion(bf16[4096,192]{1,0:T(8,128)(2,1)S(1)} %copy.47, s32[1024]{0:T(1024)S(1)} %broadcast_clamp_fusion), kind=kCustom, calls=%fused_computation.3 | custom fusion | bytes 790528 | tf_op jit(solution)/shard_map/gather | solution.py:204
  38.4 3.2 %shard_map.129 = (f32[192,1024]{1,0:T(8,128)}, f32[8,1024]{1,0:T(8,128)}) custom-call(s32[1,1024]{1,0:T(1,128)} %get-tuple-element.50.tgt_ref, bf16[192,1024]{1,0:T(8,128)(2,1)} %bitcast.137, f32[192,1024]{1,0:T(8,128)} %broadcast_in_dim.4.sum_in, f32[8,1024]{1,0:T(8,128)} %broadcast_in_dim.5.cnt_in), custom_call_target="tpu_custom_call", output_to_operand_aliasing={{0}: (2, {}), {1}: (3, {})} | custom-call | flops 419430400 | bytes 2035712 | tf_op jit(solution)/shard_map/pallas_call | solution.py:46
  42.7 3.3 %shard_map.130 = (f32[192,1024]{1,0:T(8,128)}, f32[8,1024]{1,0:T(8,128)}) custom-call(s32[1,1024]{1,0:T(1,128)} %get-tuple-element.53.tgt_ref, bf16[192,1024]{1,0:T(8,128)(2,1)} %collective-permute-done.8.rec_ref, f32[192,1024]{1,0:T(8,128)} %get-tuple-element.14.sum_in, ...), custom_call_target="tpu_custom_call", output_to_operand_aliasing={{0}: (2, {}), {1}: (3, {})} | custom-call | flops 419430400 | bytes 2035712 | tf_op jit(solution)/shard_map/pallas_call | solution.py:46
  45.9 3.3 %shard_map.131 = (f32[192,1024]{1,0:T(8,128)}, f32[8,1024]{1,0:T(8,128)}) custom-call(s32[1,1024]{1,0:T(1,128)} %get-tuple-element.51.tgt_ref, bf16[192,1024]{1,0:T(8,128)(2,1)} %collective-permute-done.7.rec_ref, f32[192,1024]{1,0:T(8,128)} %get-tuple-element.16.sum_in, ...), custom_call_target="tpu_custom_call", output_to_operand_aliasing={{0}: (2, {}), {1}: (3, {})} | custom-call | flops 419430400 | bytes 2035712 | tf_op jit(solution)/shard_map/pallas_call | solution.py:46
  49.2 1.5 collective-permute-start.2
  50.7 3.3 %shard_map.132 = (f32[192,1024]{1,0:T(8,128)}, f32[8,1024]{1,0:T(8,128)}) custom-call(s32[1,1024]{1,0:T(1,128)} %get-tuple-element.52.tgt_ref, bf16[192,1024]{1,0:T(8,128)(2,1)} %collective-permute-done.6.rec_ref, f32[192,1024]{1,0:T(8,128)} %get-tuple-element.18.sum_in, ...), custom_call_target="tpu_custom_call", output_to_operand_aliasing={{0}: (2, {}), {1}: (3, {})} | custom-call | flops 419430400 | bytes 2035712 | tf_op jit(solution)/shard_map/pallas_call | solution.py:46
  58.1 1.6 collective-permute-start.15
  61.0 13.8 %collective-permute-done.11 = bf16[192,256]{1,0:T(8,128)(2,1)S(1)} collective-permute-done((bf16[192,256]{1,0:T(8,128)(2,1)S(1)}, bf16[192,256]{1,0:T(8,128)(2,1)S(1)}, u32[]{:S(2)}, u32[]{:S(2)}) %collective-permute-start.11) | collective-permute-done | bytes 98336 | tf_op jit(solution)/shard_map/ppermute | solution.py:216
  82.9 1.6 multiply_convert_fusion.2
  85.5 2.0 %copy-done = f32[1024,1024]{1,0:T(8,128)} copy-done((f32[1024,1024]{1,0:T(8,128)}, f32[1024,1024]{1,0:T(8,128)S(1)}, u32[]{:S(2)}) %copy-start) | copy-done | bytes 4194328
  88.8 2.0 %fusion.33 = f32[256,1024]{1,0:T(8,128)S(1)} fusion(bf16[1024,1024]{1,0:T(8,128)(2,1)S(1)} %bitcast.132, f32[256,1024]{1,0:T(8,128)S(1)} %get-tuple-element.55, bf16[256,1024]{1,0:T(8,128)(2,1)} %param.19), kind=kOutput, calls=%fused_computation.110 | convolution fusion | flops 539492352 | bytes 4718592 | tf_op jit(solution)/shard_map/dot_general | solution.py:228
  90.8 1.6 multiply_convert_fusion
  93.0 1.6 bitcast_add_fusion
  96.4 3.3 %collective-permute-start.22 = (bf16[2,2,64,1024]{3,2,1,0:T(8,128)(2,1)}, bf16[2,2,64,1024]{3,2,1,0:T(8,128)(2,1)}, u32[]{:S(2)}, u32[]{:S(2)}) collective-permute-start(bf16[2,2,64,1024]{3,2,1,0:T(8,128)(2,1)} %fusion.7), channel_id=1, source_target_pairs={{0,4},{1,5},{2,6},{3,7},{4,0},{5,1},{6,2},{7,3},{8,12},{9,13},{10,... | collective-permute-start | bytes 1572872 | tf_op jit(solution)/shard_map/ppermute | solution.py:94
  99.7 9.2 %collective-permute-done.18 = bf16[256,1024]{1,0:T(8,128)(2,1)} collective-permute-done((bf16[256,1024]{1,0:T(8,128)(2,1)S(1)}, bf16[256,1024]{1,0:T(8,128)(2,1)}, u32[]{:S(2)}, u32[]{:S(2)}) %collective-permute-start.18) | collective-permute-done | bytes 524320 | tf_op jit(solution)/shard_map/ppermute | solution.py:124
  114.4 3.4 %collective-permute-start.23 = (bf16[2,64,1024]{2,1,0:T(8,128)(2,1)S(1)}, bf16[2,64,1024]{2,1,0:T(8,128)(2,1)S(1)}, u32[]{:S(2)}, u32[]{:S(2)}) collective-permute-start(bf16[2,64,1024]{2,1,0:T(8,128)(2,1)S(1)} %fusion.9), channel_id=1, source_target_pairs={{0,8},{1,9},{2,10},{3,11},{4,12},{5,13},{6,14},{7,15},{8,0},{9,1},... | collective-permute-start | bytes 786440 | tf_op jit(solution)/shard_map/ppermute | solution.py:94
  117.9 11.6 %collective-permute-done.23 = bf16[2,64,1024]{2,1,0:T(8,128)(2,1)S(1)} collective-permute-done((bf16[2,64,1024]{2,1,0:T(8,128)(2,1)S(1)}, bf16[2,64,1024]{2,1,0:T(8,128)(2,1)S(1)}, u32[]{:S(2)}, u32[]{:S(2)}) %collective-permute-start.23) | collective-permute-done | bytes 262176 | tf_op jit(solution)/shard_map/ppermute | solution.py:94
  131.7 4.0 %collective-permute-done.24 = bf16[64,1024]{1,0:T(8,128)(2,1)S(1)} collective-permute-done((bf16[64,1024]{1,0:T(8,128)(2,1)S(1)}, bf16[64,1024]{1,0:T(8,128)(2,1)S(1)}, u32[]{:S(2)}, u32[]{:S(2)}) %collective-permute-start.24) | collective-permute-done | bytes 131104 | tf_op jit(solution)/shard_map/ppermute | solution.py:94
  137.6 2.6 %copy.57 = bf16[1024,1024]{1,0:T(8,128)(2,1)} copy(bf16[1024,1024]{0,1:T(8,128)(2,1)S(1)} %bitcast.130) | data formatting | bytes 4194304 | tf_op jit(solution)/shard_map/dot_general | solution.py:242
  140.2 2.6 %fusion.4 = f32[384,4,256]{2,0,1:T(8,128)S(1)} fusion(bf16[4,256,1024]{2,1,0:T(8,128)(2,1)} %bitcast.133, bf16[192,1024]{1,0:T(8,128)(2,1)S(1)} %copy-done.10, bf16[192,1024]{1,0:T(8,128)(2,1)S(1)} %divide_convert_fusion), kind=kOutput, calls=%fused_computation.36 | convolution fusion | flops 806879232 | bytes 4456448 | tf_op jit(solution)/shard_map/dot_general | solution.py:242
  142.8 4.6 %collective-permute-start.20 = (bf16[2,384,256]{2,1,0:T(8,128)(2,1)S(1)}, bf16[2,384,256]{2,1,0:T(8,128)(2,1)S(1)}, u32[]{:S(2)}, u32[]{:S(2)}) collective-permute-start(bf16[2,384,256]{2,1,0:T(8,128)(2,1)S(1)} %fusion.8), channel_id=1, source_target_pairs={{0,4},{4,0},{8,12},{12,8},{1,5},{5,1},{9,13},{13,9},{2,6},{6,2},{1... | collective-permute-start | bytes 1179656 | tf_op jit(solution)/shard_map/ppermute | solution.py:94
  147.7 9.9 %collective-permute-done.20 = bf16[2,384,256]{2,1,0:T(8,128)(2,1)S(1)} collective-permute-done((bf16[2,384,256]{2,1,0:T(8,128)(2,1)S(1)}, bf16[2,384,256]{2,1,0:T(8,128)(2,1)S(1)}, u32[]{:S(2)}, u32[]{:S(2)}) %collective-permute-start.20) | collective-permute-done | bytes 393248 | tf_op jit(solution)/shard_map/ppermute | solution.py:94
  158.1 6.2 %collective-permute-done.26 = bf16[2,64,1024]{2,1,0:T(8,128)(2,1)S(1)} collective-permute-done((bf16[2,64,1024]{2,1,0:T(8,128)(2,1)S(1)}, bf16[2,64,1024]{2,1,0:T(8,128)(2,1)S(1)}, u32[]{:S(2)}, u32[]{:S(2)}) %collective-permute-start.26) | collective-permute-done | bytes 262176 | tf_op jit(solution)/shard_map/ppermute | solution.py:124
  165.5 1.6 collective-permute-done.21
  (130 shorter events, 40.7 us)
Async XLA Ops:
  0.6 6.2 %copy-start.15 = (s32[1,4,1024]{2,1,0:T(4,128)S(1)}, s32[1,4,1024]{2,1,0:T(4,128)}, u32[]{:S(2)}) copy-start(s32[1,4,1024]{2,1,0:T(4,128)} %param.11) | copy-start | bytes 49156
  0.6 55.6 %collective-permute-start.3 = (bf16[192,1024]{1,0:T(8,128)(2,1)}, bf16[192,1024]{1,0:T(8,128)(2,1)}, u32[]{:S(2)}, u32[]{:S(2)}) collective-permute-start(bf16[192,1024]{1,0:T(8,128)(2,1)} %param.14), channel_id=1, source_target_pairs={{0,2},{1,3},{2,0},{3,1},{4,6},{5,7},{6,4},{7,5},{8,10},{9,11},{10,... | collective-permute-start | bytes 1179656 | tf_op jit(solution)/shard_map/ppermute | solution.py:139
  3.6 56.0 %collective-permute-start.1 = (bf16[192,1024]{1,0:T(8,128)(2,1)}, bf16[192,1024]{1,0:T(8,128)(2,1)S(1)}, u32[]{:S(2)}, u32[]{:S(2)}) collective-permute-start(bf16[192,1024]{1,0:T(8,128)(2,1)} %param.14), channel_id=1, source_target_pairs={{0,1},{1,0},{2,3},{3,2},{4,5},{5,4},{6,7},{7,6},{8,9},{9,8},{10,11... | collective-permute-start | bytes 1179656 | tf_op jit(solution)/shard_map/ppermute | solution.py:139
  11.8 30.2 %collective-permute-start.8 = (bf16[192,1024]{1,0:T(8,128)(2,1)}, bf16[192,1024]{1,0:T(8,128)(2,1)}, u32[]{:S(2)}, u32[]{:S(2)}) collective-permute-start(bf16[192,1024]{1,0:T(8,128)(2,1)} %bitcast.14), channel_id=1, source_target_pairs={{0,4},{4,8},{8,12},{12,0},{1,5},{5,9},{9,13},{13,1},{2,6},{6,10},{... | collective-permute-start | bytes 1179656 | tf_op jit(solution)/shard_map/ppermute | solution.py:206
  18.3 27.7 %collective-permute-start.7 = (bf16[192,1024]{1,0:T(8,128)(2,1)}, bf16[192,1024]{1,0:T(8,128)(2,1)}, u32[]{:S(2)}, u32[]{:S(2)}) collective-permute-start(bf16[192,1024]{1,0:T(8,128)(2,1)} %bitcast.10), channel_id=1, source_target_pairs={{0,8},{4,12},{8,0},{12,4},{1,9},{5,13},{9,1},{13,5},{2,10},{6,14},... | collective-permute-start | bytes 1179656 | tf_op jit(solution)/shard_map/ppermute | solution.py:206
  24.8 6.3 %copy-start.16 = (s32[1,4,1024]{2,1,0:T(4,128)S(1)}, s32[1,4,1024]{2,1,0:T(4,128)}, u32[]{:S(2)}) copy-start(s32[1,4,1024]{2,1,0:T(4,128)} %param.12) | copy-start | bytes 49156
  25.8 23.5 %collective-permute-start.6 = (bf16[192,1024]{1,0:T(8,128)(2,1)}, bf16[192,1024]{1,0:T(8,128)(2,1)}, u32[]{:S(2)}, u32[]{:S(2)}) collective-permute-start(bf16[192,1024]{1,0:T(8,128)(2,1)} %bitcast.6), channel_id=1, source_target_pairs={{0,12},{4,0},{8,4},{12,8},{1,13},{5,1},{9,5},{13,9},{2,14},{6,2},{... | collective-permute-start | bytes 1179656 | tf_op jit(solution)/shard_map/ppermute | solution.py:206
  35.9 5.8 %copy-start.8 = (bf16[192,1024]{1,0:T(8,128)(2,1)S(1)}, bf16[192,1024]{1,0:T(8,128)(2,1)}, u32[]{:S(2)}) copy-start(bf16[192,1024]{1,0:T(8,128)(2,1)} %param.14) | copy-start | bytes 1179652
  42.1 18.8 %collective-permute-start.12 = (bf16[192,1024]{1,0:T(8,128)(2,1)S(1)}, bf16[192,1024]{1,0:T(8,128)(2,1)}, u32[]{:S(2)}, u32[]{:S(2)}) collective-permute-start(bf16[192,1024]{1,0:T(8,128)(2,1)S(1)} %copy-done.9), channel_id=1, source_target_pairs={{0,2},{1,3},{2,0},{3,1},{4,6},{5,7},{6,4},{7,5},{8,10},{9,11},{10,... | collective-permute-start | bytes 1179656 | tf_op jit(solution)/shard_map/ppermute | solution.py:139
  45.9 33.7 %collective-permute-start.10 = (bf16[192,1024]{1,0:T(8,128)(2,1)S(1)}, bf16[192,1024]{1,0:T(8,128)(2,1)S(1)}, u32[]{:S(2)}, u32[]{:S(2)}) collective-permute-start(bf16[192,1024]{1,0:T(8,128)(2,1)S(1)} %copy-done.9), channel_id=1, source_target_pairs={{0,1},{1,0},{2,3},{3,2},{4,5},{5,4},{6,7},{7,6},{8,9},{9,8},{10,11... | collective-permute-start | bytes 1179656 | tf_op jit(solution)/shard_map/ppermute | solution.py:139
  45.9 10.1 %copy-start.13 = (bf16[192,256]{1,0:T(8,128)(2,1)S(1)}, bf16[192,256]{1,0:T(8,128)(2,1)}, u32[]{:S(2)}) copy-start(bf16[192,256]{1,0:T(8,128)(2,1)} %get-tuple-element.43) | copy-start | bytes 294916
  49.2 6.8 %collective-permute-start.2 = (bf16[192,256]{1,0:T(8,128)(2,1)}, bf16[192,256]{1,0:T(8,128)(2,1)S(1)}, u32[]{:S(2)}, u32[]{:S(2)}) collective-permute-start(bf16[192,256]{1,0:T(8,128)(2,1)} %get-tuple-element.42), channel_id=1, source_target_pairs={{0,2},{1,3},{2,0},{3,1},{4,6},{5,7},{6,4},{7,5},{8,10},{9,11},{10,... | collective-permute-start | bytes 294920 | tf_op jit(solution)/shard_map/ppermute | solution.py:195
  50.7 7.4 %copy-start.5 = (bf16[256,1024]{1,0:T(8,128)(2,1)S(1)}, bf16[256,1024]{1,0:T(8,128)(2,1)}, u32[]{:S(2)}) copy-start(bf16[256,1024]{1,0:T(8,128)(2,1)} %param.16) | copy-start | bytes 1572868
  56.0 2.1 %collective-permute-start = (bf16[192,256]{1,0:T(8,128)(2,1)S(1)}, bf16[192,256]{1,0:T(8,128)(2,1)S(1)}, u32[]{:S(2)}, u32[]{:S(2)}) collective-permute-start(bf16[192,256]{1,0:T(8,128)(2,1)S(1)} %copy-done.13), channel_id=1, source_target_pairs={{0,1},{1,0},{2,3},{3,2},{4,5},{5,4},{6,7},{7,6},{8,9},{9,8},{10,11... | collective-permute-start | bytes 294920 | tf_op jit(solution)/shard_map/ppermute | solution.py:195
  56.3 21.2 %collective-permute-start.4 = (bf16[192,256]{1,0:T(8,128)(2,1)S(1)}, bf16[192,256]{1,0:T(8,128)(2,1)S(1)}, u32[]{:S(2)}, u32[]{:S(2)}) collective-permute-start(bf16[192,256]{1,0:T(8,128)(2,1)S(1)} %get-tuple-element.41), channel_id=1, source_target_pairs={{0,3},{1,2},{2,1},{3,0},{4,7},{5,6},{6,5},{7,4},{8,11},{9,10},{10,... | collective-permute-start | bytes 294920 | tf_op jit(solution)/shard_map/ppermute | solution.py:195
  58.1 18.0 %collective-permute-start.15 = (bf16[256,1024]{1,0:T(8,128)(2,1)S(1)}, bf16[256,1024]{1,0:T(8,128)(2,1)S(1)}, u32[]{:S(2)}, u32[]{:S(2)}) collective-permute-start(bf16[256,1024]{1,0:T(8,128)(2,1)S(1)} %copy-done.5), channel_id=1, source_target_pairs={{0,2},{1,3},{2,0},{3,1},{4,6},{5,7},{6,4},{7,5},{8,10},{9,11},{10,... | collective-permute-start | bytes 1572872 | tf_op jit(solution)/shard_map/ppermute | solution.py:124
  59.7 15.0 %collective-permute-start.11 = (bf16[192,256]{1,0:T(8,128)(2,1)S(1)}, bf16[192,256]{1,0:T(8,128)(2,1)S(1)}, u32[]{:S(2)}, u32[]{:S(2)}) collective-permute-start(bf16[192,256]{1,0:T(8,128)(2,1)S(1)} %get-tuple-element.39), channel_id=1, source_target_pairs={{0,2},{1,3},{2,0},{3,1},{4,6},{5,7},{6,4},{7,5},{8,10},{9,11},{10,... | collective-permute-start | bytes 294920 | tf_op jit(solution)/shard_map/ppermute | solution.py:216
  60.9 18.7 %collective-permute-start.9 = (bf16[192,256]{1,0:T(8,128)(2,1)S(1)}, bf16[192,256]{1,0:T(8,128)(2,1)S(1)}, u32[]{:S(2)}, u32[]{:S(2)}) collective-permute-start(bf16[192,256]{1,0:T(8,128)(2,1)S(1)} %get-tuple-element.40), channel_id=1, source_target_pairs={{0,1},{1,0},{2,3},{3,2},{4,5},{5,4},{6,7},{7,6},{8,9},{9,8},{10,11... | collective-permute-start | bytes 294920 | tf_op jit(solution)/shard_map/ppermute | solution.py:216
  74.7 5.2 %collective-permute-start.13 = (bf16[192,256]{1,0:T(8,128)(2,1)S(1)}, bf16[192,256]{1,0:T(8,128)(2,1)S(1)}, u32[]{:S(2)}, u32[]{:S(2)}) collective-permute-start(bf16[192,256]{1,0:T(8,128)(2,1)S(1)} %get-tuple-element.38), channel_id=1, source_target_pairs={{0,3},{1,2},{2,1},{3,0},{4,7},{5,6},{6,5},{7,4},{8,11},{9,10},{10,... | collective-permute-start | bytes 294920 | tf_op jit(solution)/shard_map/ppermute | solution.py:216
  76.1 2.8 %collective-permute-start.5 = (bf16[192,1024]{1,0:T(8,128)(2,1)}, bf16[192,1024]{1,0:T(8,128)(2,1)S(1)}, u32[]{:S(2)}, u32[]{:S(2)}) collective-permute-start(bf16[192,1024]{1,0:T(8,128)(2,1)} %collective-permute-done.3), channel_id=1, source_target_pairs={{0,1},{1,0},{2,3},{3,2},{4,5},{5,4},{6,7},{7,6},{8,9},{9,8},{10,11... | collective-permute-start | bytes 1179656 | tf_op jit(solution)/shard_map/ppermute | solution.py:139
  77.5 2.4 %collective-permute-start.14 = (bf16[192,1024]{1,0:T(8,128)(2,1)}, bf16[192,1024]{1,0:T(8,128)(2,1)S(1)}, u32[]{:S(2)}, u32[]{:S(2)}) collective-permute-start(bf16[192,1024]{1,0:T(8,128)(2,1)} %collective-permute-done.12), channel_id=1, source_target_pairs={{0,1},{1,0},{2,3},{3,2},{4,5},{5,4},{6,7},{7,6},{8,9},{9,8},{10,11... | collective-permute-start | bytes 1179656 | tf_op jit(solution)/shard_map/ppermute | solution.py:139
  78.9 3.0 %collective-permute-start.16 = (bf16[2,256,1024]{2,1,0:T(8,128)(2,1)S(1)}, bf16[2,256,1024]{2,1,0:T(8,128)(2,1)S(1)}, u32[]{:S(2)}, u32[]{:S(2)}) collective-permute-start(bf16[2,256,1024]{2,1,0:T(8,128)(2,1)S(1)} %pad_maximum_fusion.2), channel_id=1, source_target_pairs={{0,1},{1,0},{2,3},{3,2},{4,5},{5,4},{6,7},{7,6},{8,9},{9,8},{10,11... | collective-permute-start | bytes 3145736 | tf_op jit(solution)/shard_map/ppermute | solution.py:124
  88.6 3.8 %collective-permute-start.17 = (bf16[2,2,2,64,1024]{4,3,2,1,0:T(8,128)(2,1)}, bf16[2,2,2,64,1024]{4,3,2,1,0:T(8,128)(2,1)}, u32[]{:S(2)}, u32[]{:S(2)}) collective-permute-start(bf16[2,2,2,64,1024]{4,3,2,1,0:T(8,128)(2,1)} %fusion.3), channel_id=1, source_target_pairs={{0,1},{1,0},{2,3},{3,2},{4,5},{5,4},{6,7},{7,6},{8,9},{9,8},{10,11... | collective-permute-start | bytes 3145736 | tf_op jit(solution)/shard_map/ppermute | solution.py:94
  94.6 14.4 %collective-permute-start.18 = (bf16[256,1024]{1,0:T(8,128)(2,1)S(1)}, bf16[256,1024]{1,0:T(8,128)(2,1)}, u32[]{:S(2)}, u32[]{:S(2)}) collective-permute-start(bf16[256,1024]{1,0:T(8,128)(2,1)S(1)} %multiply_convert_fusion), channel_id=1, source_target_pairs={{0,2},{1,3},{2,0},{3,1},{4,6},{5,7},{6,4},{7,5},{8,10},{9,11},{10,... | collective-permute-start | bytes 1572872 | tf_op jit(solution)/shard_map/ppermute | solution.py:124
  96.4 15.8 %collective-permute-start.22 = (bf16[2,2,64,1024]{3,2,1,0:T(8,128)(2,1)}, bf16[2,2,64,1024]{3,2,1,0:T(8,128)(2,1)}, u32[]{:S(2)}, u32[]{:S(2)}) collective-permute-start(bf16[2,2,64,1024]{3,2,1,0:T(8,128)(2,1)} %fusion.7), channel_id=1, source_target_pairs={{0,4},{1,5},{2,6},{3,7},{4,0},{5,1},{6,2},{7,3},{8,12},{9,13},{10,... | collective-permute-start | bytes 1572872 | tf_op jit(solution)/shard_map/ppermute | solution.py:94
  111.3 24.5 %collective-permute-start.19 = (bf16[2,256,1024]{2,1,0:T(8,128)(2,1)}, bf16[2,256,1024]{2,1,0:T(8,128)(2,1)}, u32[]{:S(2)}, u32[]{:S(2)}) collective-permute-start(bf16[2,256,1024]{2,1,0:T(8,128)(2,1)} %pad_maximum_fusion.3), channel_id=1, source_target_pairs={{0,1},{1,0},{2,3},{3,2},{4,5},{5,4},{6,7},{7,6},{8,9},{9,8},{10,11... | collective-permute-start | bytes 3145736 | tf_op jit(solution)/shard_map/ppermute | solution.py:124
  114.4 15.1 %collective-permute-start.23 = (bf16[2,64,1024]{2,1,0:T(8,128)(2,1)S(1)}, bf16[2,64,1024]{2,1,0:T(8,128)(2,1)S(1)}, u32[]{:S(2)}, u32[]{:S(2)}) collective-permute-start(bf16[2,64,1024]{2,1,0:T(8,128)(2,1)S(1)} %fusion.9), channel_id=1, source_target_pairs={{0,8},{1,9},{2,10},{3,11},{4,12},{5,13},{6,14},{7,15},{8,0},{9,1},... | collective-permute-start | bytes 786440 | tf_op jit(solution)/shard_map/ppermute | solution.py:94
  130.7 5.0 %collective-permute-start.24 = (bf16[64,1024]{1,0:T(8,128)(2,1)S(1)}, bf16[64,1024]{1,0:T(8,128)(2,1)S(1)}, u32[]{:S(2)}, u32[]{:S(2)}) collective-permute-start(bf16[64,1024]{1,0:T(8,128)(2,1)S(1)} %fusion.13), channel_id=1, source_target_pairs={{0,2},{1,3},{2,0},{3,1},{4,6},{5,7},{6,4},{7,5},{8,10},{9,11},{10,... | collective-permute-start | bytes 393224 | tf_op jit(solution)/shard_map/ppermute | solution.py:94
  135.7 11.8 %collective-permute-start.25 = (bf16[64,1024]{1,0:T(8,128)(2,1)S(1)}, bf16[64,1024]{1,0:T(8,128)(2,1)S(1)}, u32[]{:S(2)}, u32[]{:S(2)}) collective-permute-start(bf16[64,1024]{1,0:T(8,128)(2,1)S(1)} %fusion.10), channel_id=1, source_target_pairs={{0,8},{4,12},{8,0},{12,4},{1,9},{5,13},{9,1},{13,5},{2,10},{6,14},... | collective-permute-start | bytes 393224 | tf_op jit(solution)/shard_map/ppermute | solution.py:124
  142.8 14.7 %collective-permute-start.20 = (bf16[2,384,256]{2,1,0:T(8,128)(2,1)S(1)}, bf16[2,384,256]{2,1,0:T(8,128)(2,1)S(1)}, u32[]{:S(2)}, u32[]{:S(2)}) collective-permute-start(bf16[2,384,256]{2,1,0:T(8,128)(2,1)S(1)} %fusion.8), channel_id=1, source_target_pairs={{0,4},{4,0},{8,12},{12,8},{1,5},{5,1},{9,13},{13,9},{2,6},{6,2},{1... | collective-permute-start | bytes 1179656 | tf_op jit(solution)/shard_map/ppermute | solution.py:94
  147.6 16.7 %collective-permute-start.26 = (bf16[2,64,1024]{2,1,0:T(8,128)(2,1)S(1)}, bf16[2,64,1024]{2,1,0:T(8,128)(2,1)S(1)}, u32[]{:S(2)}, u32[]{:S(2)}) collective-permute-start(bf16[2,64,1024]{2,1,0:T(8,128)(2,1)S(1)} %pad_maximum_fusion.4), channel_id=1, source_target_pairs={{0,4},{4,0},{8,12},{12,8},{1,5},{5,1},{9,13},{13,9},{2,6},{6,2},{1... | collective-permute-start | bytes 786440 | tf_op jit(solution)/shard_map/ppermute | solution.py:124
  157.7 9.4 %collective-permute-start.21 = (bf16[384,256]{1,0:T(8,128)(2,1)S(1)}, bf16[384,256]{1,0:T(8,128)(2,1)S(1)}, u32[]{:S(2)}, u32[]{:S(2)}) collective-permute-start(bf16[384,256]{1,0:T(8,128)(2,1)S(1)} %fusion.12), channel_id=1, source_target_pairs={{0,8},{4,12},{8,0},{12,4},{1,9},{5,13},{9,1},{13,5},{2,10},{6,14},... | collective-permute-start | bytes 589832 | tf_op jit(solution)/shard_map/ppermute | solution.py:94
  (14 other events, 33.4 us)

commit v13 on v12

--- a/solution.py
+++ b/solution.py
@@ -206,6 +206,10 @@
             rows_t = lax.ppermute(rows_t, "dom", _shift_pairs(n_dom, shift))
         targets = lax.dynamic_index_in_dim(edge_target[0], src, 0, keepdims=True)
         summed_t, counts = accumulate(targets, rows_t, summed_t, counts)
+        if shift == min(1, n_dom - 1):
+            summed_t, counts, layer_weights, full_upper = lax.optimization_barrier(
+                (summed_t, counts, layer_weights, full_upper)
+            )
     mean_t = (summed_t / jnp.maximum(counts[:1], 1.0)).astype(jnp.bfloat16)
     both_t = jnp.concatenate([mean_t, own_t], axis=0)
 

time: 169 us -> 201 us (1.19)
  waiting for transfers between devices: 58.5 us -> 75.1 us
  local copies, waits for them, and re-layouts: 39.5 us -> 47.6 us
  matrix products: 14.1 us -> 21.6 us
  starting transfers between devices: 29.4 us -> 25.3 us
  other arithmetic: 12 us -> 15.5 us
    ppermute x3, waiting for transfers between devices: 0.01 us -> 20.3 us  [local(): rows_t = lax.ppermute(rows_t, 'dom', _shift_pairs(n_dom, shift))]
    ppermute x6, waiting for transfers between devices: 13.8 us -> 3.82 us  [local(): chunk = lax.ppermute(chunk, 'cols', pairs)]
    dot_general x9, matrix products: 5.45 us -> 12.9 us  [contract_rows(): lax.dot_general(left_mat, right_mat, (((0,), (0,)), ((), ())), preferred_...]
    ppermute x6, waiting for transfers between devices: 15.4 us -> 21.8 us  [all_gather_blocks(): got = lax.ppermute(cur, axis, _xor_pairs(n, 1 << b))]
    gather x8, local copies, waits for them, and re-layouts: 19.7 us -> 25.8 us  [local(): rows_t = features.at[slots].get(mode='promise_in_bounds').T]
    ppermute x6, starting transfers between devices: 12.9 us -> 8.63 us  [_butterfly_reduce(): got = lax.ppermute(send.astype(send_dtype), axis, _xor_pairs(n, 1 << b))]
    another operation x11, other arithmetic: 4.49 us -> 7.92 us  [join(): return jnp.stack([low, high], axis=k - 1 - b)]
    ppermute x6, starting transfers between devices: 3.11 us -> 0.88 us  [all_gather_blocks(): got = lax.ppermute(cur, axis, _xor_pairs(n, 1 << b))]
  transfers between devices with their start and end apart: 27 -> 27, of which waited for: 9 -> 9; matrix products, arithmetic and copies ran while one was open for 32% -> 36% of each run, Pallas kernels for 8% -> 7%
where the time goes in v13:
time: 201 us; the launch traced here: 199 us
  waiting for transfers between devices  75.1 us (37%)
  local copies, waits for them, and re-layouts  47.6 us (24%)
  starting transfers between devices  25.3 us (13%)
  matrix products  21.6 us (11%)
  other arithmetic  15.5 us (8%)
  Pallas kernels  13.1 us (7%)
    ppermute x6, waiting for transfers between devices, _butterfly_reduce(): got = lax.ppermute(send.astype(send_dtype), axis, _xor_pairs(n, 1 << b))  29.2 us
    gather x8, local copies, waits for them, and re-layouts, local(): rows_t = features.at[slots].get(mode='promise_in_bounds').T  25.8 us
    ppermute x6, waiting for transfers between devices, all_gather_blocks(): got = lax.ppermute(cur, axis, _xor_pairs(n, 1 << b))  21.8 us
    ppermute x3, waiting for transfers between devices, local(): rows_t = lax.ppermute(rows_t, 'dom', _shift_pairs(n_dom, shift))  20.3 us
    pallas_call x4, Pallas kernels, accumulate(): pl.pallas_call(_accumulate_kernel, out_shape=[jax.ShapeDtypeStruct(acc_su...  13.1 us
    dot_general x9, matrix products, contract_rows(): lax.dot_general(left_mat, right_mat, (((0,), (0,)), ((), ())), preferred_...  12.9 us
    ppermute x6, starting transfers between devices, _butterfly_reduce(): got = lax.ppermute(send.astype(send_dtype), axis, _xor_pairs(n, 1 << b))  8.63 us
    another operation x11, other arithmetic, join(): return jnp.stack([low, high], axis=k - 1 - b)  7.92 us
  transfers between devices with their start and end apart: 27, of which 9 were waited for; matrix products, arithmetic and copies ran while one was open for 36% of the time, Pallas kernels for 7%

profile of v13, /device:TPU:0, one launch (start us, length us, event | category | flops | bytes accessed | tf_op | source)
XLA Modules:
  0.0 199.3 jit_solution(5563713934313112915)
XLA Ops:
  1.1 2.6 %collective-permute-start.3 = (bf16[192,1024]{1,0:T(8,128)(2,1)}, bf16[192,1024]{1,0:T(8,128)(2,1)}, u32[]{:S(2)}, u32[]{:S(2)}) collective-permute-start(bf16[192,1024]{1,0:T(8,128)(2,1)} %param.14), channel_id=1, source_target_pairs={{0,2},{1,3},{2,0},{3,1},{4,6},{5,7},{6,4},{7,5},{8,10},{9,11},{10,... | collective-permute-start | bytes 1179656 | tf_op jit(solution)/shard_map/ppermute | solution.py:139
  6.4 1.9 collective-permute-start.2
  8.3 3.1 %copy.47 = bf16[4096,192]{1,0:T(8,128)(2,1)S(1)} copy(bf16[4096,192]{0,1:T(8,128)(2,1)} %param.10) | data formatting | bytes 3145728 | tf_op args[0]
  11.5 3.9 %gather_fusion.2 = bf16[1024,192]{1,0:T(8,128)(2,1)S(1)} fusion(bf16[4096,192]{1,0:T(8,128)(2,1)S(1)} %copy.47, s32[1024]{0:T(1024)S(1)} %broadcast_clamp_fusion.1), kind=kCustom, calls=%fused_computation.2 | custom fusion | bytes 790528 | tf_op jit(solution)/shard_map/gather | solution.py:204
  18.0 2.3 %convolution_add_fusion.2 = f32[256,1024]{1,0:T(8,128)} fusion(bf16[192,1024]{1,0:T(8,128)(2,1)} %param.14, f32[1024]{0:T(1024)S(1)} %copy-done.16, bf16[1024,192]{0,1:T(8,128)(2,1)S(1)} %get-tuple-element.43, s32[]{:T(128)S(6)} %select_n.219), kind=kOutput, calls=%fused_computation.14 | convolution fusion | flops 100925440 | bytes 1544196 | tf_op jit(solution)/shard_map/dot_general | solution.py:23
  20.3 4.9 %collective-permute-done.12 = bf16[256,1024]{1,0:T(8,128)(2,1)} collective-permute-done((bf16[256,1024]{1,0:T(8,128)(2,1)}, bf16[256,1024]{1,0:T(8,128)(2,1)}, u32[]{:S(2)}, u32[]{:S(2)}) %collective-permute-start.12) | collective-permute-done | bytes 524320 | tf_op jit(solution)/shard_map/ppermute | solution.py:124
  30.6 5.0 %gather_fusion.3 = bf16[1024,192]{1,0:T(8,128)(2,1)} fusion(bf16[4096,192]{1,0:T(8,128)(2,1)S(1)} %copy.47, s32[1024]{0:T(1024)S(1)} %broadcast_clamp_fusion), kind=kCustom, calls=%fused_computation.3 | custom fusion | bytes 790528 | tf_op jit(solution)/shard_map/gather | solution.py:204
  35.6 2.0 copy.54
  37.6 5.0 %gather_fusion.1 = bf16[1024,192]{1,0:T(8,128)(2,1)} fusion(bf16[4096,192]{1,0:T(8,128)(2,1)S(1)} %copy.47, s32[1024]{0:T(1024)S(1)} %broadcast_clamp_fusion.2), kind=kCustom, calls=%fused_computation.1 | custom fusion | bytes 790528 | tf_op jit(solution)/shard_map/gather | solution.py:204
  42.5 5.0 %gather_fusion = bf16[1024,192]{1,0:T(8,128)(2,1)} fusion(bf16[4096,192]{1,0:T(8,128)(2,1)S(1)} %copy.47, s32[1024]{0:T(1024)S(1)} %broadcast_clamp_fusion.3), kind=kCustom, calls=%fused_computation | custom fusion | bytes 790528 | tf_op jit(solution)/shard_map/gather | solution.py:204
  47.5 2.0 %copy.48 = bf16[1024,192]{0,1:T(8,128)(2,1)} copy(bf16[1024,192]{1,0:T(8,128)(2,1)} %gather_fusion) | data formatting | bytes 786432 | tf_op jit(solution)/shard_map/gather | solution.py:204
  49.5 2.0 copy.50
  53.1 3.3 %shard_map.129 = (f32[192,1024]{1,0:T(8,128)}, f32[8,1024]{1,0:T(8,128)}) custom-call(s32[1,1024]{1,0:T(1,128)} %get-tuple-element.64.tgt_ref, bf16[192,1024]{1,0:T(8,128)(2,1)} %bitcast.138, f32[192,1024]{1,0:T(8,128)} %broadcast_in_dim.4.sum_in, f32[8,1024]{1,0:T(8,128)} %broadcast_in_dim.5.cnt_in), custom_call_target="tpu_custom_call", output_to_operand_aliasing={{0}: (2, {}), {1}: (3, {})} | custom-call | flops 419430400 | bytes 2035712 | tf_op jit(solution)/shard_map/pallas_call | solution.py:46
  56.5 2.0 collective-permute-start.10
  58.7 2.3 %fusion.38 = f32[256,1024]{1,0:T(8,128)} fusion(bf16[192,256]{1,0:T(8,128)(2,1)} %collective-permute-done.2, bf16[192,1024]{1,0:T(8,128)(2,1)} %collective-permute-done.3), kind=kOutput, calls=%fused_computation.113 | convolution fusion | flops 100663296 | bytes 1540096 | tf_op jit(solution)/shard_map/dot_general | solution.py:23
  61.3 3.3 %shard_map.130 = (f32[192,1024]{1,0:T(8,128)}, f32[8,1024]{1,0:T(8,128)}) custom-call(s32[1,1024]{1,0:T(1,128)} %get-tuple-element.67.tgt_ref, bf16[192,1024]{1,0:T(8,128)(2,1)} %collective-permute-done.8.rec_ref, f32[192,1024]{1,0:T(8,128)} %get-tuple-element.21.sum_in, ...), custom_call_target="tpu_custom_call", output_to_operand_aliasing={{0}: (2, {}), {1}: (3, {})} | custom-call | flops 419430400 | bytes 2035712 | tf_op jit(solution)/shard_map/pallas_call | solution.py:46
  64.6 3.8 %collective-permute-start.6 = (bf16[192,1024]{1,0:T(8,128)(2,1)}, bf16[192,1024]{1,0:T(8,128)(2,1)}, u32[]{:S(2)}, u32[]{:S(2)}) collective-permute-start(bf16[192,1024]{1,0:T(8,128)(2,1)} %bitcast.6), channel_id=1, source_target_pairs={{0,12},{4,0},{8,4},{12,8},{1,13},{5,1},{9,5},{13,9},{2,14},{6,2},{... | collective-permute-start | bytes 1179656 | tf_op jit(solution)/shard_map/ppermute | solution.py:206
  73.9 20.3 %collective-permute-done.7.rec_ref = bf16[192,1024]{1,0:T(8,128)(2,1)} collective-permute-done((bf16[192,1024]{1,0:T(8,128)(2,1)}, bf16[192,1024]{1,0:T(8,128)(2,1)}, u32[]{:S(2)}, u32[]{:S(2)}) %collective-permute-start.7) | collective-permute-done | bytes 393248 | tf_op jit(solution)/shard_map/ppermute | solution.py:206
  94.2 3.3 %shard_map.131 = (f32[192,1024]{1,0:T(8,128)}, f32[8,1024]{1,0:T(8,128)}) custom-call(s32[1,1024]{1,0:T(1,128)} %get-tuple-element.65.tgt_ref, bf16[192,1024]{1,0:T(8,128)(2,1)} %collective-permute-done.7.rec_ref, f32[192,1024]{1,0:T(8,128)} %get-tuple-element.25.sum_in, ...), custom_call_target="tpu_custom_call", output_to_operand_aliasing={{0}: (2, {}), {1}: (3, {})} | custom-call | flops 419430400 | bytes 2035712 | tf_op jit(solution)/shard_map/pallas_call | solution.py:46
  97.4 3.3 %shard_map.132 = (f32[192,1024]{1,0:T(8,128)}, f32[8,1024]{1,0:T(8,128)}) custom-call(s32[1,1024]{1,0:T(1,128)} %get-tuple-element.66.tgt_ref, bf16[192,1024]{1,0:T(8,128)(2,1)} %collective-permute-done.6.rec_ref, f32[192,1024]{1,0:T(8,128)} %get-tuple-element.27.sum_in, ...), custom_call_target="tpu_custom_call", output_to_operand_aliasing={{0}: (2, {}), {1}: (3, {})} | custom-call | flops 419430400 | bytes 2035712 | tf_op jit(solution)/shard_map/pallas_call | solution.py:46
  106.3 3.8 %collective-permute-done.15 = bf16[192,256]{1,0:T(8,128)(2,1)S(1)} collective-permute-done((bf16[192,256]{1,0:T(8,128)(2,1)S(1)}, bf16[192,256]{1,0:T(8,128)(2,1)S(1)}, u32[]{:S(2)}, u32[]{:S(2)}) %collective-permute-start.15) | collective-permute-done | bytes 98336 | tf_op jit(solution)/shard_map/ppermute | solution.py:220
  118.8 2.0 %copy-done = f32[1024,1024]{1,0:T(8,128)} copy-done((f32[1024,1024]{1,0:T(8,128)}, f32[1024,1024]{1,0:T(8,128)S(1)}, u32[]{:S(2)}) %copy-start) | copy-done | bytes 4194328
  122.0 2.3 %fusion.35 = f32[256,1024]{1,0:T(8,128)S(1)} fusion(bf16[1024,1024]{1,0:T(8,128)(2,1)S(1)} %bitcast.132, f32[256,1024]{1,0:T(8,128)} %copy-done.5, bf16[256,1024]{1,0:T(8,128)(2,1)} %param.19), kind=kOutput, calls=%fused_computation.110 | convolution fusion | flops 539492352 | bytes 4718592 | tf_op jit(solution)/shard_map/dot_general | solution.py:232
  130.6 11.9 %collective-permute-done.18 = bf16[256,1024]{1,0:T(8,128)(2,1)} collective-permute-done((bf16[256,1024]{1,0:T(8,128)(2,1)S(1)}, bf16[256,1024]{1,0:T(8,128)(2,1)}, u32[]{:S(2)}, u32[]{:S(2)}) %collective-permute-start.18) | collective-permute-done | bytes 524320 | tf_op jit(solution)/shard_map/ppermute | solution.py:124
  148.9 13.5 %collective-permute-done.23 = bf16[2,64,1024]{2,1,0:T(8,128)(2,1)S(1)} collective-permute-done((bf16[2,64,1024]{2,1,0:T(8,128)(2,1)S(1)}, bf16[2,64,1024]{2,1,0:T(8,128)(2,1)S(1)}, u32[]{:S(2)}, u32[]{:S(2)}) %collective-permute-start.23) | collective-permute-done | bytes 262176 | tf_op jit(solution)/shard_map/ppermute | solution.py:94
  164.1 4.6 %collective-permute-done.24 = bf16[64,1024]{1,0:T(8,128)(2,1)S(1)} collective-permute-done((bf16[64,1024]{1,0:T(8,128)(2,1)S(1)}, bf16[64,1024]{1,0:T(8,128)(2,1)S(1)}, u32[]{:S(2)}, u32[]{:S(2)}) %collective-permute-start.24) | collective-permute-done | bytes 131104 | tf_op jit(solution)/shard_map/ppermute | solution.py:94
  170.6 2.6 %copy.57 = bf16[1024,1024]{1,0:T(8,128)(2,1)} copy(bf16[1024,1024]{0,1:T(8,128)(2,1)S(1)} %bitcast.130) | data formatting | bytes 4194304 | tf_op jit(solution)/shard_map/dot_general | solution.py:246
  173.2 2.6 %fusion.6 = f32[384,4,256]{2,0,1:T(8,128)S(1)} fusion(bf16[4,256,1024]{2,1,0:T(8,128)(2,1)} %bitcast.133, bf16[192,1024]{1,0:T(8,128)(2,1)S(1)} %copy-done.8, bf16[192,1024]{1,0:T(8,128)(2,1)S(1)} %divide_convert_fusion), kind=kOutput, calls=%fused_computation.36 | convolution fusion | flops 806879232 | bytes 4456448 | tf_op jit(solution)/shard_map/dot_general | solution.py:246
  175.9 2.8 %collective-permute-start.20 = (bf16[2,384,256]{2,1,0:T(8,128)(2,1)S(1)}, bf16[2,384,256]{2,1,0:T(8,128)(2,1)S(1)}, u32[]{:S(2)}, u32[]{:S(2)}) collective-permute-start(bf16[2,384,256]{2,1,0:T(8,128)(2,1)S(1)} %fusion.10), channel_id=1, source_target_pairs={{0,4},{4,0},{8,12},{12,8},{1,5},{5,1},{9,13},{13,9},{2,6},{6,2},{1... | collective-permute-start | bytes 1179656 | tf_op jit(solution)/shard_map/ppermute | solution.py:94
  178.9 9.9 %collective-permute-done.20 = bf16[2,384,256]{2,1,0:T(8,128)(2,1)S(1)} collective-permute-done((bf16[2,384,256]{2,1,0:T(8,128)(2,1)S(1)}, bf16[2,384,256]{2,1,0:T(8,128)(2,1)S(1)}, u32[]{:S(2)}, u32[]{:S(2)}) %collective-permute-start.20) | collective-permute-done | bytes 393248 | tf_op jit(solution)/shard_map/ppermute | solution.py:94
  188.9 2.2 %collective-permute-start.21 = (bf16[384,256]{1,0:T(8,128)(2,1)S(1)}, bf16[384,256]{1,0:T(8,128)(2,1)S(1)}, u32[]{:S(2)}, u32[]{:S(2)}) collective-permute-start(bf16[384,256]{1,0:T(8,128)(2,1)S(1)} %fusion.14), channel_id=1, source_target_pairs={{0,8},{4,12},{8,0},{12,4},{1,9},{5,13},{9,1},{13,5},{2,10},{6,14},... | collective-permute-start | bytes 589832 | tf_op jit(solution)/shard_map/ppermute | solution.py:94
  191.1 5.0 %collective-permute-done.26 = bf16[2,64,1024]{2,1,0:T(8,128)(2,1)S(1)} collective-permute-done((bf16[2,64,1024]{2,1,0:T(8,128)(2,1)S(1)}, bf16[2,64,1024]{2,1,0:T(8,128)(2,1)S(1)}, u32[]{:S(2)}, u32[]{:S(2)}) %collective-permute-start.26) | collective-permute-done | bytes 262176 | tf_op jit(solution)/shard_map/ppermute | solution.py:124
  (128 shorter events, 53.9 us)
Async XLA Ops:
  0.6 67.7 %collective-permute-start.1 = (bf16[192,1024]{1,0:T(8,128)(2,1)}, bf16[192,1024]{1,0:T(8,128)(2,1)S(1)}, u32[]{:S(2)}, u32[]{:S(2)}) collective-permute-start(bf16[192,1024]{1,0:T(8,128)(2,1)} %param.14), channel_id=1, source_target_pairs={{0,1},{1,0},{2,3},{3,2},{4,5},{5,4},{6,7},{7,6},{8,9},{9,8},{10,11... | collective-permute-start | bytes 1179656 | tf_op jit(solution)/shard_map/ppermute | solution.py:139
  1.1 57.3 %collective-permute-start.3 = (bf16[192,1024]{1,0:T(8,128)(2,1)}, bf16[192,1024]{1,0:T(8,128)(2,1)}, u32[]{:S(2)}, u32[]{:S(2)}) collective-permute-start(bf16[192,1024]{1,0:T(8,128)(2,1)} %param.14), channel_id=1, source_target_pairs={{0,2},{1,3},{2,0},{3,1},{4,6},{5,7},{6,4},{7,5},{8,10},{9,11},{10,... | collective-permute-start | bytes 1179656 | tf_op jit(solution)/shard_map/ppermute | solution.py:139
  3.7 21.5 %collective-permute-start.12 = (bf16[256,1024]{1,0:T(8,128)(2,1)}, bf16[256,1024]{1,0:T(8,128)(2,1)}, u32[]{:S(2)}, u32[]{:S(2)}) collective-permute-start(bf16[256,1024]{1,0:T(8,128)(2,1)} %param.16), channel_id=1, source_target_pairs={{0,2},{1,3},{2,0},{3,1},{4,6},{5,7},{6,4},{7,5},{8,10},{9,11},{10,... | collective-permute-start | bytes 1572872 | tf_op jit(solution)/shard_map/ppermute | solution.py:124
  5.7 5.8 %copy-start.15 = (s32[1,4,1024]{2,1,0:T(4,128)S(1)}, s32[1,4,1024]{2,1,0:T(4,128)}, u32[]{:S(2)}) copy-start(s32[1,4,1024]{2,1,0:T(4,128)} %param.11) | copy-start | bytes 49156
  6.4 50.1 %collective-permute-start.2 = (bf16[192,256]{1,0:T(8,128)(2,1)}, bf16[192,256]{1,0:T(8,128)(2,1)}, u32[]{:S(2)}, u32[]{:S(2)}) collective-permute-start(bf16[192,256]{1,0:T(8,128)(2,1)} %get-tuple-element.53), channel_id=1, source_target_pairs={{0,2},{1,3},{2,0},{3,1},{4,6},{5,7},{6,4},{7,5},{8,10},{9,11},{10,... | collective-permute-start | bytes 294920 | tf_op jit(solution)/shard_map/ppermute | solution.py:195
  11.5 6.5 %copy-start.16 = (f32[1024]{0:T(1024)S(1)}, f32[1024]{0:T(1024)}, u32[]{:S(2)}) copy-start(f32[1024]{0:T(1024)} %param.15) | copy-start | bytes 12292
  16.4 44.6 %collective-permute-start.8 = (bf16[192,1024]{1,0:T(8,128)(2,1)}, bf16[192,1024]{1,0:T(8,128)(2,1)}, u32[]{:S(2)}, u32[]{:S(2)}) collective-permute-start(bf16[192,1024]{1,0:T(8,128)(2,1)} %bitcast.137), channel_id=1, source_target_pairs={{0,4},{4,8},{8,12},{12,0},{1,5},{5,9},{9,13},{13,1},{2,6},{6,10},{... | collective-permute-start | bytes 1179656 | tf_op jit(solution)/shard_map/ppermute | solution.py:206
  20.3 7.3 %copy-start.14 = (s32[256,15]{0,1:T(8,128)S(1)}, s32[256,15]{0,1:T(8,128)}, u32[]{:S(2)}) copy-start(s32[256,15]{0,1:T(8,128)} %param.18) | copy-start | bytes 46084
  27.6 42.4 %collective-permute-start.13 = (bf16[2,256,1024]{2,1,0:T(8,128)(2,1)}, bf16[2,256,1024]{2,1,0:T(8,128)(2,1)}, u32[]{:S(2)}, u32[]{:S(2)}) collective-permute-start(bf16[2,256,1024]{2,1,0:T(8,128)(2,1)} %pad_maximum_fusion.2), channel_id=1, source_target_pairs={{0,1},{1,0},{2,3},{3,2},{4,5},{5,4},{6,7},{7,6},{8,9},{9,8},{10,11... | collective-permute-start | bytes 3145736 | tf_op jit(solution)/shard_map/ppermute | solution.py:124
  47.5 10.9 %copy-start.12 = (bf16[192,256]{1,0:T(8,128)(2,1)S(1)}, bf16[192,256]{1,0:T(8,128)(2,1)}, u32[]{:S(2)}) copy-start(bf16[192,256]{1,0:T(8,128)(2,1)} %get-tuple-element.54) | copy-start | bytes 294916
  53.1 15.2 %copy-start.2 = (f32[256,1024]{1,0:T(8,128)S(1)}, f32[256,1024]{1,0:T(8,128)}, u32[]{:S(2)}) copy-start(f32[256,1024]{1,0:T(8,128)} %convolution_add_fusion.2) | copy-start | bytes 3145732
  56.5 13.5 %collective-permute-start.10 = (bf16[192,1024]{1,0:T(8,128)(2,1)}, bf16[192,1024]{1,0:T(8,128)(2,1)}, u32[]{:S(2)}, u32[]{:S(2)}) collective-permute-start(bf16[192,1024]{1,0:T(8,128)(2,1)} %param.13), channel_id=1, source_target_pairs={{0,2},{1,3},{2,0},{3,1},{4,6},{5,7},{6,4},{7,5},{8,10},{9,11},{10,... | collective-permute-start | bytes 1179656 | tf_op jit(solution)/shard_map/ppermute | solution.py:139
  58.4 6.1 %collective-permute-start = (bf16[192,256]{1,0:T(8,128)(2,1)S(1)}, bf16[192,256]{1,0:T(8,128)(2,1)S(1)}, u32[]{:S(2)}, u32[]{:S(2)}) collective-permute-start(bf16[192,256]{1,0:T(8,128)(2,1)S(1)} %copy-done.12), channel_id=1, source_target_pairs={{0,1},{1,0},{2,3},{3,2},{4,5},{5,4},{6,7},{7,6},{8,9},{9,8},{10,11... | collective-permute-start | bytes 294920 | tf_op jit(solution)/shard_map/ppermute | solution.py:195
  61.0 12.6 %collective-permute-start.9 = (bf16[192,1024]{1,0:T(8,128)(2,1)}, bf16[192,1024]{1,0:T(8,128)(2,1)}, u32[]{:S(2)}, u32[]{:S(2)}) collective-permute-start(bf16[192,1024]{1,0:T(8,128)(2,1)} %param.13), channel_id=1, source_target_pairs={{0,1},{1,0},{2,3},{3,2},{4,5},{5,4},{6,7},{7,6},{8,9},{9,8},{10,11... | collective-permute-start | bytes 1179656 | tf_op jit(solution)/shard_map/ppermute | solution.py:139
  64.6 32.9 %collective-permute-start.6 = (bf16[192,1024]{1,0:T(8,128)(2,1)}, bf16[192,1024]{1,0:T(8,128)(2,1)}, u32[]{:S(2)}, u32[]{:S(2)}) collective-permute-start(bf16[192,1024]{1,0:T(8,128)(2,1)} %bitcast.6), channel_id=1, source_target_pairs={{0,12},{4,0},{8,4},{12,8},{1,13},{5,1},{9,5},{13,9},{2,14},{6,2},{... | collective-permute-start | bytes 1179656 | tf_op jit(solution)/shard_map/ppermute | solution.py:206
  68.3 25.8 %collective-permute-start.7 = (bf16[192,1024]{1,0:T(8,128)(2,1)}, bf16[192,1024]{1,0:T(8,128)(2,1)}, u32[]{:S(2)}, u32[]{:S(2)}) collective-permute-start(bf16[192,1024]{1,0:T(8,128)(2,1)} %bitcast.10), channel_id=1, source_target_pairs={{0,8},{4,12},{8,0},{12,4},{1,9},{5,13},{9,1},{13,5},{2,10},{6,14},... | collective-permute-start | bytes 1179656 | tf_op jit(solution)/shard_map/ppermute | solution.py:206
  70.0 3.9 %collective-permute-start.5 = (bf16[192,1024]{1,0:T(8,128)(2,1)}, bf16[192,1024]{1,0:T(8,128)(2,1)}, u32[]{:S(2)}, u32[]{:S(2)}) collective-permute-start(bf16[192,1024]{1,0:T(8,128)(2,1)} %collective-permute-done.3), channel_id=1, source_target_pairs={{0,1},{1,0},{2,3},{3,2},{4,5},{5,4},{6,7},{7,6},{8,9},{9,8},{10,11... | collective-permute-start | bytes 1179656 | tf_op jit(solution)/shard_map/ppermute | solution.py:139
  70.1 3.8 %collective-permute-start.11 = (bf16[192,1024]{1,0:T(8,128)(2,1)}, bf16[192,1024]{1,0:T(8,128)(2,1)S(1)}, u32[]{:S(2)}, u32[]{:S(2)}) collective-permute-start(bf16[192,1024]{1,0:T(8,128)(2,1)} %collective-permute-done.10), channel_id=1, source_target_pairs={{0,1},{1,0},{2,3},{3,2},{4,5},{5,4},{6,7},{7,6},{8,9},{9,8},{10,11... | collective-permute-start | bytes 1179656 | tf_op jit(solution)/shard_map/ppermute | solution.py:139
  73.6 39.4 %collective-permute-start.4 = (bf16[192,256]{1,0:T(8,128)(2,1)S(1)}, bf16[192,256]{1,0:T(8,128)(2,1)S(1)}, u32[]{:S(2)}, u32[]{:S(2)}) collective-permute-start(bf16[192,256]{1,0:T(8,128)(2,1)S(1)} %copy-done.11), channel_id=1, source_target_pairs={{0,3},{1,2},{2,1},{3,0},{4,7},{5,6},{6,5},{7,4},{8,11},{9,10},{10,... | collective-permute-start | bytes 294920 | tf_op jit(solution)/shard_map/ppermute | solution.py:195
  102.7 9.0 %collective-permute-start.14 = (bf16[192,256]{1,0:T(8,128)(2,1)S(1)}, bf16[192,256]{1,0:T(8,128)(2,1)S(1)}, u32[]{:S(2)}, u32[]{:S(2)}) collective-permute-start(bf16[192,256]{1,0:T(8,128)(2,1)S(1)} %get-tuple-element.55), channel_id=1, source_target_pairs={{0,1},{1,0},{2,3},{3,2},{4,5},{5,4},{6,7},{7,6},{8,9},{9,8},{10,11... | collective-permute-start | bytes 294920 | tf_op jit(solution)/shard_map/ppermute | solution.py:220
  102.8 8.6 %collective-permute-start.16 = (bf16[192,256]{1,0:T(8,128)(2,1)S(1)}, bf16[192,256]{1,0:T(8,128)(2,1)S(1)}, u32[]{:S(2)}, u32[]{:S(2)}) collective-permute-start(bf16[192,256]{1,0:T(8,128)(2,1)S(1)} %get-tuple-element.56), channel_id=1, source_target_pairs={{0,3},{1,2},{2,1},{3,0},{4,7},{5,6},{6,5},{7,4},{8,11},{9,10},{10,... | collective-permute-start | bytes 294920 | tf_op jit(solution)/shard_map/ppermute | solution.py:220
  103.4 6.6 %collective-permute-start.15 = (bf16[192,256]{1,0:T(8,128)(2,1)S(1)}, bf16[192,256]{1,0:T(8,128)(2,1)S(1)}, u32[]{:S(2)}, u32[]{:S(2)}) collective-permute-start(bf16[192,256]{1,0:T(8,128)(2,1)S(1)} %get-tuple-element.57), channel_id=1, source_target_pairs={{0,2},{1,3},{2,0},{3,1},{4,6},{5,7},{6,4},{7,5},{8,10},{9,11},{10,... | collective-permute-start | bytes 294920 | tf_op jit(solution)/shard_map/ppermute | solution.py:220
  122.0 3.6 %collective-permute-start.17 = (bf16[2,2,2,64,1024]{4,3,2,1,0:T(8,128)(2,1)}, bf16[2,2,2,64,1024]{4,3,2,1,0:T(8,128)(2,1)}, u32[]{:S(2)}, u32[]{:S(2)}) collective-permute-start(bf16[2,2,2,64,1024]{4,3,2,1,0:T(8,128)(2,1)} %fusion.5), channel_id=1, source_target_pairs={{0,1},{1,0},{2,3},{3,2},{4,5},{5,4},{6,7},{7,6},{8,9},{9,8},{10,11... | collective-permute-start | bytes 3145736 | tf_op jit(solution)/shard_map/ppermute | solution.py:94
  128.0 14.5 %collective-permute-start.18 = (bf16[256,1024]{1,0:T(8,128)(2,1)S(1)}, bf16[256,1024]{1,0:T(8,128)(2,1)}, u32[]{:S(2)}, u32[]{:S(2)}) collective-permute-start(bf16[256,1024]{1,0:T(8,128)(2,1)S(1)} %multiply_convert_fusion), channel_id=1, source_target_pairs={{0,2},{1,3},{2,0},{3,1},{4,6},{5,7},{6,4},{7,5},{8,10},{9,11},{10,... | collective-permute-start | bytes 1572872 | tf_op jit(solution)/shard_map/ppermute | solution.py:124
  129.5 15.4 %collective-permute-start.22 = (bf16[2,2,64,1024]{3,2,1,0:T(8,128)(2,1)}, bf16[2,2,64,1024]{3,2,1,0:T(8,128)(2,1)}, u32[]{:S(2)}, u32[]{:S(2)}) collective-permute-start(bf16[2,2,64,1024]{3,2,1,0:T(8,128)(2,1)} %fusion.9), channel_id=1, source_target_pairs={{0,4},{1,5},{2,6},{3,7},{4,0},{5,1},{6,2},{7,3},{8,12},{9,13},{10,... | collective-permute-start | bytes 1572872 | tf_op jit(solution)/shard_map/ppermute | solution.py:94
  144.9 24.0 %collective-permute-start.19 = (bf16[2,256,1024]{2,1,0:T(8,128)(2,1)}, bf16[2,256,1024]{2,1,0:T(8,128)(2,1)}, u32[]{:S(2)}, u32[]{:S(2)}) collective-permute-start(bf16[2,256,1024]{2,1,0:T(8,128)(2,1)} %pad_maximum_fusion.3), channel_id=1, source_target_pairs={{0,1},{1,0},{2,3},{3,2},{4,5},{5,4},{6,7},{7,6},{8,9},{9,8},{10,11... | collective-permute-start | bytes 3145736 | tf_op jit(solution)/shard_map/ppermute | solution.py:124
  147.1 15.3 %collective-permute-start.23 = (bf16[2,64,1024]{2,1,0:T(8,128)(2,1)S(1)}, bf16[2,64,1024]{2,1,0:T(8,128)(2,1)S(1)}, u32[]{:S(2)}, u32[]{:S(2)}) collective-permute-start(bf16[2,64,1024]{2,1,0:T(8,128)(2,1)S(1)} %fusion.11), channel_id=1, source_target_pairs={{0,8},{1,9},{2,10},{3,11},{4,12},{5,13},{6,14},{7,15},{8,0},{9,1},... | collective-permute-start | bytes 786440 | tf_op jit(solution)/shard_map/ppermute | solution.py:94
  163.5 5.2 %collective-permute-start.24 = (bf16[64,1024]{1,0:T(8,128)(2,1)S(1)}, bf16[64,1024]{1,0:T(8,128)(2,1)S(1)}, u32[]{:S(2)}, u32[]{:S(2)}) collective-permute-start(bf16[64,1024]{1,0:T(8,128)(2,1)S(1)} %fusion.15), channel_id=1, source_target_pairs={{0,2},{1,3},{2,0},{3,1},{4,6},{5,7},{6,4},{7,5},{8,10},{9,11},{10,... | collective-permute-start | bytes 393224 | tf_op jit(solution)/shard_map/ppermute | solution.py:94
  168.8 10.0 %collective-permute-start.25 = (bf16[64,1024]{1,0:T(8,128)(2,1)S(1)}, bf16[64,1024]{1,0:T(8,128)(2,1)S(1)}, u32[]{:S(2)}, u32[]{:S(2)}) collective-permute-start(bf16[64,1024]{1,0:T(8,128)(2,1)S(1)} %fusion.12), channel_id=1, source_target_pairs={{0,8},{4,12},{8,0},{12,4},{1,9},{5,13},{9,1},{13,5},{2,10},{6,14},... | collective-permute-start | bytes 393224 | tf_op jit(solution)/shard_map/ppermute | solution.py:124
  175.9 12.9 %collective-permute-start.20 = (bf16[2,384,256]{2,1,0:T(8,128)(2,1)S(1)}, bf16[2,384,256]{2,1,0:T(8,128)(2,1)S(1)}, u32[]{:S(2)}, u32[]{:S(2)}) collective-permute-start(bf16[2,384,256]{2,1,0:T(8,128)(2,1)S(1)} %fusion.10), channel_id=1, source_target_pairs={{0,4},{4,0},{8,12},{12,8},{1,5},{5,1},{9,13},{13,9},{2,6},{6,2},{1... | collective-permute-start | bytes 1179656 | tf_op jit(solution)/shard_map/ppermute | solution.py:94
  178.8 17.3 %collective-permute-start.26 = (bf16[2,64,1024]{2,1,0:T(8,128)(2,1)S(1)}, bf16[2,64,1024]{2,1,0:T(8,128)(2,1)S(1)}, u32[]{:S(2)}, u32[]{:S(2)}) collective-permute-start(bf16[2,64,1024]{2,1,0:T(8,128)(2,1)S(1)} %pad_maximum_fusion.4), channel_id=1, source_target_pairs={{0,4},{4,0},{8,12},{12,8},{1,5},{5,1},{9,13},{13,9},{2,6},{6,2},{1... | collective-permute-start | bytes 786440 | tf_op jit(solution)/shard_map/ppermute | solution.py:124
  188.9 9.6 %collective-permute-start.21 = (bf16[384,256]{1,0:T(8,128)(2,1)S(1)}, bf16[384,256]{1,0:T(8,128)(2,1)S(1)}, u32[]{:S(2)}, u32[]{:S(2)}) collective-permute-start(bf16[384,256]{1,0:T(8,128)(2,1)S(1)} %fusion.14), channel_id=1, source_target_pairs={{0,8},{4,12},{8,0},{12,4},{1,9},{5,13},{9,1},{13,5},{2,10},{6,14},... | collective-permute-start | bytes 589832 | tf_op jit(solution)/shard_map/ppermute | solution.py:94
  (13 other events, 25.2 us)

commit v14 on v8

--- a/solution.py
+++ b/solution.py
@@ -96,10 +96,10 @@
     return cur
 
 
-def reduce_scatter_grid(x, n_dom, n_cols, send_dtype, carried):
+def reduce_scatter_grid(x, n_dom, n_cols, send_dtype, carried, later):
     if not (_is_pow2(n_dom) and _is_pow2(n_cols)):
         part = reduce_scatter_blocks(x, "cols", n_cols, send_dtype)
-        return reduce_scatter_blocks(part, "dom", n_dom, send_dtype), carried
+        return reduce_scatter_blocks(part, "dom", n_dom, send_dtype), later(carried)
     kc = n_cols.bit_length() - 1
     kd = n_dom.bit_length() - 1
     axis_bits = [kc - 1 - i for i in range(kc)] + [kc + kd - 1 - i for i in range(kd)]
@@ -109,8 +109,12 @@
     n = n_dom * n_cols
     cur = _butterfly_reduce(cur, axes, n, axis_bits, order[:1], send_dtype)
     cur, carried = lax.optimization_barrier((cur, carried))
-    rest = [b for b in axis_bits if b != order[0]]
-    return _butterfly_reduce(cur, axes, n, rest, order[1:], send_dtype), carried
+    axis_bits = [b for b in axis_bits if b != order[0]]
+    cur = _butterfly_reduce(cur, axes, n, axis_bits, order[1:2], send_dtype)
+    axis_bits = [b for b in axis_bits if b not in order[:2]]
+    result = later(carried)
+    cur, result = lax.optimization_barrier((cur, result))
+    return _butterfly_reduce(cur, axes, n, axis_bits, order[2:], send_dtype), result
 
 
 def all_gather_blocks(x, axis, n):
@@ -211,15 +215,19 @@
     back_one = jnp.dot(mix_matrix.T, back_mixed, precision=lax.Precision.HIGHEST)
     slope_one = (back_one * swish_slope(pre_one)).astype(jnp.bfloat16)
     dom_rows = up_rows // n_dom
-    upper_part, slope_one = reduce_scatter_grid(
+
+    def layer_grads(slope_rows):
+        slab_rows = all_gather_blocks(slope_rows, "cols", n_cols).reshape(tgt_dev, hidden)
+        return jnp.dot(both_t, slab_rows, preferred_element_type=jnp.float32)
+
+    upper_part, stacked = reduce_scatter_grid(
         local_grad.reshape(n_cols, n_dom, dom_rows, hidden),
         n_dom,
         n_cols,
         jnp.bfloat16,
         slope_one,
-    )
-    slab_rows = all_gather_blocks(slope_one, "cols", n_cols).reshape(tgt_dev, hidden)
-    stacked = jnp.dot(both_t, slab_rows, preferred_element_type=jnp.float32)
+        layer_grads,
+    )
     dom_cols = hidden // n_dom
     grad_upper = all_gather_blocks(upper_part.astype(jnp.bfloat16), "dom", n_dom)
     grad_upper = grad_upper.reshape(up_rows, hidden).astype(jnp.float32)

time: 163 us -> 171 us (1.049)
  waiting for transfers between devices: 54.1 us -> 64.6 us
    ppermute x10, waiting for transfers between devices: 19 us -> 27.6 us  [all_gather_blocks(): got = lax.ppermute(cur, axis, _xor_pairs(n, 1 << b))]
    dot_general x1 -> x0, local copies, waits for them, and re-layouts: 2.6 us -> none  [local(): stacked = jnp.dot(both_t, slab_rows, preferred_element_type=jnp.float32)]
    ppermute x6, waiting for transfers between devices: 31.6 us -> 33.5 us  [_butterfly_reduce(): got = lax.ppermute(send.astype(send_dtype), axis, _xor_pairs(n, 1 << b))]
  transfers between devices with their start and end apart: 25 -> 25, of which waited for: 8 -> 9; matrix products, arithmetic and copies ran while one was open for 34% -> 28% of each run, Pallas kernels for 8% -> 8%
where the time goes in v14:
time: 171 us; the launch traced here: 170 us
  waiting for transfers between devices  64.6 us (38%)
  local copies, waits for them, and re-layouts  39.4 us (23%)
  starting transfers between devices  22.8 us (13%)
  other arithmetic  15.3 us (9%)
  matrix products  13.6 us (8%)
  Pallas kernels  13 us (8%)
    ppermute x6, waiting for transfers between devices, _butterfly_reduce(): got = lax.ppermute(send.astype(send_dtype), axis, _xor_pairs(n, 1 << b))  33.5 us
    ppermute x10, waiting for transfers between devices, all_gather_blocks(): got = lax.ppermute(cur, axis, _xor_pairs(n, 1 << b))  27.6 us
    gather x8, local copies, waits for them, and re-layouts, local(): rows_t = features.at[slots].get(mode='promise_in_bounds').T  18.8 us
    pallas_call x4, Pallas kernels, accumulate(): pl.pallas_call(_accumulate_kernel, out_shape=[jax.ShapeDtypeStruct(acc_su...  13 us
    unnamed x35, local copies, waits for them, and re-layouts  9.08 us
    another operation x18, other arithmetic, join(): return jnp.stack([low, high], axis=k - 1 - b)  7.88 us
    ppermute x10, starting transfers between devices, all_gather_blocks(): got = lax.ppermute(cur, axis, _xor_pairs(n, 1 << b))  6.94 us
    ppermute x3, starting transfers between devices, local(): rows_t = lax.ppermute(rows_t, 'dom', _shift_pairs(n_dom, shift))  5.81 us
  transfers between devices with their start and end apart: 25, of which 9 were waited for; matrix products, arithmetic and copies ran while one was open for 28% of the time, Pallas kernels for 8%

profile of v14, /device:TPU:0, one launch (start us, length us, event | category | flops | bytes accessed | tf_op | source)
XLA Modules:
  0.0 170.2 jit_solution(10743319855906153997)
XLA Ops:
  0.7 1.8 %slice_bitcast_fusion = (bf16[192,1024]{1,0:T(8,128)(2,1)}, bf16[1024,192]{0,1:T(8,128)(2,1)S(1)}) fusion(bf16[4096,192]{0,1:T(8,128)(2,1)} %param.10), kind=kLoop, calls=%fused_computation.148 | loop fusion | bytes 1179648 | tf_op jit(solution)/shard_map/transpose | solution.py:168
  3.2 2.4 %collective-permute-start.4 = (bf16[192,256]{1,0:T(8,128)(2,1)}, bf16[192,256]{1,0:T(8,128)(2,1)}, u32[]{:S(2)}, u32[]{:S(2)}) collective-permute-start(bf16[192,256]{1,0:T(8,128)(2,1)} %get-tuple-element.54), channel_id=1, source_target_pairs={{0,3},{1,0},{2,1},{3,2},{4,7},{5,4},{6,5},{7,6},{8,11},{9,8},{10,9... | collective-permute-start | bytes 294920 | tf_op jit(solution)/shard_map/ppermute | solution.py:175
  7.6 3.1 %copy.48 = bf16[4096,192]{1,0:T(8,128)(2,1)S(1)} copy(bf16[4096,192]{0,1:T(8,128)(2,1)} %param.10) | data formatting | bytes 3145728 | tf_op args[0]
  10.9 3.9 %gather_fusion.2 = bf16[1024,192]{1,0:T(8,128)(2,1)S(1)} fusion(bf16[4096,192]{1,0:T(8,128)(2,1)S(1)} %copy.48, s32[1024]{0:T(1024)S(1)} %broadcast_clamp_fusion.1), kind=kCustom, calls=%fused_computation.2 | custom fusion | bytes 790528 | tf_op jit(solution)/shard_map/gather | solution.py:185
  15.8 1.6 collective-permute-start.7
  17.3 3.9 %gather_fusion.1 = bf16[1024,192]{1,0:T(8,128)(2,1)S(1)} fusion(bf16[4096,192]{1,0:T(8,128)(2,1)S(1)} %copy.48, s32[1024]{0:T(1024)S(1)} %broadcast_clamp_fusion.2), kind=kCustom, calls=%fused_computation.1 | custom fusion | bytes 790528 | tf_op jit(solution)/shard_map/gather | solution.py:185
  21.5 2.7 %collective-permute-start.6 = (bf16[192,1024]{1,0:T(8,128)(2,1)S(1)}, bf16[192,1024]{1,0:T(8,128)(2,1)}, u32[]{:S(2)}, u32[]{:S(2)}) collective-permute-start(bf16[192,1024]{1,0:T(8,128)(2,1)S(1)} %bitcast.175), channel_id=1, source_target_pairs={{0,8},{4,12},{8,0},{12,4},{1,9},{5,13},{9,1},{13,5},{2,10},{6,14},... | collective-permute-start | bytes 1179656 | tf_op jit(solution)/shard_map/ppermute | solution.py:187
  24.3 3.9 %gather_fusion.3 = bf16[1024,192]{1,0:T(8,128)(2,1)S(1)} fusion(bf16[4096,192]{1,0:T(8,128)(2,1)S(1)} %copy.48, s32[1024]{0:T(1024)S(1)} %broadcast_clamp_fusion), kind=kCustom, calls=%fused_computation.3 | custom fusion | bytes 790528 | tf_op jit(solution)/shard_map/gather | solution.py:185
  29.2 3.9 %gather_fusion = bf16[1024,192]{1,0:T(8,128)(2,1)S(1)} fusion(bf16[4096,192]{1,0:T(8,128)(2,1)S(1)} %copy.48, s32[1024]{0:T(1024)S(1)} %broadcast_clamp_fusion.3), kind=kCustom, calls=%fused_computation | custom fusion | bytes 790528 | tf_op jit(solution)/shard_map/gather | solution.py:185
  36.3 3.3 %shard_map.129 = (f32[192,1024]{1,0:T(8,128)}, f32[8,1024]{1,0:T(8,128)}) custom-call(s32[1,1024]{1,0:T(1,128)} %get-tuple-element.62.tgt_ref, bf16[192,1024]{1,0:T(8,128)(2,1)} %bitcast.176, f32[192,1024]{1,0:T(8,128)} %broadcast_in_dim.4.sum_in, f32[8,1024]{1,0:T(8,128)} %broadcast_in_dim.5.cnt_in), custom_call_target="tpu_custom_call", output_to_operand_aliasing={{0}: (2, {}), {1}: (3, {})} | custom-call | flops 419430400 | bytes 2035712 | tf_op jit(solution)/shard_map/pallas_call | solution.py:46
  41.6 3.2 %shard_map.130 = (f32[192,1024]{1,0:T(8,128)}, f32[8,1024]{1,0:T(8,128)}) custom-call(s32[1,1024]{1,0:T(1,128)} %get-tuple-element.65.tgt_ref, bf16[192,1024]{1,0:T(8,128)(2,1)} %collective-permute-done.7.rec_ref, f32[192,1024]{1,0:T(8,128)} %get-tuple-element.16.sum_in, ...), custom_call_target="tpu_custom_call", output_to_operand_aliasing={{0}: (2, {}), {1}: (3, {})} | custom-call | flops 419430400 | bytes 2035712 | tf_op jit(solution)/shard_map/pallas_call | solution.py:46
  44.9 1.6 collective-permute-start.5
  46.5 3.2 %shard_map.131 = (f32[192,1024]{1,0:T(8,128)}, f32[8,1024]{1,0:T(8,128)}) custom-call(s32[1,1024]{1,0:T(1,128)} %get-tuple-element.63.tgt_ref, bf16[192,1024]{1,0:T(8,128)(2,1)} %collective-permute-done.6.rec_ref, f32[192,1024]{1,0:T(8,128)} %get-tuple-element.18.sum_in, ...), custom_call_target="tpu_custom_call", output_to_operand_aliasing={{0}: (2, {}), {1}: (3, {})} | custom-call | flops 419430400 | bytes 2035712 | tf_op jit(solution)/shard_map/pallas_call | solution.py:46
  49.7 1.6 collective-permute-start.13
  52.6 3.5 %collective-permute-done.5.rec_ref = bf16[192,1024]{1,0:T(8,128)(2,1)S(1)} collective-permute-done((bf16[192,1024]{1,0:T(8,128)(2,1)}, bf16[192,1024]{1,0:T(8,128)(2,1)S(1)}, u32[]{:S(2)}, u32[]{:S(2)}) %collective-permute-start.5) | collective-permute-done | bytes 393248 | tf_op jit(solution)/shard_map/ppermute | solution.py:187
  56.8 3.2 %shard_map.132 = (f32[192,1024]{1,0:T(8,128)}, f32[8,1024]{1,0:T(8,128)}) custom-call(s32[1,1024]{1,0:T(1,128)} %get-tuple-element.64.tgt_ref, bf16[192,1024]{1,0:T(8,128)(2,1)} %copy-done.15, f32[192,1024]{1,0:T(8,128)} %get-tuple-element.20.sum_in, f32[8,1024]{1,0:T(8,128)} %get-tuple-element.21.cnt_in), custom_call_target="tpu_custom_call", output_to_operand_aliasing={{0}: (2, {}), {1}: (3, {})} | custom-call | flops 419430400 | bytes 2035712 | tf_op jit(solution)/shard_map/pallas_call | solution.py:46
  62.2 2.7 %collective-permute-done.13 = bf16[256,1024]{1,0:T(8,128)(2,1)} collective-permute-done((bf16[256,1024]{1,0:T(8,128)(2,1)}, bf16[256,1024]{1,0:T(8,128)(2,1)}, u32[]{:S(2)}, u32[]{:S(2)}) %collective-permute-start.13) | collective-permute-done | bytes 524320 | tf_op jit(solution)/shard_map/ppermute | solution.py:128
  79.0 1.7 multiply_convert_fusion.2
  81.6 2.0 %copy-done = f32[1024,1024]{1,0:T(8,128)} copy-done((f32[1024,1024]{1,0:T(8,128)}, f32[1024,1024]{1,0:T(8,128)S(1)}, u32[]{:S(2)}) %copy-start) | copy-done | bytes 4194328
  84.7 2.3 %fusion.62 = f32[256,1024]{1,0:T(8,128)S(1)} fusion(bf16[1024,1024]{1,0:T(8,128)(2,1)S(1)} %bitcast.171, f32[256,1024]{1,0:T(8,128)} %copy-done.4, bf16[256,1024]{1,0:T(8,128)(2,1)} %param.19), kind=kOutput, calls=%fused_computation.149 | convolution fusion | flops 539492352 | bytes 4718592 | tf_op jit(solution)/shard_map/dot_general | solution.py:212
  89.2 1.6 bitcast_add_fusion
  91.8 13.4 %collective-permute-done.17 = bf16[256,1024]{1,0:T(8,128)(2,1)S(1)} collective-permute-done((bf16[256,1024]{1,0:T(8,128)(2,1)S(1)}, bf16[256,1024]{1,0:T(8,128)(2,1)S(1)}, u32[]{:S(2)}, u32[]{:S(2)}) %collective-permute-start.17) | collective-permute-done | bytes 524320 | tf_op jit(solution)/shard_map/ppermute | solution.py:128
  107.6 14.2 %collective-permute-done.16 = bf16[2,2,64,1024]{3,2,1,0:T(8,128)(2,1)} collective-permute-done((bf16[2,2,64,1024]{3,2,1,0:T(8,128)(2,1)}, bf16[2,2,64,1024]{3,2,1,0:T(8,128)(2,1)}, u32[]{:S(2)}, u32[]{:S(2)}) %collective-permute-start.16) | collective-permute-done | bytes 524320 | tf_op jit(solution)/shard_map/ppermute | solution.py:94
  123.0 1.7 %select_bitcast_fusion.1 = (bf16[2,1,256,1024]{3,2,0,1:T(8,128)(2,1)S(1)}, bf16[2,1,256,1024]{3,2,0,1:T(8,128)(2,1)S(1)}) fusion(bf16[2,256,1024]{2,1,0:T(8,128)(2,1)} %collective-permute-done.18, pred[]{:T(512)S(6)} %eq.73, bf16[1,256,1024]{2,1,0:T(8,128)(2,1)S(1)} %get-tuple-element.39, bf16[1,256,1024]{2,1,0:T(8,128)(2,1)S(1)} %get-tuple-element.38), kind=kLoop, calls=%fused_computation.28 | loop fusion | flops 1572864 | bytes 4194305 | tf_op jit(solution)/shard_map/stack | solution.py:133
  126.0 2.2 %fusion.6 = f32[384,1024]{1,0:T(8,128)} fusion(bf16[1024,1024]{1,0:T(8,128)(2,1)S(1)} %bitcast.172, bf16[192,1024]{1,0:T(8,128)(2,1)S(1)} %copy-done.6, bf16[192,1024]{1,0:T(8,128)(2,1)S(1)} %divide_convert_fusion), kind=kOutput, calls=%fused_computation.40 | convolution fusion | flops 806879232 | bytes 4456448 | tf_op jit(solution)/shard_map/dot_general | solution.py:221
  128.3 1.6 copy.63
  131.3 11.4 %collective-permute-done.21 = bf16[2,64,1024]{2,1,0:T(8,128)(2,1)} collective-permute-done((bf16[2,64,1024]{2,1,0:T(8,128)(2,1)S(1)}, bf16[2,64,1024]{2,1,0:T(8,128)(2,1)}, u32[]{:S(2)}, u32[]{:S(2)}) %collective-permute-start.21) | collective-permute-done | bytes 262176 | tf_op jit(solution)/shard_map/ppermute | solution.py:94
  144.8 4.4 %collective-permute-done.22 = bf16[64,1024]{1,0:T(8,128)(2,1)S(1)} collective-permute-done((bf16[64,1024]{1,0:T(8,128)(2,1)S(1)}, bf16[64,1024]{1,0:T(8,128)(2,1)S(1)}, u32[]{:S(2)}, u32[]{:S(2)}) %collective-permute-start.22) | collective-permute-done | bytes 131104 | tf_op jit(solution)/shard_map/ppermute | solution.py:94
  149.5 3.0 %collective-permute-start.20 = (bf16[384,256]{1,0:T(8,128)(2,1)S(1)}, bf16[384,256]{1,0:T(8,128)(2,1)S(1)}, u32[]{:S(2)}, u32[]{:S(2)}) collective-permute-start(bf16[384,256]{1,0:T(8,128)(2,1)S(1)} %fusion.36), channel_id=1, source_target_pairs={{0,8},{4,12},{8,0},{12,4},{1,9},{5,13},{9,1},{13,5},{2,10},{6,14},... | collective-permute-start | bytes 589832 | tf_op jit(solution)/shard_map/ppermute | solution.py:94
  152.5 6.8 %collective-permute-done.23 = bf16[64,1024]{1,0:T(8,128)(2,1)S(1)} collective-permute-done((bf16[64,1024]{1,0:T(8,128)(2,1)S(1)}, bf16[64,1024]{1,0:T(8,128)(2,1)S(1)}, u32[]{:S(2)}, u32[]{:S(2)}) %collective-permute-start.23) | collective-permute-done | bytes 131104 | tf_op jit(solution)/shard_map/ppermute | solution.py:128
  160.1 3.4 %collective-permute-done.20 = bf16[384,256]{1,0:T(8,128)(2,1)S(1)} collective-permute-done((bf16[384,256]{1,0:T(8,128)(2,1)S(1)}, bf16[384,256]{1,0:T(8,128)(2,1)S(1)}, u32[]{:S(2)}, u32[]{:S(2)}) %collective-permute-start.20) | collective-permute-done | bytes 196640 | tf_op jit(solution)/shard_map/ppermute | solution.py:94
  164.3 4.7 %collective-permute-done.24 = bf16[2,64,1024]{2,1,0:T(8,128)(2,1)S(1)} collective-permute-done((bf16[2,64,1024]{2,1,0:T(8,128)(2,1)S(1)}, bf16[2,64,1024]{2,1,0:T(8,128)(2,1)S(1)}, u32[]{:S(2)}, u32[]{:S(2)}) %collective-permute-start.24) | collective-permute-done | bytes 262176 | tf_op jit(solution)/shard_map/ppermute | solution.py:128
  (130 shorter events, 44.7 us)
Async XLA Ops:
  2.5 8.3 %copy-start.12 = (s32[1,4,1024]{2,1,0:T(4,128)S(1)}, s32[1,4,1024]{2,1,0:T(4,128)}, u32[]{:S(2)}) copy-start(s32[1,4,1024]{2,1,0:T(4,128)} %param.11) | copy-start | bytes 49156
  3.2 67.3 %collective-permute-start.4 = (bf16[192,256]{1,0:T(8,128)(2,1)}, bf16[192,256]{1,0:T(8,128)(2,1)}, u32[]{:S(2)}, u32[]{:S(2)}) collective-permute-start(bf16[192,256]{1,0:T(8,128)(2,1)} %get-tuple-element.54), channel_id=1, source_target_pairs={{0,3},{1,0},{2,1},{3,2},{4,7},{5,4},{6,5},{7,6},{8,11},{9,8},{10,9... | collective-permute-start | bytes 294920 | tf_op jit(solution)/shard_map/ppermute | solution.py:175
  5.6 44.1 %collective-permute-start = (bf16[192,1024]{1,0:T(8,128)(2,1)}, bf16[192,1024]{1,0:T(8,128)(2,1)}, u32[]{:S(2)}, u32[]{:S(2)}) collective-permute-start(bf16[192,1024]{1,0:T(8,128)(2,1)} %param.14), channel_id=1, source_target_pairs={{0,2},{1,3},{2,0},{3,1},{4,6},{5,7},{6,4},{7,5},{8,10},{9,11},{10,... | collective-permute-start | bytes 1179656 | tf_op jit(solution)/shard_map/ppermute | solution.py:128
  6.2 43.5 %collective-permute-start.8 = (bf16[192,1024]{1,0:T(8,128)(2,1)}, bf16[192,1024]{1,0:T(8,128)(2,1)}, u32[]{:S(2)}, u32[]{:S(2)}) collective-permute-start(bf16[192,1024]{1,0:T(8,128)(2,1)} %param.13), channel_id=1, source_target_pairs={{0,2},{1,3},{2,0},{3,1},{4,6},{5,7},{6,4},{7,5},{8,10},{9,11},{10,... | collective-permute-start | bytes 1179656 | tf_op jit(solution)/shard_map/ppermute | solution.py:128
  15.8 25.3 %collective-permute-start.7 = (bf16[192,1024]{1,0:T(8,128)(2,1)}, bf16[192,1024]{1,0:T(8,128)(2,1)}, u32[]{:S(2)}, u32[]{:S(2)}) collective-permute-start(bf16[192,1024]{1,0:T(8,128)(2,1)} %bitcast.24), channel_id=1, source_target_pairs={{0,4},{4,8},{8,12},{12,0},{1,5},{5,9},{9,13},{13,1},{2,6},{6,10},{... | collective-permute-start | bytes 1179656 | tf_op jit(solution)/shard_map/ppermute | solution.py:187
  21.5 23.4 %collective-permute-start.6 = (bf16[192,1024]{1,0:T(8,128)(2,1)S(1)}, bf16[192,1024]{1,0:T(8,128)(2,1)}, u32[]{:S(2)}, u32[]{:S(2)}) collective-permute-start(bf16[192,1024]{1,0:T(8,128)(2,1)S(1)} %bitcast.175), channel_id=1, source_target_pairs={{0,8},{4,12},{8,0},{12,4},{1,9},{5,13},{9,1},{13,5},{2,10},{6,14},... | collective-permute-start | bytes 1179656 | tf_op jit(solution)/shard_map/ppermute | solution.py:187
  29.2 4.9 %copy-start.13 = (s32[1,4,1024]{2,1,0:T(4,128)S(1)}, s32[1,4,1024]{2,1,0:T(4,128)}, u32[]{:S(2)}) copy-start(s32[1,4,1024]{2,1,0:T(4,128)} %param.12) | copy-start | bytes 49156
  33.1 6.5 %copy-start.11 = (s32[256,15]{0,1:T(8,128)S(1)}, s32[256,15]{0,1:T(8,128)}, u32[]{:S(2)}) copy-start(s32[256,15]{0,1:T(8,128)} %param.18) | copy-start | bytes 46084
  36.3 15.0 %copy-start.7 = (bf16[192,1024]{1,0:T(8,128)(2,1)S(1)}, bf16[192,1024]{1,0:T(8,128)(2,1)}, u32[]{:S(2)}) copy-start(bf16[192,1024]{1,0:T(8,128)(2,1)} %param.13) | copy-start | bytes 1179652
  36.3 15.0 %copy-start.8 = (bf16[192,1024]{1,0:T(8,128)(2,1)S(1)}, bf16[192,1024]{1,0:T(8,128)(2,1)}, u32[]{:S(2)}) copy-start(bf16[192,1024]{1,0:T(8,128)(2,1)} %param.14) | copy-start | bytes 1179652
  41.1 31.2 %collective-permute-start.3 = (bf16[192,256]{1,0:T(8,128)(2,1)}, bf16[192,256]{1,0:T(8,128)(2,1)S(1)}, u32[]{:S(2)}, u32[]{:S(2)}) collective-permute-start(bf16[192,256]{1,0:T(8,128)(2,1)} %get-tuple-element.55), channel_id=1, source_target_pairs={{0,2},{1,3},{2,0},{3,1},{4,6},{5,7},{6,4},{7,5},{8,10},{9,11},{10,... | collective-permute-start | bytes 294920 | tf_op jit(solution)/shard_map/ppermute | solution.py:175
  44.9 11.2 %collective-permute-start.5 = (bf16[192,1024]{1,0:T(8,128)(2,1)}, bf16[192,1024]{1,0:T(8,128)(2,1)S(1)}, u32[]{:S(2)}, u32[]{:S(2)}) collective-permute-start(bf16[192,1024]{1,0:T(8,128)(2,1)} %bitcast.16), channel_id=1, source_target_pairs={{0,12},{4,0},{8,4},{12,8},{1,13},{5,1},{9,5},{13,9},{2,14},{6,2},{... | collective-permute-start | bytes 1179656 | tf_op jit(solution)/shard_map/ppermute | solution.py:187
  49.7 24.5 %collective-permute-start.2 = (bf16[192,256]{1,0:T(8,128)(2,1)}, bf16[192,256]{1,0:T(8,128)(2,1)}, u32[]{:S(2)}, u32[]{:S(2)}) collective-permute-start(bf16[192,256]{1,0:T(8,128)(2,1)} %get-tuple-element.53), channel_id=1, source_target_pairs={{0,1},{1,2},{2,3},{3,0},{4,5},{5,6},{6,7},{7,4},{8,9},{9,10},{10,1... | collective-permute-start | bytes 294920 | tf_op jit(solution)/shard_map/ppermute | solution.py:175
  49.7 15.1 %collective-permute-start.13 = (bf16[256,1024]{1,0:T(8,128)(2,1)}, bf16[256,1024]{1,0:T(8,128)(2,1)}, u32[]{:S(2)}, u32[]{:S(2)}) collective-permute-start(bf16[256,1024]{1,0:T(8,128)(2,1)} %param.16), channel_id=1, source_target_pairs={{0,2},{1,3},{2,0},{3,1},{4,6},{5,7},{6,4},{7,5},{8,10},{9,11},{10,... | collective-permute-start | bytes 1572872 | tf_op jit(solution)/shard_map/ppermute | solution.py:128
  56.1 10.4 %collective-permute-start.1 = (bf16[2,192,1024]{2,1,0:T(8,128)(2,1)S(1)}, bf16[2,192,1024]{2,1,0:T(8,128)(2,1)}, u32[]{:S(2)}, u32[]{:S(2)}) collective-permute-start(bf16[2,192,1024]{2,1,0:T(8,128)(2,1)S(1)} %pad_maximum_fusion.6), channel_id=1, source_target_pairs={{0,1},{1,0},{2,3},{3,2},{4,5},{5,4},{6,7},{7,6},{8,9},{9,8},{10,11... | collective-permute-start | bytes 2359304 | tf_op jit(solution)/shard_map/ppermute | solution.py:128
  64.8 4.6 %collective-permute-start.9 = (bf16[2,192,1024]{2,1,0:T(8,128)(2,1)S(1)}, bf16[2,192,1024]{2,1,0:T(8,128)(2,1)S(1)}, u32[]{:S(2)}, u32[]{:S(2)}) collective-permute-start(bf16[2,192,1024]{2,1,0:T(8,128)(2,1)S(1)} %pad_maximum_fusion.7), channel_id=1, source_target_pairs={{0,1},{1,0},{2,3},{3,2},{4,5},{5,4},{6,7},{7,6},{8,9},{9,8},{10,11... | collective-permute-start | bytes 2359304 | tf_op jit(solution)/shard_map/ppermute | solution.py:128
  66.5 9.0 %collective-permute-start.11 = (bf16[192,256]{1,0:T(8,128)(2,1)S(1)}, bf16[192,256]{1,0:T(8,128)(2,1)S(1)}, u32[]{:S(2)}, u32[]{:S(2)}) collective-permute-start(bf16[192,256]{1,0:T(8,128)(2,1)S(1)} %get-tuple-element.52), channel_id=1, source_target_pairs={{0,2},{1,3},{2,0},{3,1},{4,6},{5,7},{6,4},{7,5},{8,10},{9,11},{10,... | collective-permute-start | bytes 294920 | tf_op jit(solution)/shard_map/ppermute | solution.py:199
  69.5 6.3 %collective-permute-start.12 = (bf16[192,256]{1,0:T(8,128)(2,1)S(1)}, bf16[192,256]{1,0:T(8,128)(2,1)S(1)}, u32[]{:S(2)}, u32[]{:S(2)}) collective-permute-start(bf16[192,256]{1,0:T(8,128)(2,1)S(1)} %get-tuple-element.51), channel_id=1, source_target_pairs={{0,3},{1,0},{2,1},{3,2},{4,7},{5,4},{6,5},{7,6},{8,11},{9,8},{10,9... | collective-permute-start | bytes 294920 | tf_op jit(solution)/shard_map/ppermute | solution.py:199
  70.5 5.7 %collective-permute-start.10 = (bf16[192,256]{1,0:T(8,128)(2,1)S(1)}, bf16[192,256]{1,0:T(8,128)(2,1)S(1)}, u32[]{:S(2)}, u32[]{:S(2)}) collective-permute-start(bf16[192,256]{1,0:T(8,128)(2,1)S(1)} %get-tuple-element.50), channel_id=1, source_target_pairs={{0,1},{1,2},{2,3},{3,0},{4,5},{5,6},{6,7},{7,4},{8,9},{9,10},{10,1... | collective-permute-start | bytes 294920 | tf_op jit(solution)/shard_map/ppermute | solution.py:199
  72.3 5.7 %collective-permute-start.14 = (bf16[2,256,1024]{2,1,0:T(8,128)(2,1)S(1)}, bf16[2,256,1024]{2,1,0:T(8,128)(2,1)S(1)}, u32[]{:S(2)}, u32[]{:S(2)}) collective-permute-start(bf16[2,256,1024]{2,1,0:T(8,128)(2,1)S(1)} %pad_maximum_fusion.4), channel_id=1, source_target_pairs={{0,1},{1,0},{2,3},{3,2},{4,5},{5,4},{6,7},{7,6},{8,9},{9,8},{10,11... | collective-permute-start | bytes 3145736 | tf_op jit(solution)/shard_map/ppermute | solution.py:128
  84.7 3.6 %collective-permute-start.15 = (bf16[2,2,2,64,1024]{4,3,2,1,0:T(8,128)(2,1)}, bf16[2,2,2,64,1024]{4,3,2,1,0:T(8,128)(2,1)}, u32[]{:S(2)}, u32[]{:S(2)}) collective-permute-start(bf16[2,2,2,64,1024]{4,3,2,1,0:T(8,128)(2,1)} %fusion.5), channel_id=1, source_target_pairs={{0,1},{1,0},{2,3},{3,2},{4,5},{5,4},{6,7},{7,6},{8,9},{9,8},{10,11... | collective-permute-start | bytes 3145736 | tf_op jit(solution)/shard_map/ppermute | solution.py:94
  90.8 14.4 %collective-permute-start.17 = (bf16[256,1024]{1,0:T(8,128)(2,1)S(1)}, bf16[256,1024]{1,0:T(8,128)(2,1)S(1)}, u32[]{:S(2)}, u32[]{:S(2)}) collective-permute-start(bf16[256,1024]{1,0:T(8,128)(2,1)S(1)} %multiply_convert_fusion), channel_id=1, source_target_pairs={{0,2},{1,3},{2,0},{3,1},{4,6},{5,7},{6,4},{7,5},{8,10},{9,11},{10,... | collective-permute-start | bytes 1572872 | tf_op jit(solution)/shard_map/ppermute | solution.py:128
  106.3 16.7 %collective-permute-start.18 = (bf16[2,256,1024]{2,1,0:T(8,128)(2,1)}, bf16[2,256,1024]{2,1,0:T(8,128)(2,1)}, u32[]{:S(2)}, u32[]{:S(2)}) collective-permute-start(bf16[2,256,1024]{2,1,0:T(8,128)(2,1)} %pad_maximum_fusion.5), channel_id=1, source_target_pairs={{0,1},{1,0},{2,3},{3,2},{4,5},{5,4},{6,7},{7,6},{8,9},{9,8},{10,11... | collective-permute-start | bytes 3145736 | tf_op jit(solution)/shard_map/ppermute | solution.py:128
  107.2 14.7 %collective-permute-start.16 = (bf16[2,2,64,1024]{3,2,1,0:T(8,128)(2,1)}, bf16[2,2,64,1024]{3,2,1,0:T(8,128)(2,1)}, u32[]{:S(2)}, u32[]{:S(2)}) collective-permute-start(bf16[2,2,64,1024]{3,2,1,0:T(8,128)(2,1)} %fusion.10), channel_id=1, source_target_pairs={{0,4},{1,5},{2,6},{3,7},{4,0},{5,1},{6,2},{7,3},{8,12},{9,13},{10,... | collective-permute-start | bytes 1572872 | tf_op jit(solution)/shard_map/ppermute | solution.py:94
  123.0 5.1 %copy-start.2 = (f32[2,2,64,1024]{3,2,1,0:T(8,128)}, f32[2,2,64,1024]{3,2,1,0:T(8,128)S(1)}, u32[]{:S(2)}) copy-start(f32[2,2,64,1024]{3,2,1,0:T(8,128)S(1)} %bitcast_add_fusion.1) | copy-start | bytes 3145732
  128.2 14.6 %copy-start.3 = (f32[2,2,64,1024]{3,2,1,0:T(8,128)S(1)}, f32[2,2,64,1024]{3,2,1,0:T(8,128)}, u32[]{:S(2)}) copy-start(f32[2,2,64,1024]{3,2,1,0:T(8,128)} %copy-done.2) | copy-start | bytes 3145732
  128.2 14.6 %collective-permute-start.21 = (bf16[2,64,1024]{2,1,0:T(8,128)(2,1)S(1)}, bf16[2,64,1024]{2,1,0:T(8,128)(2,1)}, u32[]{:S(2)}, u32[]{:S(2)}) collective-permute-start(bf16[2,64,1024]{2,1,0:T(8,128)(2,1)S(1)} %fusion.33), channel_id=1, source_target_pairs={{0,8},{1,9},{2,10},{3,11},{4,12},{5,13},{6,14},{7,15},{8,0},{9,1},... | collective-permute-start | bytes 786440 | tf_op jit(solution)/shard_map/ppermute | solution.py:94
  130.8 18.6 %collective-permute-start.19 = (bf16[2,384,256]{2,1,0:T(8,128)(2,1)}, bf16[2,384,256]{2,1,0:T(8,128)(2,1)S(1)}, u32[]{:S(2)}, u32[]{:S(2)}) collective-permute-start(bf16[2,384,256]{2,1,0:T(8,128)(2,1)} %fusion.11), channel_id=1, source_target_pairs={{0,4},{4,0},{8,12},{12,8},{1,5},{5,1},{9,13},{13,9},{2,6},{6,2},{1... | collective-permute-start | bytes 1179656 | tf_op jit(solution)/shard_map/ppermute | solution.py:94
  143.8 5.4 %collective-permute-start.22 = (bf16[64,1024]{1,0:T(8,128)(2,1)S(1)}, bf16[64,1024]{1,0:T(8,128)(2,1)S(1)}, u32[]{:S(2)}, u32[]{:S(2)}) collective-permute-start(bf16[64,1024]{1,0:T(8,128)(2,1)S(1)} %fusion.37), channel_id=1, source_target_pairs={{0,2},{1,3},{2,0},{3,1},{4,6},{5,7},{6,4},{7,5},{8,10},{9,11},{10,... | collective-permute-start | bytes 393224 | tf_op jit(solution)/shard_map/ppermute | solution.py:94
  149.3 10.0 %collective-permute-start.23 = (bf16[64,1024]{1,0:T(8,128)(2,1)S(1)}, bf16[64,1024]{1,0:T(8,128)(2,1)S(1)}, u32[]{:S(2)}, u32[]{:S(2)}) collective-permute-start(bf16[64,1024]{1,0:T(8,128)(2,1)S(1)} %fusion.34), channel_id=1, source_target_pairs={{0,8},{4,12},{8,0},{12,4},{1,9},{5,13},{9,1},{13,5},{2,10},{6,14},... | collective-permute-start | bytes 393224 | tf_op jit(solution)/shard_map/ppermute | solution.py:128
  149.5 14.0 %collective-permute-start.20 = (bf16[384,256]{1,0:T(8,128)(2,1)S(1)}, bf16[384,256]{1,0:T(8,128)(2,1)S(1)}, u32[]{:S(2)}, u32[]{:S(2)}) collective-permute-start(bf16[384,256]{1,0:T(8,128)(2,1)S(1)} %fusion.36), channel_id=1, source_target_pairs={{0,8},{4,12},{8,0},{12,4},{1,9},{5,13},{9,1},{13,5},{2,10},{6,14},... | collective-permute-start | bytes 589832 | tf_op jit(solution)/shard_map/ppermute | solution.py:94
  159.3 9.7 %collective-permute-start.24 = (bf16[2,64,1024]{2,1,0:T(8,128)(2,1)S(1)}, bf16[2,64,1024]{2,1,0:T(8,128)(2,1)S(1)}, u32[]{:S(2)}, u32[]{:S(2)}) collective-permute-start(bf16[2,64,1024]{2,1,0:T(8,128)(2,1)S(1)} %pad_maximum_fusion.8), channel_id=1, source_target_pairs={{0,4},{4,0},{8,12},{12,8},{1,5},{5,1},{9,13},{13,9},{2,6},{6,2},{1... | collective-permute-start | bytes 786440 | tf_op jit(solution)/shard_map/ppermute | solution.py:128
  (10 other events, 13.2 us)

commit v15 on v8

--- a/solution.py
+++ b/solution.py
@@ -162,15 +162,7 @@
     me_dom = lax.axis_index("dom")
     me_col = lax.axis_index("cols")
     own_t = features[:tgt_dev].T
-    own_pre = bias_one
-    for shift in range(n_cols):
-        dest = (me_col + shift) % n_cols
-        src = (me_col - shift) % n_cols
-        chunk = lax.dynamic_slice_in_dim(own_t, dest * tgt_loc, tgt_loc, axis=1)
-        if shift:
-            chunk = lax.ppermute(chunk, "cols", _shift_pairs(n_cols, shift))
-        weight = lax.dynamic_index_in_dim(self_full, src, 0, keepdims=False)
-        own_pre = own_pre + contract_rows(chunk, weight)
+    both_full = jnp.concatenate([neigh_full, self_full], axis=1)
 
     summed_t = jnp.zeros((width, tgt_dev), jnp.float32)
     counts = jnp.zeros((8, tgt_dev), jnp.float32)
@@ -186,14 +178,14 @@
     mean_t = (summed_t / jnp.maximum(counts[:1], 1.0)).astype(jnp.bfloat16)
     both_t = jnp.concatenate([mean_t, own_t], axis=0)
 
-    pre_one = own_pre
+    pre_one = bias_one
     for shift in range(n_cols):
         dest = (me_col + shift) % n_cols
         src = (me_col - shift) % n_cols
-        chunk = lax.dynamic_slice_in_dim(mean_t, dest * tgt_loc, tgt_loc, axis=1)
+        chunk = lax.dynamic_slice_in_dim(both_t, dest * tgt_loc, tgt_loc, axis=1)
         if shift:
             chunk = lax.ppermute(chunk, "cols", _shift_pairs(n_cols, shift))
-        weight = lax.dynamic_index_in_dim(neigh_full, src, 0, keepdims=False)
+        weight = lax.dynamic_index_in_dim(both_full, src, 0, keepdims=False)
         pre_one = pre_one + contract_rows(chunk, weight)
     hidden_one = jax.nn.silu(pre_one).astype(jnp.bfloat16)
     mix_matrix = mixing(upper_neighbours, tgt_loc)

time: 163 us -> 159 us (0.975)
  matrix products: 14 us -> 11.2 us
  local copies, waits for them, and re-layouts: 39.8 us -> 37.8 us
    ppermute x6, waiting for transfers between devices: 31.6 us -> 35.2 us  [_butterfly_reduce(): got = lax.ppermute(send.astype(send_dtype), axis, _xor_pairs(n, 1 << b))]
    ppermute x3, waiting for transfers between devices: 3.49 us -> 0.01 us  [local(): rows_t = lax.ppermute(rows_t, 'dom', _shift_pairs(n_dom, shift))]
    ppermute x6 -> x3, starting transfers between devices: 4.9 us -> 2.07 us  [local(): chunk = lax.ppermute(chunk, 'cols', _shift_pairs(n_cols, shift))]
    dot_general x9 -> x5, matrix products: 5.42 us -> 2.84 us  [contract_rows(): lax.dot_general(left_mat, right_mat, (((0,), (0,)), ((), ())), preferred_...]
    ppermute x6 -> x3, waiting for transfers between devices: 0.02 us -> 2.21 us  [local(): chunk = lax.ppermute(chunk, 'cols', _shift_pairs(n_cols, shift))]
    unnamed x35 -> x37, local copies, waits for them, and re-layouts: 9.24 us -> 8.02 us
  transfers between devices with their start and end apart: 25 -> 22, of which waited for: 8 -> 9; matrix products, arithmetic and copies ran while one was open for 34% -> 30% of each run, Pallas kernels for 8% -> 8%
where the time goes in v15:
time: 159 us; the launch traced here: 158 us
  waiting for transfers between devices  55.1 us (35%)
  local copies, waits for them, and re-layouts  37.8 us (24%)
  starting transfers between devices  22.4 us (14%)
  other arithmetic  17.5 us (11%)
  Pallas kernels  13.1 us (8%)
  matrix products  11.2 us (7%)
    ppermute x6, waiting for transfers between devices, _butterfly_reduce(): got = lax.ppermute(send.astype(send_dtype), axis, _xor_pairs(n, 1 << b))  35.2 us
    gather x8, local copies, waits for them, and re-layouts, local(): rows_t = features.at[slots].get(mode='promise_in_bounds').T  19.5 us
    ppermute x10, waiting for transfers between devices, all_gather_blocks(): got = lax.ppermute(cur, axis, _xor_pairs(n, 1 << b))  17.7 us
    pallas_call x4, Pallas kernels, accumulate(): pl.pallas_call(_accumulate_kernel, out_shape=[jax.ShapeDtypeStruct(acc_su...  13.1 us
    another operation x18, other arithmetic, join(): return jnp.stack([low, high], axis=k - 1 - b)  9.83 us
    ppermute x10, starting transfers between devices, all_gather_blocks(): got = lax.ppermute(cur, axis, _xor_pairs(n, 1 << b))  8.17 us
    unnamed x37, local copies, waits for them, and re-layouts  8.02 us
    ppermute x3, starting transfers between devices, local(): rows_t = lax.ppermute(rows_t, 'dom', _shift_pairs(n_dom, shift))  6.96 us
  transfers between devices with their start and end apart: 22, of which 9 were waited for; matrix products, arithmetic and copies ran while one was open for 30% of the time, Pallas kernels for 8%

profile of v15, /device:TPU:0, one launch (start us, length us, event | category | flops | bytes accessed | tf_op | source)
XLA Modules:
  0.0 158.3 jit_solution(1869728440705803594)
XLA Ops:
  0.7 3.2 %copy.49 = bf16[4096,192]{1,0:T(8,128)(2,1)S(1)} copy(bf16[4096,192]{0,1:T(8,128)(2,1)} %param.10) | data formatting | bytes 3145728 | tf_op args[0]
  3.9 3.9 %gather_fusion.2 = bf16[1024,192]{1,0:T(8,128)(2,1)S(1)} fusion(bf16[4096,192]{1,0:T(8,128)(2,1)S(1)} %copy.49, s32[1024]{0:T(1024)S(1)} %broadcast_clamp_fusion.1), kind=kCustom, calls=%fused_computation.2 | custom fusion | bytes 790528 | tf_op jit(solution)/shard_map/gather | solution.py:173
  8.8 3.0 %collective-permute-start.2 = (bf16[192,1024]{1,0:T(8,128)(2,1)}, bf16[192,1024]{1,0:T(8,128)(2,1)}, u32[]{:S(2)}, u32[]{:S(2)}) collective-permute-start(bf16[192,1024]{1,0:T(8,128)(2,1)} %bitcast.11), channel_id=1, source_target_pairs={{0,4},{4,8},{8,12},{12,0},{1,5},{5,9},{9,13},{13,1},{2,6},{6,10},{... | collective-permute-start | bytes 1179656 | tf_op jit(solution)/shard_map/ppermute | solution.py:175
  11.9 3.9 %gather_fusion.1 = bf16[1024,192]{1,0:T(8,128)(2,1)S(1)} fusion(bf16[4096,192]{1,0:T(8,128)(2,1)S(1)} %copy.49, s32[1024]{0:T(1024)S(1)} %broadcast_clamp_fusion.2), kind=kCustom, calls=%fused_computation.1 | custom fusion | bytes 790528 | tf_op jit(solution)/shard_map/gather | solution.py:173
  16.7 2.6 %collective-permute-start.1 = (bf16[192,1024]{1,0:T(8,128)(2,1)}, bf16[192,1024]{1,0:T(8,128)(2,1)}, u32[]{:S(2)}, u32[]{:S(2)}) collective-permute-start(bf16[192,1024]{1,0:T(8,128)(2,1)} %bitcast.7), channel_id=1, source_target_pairs={{0,8},{4,12},{8,0},{12,4},{1,9},{5,13},{9,1},{13,5},{2,10},{6,14},... | collective-permute-start | bytes 1179656 | tf_op jit(solution)/shard_map/ppermute | solution.py:175
  19.3 3.9 %gather_fusion = bf16[1024,192]{1,0:T(8,128)(2,1)S(1)} fusion(bf16[4096,192]{1,0:T(8,128)(2,1)S(1)} %copy.49, s32[1024]{0:T(1024)S(1)} %broadcast_clamp_fusion.3), kind=kCustom, calls=%fused_computation | custom fusion | bytes 790528 | tf_op jit(solution)/shard_map/gather | solution.py:173
  25.6 1.5 collective-permute-start.3
  27.6 3.9 %gather_fusion.3 = bf16[1024,192]{1,0:T(8,128)(2,1)S(1)} fusion(bf16[4096,192]{1,0:T(8,128)(2,1)S(1)} %copy.49, s32[1024]{0:T(1024)S(1)} %broadcast_clamp_fusion), kind=kCustom, calls=%fused_computation.3 | custom fusion | bytes 790528 | tf_op jit(solution)/shard_map/gather | solution.py:173
  34.7 3.3 %shard_map.129 = (f32[192,1024]{1,0:T(8,128)}, f32[8,1024]{1,0:T(8,128)}) custom-call(s32[1,1024]{1,0:T(1,128)} %get-tuple-element.53.tgt_ref, bf16[192,1024]{1,0:T(8,128)(2,1)} %bitcast.160, f32[192,1024]{1,0:T(8,128)} %broadcast_in_dim.4.sum_in, f32[8,1024]{1,0:T(8,128)} %broadcast_in_dim.5.cnt_in), custom_call_target="tpu_custom_call", output_to_operand_aliasing={{0}: (2, {}), {1}: (3, {})} | custom-call | flops 419430400 | bytes 2035712 | tf_op jit(solution)/shard_map/pallas_call | solution.py:46
  38.0 1.5 convert_reduce_fusion
  40.5 1.6 collective-permute-start.10
  42.1 4.1 %collective-permute-done.5 = bf16[192,1024]{1,0:T(8,128)(2,1)} collective-permute-done((bf16[192,1024]{1,0:T(8,128)(2,1)S(1)}, bf16[192,1024]{1,0:T(8,128)(2,1)}, u32[]{:S(2)}, u32[]{:S(2)}) %collective-permute-start.5) | collective-permute-done | bytes 393248 | tf_op jit(solution)/shard_map/ppermute | solution.py:124
  48.2 3.3 %shard_map.130 = (f32[192,1024]{1,0:T(8,128)}, f32[8,1024]{1,0:T(8,128)}) custom-call(s32[1,1024]{1,0:T(1,128)} %get-tuple-element.56.tgt_ref, bf16[192,1024]{1,0:T(8,128)(2,1)} %collective-permute-done.2.rec_ref, f32[192,1024]{1,0:T(8,128)} %get-tuple-element.14.sum_in, ...), custom_call_target="tpu_custom_call", output_to_operand_aliasing={{0}: (2, {}), {1}: (3, {})} | custom-call | flops 419430400 | bytes 2035712 | tf_op jit(solution)/shard_map/pallas_call | solution.py:46
  51.5 3.3 %shard_map.131 = (f32[192,1024]{1,0:T(8,128)}, f32[8,1024]{1,0:T(8,128)}) custom-call(s32[1,1024]{1,0:T(1,128)} %get-tuple-element.54.tgt_ref, bf16[192,1024]{1,0:T(8,128)(2,1)} %collective-permute-done.1.rec_ref, f32[192,1024]{1,0:T(8,128)} %get-tuple-element.16.sum_in, ...), custom_call_target="tpu_custom_call", output_to_operand_aliasing={{0}: (2, {}), {1}: (3, {})} | custom-call | flops 419430400 | bytes 2035712 | tf_op jit(solution)/shard_map/pallas_call | solution.py:46
  54.7 3.3 %shard_map.132 = (f32[192,1024]{1,0:T(8,128)}, f32[8,1024]{1,0:T(8,128)}) custom-call(s32[1,1024]{1,0:T(1,128)} %get-tuple-element.55.tgt_ref, bf16[192,1024]{1,0:T(8,128)(2,1)} %collective-permute-done.rec_ref, f32[192,1024]{1,0:T(8,128)} %get-tuple-element.18.sum_in, f32[8,1024]{1,0:T(8,128)} %get-tuple-element.19.cnt_in), custom_call_target="tpu_custom_call", output_to_operand_aliasing={{0}: (2, {}), {1}: (3, {})} | custom-call | flops 419430400 | bytes 2035712 | tf_op jit(solution)/shard_map/pallas_call | solution.py:46
  60.1 1.6 collective-permute-start.8
  68.4 1.8 %collective-permute-done.9 = bf16[384,256]{1,0:T(8,128)(2,1)S(1)} collective-permute-done((bf16[384,256]{1,0:T(8,128)(2,1)S(1)}, bf16[384,256]{1,0:T(8,128)(2,1)S(1)}, u32[]{:S(2)}, u32[]{:S(2)}) %collective-permute-start.9) | collective-permute-done | bytes 196640 | tf_op jit(solution)/shard_map/ppermute | solution.py:187
  74.1 1.6 %multiply_convert_fusion.2 = (bf16[256,1024]{1,0:T(8,128)(2,1)}, f32[256,1024]{1,0:T(8,128)S(1)}) fusion(f32[1024]{0:T(1024)S(1)} %copy-done.17, bf16[256,1024]{1,0:T(8,128)(2,1)S(1)} %convolution_convert_fusion, bf16[1024,1024]{1,0:T(8,128)(2,1)S(1)} %bitcast.154), kind=kOutput, calls=%fused_computation.44 | convolution fusion | flops 538443776 | bytes 4198400 | tf_op jit(solution)/shard_map/dot_general | solution.py:195
  76.7 2.0 %copy-done = f32[1024,1024]{1,0:T(8,128)} copy-done((f32[1024,1024]{1,0:T(8,128)}, f32[1024,1024]{1,0:T(8,128)S(1)}, u32[]{:S(2)}) %copy-start) | copy-done | bytes 4194328
  80.6 2.0 %fusion.54 = f32[256,1024]{1,0:T(8,128)S(1)} fusion(bf16[1024,1024]{1,0:T(8,128)(2,1)S(1)} %bitcast.155, f32[256,1024]{1,0:T(8,128)S(1)} %get-tuple-element.58, bf16[256,1024]{1,0:T(8,128)(2,1)} %param.19), kind=kOutput, calls=%fused_computation.144 | convolution fusion | flops 539492352 | bytes 4718592 | tf_op jit(solution)/shard_map/dot_general | solution.py:200
  84.8 1.6 bitcast_add_fusion
  86.4 1.6 collective-permute-start.13
  89.6 10.9 %collective-permute-done.13 = bf16[256,1024]{1,0:T(8,128)(2,1)} collective-permute-done((bf16[256,1024]{1,0:T(8,128)(2,1)S(1)}, bf16[256,1024]{1,0:T(8,128)(2,1)}, u32[]{:S(2)}, u32[]{:S(2)}) %collective-permute-start.13) | collective-permute-done | bytes 524320 | tf_op jit(solution)/shard_map/ppermute | solution.py:124
  105.4 14.9 %collective-permute-done.18 = bf16[2,64,1024]{2,1,0:T(8,128)(2,1)S(1)} collective-permute-done((bf16[2,64,1024]{2,1,0:T(8,128)(2,1)S(1)}, bf16[2,64,1024]{2,1,0:T(8,128)(2,1)S(1)}, u32[]{:S(2)}, u32[]{:S(2)}) %collective-permute-start.18) | collective-permute-done | bytes 262176 | tf_op jit(solution)/shard_map/ppermute | solution.py:94
  121.4 1.6 collective-permute-start.19
  123.0 3.8 %collective-permute-done.19 = bf16[64,1024]{1,0:T(8,128)(2,1)S(1)} collective-permute-done((bf16[64,1024]{1,0:T(8,128)(2,1)S(1)}, bf16[64,1024]{1,0:T(8,128)(2,1)S(1)}, u32[]{:S(2)}, u32[]{:S(2)}) %collective-permute-start.19) | collective-permute-done | bytes 131104 | tf_op jit(solution)/shard_map/ppermute | solution.py:94
  126.9 1.4 select_bitcast_fusion.1
  128.7 2.6 %copy.61 = bf16[1024,1024]{1,0:T(8,128)(2,1)} copy(bf16[1024,1024]{0,1:T(8,128)(2,1)S(1)} %bitcast.153) | data formatting | bytes 4194304 | tf_op jit(solution)/shard_map/dot_general | solution.py:214
  131.3 2.6 %fusion.4 = f32[384,4,256]{2,0,1:T(8,128)S(1)} fusion(bf16[4,256,1024]{2,1,0:T(8,128)(2,1)} %bitcast.156, bf16[192,1024]{1,0:T(8,128)(2,1)S(1)} %slice_bitcast_fusion, bf16[192,1024]{1,0:T(8,128)(2,1)S(1)} %copy-done.3), kind=kOutput, calls=%fused_computation.51 | convolution fusion | flops 806879232 | bytes 4456448 | tf_op jit(solution)/shard_map/dot_general | solution.py:214
  136.2 12.0 %collective-permute-done.15 = bf16[2,384,256]{2,1,0:T(8,128)(2,1)S(1)} collective-permute-done((bf16[2,384,256]{2,1,0:T(8,128)(2,1)S(1)}, bf16[2,384,256]{2,1,0:T(8,128)(2,1)S(1)}, u32[]{:S(2)}, u32[]{:S(2)}) %collective-permute-start.15) | collective-permute-done | bytes 393248 | tf_op jit(solution)/shard_map/ppermute | solution.py:94
  149.1 2.6 %collective-permute-done.21 = bf16[2,64,1024]{2,1,0:T(8,128)(2,1)S(1)} collective-permute-done((bf16[2,64,1024]{2,1,0:T(8,128)(2,1)S(1)}, bf16[2,64,1024]{2,1,0:T(8,128)(2,1)S(1)}, u32[]{:S(2)}, u32[]{:S(2)}) %collective-permute-start.21) | collective-permute-done | bytes 262176 | tf_op jit(solution)/shard_map/ppermute | solution.py:124
  153.0 4.5 %collective-permute-done.16 = bf16[384,256]{1,0:T(8,128)(2,1)S(1)} collective-permute-done((bf16[384,256]{1,0:T(8,128)(2,1)S(1)}, bf16[384,256]{1,0:T(8,128)(2,1)S(1)}, u32[]{:S(2)}, u32[]{:S(2)}) %collective-permute-start.16) | collective-permute-done | bytes 196640 | tf_op jit(solution)/shard_map/ppermute | solution.py:94
  (121 shorter events, 41.8 us)
Async XLA Ops:
  0.6 3.3 %copy-start.14 = (s32[1,4,1024]{2,1,0:T(4,128)S(1)}, s32[1,4,1024]{2,1,0:T(4,128)}, u32[]{:S(2)}) copy-start(s32[1,4,1024]{2,1,0:T(4,128)} %param.11) | copy-start | bytes 49156
  8.8 38.8 %collective-permute-start.2 = (bf16[192,1024]{1,0:T(8,128)(2,1)}, bf16[192,1024]{1,0:T(8,128)(2,1)}, u32[]{:S(2)}, u32[]{:S(2)}) collective-permute-start(bf16[192,1024]{1,0:T(8,128)(2,1)} %bitcast.11), channel_id=1, source_target_pairs={{0,4},{4,8},{8,12},{12,0},{1,5},{5,9},{9,13},{13,1},{2,6},{6,10},{... | collective-permute-start | bytes 1179656 | tf_op jit(solution)/shard_map/ppermute | solution.py:175
  16.7 34.7 %collective-permute-start.1 = (bf16[192,1024]{1,0:T(8,128)(2,1)}, bf16[192,1024]{1,0:T(8,128)(2,1)}, u32[]{:S(2)}, u32[]{:S(2)}) collective-permute-start(bf16[192,1024]{1,0:T(8,128)(2,1)} %bitcast.7), channel_id=1, source_target_pairs={{0,8},{4,12},{8,0},{12,4},{1,9},{5,13},{9,1},{13,5},{2,10},{6,14},... | collective-permute-start | bytes 1179656 | tf_op jit(solution)/shard_map/ppermute | solution.py:175
  19.3 6.2 %copy-start.10 = (bf16[192,1024]{1,0:T(8,128)(2,1)S(1)}, bf16[192,1024]{1,0:T(8,128)(2,1)}, u32[]{:S(2)}) copy-start(bf16[192,1024]{1,0:T(8,128)(2,1)} %param.13) | copy-start | bytes 1179652
  19.3 7.7 %copy-start.9 = (bf16[192,1024]{1,0:T(8,128)(2,1)S(1)}, bf16[192,1024]{1,0:T(8,128)(2,1)}, u32[]{:S(2)}) copy-start(bf16[192,1024]{1,0:T(8,128)(2,1)} %param.14) | copy-start | bytes 1179652
  24.2 30.5 %collective-permute-start = (bf16[192,1024]{1,0:T(8,128)(2,1)}, bf16[192,1024]{1,0:T(8,128)(2,1)}, u32[]{:S(2)}, u32[]{:S(2)}) collective-permute-start(bf16[192,1024]{1,0:T(8,128)(2,1)} %bitcast.3), channel_id=1, source_target_pairs={{0,12},{4,0},{8,4},{12,8},{1,13},{5,1},{9,5},{13,9},{2,14},{6,2},{... | collective-permute-start | bytes 1179656 | tf_op jit(solution)/shard_map/ppermute | solution.py:175
  25.6 14.9 %collective-permute-start.3 = (bf16[192,1024]{1,0:T(8,128)(2,1)S(1)}, bf16[192,1024]{1,0:T(8,128)(2,1)}, u32[]{:S(2)}, u32[]{:S(2)}) collective-permute-start(bf16[192,1024]{1,0:T(8,128)(2,1)S(1)} %copy-done.10), channel_id=1, source_target_pairs={{0,2},{1,3},{2,0},{3,1},{4,6},{5,7},{6,4},{7,5},{8,10},{9,11},{10,... | collective-permute-start | bytes 1179656 | tf_op jit(solution)/shard_map/ppermute | solution.py:124
  27.1 19.1 %collective-permute-start.5 = (bf16[192,1024]{1,0:T(8,128)(2,1)S(1)}, bf16[192,1024]{1,0:T(8,128)(2,1)}, u32[]{:S(2)}, u32[]{:S(2)}) collective-permute-start(bf16[192,1024]{1,0:T(8,128)(2,1)S(1)} %copy-done.9), channel_id=1, source_target_pairs={{0,2},{1,3},{2,0},{3,1},{4,6},{5,7},{6,4},{7,5},{8,10},{9,11},{10,... | collective-permute-start | bytes 1179656 | tf_op jit(solution)/shard_map/ppermute | solution.py:124
  27.6 4.9 %copy-start.15 = (s32[1,4,1024]{2,1,0:T(4,128)S(1)}, s32[1,4,1024]{2,1,0:T(4,128)}, u32[]{:S(2)}) copy-start(s32[1,4,1024]{2,1,0:T(4,128)} %param.12) | copy-start | bytes 49156
  31.6 6.4 %copy-start.13 = (s32[256,15]{0,1:T(8,128)S(1)}, s32[256,15]{0,1:T(8,128)}, u32[]{:S(2)}) copy-start(s32[256,15]{0,1:T(8,128)} %param.18) | copy-start | bytes 46084
  40.5 21.1 %collective-permute-start.10 = (bf16[256,1024]{1,0:T(8,128)(2,1)}, bf16[256,1024]{1,0:T(8,128)(2,1)}, u32[]{:S(2)}, u32[]{:S(2)}) collective-permute-start(bf16[256,1024]{1,0:T(8,128)(2,1)} %param.16), channel_id=1, source_target_pairs={{0,2},{1,3},{2,0},{3,1},{4,6},{5,7},{6,4},{7,5},{8,10},{9,11},{10,... | collective-permute-start | bytes 1572872 | tf_op jit(solution)/shard_map/ppermute | solution.py:124
  47.5 16.1 %collective-permute-start.6 = (bf16[2,192,1024]{2,1,0:T(8,128)(2,1)S(1)}, bf16[2,192,1024]{2,1,0:T(8,128)(2,1)}, u32[]{:S(2)}, u32[]{:S(2)}) collective-permute-start(bf16[2,192,1024]{2,1,0:T(8,128)(2,1)S(1)} %pad_maximum_fusion.8), channel_id=1, source_target_pairs={{0,1},{1,0},{2,3},{3,2},{4,5},{5,4},{6,7},{7,6},{8,9},{9,8},{10,11... | collective-permute-start | bytes 2359304 | tf_op jit(solution)/shard_map/ppermute | solution.py:124
  47.7 18.2 %collective-permute-start.4 = (bf16[2,192,1024]{2,1,0:T(8,128)(2,1)S(1)}, bf16[2,192,1024]{2,1,0:T(8,128)(2,1)}, u32[]{:S(2)}, u32[]{:S(2)}) collective-permute-start(bf16[2,192,1024]{2,1,0:T(8,128)(2,1)S(1)} %pad_maximum_fusion.7), channel_id=1, source_target_pairs={{0,1},{1,0},{2,3},{3,2},{4,5},{5,4},{6,7},{7,6},{8,9},{9,8},{10,11... | collective-permute-start | bytes 2359304 | tf_op jit(solution)/shard_map/ppermute | solution.py:124
  60.0 10.7 %copy-start.2 = (bf16[192,1024]{1,0:T(8,128)(2,1)}, bf16[192,1024]{1,0:T(8,128)(2,1)S(1)}, u32[]{:S(2)}) copy-start(bf16[192,1024]{1,0:T(8,128)(2,1)S(1)} %divide_convert_fusion) | copy-start | bytes 1179652
  60.1 7.8 %collective-permute-start.8 = (bf16[384,256]{1,0:T(8,128)(2,1)S(1)}, bf16[384,256]{1,0:T(8,128)(2,1)S(1)}, u32[]{:S(2)}, u32[]{:S(2)}) collective-permute-start(bf16[384,256]{1,0:T(8,128)(2,1)S(1)} %get-tuple-element.37), channel_id=1, source_target_pairs={{0,2},{1,3},{2,0},{3,1},{4,6},{5,7},{6,4},{7,5},{8,10},{9,11},{10,... | collective-permute-start | bytes 589832 | tf_op jit(solution)/shard_map/ppermute | solution.py:187
  61.6 8.6 %collective-permute-start.9 = (bf16[384,256]{1,0:T(8,128)(2,1)S(1)}, bf16[384,256]{1,0:T(8,128)(2,1)S(1)}, u32[]{:S(2)}, u32[]{:S(2)}) collective-permute-start(bf16[384,256]{1,0:T(8,128)(2,1)S(1)} %get-tuple-element.38), channel_id=1, source_target_pairs={{0,3},{1,0},{2,1},{3,2},{4,7},{5,4},{6,5},{7,6},{8,11},{9,8},{10,9... | collective-permute-start | bytes 589832 | tf_op jit(solution)/shard_map/ppermute | solution.py:187
  61.6 9.5 %collective-permute-start.7 = (bf16[384,256]{1,0:T(8,128)(2,1)S(1)}, bf16[384,256]{1,0:T(8,128)(2,1)S(1)}, u32[]{:S(2)}, u32[]{:S(2)}) collective-permute-start(bf16[384,256]{1,0:T(8,128)(2,1)S(1)} %get-tuple-element.36), channel_id=1, source_target_pairs={{0,1},{1,2},{2,3},{3,0},{4,5},{5,6},{6,7},{7,4},{8,9},{9,10},{10,1... | collective-permute-start | bytes 589832 | tf_op jit(solution)/shard_map/ppermute | solution.py:187
  63.5 9.5 %collective-permute-start.11 = (bf16[2,256,1024]{2,1,0:T(8,128)(2,1)S(1)}, bf16[2,256,1024]{2,1,0:T(8,128)(2,1)S(1)}, u32[]{:S(2)}, u32[]{:S(2)}) collective-permute-start(bf16[2,256,1024]{2,1,0:T(8,128)(2,1)S(1)} %pad_maximum_fusion.5), channel_id=1, source_target_pairs={{0,1},{1,0},{2,3},{3,2},{4,5},{5,4},{6,7},{7,6},{8,9},{9,8},{10,11... | collective-permute-start | bytes 3145736 | tf_op jit(solution)/shard_map/ppermute | solution.py:124
  68.4 2.3 %copy-start.16 = (f32[1024]{0:T(1024)S(1)}, f32[1024]{0:T(1024)}, u32[]{:S(2)}) copy-start(f32[1024]{0:T(1024)} %param.15) | copy-start | bytes 12292
  79.8 4.2 %collective-permute-start.12 = (bf16[2,2,2,64,1024]{4,3,2,1,0:T(8,128)(2,1)}, bf16[2,2,2,64,1024]{4,3,2,1,0:T(8,128)(2,1)}, u32[]{:S(2)}, u32[]{:S(2)}) collective-permute-start(bf16[2,2,2,64,1024]{4,3,2,1,0:T(8,128)(2,1)} %fusion.2), channel_id=1, source_target_pairs={{0,1},{1,0},{2,3},{3,2},{4,5},{5,4},{6,7},{7,6},{8,9},{9,8},{10,11... | collective-permute-start | bytes 3145736 | tf_op jit(solution)/shard_map/ppermute | solution.py:94
  82.7 2.2 %copy-start.1 = (f32[1024,1024]{1,0:T(8,128)S(1)}, f32[1024,1024]{1,0:T(8,128)}, u32[]{:S(2)}) copy-start(f32[1024,1024]{1,0:T(8,128)} %copy-done) | copy-start | bytes 12582916
  84.0 2.4 %copy-start.8 = (bf16[256,1024]{1,0:T(8,128)(2,1)}, bf16[256,1024]{1,0:T(8,128)(2,1)S(1)}, u32[]{:S(2)}) copy-start(bf16[256,1024]{1,0:T(8,128)(2,1)S(1)} %multiply_convert_fusion) | copy-start | bytes 1572868
  86.4 14.0 %collective-permute-start.13 = (bf16[256,1024]{1,0:T(8,128)(2,1)S(1)}, bf16[256,1024]{1,0:T(8,128)(2,1)}, u32[]{:S(2)}, u32[]{:S(2)}) collective-permute-start(bf16[256,1024]{1,0:T(8,128)(2,1)S(1)} %multiply_convert_fusion), channel_id=1, source_target_pairs={{0,2},{1,3},{2,0},{3,1},{4,6},{5,7},{6,4},{7,5},{8,10},{9,11},{10,... | collective-permute-start | bytes 1572872 | tf_op jit(solution)/shard_map/ppermute | solution.py:124
  88.9 13.9 %collective-permute-start.17 = (bf16[2,2,64,1024]{3,2,1,0:T(8,128)(2,1)}, bf16[2,2,64,1024]{3,2,1,0:T(8,128)(2,1)}, u32[]{:S(2)}, u32[]{:S(2)}) collective-permute-start(bf16[2,2,64,1024]{3,2,1,0:T(8,128)(2,1)} %fusion.20), channel_id=1, source_target_pairs={{0,4},{1,5},{2,6},{3,7},{4,0},{5,1},{6,2},{7,3},{8,12},{9,13},{10,... | collective-permute-start | bytes 1572872 | tf_op jit(solution)/shard_map/ppermute | solution.py:94
  102.8 24.2 %collective-permute-start.14 = (bf16[2,256,1024]{2,1,0:T(8,128)(2,1)}, bf16[2,256,1024]{2,1,0:T(8,128)(2,1)}, u32[]{:S(2)}, u32[]{:S(2)}) collective-permute-start(bf16[2,256,1024]{2,1,0:T(8,128)(2,1)} %pad_maximum_fusion.6), channel_id=1, source_target_pairs={{0,1},{1,0},{2,3},{3,2},{4,5},{5,4},{6,7},{7,6},{8,9},{9,8},{10,11... | collective-permute-start | bytes 3145736 | tf_op jit(solution)/shard_map/ppermute | solution.py:124
  105.0 15.3 %collective-permute-start.18 = (bf16[2,64,1024]{2,1,0:T(8,128)(2,1)S(1)}, bf16[2,64,1024]{2,1,0:T(8,128)(2,1)S(1)}, u32[]{:S(2)}, u32[]{:S(2)}) collective-permute-start(bf16[2,64,1024]{2,1,0:T(8,128)(2,1)S(1)} %fusion.22), channel_id=1, source_target_pairs={{0,8},{1,9},{2,10},{3,11},{4,12},{5,13},{6,14},{7,15},{8,0},{9,1},... | collective-permute-start | bytes 786440 | tf_op jit(solution)/shard_map/ppermute | solution.py:94
  121.4 5.4 %collective-permute-start.19 = (bf16[64,1024]{1,0:T(8,128)(2,1)S(1)}, bf16[64,1024]{1,0:T(8,128)(2,1)S(1)}, u32[]{:S(2)}, u32[]{:S(2)}) collective-permute-start(bf16[64,1024]{1,0:T(8,128)(2,1)S(1)} %fusion.31), channel_id=1, source_target_pairs={{0,2},{1,3},{2,0},{3,1},{4,6},{5,7},{6,4},{7,5},{8,10},{9,11},{10,... | collective-permute-start | bytes 393224 | tf_op jit(solution)/shard_map/ppermute | solution.py:94
  126.8 8.0 %collective-permute-start.20 = (bf16[64,1024]{1,0:T(8,128)(2,1)S(1)}, bf16[64,1024]{1,0:T(8,128)(2,1)S(1)}, u32[]{:S(2)}, u32[]{:S(2)}) collective-permute-start(bf16[64,1024]{1,0:T(8,128)(2,1)S(1)} %fusion.23), channel_id=1, source_target_pairs={{0,8},{4,12},{8,0},{12,4},{1,9},{5,13},{9,1},{13,5},{2,10},{6,14},... | collective-permute-start | bytes 393224 | tf_op jit(solution)/shard_map/ppermute | solution.py:124
  128.7 2.6 %copy-start.3 = (bf16[192,1024]{1,0:T(8,128)(2,1)S(1)}, bf16[192,1024]{1,0:T(8,128)(2,1)}, u32[]{:S(2)}) copy-start(bf16[192,1024]{1,0:T(8,128)(2,1)} %copy-done.2) | copy-start | bytes 1179652
  133.9 14.2 %collective-permute-start.15 = (bf16[2,384,256]{2,1,0:T(8,128)(2,1)S(1)}, bf16[2,384,256]{2,1,0:T(8,128)(2,1)S(1)}, u32[]{:S(2)}, u32[]{:S(2)}) collective-permute-start(bf16[2,384,256]{2,1,0:T(8,128)(2,1)S(1)} %fusion.21), channel_id=1, source_target_pairs={{0,4},{4,0},{8,12},{12,8},{1,5},{5,1},{9,13},{13,9},{2,6},{6,2},{1... | collective-permute-start | bytes 1179656 | tf_op jit(solution)/shard_map/ppermute | solution.py:94
  134.9 16.9 %collective-permute-start.21 = (bf16[2,64,1024]{2,1,0:T(8,128)(2,1)S(1)}, bf16[2,64,1024]{2,1,0:T(8,128)(2,1)S(1)}, u32[]{:S(2)}, u32[]{:S(2)}) collective-permute-start(bf16[2,64,1024]{2,1,0:T(8,128)(2,1)S(1)} %pad_maximum_fusion.9), channel_id=1, source_target_pairs={{0,4},{4,0},{8,12},{12,8},{1,5},{5,1},{9,13},{13,9},{2,6},{6,2},{1... | collective-permute-start | bytes 786440 | tf_op jit(solution)/shard_map/ppermute | solution.py:124
  148.3 9.2 %collective-permute-start.16 = (bf16[384,256]{1,0:T(8,128)(2,1)S(1)}, bf16[384,256]{1,0:T(8,128)(2,1)S(1)}, u32[]{:S(2)}, u32[]{:S(2)}) collective-permute-start(bf16[384,256]{1,0:T(8,128)(2,1)S(1)} %fusion.25), channel_id=1, source_target_pairs={{0,8},{4,12},{8,0},{12,4},{1,9},{5,13},{9,1},{13,5},{2,10},{6,14},... | collective-permute-start | bytes 589832 | tf_op jit(solution)/shard_map/ppermute | solution.py:94
  (8 other events, 11.3 us)

commit v16 on v15

--- a/solution.py
+++ b/solution.py
@@ -154,15 +154,14 @@
     w_rows = neigh_weight.shape[0]
     up_rows = upper_weight.shape[0]
 
-    neigh_full, self_full, full_upper = all_gather_blocks(
-        (neigh_weight, self_weight, upper_weight), "cols", n_cols
+    both_full, full_upper = all_gather_blocks(
+        (jnp.concatenate([neigh_weight, self_weight], axis=0), upper_weight), "cols", n_cols
     )
     full_upper = full_upper.reshape(n_cols * up_rows, hidden)
 
     me_dom = lax.axis_index("dom")
     me_col = lax.axis_index("cols")
     own_t = features[:tgt_dev].T
-    both_full = jnp.concatenate([neigh_full, self_full], axis=1)
 
     summed_t = jnp.zeros((width, tgt_dev), jnp.float32)
     counts = jnp.zeros((8, tgt_dev), jnp.float32)

time: 159 us -> 171 us (1.075)
  local copies, waits for them, and re-layouts: 37.8 us -> 44.1 us
  other arithmetic: 17.5 us -> 20.2 us
  waiting for transfers between devices: 55.1 us -> 57.3 us
    ppermute x6, starting transfers between devices: 5.16 us -> 9.6 us  [_butterfly_reduce(): got = lax.ppermute(send.astype(send_dtype), axis, _xor_pairs(n, 1 << b))]
    ppermute x10 -> x8, starting transfers between devices: 8.17 us -> 3.74 us  [all_gather_blocks(): got = lax.ppermute(cur, axis, _xor_pairs(n, 1 << b))]
    ppermute x10 -> x8, waiting for transfers between devices: 17.7 us -> 21.4 us  [all_gather_blocks(): got = lax.ppermute(cur, axis, _xor_pairs(n, 1 << b))]
    another operation x18 -> x15, other arithmetic: 9.83 us -> 12.6 us  [join(): return jnp.stack([low, high], axis=k - 1 - b)]
    ppermute x6, waiting for transfers between devices: 35.2 us -> 32.5 us  [_butterfly_reduce(): got = lax.ppermute(send.astype(send_dtype), axis, _xor_pairs(n, 1 << b))]
    unnamed x37 -> x52, local copies, waits for them, and re-layouts: 8.02 us -> 10.4 us
    gather x8, local copies, waits for them, and re-layouts: 19.5 us -> 21.7 us  [local(): rows_t = features.at[slots].get(mode='promise_in_bounds').T]
    concatenate x0 -> x1, local copies, waits for them, and re-layouts: none -> 1.76 us  [local(): jnp.concatenate([neigh_weight, self_weight], axis=0)]
  transfers between devices with their start and end apart: 22 -> 20, of which waited for: 9 -> 9; matrix products, arithmetic and copies ran while one was open for 30% -> 32% of each run, Pallas kernels for 8% -> 8%
where the time goes in v16:
time: 171 us; the launch traced here: 170 us
  waiting for transfers between devices  57.3 us (34%)
  local copies, waits for them, and re-layouts  44.1 us (26%)
  starting transfers between devices  22.4 us (13%)
  other arithmetic  20.2 us (12%)
  Pallas kernels  13.2 us (8%)
  matrix products  11.1 us (6%)
    ppermute x6, waiting for transfers between devices, _butterfly_reduce(): got = lax.ppermute(send.astype(send_dtype), axis, _xor_pairs(n, 1 << b))  32.5 us
    gather x8, local copies, waits for them, and re-layouts, local(): rows_t = features.at[slots].get(mode='promise_in_bounds').T  21.7 us
    ppermute x8, waiting for transfers between devices, all_gather_blocks(): got = lax.ppermute(cur, axis, _xor_pairs(n, 1 << b))  21.4 us
    pallas_call x4, Pallas kernels, accumulate(): pl.pallas_call(_accumulate_kernel, out_shape=[jax.ShapeDtypeStruct(acc_su...  13.2 us
    another operation x15, other arithmetic, join(): return jnp.stack([low, high], axis=k - 1 - b)  12.6 us
    unnamed x52, local copies, waits for them, and re-layouts  10.4 us
    ppermute x6, starting transfers between devices, _butterfly_reduce(): got = lax.ppermute(send.astype(send_dtype), axis, _xor_pairs(n, 1 << b))  9.6 us
    ppermute x3, starting transfers between devices, local(): rows_t = lax.ppermute(rows_t, 'dom', _shift_pairs(n_dom, shift))  6.96 us
  transfers between devices with their start and end apart: 20, of which 9 were waited for; matrix products, arithmetic and copies ran while one was open for 32% of the time, Pallas kernels for 8%

profile of v16, /device:TPU:0, one launch (start us, length us, event | category | flops | bytes accessed | tf_op | source)
XLA Modules:
  0.0 169.7 jit_solution(15993565419935244838)
XLA Ops:
  0.7 3.2 %copy.48 = bf16[4096,192]{1,0:T(8,128)(2,1)S(1)} copy(bf16[4096,192]{0,1:T(8,128)(2,1)} %param.10) | data formatting | bytes 3145728 | tf_op args[0]
  4.0 3.9 %gather_fusion.2 = bf16[1024,192]{1,0:T(8,128)(2,1)S(1)} fusion(bf16[4096,192]{1,0:T(8,128)(2,1)S(1)} %copy.48, s32[1024]{0:T(1024)S(1)} %get-tuple-element.56), kind=kCustom, calls=%fused_computation.2 | custom fusion | bytes 790528 | tf_op jit(solution)/shard_map/gather | solution.py:172
  8.9 3.0 %collective-permute-start.2 = (bf16[192,1024]{1,0:T(8,128)(2,1)}, bf16[192,1024]{1,0:T(8,128)(2,1)}, u32[]{:S(2)}, u32[]{:S(2)}) collective-permute-start(bf16[192,1024]{1,0:T(8,128)(2,1)} %bitcast.11), channel_id=1, source_target_pairs={{0,4},{4,8},{8,12},{12,0},{1,5},{5,9},{9,13},{13,1},{2,6},{6,10},{... | collective-permute-start | bytes 1179656 | tf_op jit(solution)/shard_map/ppermute | solution.py:174
  14.2 1.8 %constant_dynamic-update-slice_fusion = bf16[384,1024]{1,0:T(8,128)(2,1)} fusion(bf16[384,1024]{1,0:T(8,128)(2,1)} %constant_dynamic-update-slice_fusion.1, bf16[192,1024]{1,0:T(8,128)(2,1)} %param.14), kind=kLoop, calls=%fused_computation.117 | loop fusion | bytes 786432 | tf_op jit(solution)/shard_map/concatenate | solution.py:158
  16.5 3.9 %gather_fusion.1 = bf16[1024,192]{1,0:T(8,128)(2,1)S(1)} fusion(bf16[4096,192]{1,0:T(8,128)(2,1)S(1)} %copy.48, s32[1024]{0:T(1024)S(1)} %get-tuple-element.57), kind=kCustom, calls=%fused_computation.1 | custom fusion | bytes 790528 | tf_op jit(solution)/shard_map/gather | solution.py:172
  21.4 2.6 %collective-permute-start.1 = (bf16[192,1024]{1,0:T(8,128)(2,1)}, bf16[192,1024]{1,0:T(8,128)(2,1)}, u32[]{:S(2)}, u32[]{:S(2)}) collective-permute-start(bf16[192,1024]{1,0:T(8,128)(2,1)} %bitcast.7), channel_id=1, source_target_pairs={{0,8},{4,12},{8,0},{12,4},{1,9},{5,13},{9,1},{13,5},{2,10},{6,14},... | collective-permute-start | bytes 1179656 | tf_op jit(solution)/shard_map/ppermute | solution.py:174
  24.0 3.9 %gather_fusion = bf16[1024,192]{1,0:T(8,128)(2,1)S(1)} fusion(bf16[4096,192]{1,0:T(8,128)(2,1)S(1)} %copy.48, s32[1024]{0:T(1024)S(1)} %get-tuple-element.58), kind=kCustom, calls=%fused_computation | custom fusion | bytes 790528 | tf_op jit(solution)/shard_map/gather | solution.py:172
  34.1 8.1 %collective-permute-done.3 = bf16[384,1024]{1,0:T(8,128)(2,1)} collective-permute-done((bf16[384,1024]{1,0:T(8,128)(2,1)}, bf16[384,1024]{1,0:T(8,128)(2,1)}, u32[]{:S(2)}, u32[]{:S(2)}) %collective-permute-start.3) | collective-permute-done | bytes 786464 | tf_op jit(solution)/shard_map/ppermute | solution.py:124
  46.5 5.0 %gather_fusion.3 = bf16[1024,192]{1,0:T(8,128)(2,1)} fusion(bf16[4096,192]{1,0:T(8,128)(2,1)S(1)} %copy.48, s32[1024]{0:T(1024)S(1)} %get-tuple-element.55), kind=kCustom, calls=%fused_computation.3 | custom fusion | bytes 790528 | tf_op jit(solution)/shard_map/gather | solution.py:172
  51.5 2.0 %copy.55 = bf16[1024,192]{0,1:T(8,128)(2,1)} copy(bf16[1024,192]{1,0:T(8,128)(2,1)} %gather_fusion.3) | data formatting | bytes 786432 | tf_op jit(solution)/shard_map/gather | solution.py:172
  55.1 3.3 %shard_map.129 = (f32[192,1024]{1,0:T(8,128)}, f32[8,1024]{1,0:T(8,128)}) custom-call(s32[1,1024]{1,0:T(1,128)} %get-tuple-element.49.tgt_ref, bf16[192,1024]{1,0:T(8,128)(2,1)} %bitcast.147, f32[192,1024]{1,0:T(8,128)} %broadcast_in_dim.4.sum_in, f32[8,1024]{1,0:T(8,128)} %broadcast_in_dim.5.cnt_in), custom_call_target="tpu_custom_call", output_to_operand_aliasing={{0}: (2, {}), {1}: (3, {})} | custom-call | flops 419430400 | bytes 2035712 | tf_op jit(solution)/shard_map/pallas_call | solution.py:46
  59.5 3.4 %shard_map.130 = (f32[192,1024]{1,0:T(8,128)}, f32[8,1024]{1,0:T(8,128)}) custom-call(s32[1,1024]{1,0:T(1,128)} %get-tuple-element.52.tgt_ref, bf16[192,1024]{1,0:T(8,128)(2,1)} %collective-permute-done.2.rec_ref, f32[192,1024]{1,0:T(8,128)} %get-tuple-element.14.sum_in, ...), custom_call_target="tpu_custom_call", output_to_operand_aliasing={{0}: (2, {}), {1}: (3, {})} | custom-call | flops 419430400 | bytes 2035712 | tf_op jit(solution)/shard_map/pallas_call | solution.py:46
  62.9 3.3 %shard_map.131 = (f32[192,1024]{1,0:T(8,128)}, f32[8,1024]{1,0:T(8,128)}) custom-call(s32[1,1024]{1,0:T(1,128)} %get-tuple-element.50.tgt_ref, bf16[192,1024]{1,0:T(8,128)(2,1)} %collective-permute-done.1.rec_ref, f32[192,1024]{1,0:T(8,128)} %get-tuple-element.16.sum_in, ...), custom_call_target="tpu_custom_call", output_to_operand_aliasing={{0}: (2, {}), {1}: (3, {})} | custom-call | flops 419430400 | bytes 2035712 | tf_op jit(solution)/shard_map/pallas_call | solution.py:46
  66.1 3.3 %shard_map.132 = (f32[192,1024]{1,0:T(8,128)}, f32[8,1024]{1,0:T(8,128)}) custom-call(s32[1,1024]{1,0:T(1,128)} %get-tuple-element.51.tgt_ref, bf16[192,1024]{1,0:T(8,128)(2,1)} %collective-permute-done.rec_ref, f32[192,1024]{1,0:T(8,128)} %get-tuple-element.18.sum_in, f32[8,1024]{1,0:T(8,128)} %get-tuple-element.19.cnt_in), custom_call_target="tpu_custom_call", output_to_operand_aliasing={{0}: (2, {}), {1}: (3, {})} | custom-call | flops 419430400 | bytes 2035712 | tf_op jit(solution)/shard_map/pallas_call | solution.py:46
  71.5 1.6 collective-permute-start.6
  76.4 1.6 select_bitcast_fusion.1
  79.7 2.4 %collective-permute-done.7 = bf16[384,256]{1,0:T(8,128)(2,1)S(1)} collective-permute-done((bf16[384,256]{1,0:T(8,128)(2,1)S(1)}, bf16[384,256]{1,0:T(8,128)(2,1)S(1)}, u32[]{:S(2)}, u32[]{:S(2)}) %collective-permute-start.7) | collective-permute-done | bytes 196640 | tf_op jit(solution)/shard_map/ppermute | solution.py:186
  85.0 1.6 multiply_convert_fusion.2
  87.6 2.1 %copy-done = f32[1024,1024]{1,0:T(8,128)} copy-done((f32[1024,1024]{1,0:T(8,128)}, f32[1024,1024]{1,0:T(8,128)S(1)}, u32[]{:S(2)}) %copy-start) | copy-done | bytes 4194328
  91.8 2.0 %fusion.47 = f32[256,1024]{1,0:T(8,128)S(1)} fusion(bf16[1024,1024]{1,0:T(8,128)(2,1)S(1)} %bitcast.142, f32[256,1024]{1,0:T(8,128)S(1)} %get-tuple-element.54, bf16[256,1024]{1,0:T(8,128)(2,1)} %param.19), kind=kOutput, calls=%fused_computation.129 | convolution fusion | flops 539492352 | bytes 4718592 | tf_op jit(solution)/shard_map/dot_general | solution.py:199
  96.0 1.6 bitcast_add_fusion
  100.0 1.6 collective-permute-start.15
  101.5 10.0 %collective-permute-done.11 = bf16[256,1024]{1,0:T(8,128)(2,1)} collective-permute-done((bf16[256,1024]{1,0:T(8,128)(2,1)S(1)}, bf16[256,1024]{1,0:T(8,128)(2,1)}, u32[]{:S(2)}, u32[]{:S(2)}) %collective-permute-start.11) | collective-permute-done | bytes 524320 | tf_op jit(solution)/shard_map/ppermute | solution.py:124
  116.2 2.7 %collective-permute-start.16 = (bf16[2,64,1024]{2,1,0:T(8,128)(2,1)S(1)}, bf16[2,64,1024]{2,1,0:T(8,128)(2,1)S(1)}, u32[]{:S(2)}, u32[]{:S(2)}) collective-permute-start(bf16[2,64,1024]{2,1,0:T(8,128)(2,1)S(1)} %fusion.18), channel_id=1, source_target_pairs={{0,8},{1,9},{2,10},{3,11},{4,12},{5,13},{6,14},{7,15},{8,0},{9,1},... | collective-permute-start | bytes 786440 | tf_op jit(solution)/shard_map/ppermute | solution.py:94
  118.8 12.6 %collective-permute-done.16 = bf16[2,64,1024]{2,1,0:T(8,128)(2,1)S(1)} collective-permute-done((bf16[2,64,1024]{2,1,0:T(8,128)(2,1)S(1)}, bf16[2,64,1024]{2,1,0:T(8,128)(2,1)S(1)}, u32[]{:S(2)}, u32[]{:S(2)}) %collective-permute-start.16) | collective-permute-done | bytes 262176 | tf_op jit(solution)/shard_map/ppermute | solution.py:94
  134.1 3.7 %collective-permute-done.17 = bf16[64,1024]{1,0:T(8,128)(2,1)S(1)} collective-permute-done((bf16[64,1024]{1,0:T(8,128)(2,1)S(1)}, bf16[64,1024]{1,0:T(8,128)(2,1)S(1)}, u32[]{:S(2)}, u32[]{:S(2)}) %collective-permute-start.17) | collective-permute-done | bytes 131104 | tf_op jit(solution)/shard_map/ppermute | solution.py:94
  139.7 2.6 %copy.59 = bf16[1024,1024]{1,0:T(8,128)(2,1)} copy(bf16[1024,1024]{0,1:T(8,128)(2,1)S(1)} %bitcast.140) | data formatting | bytes 4194304 | tf_op jit(solution)/shard_map/dot_general | solution.py:213
  142.3 2.6 %fusion.4 = f32[384,4,256]{2,0,1:T(8,128)S(1)} fusion(bf16[4,256,1024]{2,1,0:T(8,128)(2,1)} %bitcast.143, bf16[192,1024]{1,0:T(8,128)(2,1)S(1)} %copy-done.7, bf16[192,1024]{1,0:T(8,128)(2,1)S(1)} %copy-done.9), kind=kOutput, calls=%fused_computation.45 | convolution fusion | flops 806879232 | bytes 4456448 | tf_op jit(solution)/shard_map/dot_general | solution.py:213
  145.0 2.9 %collective-permute-start.13 = (bf16[2,384,256]{2,1,0:T(8,128)(2,1)S(1)}, bf16[2,384,256]{2,1,0:T(8,128)(2,1)S(1)}, u32[]{:S(2)}, u32[]{:S(2)}) collective-permute-start(bf16[2,384,256]{2,1,0:T(8,128)(2,1)S(1)} %fusion.17), channel_id=1, source_target_pairs={{0,4},{4,0},{8,12},{12,8},{1,5},{5,1},{9,13},{13,9},{2,6},{6,2},{1... | collective-permute-start | bytes 1179656 | tf_op jit(solution)/shard_map/ppermute | solution.py:94
  148.1 12.0 %collective-permute-done.13 = bf16[2,384,256]{2,1,0:T(8,128)(2,1)S(1)} collective-permute-done((bf16[2,384,256]{2,1,0:T(8,128)(2,1)S(1)}, bf16[2,384,256]{2,1,0:T(8,128)(2,1)S(1)}, u32[]{:S(2)}, u32[]{:S(2)}) %collective-permute-start.13) | collective-permute-done | bytes 393248 | tf_op jit(solution)/shard_map/ppermute | solution.py:94
  160.2 3.2 %collective-permute-done.19 = bf16[2,64,1024]{2,1,0:T(8,128)(2,1)S(1)} collective-permute-done((bf16[2,64,1024]{2,1,0:T(8,128)(2,1)S(1)}, bf16[2,64,1024]{2,1,0:T(8,128)(2,1)S(1)}, u32[]{:S(2)}, u32[]{:S(2)}) %collective-permute-start.19) | collective-permute-done | bytes 262176 | tf_op jit(solution)/shard_map/ppermute | solution.py:124
  164.7 4.2 %collective-permute-done.14 = bf16[384,256]{1,0:T(8,128)(2,1)S(1)} collective-permute-done((bf16[384,256]{1,0:T(8,128)(2,1)S(1)}, bf16[384,256]{1,0:T(8,128)(2,1)S(1)}, u32[]{:S(2)}, u32[]{:S(2)}) %collective-permute-start.14) | collective-permute-done | bytes 196640 | tf_op jit(solution)/shard_map/ppermute | solution.py:94
  (127 shorter events, 46.7 us)
Async XLA Ops:
  0.6 3.3 %copy-start.21 = (s32[1,4,1024]{2,1,0:T(4,128)S(1)}, s32[1,4,1024]{2,1,0:T(4,128)}, u32[]{:S(2)}) copy-start(s32[1,4,1024]{2,1,0:T(4,128)} %param.11) | copy-start | bytes 49156
  3.9 8.0 %copy-start.15 = (bf16[256,1024]{1,0:T(8,128)(2,1)S(1)}, bf16[256,1024]{1,0:T(8,128)(2,1)}, u32[]{:S(2)}) copy-start(bf16[256,1024]{1,0:T(8,128)(2,1)} %param.16) | copy-start | bytes 1572868
  4.0 9.5 %copy-start.18 = (bf16[192,1024]{1,0:T(8,128)(2,1)S(1)}, bf16[192,1024]{1,0:T(8,128)(2,1)}, u32[]{:S(2)}) copy-start(bf16[192,1024]{1,0:T(8,128)(2,1)} %param.13) | copy-start | bytes 1179652
  8.9 50.5 %collective-permute-start.2 = (bf16[192,1024]{1,0:T(8,128)(2,1)}, bf16[192,1024]{1,0:T(8,128)(2,1)}, u32[]{:S(2)}, u32[]{:S(2)}) collective-permute-start(bf16[192,1024]{1,0:T(8,128)(2,1)} %bitcast.11), channel_id=1, source_target_pairs={{0,4},{4,8},{8,12},{12,0},{1,5},{5,9},{9,13},{13,1},{2,6},{6,10},{... | collective-permute-start | bytes 1179656 | tf_op jit(solution)/shard_map/ppermute | solution.py:174
  11.9 19.8 %collective-permute-start.8 = (bf16[256,1024]{1,0:T(8,128)(2,1)S(1)}, bf16[256,1024]{1,0:T(8,128)(2,1)}, u32[]{:S(2)}, u32[]{:S(2)}) collective-permute-start(bf16[256,1024]{1,0:T(8,128)(2,1)S(1)} %copy-done.15), channel_id=1, source_target_pairs={{0,2},{1,3},{2,0},{3,1},{4,6},{5,7},{6,4},{7,5},{8,10},{9,11},{10,... | collective-permute-start | bytes 1572872 | tf_op jit(solution)/shard_map/ppermute | solution.py:124
  16.0 26.3 %collective-permute-start.3 = (bf16[384,1024]{1,0:T(8,128)(2,1)}, bf16[384,1024]{1,0:T(8,128)(2,1)}, u32[]{:S(2)}, u32[]{:S(2)}) collective-permute-start(bf16[384,1024]{1,0:T(8,128)(2,1)} %constant_dynamic-update-slice_fusion), channel_id=1, source_target_pairs={{0,2},{1,3},{2,0},{3,1},{4,6},{5,7},{6,4},{7,5},{8,10},{9,11},{10,... | collective-permute-start | bytes 2359304 | tf_op jit(solution)/shard_map/ppermute | solution.py:124
  21.4 41.5 %collective-permute-start.1 = (bf16[192,1024]{1,0:T(8,128)(2,1)}, bf16[192,1024]{1,0:T(8,128)(2,1)}, u32[]{:S(2)}, u32[]{:S(2)}) collective-permute-start(bf16[192,1024]{1,0:T(8,128)(2,1)} %bitcast.7), channel_id=1, source_target_pairs={{0,8},{4,12},{8,0},{12,4},{1,9},{5,13},{9,1},{13,5},{2,10},{6,14},... | collective-permute-start | bytes 1179656 | tf_op jit(solution)/shard_map/ppermute | solution.py:174
  24.0 6.2 %copy-start.20 = (s32[256,15]{0,1:T(8,128)S(1)}, s32[256,15]{0,1:T(8,128)}, u32[]{:S(2)}) copy-start(s32[256,15]{0,1:T(8,128)} %param.18) | copy-start | bytes 46084
  28.9 37.3 %collective-permute-start = (bf16[192,1024]{1,0:T(8,128)(2,1)}, bf16[192,1024]{1,0:T(8,128)(2,1)}, u32[]{:S(2)}, u32[]{:S(2)}) collective-permute-start(bf16[192,1024]{1,0:T(8,128)(2,1)} %bitcast.3), channel_id=1, source_target_pairs={{0,12},{4,0},{8,4},{12,8},{1,13},{5,1},{9,5},{13,9},{2,14},{6,2},{... | collective-permute-start | bytes 1179656 | tf_op jit(solution)/shard_map/ppermute | solution.py:174
  34.1 39.5 %collective-permute-start.9 = (bf16[2,256,1024]{2,1,0:T(8,128)(2,1)}, bf16[2,256,1024]{2,1,0:T(8,128)(2,1)}, u32[]{:S(2)}, u32[]{:S(2)}) collective-permute-start(bf16[2,256,1024]{2,1,0:T(8,128)(2,1)} %pad_maximum_fusion.5), channel_id=1, source_target_pairs={{0,1},{1,0},{2,3},{3,2},{4,5},{5,4},{6,7},{7,6},{8,9},{9,8},{10,11... | collective-permute-start | bytes 3145736 | tf_op jit(solution)/shard_map/ppermute | solution.py:124
  45.9 29.4 %collective-permute-start.4 = (bf16[2,384,1024]{2,1,0:T(8,128)(2,1)}, bf16[2,384,1024]{2,1,0:T(8,128)(2,1)}, u32[]{:S(2)}, u32[]{:S(2)}) collective-permute-start(bf16[2,384,1024]{2,1,0:T(8,128)(2,1)} %pad_maximum_fusion.3), channel_id=1, source_target_pairs={{0,1},{1,0},{2,3},{3,2},{4,5},{5,4},{6,7},{7,6},{8,9},{9,8},{10,11... | collective-permute-start | bytes 4718600 | tf_op jit(solution)/shard_map/ppermute | solution.py:124
  59.4 23.1 %copy-start.6 = (bf16[192,1024]{1,0:T(8,128)(2,1)}, bf16[192,1024]{1,0:T(8,128)(2,1)S(1)}, u32[]{:S(2)}) copy-start(bf16[192,1024]{1,0:T(8,128)(2,1)S(1)} %slice_bitcast_fusion) | copy-start | bytes 1179652
  66.1 7.5 %copy-start.5 = (bf16[1,256,1024]{2,1,0:T(8,128)(2,1)S(1)}, bf16[1,256,1024]{2,1,0:T(8,128)(2,1)}, u32[]{:S(2)}) copy-start(bf16[1,256,1024]{2,1,0:T(8,128)(2,1)} %copy-done.4) | copy-start | bytes 1572868
  71.4 11.2 %copy-start.8 = (bf16[192,1024]{1,0:T(8,128)(2,1)}, bf16[192,1024]{1,0:T(8,128)(2,1)S(1)}, u32[]{:S(2)}) copy-start(bf16[192,1024]{1,0:T(8,128)(2,1)S(1)} %divide_convert_fusion) | copy-start | bytes 1179652
  71.5 7.8 %collective-permute-start.6 = (bf16[384,256]{1,0:T(8,128)(2,1)S(1)}, bf16[384,256]{1,0:T(8,128)(2,1)S(1)}, u32[]{:S(2)}, u32[]{:S(2)}) collective-permute-start(bf16[384,256]{1,0:T(8,128)(2,1)S(1)} %get-tuple-element.37), channel_id=1, source_target_pairs={{0,2},{1,3},{2,0},{3,1},{4,6},{5,7},{6,4},{7,5},{8,10},{9,11},{10,... | collective-permute-start | bytes 589832 | tf_op jit(solution)/shard_map/ppermute | solution.py:186
  73.1 9.0 %collective-permute-start.7 = (bf16[384,256]{1,0:T(8,128)(2,1)S(1)}, bf16[384,256]{1,0:T(8,128)(2,1)S(1)}, u32[]{:S(2)}, u32[]{:S(2)}) collective-permute-start(bf16[384,256]{1,0:T(8,128)(2,1)S(1)} %get-tuple-element.38), channel_id=1, source_target_pairs={{0,3},{1,0},{2,1},{3,2},{4,7},{5,4},{6,5},{7,6},{8,11},{9,8},{10,9... | collective-permute-start | bytes 589832 | tf_op jit(solution)/shard_map/ppermute | solution.py:186
  73.4 9.7 %collective-permute-start.5 = (bf16[384,256]{1,0:T(8,128)(2,1)S(1)}, bf16[384,256]{1,0:T(8,128)(2,1)S(1)}, u32[]{:S(2)}, u32[]{:S(2)}) collective-permute-start(bf16[384,256]{1,0:T(8,128)(2,1)S(1)} %get-tuple-element.36), channel_id=1, source_target_pairs={{0,1},{1,2},{2,3},{3,0},{4,5},{5,6},{6,7},{7,4},{8,9},{9,10},{10,1... | collective-permute-start | bytes 589832 | tf_op jit(solution)/shard_map/ppermute | solution.py:186
  75.3 9.7 %copy-start.11 = (bf16[2,2,256,1024]{3,2,1,0:T(8,128)(2,1)}, bf16[2,2,256,1024]{3,2,1,0:T(8,128)(2,1)S(1)}, u32[]{:S(2)}) copy-start(bf16[2,2,256,1024]{3,2,1,0:T(8,128)(2,1)S(1)} %copy.57) | copy-start | bytes 6291460
  78.3 4.3 %copy-start.23 = (f32[1024]{0:T(1024)S(1)}, f32[1024]{0:T(1024)}, u32[]{:S(2)}) copy-start(f32[1024]{0:T(1024)} %param.15) | copy-start | bytes 12292
  87.6 4.2 %copy-start.12 = (bf16[2,2,256,1024]{3,2,1,0:T(8,128)(2,1)S(1)}, bf16[2,2,256,1024]{3,2,1,0:T(8,128)(2,1)}, u32[]{:S(2)}) copy-start(bf16[2,2,256,1024]{3,2,1,0:T(8,128)(2,1)} %copy-done.11) | copy-start | bytes 6291460
  90.9 4.2 %collective-permute-start.10 = (bf16[2,2,2,64,1024]{4,3,2,1,0:T(8,128)(2,1)}, bf16[2,2,2,64,1024]{4,3,2,1,0:T(8,128)(2,1)}, u32[]{:S(2)}, u32[]{:S(2)}) collective-permute-start(bf16[2,2,2,64,1024]{4,3,2,1,0:T(8,128)(2,1)} %fusion.2), channel_id=1, source_target_pairs={{0,1},{1,0},{2,3},{3,2},{4,5},{5,4},{6,7},{7,6},{8,9},{9,8},{10,11... | collective-permute-start | bytes 3145736 | tf_op jit(solution)/shard_map/ppermute | solution.py:94
  97.6 14.0 %collective-permute-start.11 = (bf16[256,1024]{1,0:T(8,128)(2,1)S(1)}, bf16[256,1024]{1,0:T(8,128)(2,1)}, u32[]{:S(2)}, u32[]{:S(2)}) collective-permute-start(bf16[256,1024]{1,0:T(8,128)(2,1)S(1)} %multiply_convert_fusion), channel_id=1, source_target_pairs={{0,2},{1,3},{2,0},{3,1},{4,6},{5,7},{6,4},{7,5},{8,10},{9,11},{10,... | collective-permute-start | bytes 1572872 | tf_op jit(solution)/shard_map/ppermute | solution.py:124
  100.0 13.9 %collective-permute-start.15 = (bf16[2,2,64,1024]{3,2,1,0:T(8,128)(2,1)}, bf16[2,2,64,1024]{3,2,1,0:T(8,128)(2,1)}, u32[]{:S(2)}, u32[]{:S(2)}) collective-permute-start(bf16[2,2,64,1024]{3,2,1,0:T(8,128)(2,1)} %fusion.16), channel_id=1, source_target_pairs={{0,4},{1,5},{2,6},{3,7},{4,0},{5,1},{6,2},{7,3},{8,12},{9,13},{10,... | collective-permute-start | bytes 1572872 | tf_op jit(solution)/shard_map/ppermute | solution.py:94
  113.9 24.0 %collective-permute-start.12 = (bf16[2,256,1024]{2,1,0:T(8,128)(2,1)}, bf16[2,256,1024]{2,1,0:T(8,128)(2,1)}, u32[]{:S(2)}, u32[]{:S(2)}) collective-permute-start(bf16[2,256,1024]{2,1,0:T(8,128)(2,1)} %pad_maximum_fusion.6), channel_id=1, source_target_pairs={{0,1},{1,0},{2,3},{3,2},{4,5},{5,4},{6,7},{7,6},{8,9},{9,8},{10,11... | collective-permute-start | bytes 3145736 | tf_op jit(solution)/shard_map/ppermute | solution.py:124
  116.2 15.3 %collective-permute-start.16 = (bf16[2,64,1024]{2,1,0:T(8,128)(2,1)S(1)}, bf16[2,64,1024]{2,1,0:T(8,128)(2,1)S(1)}, u32[]{:S(2)}, u32[]{:S(2)}) collective-permute-start(bf16[2,64,1024]{2,1,0:T(8,128)(2,1)S(1)} %fusion.18), channel_id=1, source_target_pairs={{0,8},{1,9},{2,10},{3,11},{4,12},{5,13},{6,14},{7,15},{8,0},{9,1},... | collective-permute-start | bytes 786440 | tf_op jit(solution)/shard_map/ppermute | solution.py:94
  132.6 5.2 %collective-permute-start.17 = (bf16[64,1024]{1,0:T(8,128)(2,1)S(1)}, bf16[64,1024]{1,0:T(8,128)(2,1)S(1)}, u32[]{:S(2)}, u32[]{:S(2)}) collective-permute-start(bf16[64,1024]{1,0:T(8,128)(2,1)S(1)} %fusion.27), channel_id=1, source_target_pairs={{0,2},{1,3},{2,0},{3,1},{4,6},{5,7},{6,4},{7,5},{8,10},{9,11},{10,... | collective-permute-start | bytes 393224 | tf_op jit(solution)/shard_map/ppermute | solution.py:94
  137.8 10.1 %collective-permute-start.18 = (bf16[64,1024]{1,0:T(8,128)(2,1)S(1)}, bf16[64,1024]{1,0:T(8,128)(2,1)S(1)}, u32[]{:S(2)}, u32[]{:S(2)}) collective-permute-start(bf16[64,1024]{1,0:T(8,128)(2,1)S(1)} %fusion.19), channel_id=1, source_target_pairs={{0,8},{4,12},{8,0},{12,4},{1,9},{5,13},{9,1},{13,5},{2,10},{6,14},... | collective-permute-start | bytes 393224 | tf_op jit(solution)/shard_map/ppermute | solution.py:124
  139.7 2.6 %copy-start.7 = (bf16[192,1024]{1,0:T(8,128)(2,1)S(1)}, bf16[192,1024]{1,0:T(8,128)(2,1)}, u32[]{:S(2)}) copy-start(bf16[192,1024]{1,0:T(8,128)(2,1)} %copy-done.6) | copy-start | bytes 1179652
  139.7 2.6 %copy-start.9 = (bf16[192,1024]{1,0:T(8,128)(2,1)S(1)}, bf16[192,1024]{1,0:T(8,128)(2,1)}, u32[]{:S(2)}) copy-start(bf16[192,1024]{1,0:T(8,128)(2,1)} %copy-done.8) | copy-start | bytes 1179652
  145.0 15.1 %collective-permute-start.13 = (bf16[2,384,256]{2,1,0:T(8,128)(2,1)S(1)}, bf16[2,384,256]{2,1,0:T(8,128)(2,1)S(1)}, u32[]{:S(2)}, u32[]{:S(2)}) collective-permute-start(bf16[2,384,256]{2,1,0:T(8,128)(2,1)S(1)} %fusion.17), channel_id=1, source_target_pairs={{0,4},{4,0},{8,12},{12,8},{1,5},{5,1},{9,13},{13,9},{2,6},{6,2},{1... | collective-permute-start | bytes 1179656 | tf_op jit(solution)/shard_map/ppermute | solution.py:94
  148.0 15.5 %collective-permute-start.19 = (bf16[2,64,1024]{2,1,0:T(8,128)(2,1)S(1)}, bf16[2,64,1024]{2,1,0:T(8,128)(2,1)S(1)}, u32[]{:S(2)}, u32[]{:S(2)}) collective-permute-start(bf16[2,64,1024]{2,1,0:T(8,128)(2,1)S(1)} %pad_maximum_fusion.7), channel_id=1, source_target_pairs={{0,4},{4,0},{8,12},{12,8},{1,5},{5,1},{9,13},{13,9},{2,6},{6,2},{1... | collective-permute-start | bytes 786440 | tf_op jit(solution)/shard_map/ppermute | solution.py:124
  160.2 8.7 %collective-permute-start.14 = (bf16[384,256]{1,0:T(8,128)(2,1)S(1)}, bf16[384,256]{1,0:T(8,128)(2,1)S(1)}, u32[]{:S(2)}, u32[]{:S(2)}) collective-permute-start(bf16[384,256]{1,0:T(8,128)(2,1)S(1)} %fusion.21), channel_id=1, source_target_pairs={{0,8},{4,12},{8,0},{12,4},{1,9},{5,13},{9,1},{13,5},{2,10},{6,14},... | collective-permute-start | bytes 589832 | tf_op jit(solution)/shard_map/ppermute | solution.py:94
  (13 other events, 19.7 us)

commit v17 on v15

--- a/solution.py
+++ b/solution.py
@@ -130,6 +130,16 @@
 
         cur = jax.tree.map(join, cur, got)
     return jax.tree.map(lambda leaf, orig: leaf.reshape((n,) + orig.shape), cur, x)
+
+
+def gather_block_list(x, axis, n):
+    held = {0: x}
+    for b in reversed(range(n.bit_length() - 1)):
+        keys = sorted(held)
+        came = lax.ppermute(tuple(held[q] for q in keys), axis, _xor_pairs(n, 1 << b))
+        for q, blocks in zip(keys, came):
+            held[q | (1 << b)] = blocks
+    return [held[q] for q in range(n)]
 
 
 def local(
@@ -210,8 +220,17 @@
         jnp.bfloat16,
         slope_one,
     )
-    slab_rows = all_gather_blocks(slope_one, "cols", n_cols).reshape(tgt_dev, hidden)
-    stacked = jnp.dot(both_t, slab_rows, preferred_element_type=jnp.float32)
+    if _is_pow2(n_cols):
+        slope_blocks = gather_block_list((slope_one,), "cols", n_cols)
+        stacked = jnp.zeros((2 * width, hidden), jnp.float32)
+        for j, (block,) in enumerate(slope_blocks):
+            owner_cols = lax.dynamic_slice_in_dim(
+                both_t, (me_col ^ j) * tgt_loc, tgt_loc, axis=1
+            )
+            stacked = stacked + jnp.dot(owner_cols, block, preferred_element_type=jnp.float32)
+    else:
+        slab_rows = all_gather_blocks(slope_one, "cols", n_cols).reshape(tgt_dev, hidden)
+        stacked = jnp.dot(both_t, slab_rows, preferred_element_type=jnp.float32)
     dom_cols = hidden // n_dom
     grad_upper = all_gather_blocks(upper_part.astype(jnp.bfloat16), "dom", n_dom)
     grad_upper = grad_upper.reshape(up_rows, hidden).astype(jnp.float32)

time: 159 us -> 148 us (0.931)
  local copies, waits for them, and re-layouts: 37.8 us -> 31.7 us
  other arithmetic: 17.5 us -> 13.5 us
    ppermute x10 -> x8, waiting for transfers between devices: 17.7 us -> 14.5 us  [all_gather_blocks(): got = lax.ppermute(cur, axis, _xor_pairs(n, 1 << b))]
    another operation x18 -> x14, other arithmetic: 9.83 us -> 6.82 us  [join(): return jnp.stack([low, high], axis=k - 1 - b)]
    ppermute x10 -> x8, starting transfers between devices: 8.17 us -> 5.34 us  [all_gather_blocks(): got = lax.ppermute(cur, axis, _xor_pairs(n, 1 << b))]
    dot_general x1 -> x0, local copies, waits for them, and re-layouts: 2.58 us -> none  [local(): stacked = jnp.dot(both_t, slab_rows, preferred_element_type=jnp.float32)]
    ppermute x6, waiting for transfers between devices: 35.2 us -> 37.5 us  [_butterfly_reduce(): got = lax.ppermute(send.astype(send_dtype), axis, _xor_pairs(n, 1 << b))]
    unnamed x37 -> x31, local copies, waits for them, and re-layouts: 8.02 us -> 6.3 us
  transfers between devices with their start and end apart: 22 -> 23, of which waited for: 9 -> 10; matrix products, arithmetic and copies ran while one was open for 30% -> 27% of each run, Pallas kernels for 8% -> 9%
where the time goes in v17:
time: 148 us; the launch traced here: 147 us
  waiting for transfers between devices  54.3 us (37%)
  local copies, waits for them, and re-layouts  31.7 us (21%)
  starting transfers between devices  21.2 us (14%)
  other arithmetic  13.5 us (9%)
  Pallas kernels  13.1 us (9%)
  matrix products  12.2 us (8%)
    ppermute x6, waiting for transfers between devices, _butterfly_reduce(): got = lax.ppermute(send.astype(send_dtype), axis, _xor_pairs(n, 1 << b))  37.5 us
    gather x8, local copies, waits for them, and re-layouts, local(): rows_t = features.at[slots].get(mode='promise_in_bounds').T  18.8 us
    ppermute x8, waiting for transfers between devices, all_gather_blocks(): got = lax.ppermute(cur, axis, _xor_pairs(n, 1 << b))  14.5 us
    pallas_call x4, Pallas kernels, accumulate(): pl.pallas_call(_accumulate_kernel, out_shape=[jax.ShapeDtypeStruct(acc_su...  13.1 us
    ppermute x3, starting transfers between devices, local(): rows_t = lax.ppermute(rows_t, 'dom', _shift_pairs(n_dom, shift))  7.01 us
    another operation x14, other arithmetic, join(): return jnp.stack([low, high], axis=k - 1 - b)  6.82 us
    unnamed x31, local copies, waits for them, and re-layouts  6.3 us
    ppermute x8, starting transfers between devices, all_gather_blocks(): got = lax.ppermute(cur, axis, _xor_pairs(n, 1 << b))  5.34 us
  transfers between devices with their start and end apart: 23, of which 10 were waited for; matrix products, arithmetic and copies ran while one was open for 27% of the time, Pallas kernels for 9%

profile of v17, /device:TPU:0, one launch (start us, length us, event | category | flops | bytes accessed | tf_op | source)
XLA Modules:
  0.0 147.1 jit_solution(9688848714419285575)
XLA Ops:
  0.7 3.2 %copy.46 = bf16[4096,192]{1,0:T(8,128)(2,1)S(1)} copy(bf16[4096,192]{0,1:T(8,128)(2,1)} %param.10) | data formatting | bytes 3145728 | tf_op args[0]
  3.9 3.9 %gather_fusion.2 = bf16[1024,192]{1,0:T(8,128)(2,1)S(1)} fusion(bf16[4096,192]{1,0:T(8,128)(2,1)S(1)} %copy.46, s32[1024]{0:T(1024)S(1)} %broadcast_clamp_fusion.1), kind=kCustom, calls=%fused_computation.2 | custom fusion | bytes 790528 | tf_op jit(solution)/shard_map/gather | solution.py:183
  8.8 3.0 %collective-permute-start.2 = (bf16[192,1024]{1,0:T(8,128)(2,1)}, bf16[192,1024]{1,0:T(8,128)(2,1)}, u32[]{:S(2)}, u32[]{:S(2)}) collective-permute-start(bf16[192,1024]{1,0:T(8,128)(2,1)} %bitcast.11), channel_id=1, source_target_pairs={{0,4},{4,8},{8,12},{12,0},{1,5},{5,9},{9,13},{13,1},{2,6},{6,10},{... | collective-permute-start | bytes 1179656 | tf_op jit(solution)/shard_map/ppermute | solution.py:185
  11.9 3.9 %gather_fusion.1 = bf16[1024,192]{1,0:T(8,128)(2,1)S(1)} fusion(bf16[4096,192]{1,0:T(8,128)(2,1)S(1)} %copy.46, s32[1024]{0:T(1024)S(1)} %broadcast_clamp_fusion.2), kind=kCustom, calls=%fused_computation.1 | custom fusion | bytes 790528 | tf_op jit(solution)/shard_map/gather | solution.py:183
  16.7 2.6 %collective-permute-start.1 = (bf16[192,1024]{1,0:T(8,128)(2,1)}, bf16[192,1024]{1,0:T(8,128)(2,1)}, u32[]{:S(2)}, u32[]{:S(2)}) collective-permute-start(bf16[192,1024]{1,0:T(8,128)(2,1)} %bitcast.7), channel_id=1, source_target_pairs={{0,8},{4,12},{8,0},{12,4},{1,9},{5,13},{9,1},{13,5},{2,10},{6,14},... | collective-permute-start | bytes 1179656 | tf_op jit(solution)/shard_map/ppermute | solution.py:185
  19.3 3.9 %gather_fusion = bf16[1024,192]{1,0:T(8,128)(2,1)S(1)} fusion(bf16[4096,192]{1,0:T(8,128)(2,1)S(1)} %copy.46, s32[1024]{0:T(1024)S(1)} %broadcast_clamp_fusion.3), kind=kCustom, calls=%fused_computation | custom fusion | bytes 790528 | tf_op jit(solution)/shard_map/gather | solution.py:183
  24.9 1.5 %collective-permute-start.3 = (bf16[192,1024]{1,0:T(8,128)(2,1)}, bf16[192,1024]{1,0:T(8,128)(2,1)}, u32[]{:S(2)}, u32[]{:S(2)}) collective-permute-start(bf16[192,1024]{1,0:T(8,128)(2,1)} %param.13), channel_id=1, source_target_pairs={{0,2},{1,3},{2,0},{3,1},{4,6},{5,7},{6,4},{7,5},{8,10},{9,11},{10,... | collective-permute-start | bytes 1179656 | tf_op jit(solution)/shard_map/ppermute | solution.py:124
  26.9 3.9 %gather_fusion.3 = bf16[1024,192]{1,0:T(8,128)(2,1)S(1)} fusion(bf16[4096,192]{1,0:T(8,128)(2,1)S(1)} %copy.46, s32[1024]{0:T(1024)S(1)} %broadcast_clamp_fusion), kind=kCustom, calls=%fused_computation.3 | custom fusion | bytes 790528 | tf_op jit(solution)/shard_map/gather | solution.py:183
  34.0 3.3 %shard_map.129 = (f32[192,1024]{1,0:T(8,128)}, f32[8,1024]{1,0:T(8,128)}) custom-call(s32[1,1024]{1,0:T(1,128)} %get-tuple-element.49.tgt_ref, bf16[192,1024]{1,0:T(8,128)(2,1)} %bitcast.150, f32[192,1024]{1,0:T(8,128)} %broadcast_in_dim.4.sum_in, f32[8,1024]{1,0:T(8,128)} %broadcast_in_dim.5.cnt_in), custom_call_target="tpu_custom_call", output_to_operand_aliasing={{0}: (2, {}), {1}: (3, {})} | custom-call | flops 419430400 | bytes 2035712 | tf_op jit(solution)/shard_map/pallas_call | solution.py:46
  37.3 1.5 %convert_reduce_fusion = f32[256,256]{1,0:T(8,128)} fusion(s32[256,15]{0,1:T(8,128)S(1)} %copy-done.10), kind=kLoop, calls=%fused_computation.12 | loop fusion | flops 2883584 | bytes 277504 | tf_op jit(solution)/shard_map/reduce_sum | solution.py:16
  39.8 1.6 %collective-permute-start.10 = (bf16[256,1024]{1,0:T(8,128)(2,1)}, bf16[256,1024]{1,0:T(8,128)(2,1)}, u32[]{:S(2)}, u32[]{:S(2)}) collective-permute-start(bf16[256,1024]{1,0:T(8,128)(2,1)} %param.16), channel_id=1, source_target_pairs={{0,2},{1,3},{2,0},{3,1},{4,6},{5,7},{6,4},{7,5},{8,10},{9,11},{10,... | collective-permute-start | bytes 1572872 | tf_op jit(solution)/shard_map/ppermute | solution.py:124
  41.4 4.3 %collective-permute-done.5 = bf16[192,1024]{1,0:T(8,128)(2,1)} collective-permute-done((bf16[192,1024]{1,0:T(8,128)(2,1)S(1)}, bf16[192,1024]{1,0:T(8,128)(2,1)}, u32[]{:S(2)}, u32[]{:S(2)}) %collective-permute-start.5) | collective-permute-done | bytes 393248 | tf_op jit(solution)/shard_map/ppermute | solution.py:124
  48.5 3.3 %shard_map.130 = (f32[192,1024]{1,0:T(8,128)}, f32[8,1024]{1,0:T(8,128)}) custom-call(s32[1,1024]{1,0:T(1,128)} %get-tuple-element.52.tgt_ref, bf16[192,1024]{1,0:T(8,128)(2,1)} %collective-permute-done.2.rec_ref, f32[192,1024]{1,0:T(8,128)} %get-tuple-element.14.sum_in, ...), custom_call_target="tpu_custom_call", output_to_operand_aliasing={{0}: (2, {}), {1}: (3, {})} | custom-call | flops 419430400 | bytes 2035712 | tf_op jit(solution)/shard_map/pallas_call | solution.py:46
  51.8 3.3 %shard_map.131 = (f32[192,1024]{1,0:T(8,128)}, f32[8,1024]{1,0:T(8,128)}) custom-call(s32[1,1024]{1,0:T(1,128)} %get-tuple-element.50.tgt_ref, bf16[192,1024]{1,0:T(8,128)(2,1)} %collective-permute-done.1.rec_ref, f32[192,1024]{1,0:T(8,128)} %get-tuple-element.16.sum_in, ...), custom_call_target="tpu_custom_call", output_to_operand_aliasing={{0}: (2, {}), {1}: (3, {})} | custom-call | flops 419430400 | bytes 2035712 | tf_op jit(solution)/shard_map/pallas_call | solution.py:46
  55.0 3.3 %shard_map.132 = (f32[192,1024]{1,0:T(8,128)}, f32[8,1024]{1,0:T(8,128)}) custom-call(s32[1,1024]{1,0:T(1,128)} %get-tuple-element.51.tgt_ref, bf16[192,1024]{1,0:T(8,128)(2,1)} %collective-permute-done.rec_ref, f32[192,1024]{1,0:T(8,128)} %get-tuple-element.18.sum_in, f32[8,1024]{1,0:T(8,128)} %get-tuple-element.19.cnt_in), custom_call_target="tpu_custom_call", output_to_operand_aliasing={{0}: (2, {}), {1}: (3, {})} | custom-call | flops 419430400 | bytes 2035712 | tf_op jit(solution)/shard_map/pallas_call | solution.py:46
  60.4 1.6 %collective-permute-start.8 = (bf16[384,256]{1,0:T(8,128)(2,1)S(1)}, bf16[384,256]{1,0:T(8,128)(2,1)S(1)}, u32[]{:S(2)}, u32[]{:S(2)}) collective-permute-start(bf16[384,256]{1,0:T(8,128)(2,1)S(1)} %get-tuple-element.33), channel_id=1, source_target_pairs={{0,2},{1,3},{2,0},{3,1},{4,6},{5,7},{6,4},{7,5},{8,10},{9,11},{10,... | collective-permute-start | bytes 589832 | tf_op jit(solution)/shard_map/ppermute | solution.py:197
  68.7 1.8 %collective-permute-done.9 = bf16[384,256]{1,0:T(8,128)(2,1)S(1)} collective-permute-done((bf16[384,256]{1,0:T(8,128)(2,1)S(1)}, bf16[384,256]{1,0:T(8,128)(2,1)S(1)}, u32[]{:S(2)}, u32[]{:S(2)}) %collective-permute-start.9) | collective-permute-done | bytes 196640 | tf_op jit(solution)/shard_map/ppermute | solution.py:197
  74.2 1.7 %multiply_convert_fusion.2 = (bf16[256,1024]{1,0:T(8,128)(2,1)}, f32[256,1024]{1,0:T(8,128)S(1)}) fusion(f32[1024]{0:T(1024)S(1)} %copy-done.14, bf16[256,1024]{1,0:T(8,128)(2,1)S(1)} %convolution_convert_fusion, bf16[1024,1024]{1,0:T(8,128)(2,1)S(1)} %bitcast.146), kind=kOutput, calls=%fused_computation.49 | convolution fusion | flops 538443776 | bytes 4198400 | tf_op jit(solution)/shard_map/dot_general | solution.py:205
  76.8 2.0 %copy-done = f32[1024,1024]{1,0:T(8,128)} copy-done((f32[1024,1024]{1,0:T(8,128)}, f32[1024,1024]{1,0:T(8,128)S(1)}, u32[]{:S(2)}) %copy-start) | copy-done | bytes 4194328
  80.8 2.2 %fusion.69 = f32[256,1024]{1,0:T(8,128)S(1)} fusion(bf16[1024,1024]{1,0:T(8,128)(2,1)S(1)} %bitcast.147, f32[256,1024]{1,0:T(8,128)} %copy-done.2, bf16[256,1024]{1,0:T(8,128)(2,1)S(1)} %copy-done.5), kind=kOutput, calls=%fused_computation.159 | convolution fusion | flops 539492352 | bytes 4718592 | tf_op jit(solution)/shard_map/dot_general | solution.py:210
  83.0 2.1 %multiply_convert_fusion = bf16[256,1024]{1,0:T(8,128)(2,1)} fusion(f32[256,1024]{1,0:T(8,128)S(1)} %copy-done.4, f32[256,1024]{1,0:T(8,128)S(1)} %fusion.69, f32[256,256]{1,0:T(8,128)S(1)} %copy-done.9), kind=kOutput, calls=%fused_computation.47 | convolution fusion | flops 807927808 | bytes 2883584 | tf_op jit(solution)/shard_map/dot_general | solution.py:213
  85.2 1.6 %bitcast_add_fusion = f32[2,2,2,64,1024]{4,3,2,1,0:T(8,128)S(1)} fusion(bf16[2,2,2,64,1024]{4,3,2,1,0:T(8,128)(2,1)} %collective-permute-done.12, f32[2,2,2,2,64,1024]{5,4,3,2,1,0:T(8,128)S(1)} %bitcast.142, s32[]{:T(128)S(6)} %select_n.344), kind=kLoop, calls=%fused_computation.15 | loop fusion | flops 1048576 | bytes 5242884 | tf_op jit(solution)/shard_map/add | solution.py:95
  87.6 1.5 %collective-permute-start.14 = (bf16[256,1024]{1,0:T(8,128)(2,1)}, bf16[256,1024]{1,0:T(8,128)(2,1)S(1)}, u32[]{:S(2)}, u32[]{:S(2)}) collective-permute-start(bf16[256,1024]{1,0:T(8,128)(2,1)} %multiply_convert_fusion), channel_id=1, source_target_pairs={{0,2},{1,3},{2,0},{3,1},{4,6},{5,7},{6,4},{7,5},{8,10},{9,11},{10,... | collective-permute-start | bytes 1572872 | tf_op jit(solution)/shard_map/ppermute | solution.py:139
  89.1 1.4 fusion.31
  90.5 10.3 %collective-permute-done.18 = bf16[2,2,64,1024]{3,2,1,0:T(8,128)(2,1)} collective-permute-done((bf16[2,2,64,1024]{3,2,1,0:T(8,128)(2,1)S(1)}, bf16[2,2,64,1024]{3,2,1,0:T(8,128)(2,1)}, u32[]{:S(2)}, u32[]{:S(2)}) %collective-permute-start.18) | collective-permute-done | bytes 524320 | tf_op jit(solution)/shard_map/ppermute | solution.py:94
  102.7 13.4 %collective-permute-done.19 = bf16[2,64,1024]{2,1,0:T(8,128)(2,1)S(1)} collective-permute-done((bf16[2,64,1024]{2,1,0:T(8,128)(2,1)S(1)}, bf16[2,64,1024]{2,1,0:T(8,128)(2,1)S(1)}, u32[]{:S(2)}, u32[]{:S(2)}) %collective-permute-start.19) | collective-permute-done | bytes 262176 | tf_op jit(solution)/shard_map/ppermute | solution.py:94
  116.2 1.6 %collective-permute-start.20 = (bf16[64,1024]{1,0:T(8,128)(2,1)S(1)}, bf16[64,1024]{1,0:T(8,128)(2,1)S(1)}, u32[]{:S(2)}, u32[]{:S(2)}) collective-permute-start(bf16[64,1024]{1,0:T(8,128)(2,1)S(1)} %fusion.39), channel_id=1, source_target_pairs={{0,2},{1,3},{2,0},{3,1},{4,6},{5,7},{6,4},{7,5},{8,10},{9,11},{10,... | collective-permute-start | bytes 393224 | tf_op jit(solution)/shard_map/ppermute | solution.py:94
  118.1 3.4 %collective-permute-done.20 = bf16[64,1024]{1,0:T(8,128)(2,1)S(1)} collective-permute-done((bf16[64,1024]{1,0:T(8,128)(2,1)S(1)}, bf16[64,1024]{1,0:T(8,128)(2,1)S(1)}, u32[]{:S(2)}, u32[]{:S(2)}) %collective-permute-start.20) | collective-permute-done | bytes 131104 | tf_op jit(solution)/shard_map/ppermute | solution.py:94
  122.9 4.7 %collective-permute-done.21 = bf16[64,1024]{1,0:T(8,128)(2,1)S(1)} collective-permute-done((bf16[64,1024]{1,0:T(8,128)(2,1)S(1)}, bf16[64,1024]{1,0:T(8,128)(2,1)S(1)}, u32[]{:S(2)}, u32[]{:S(2)}) %collective-permute-start.21) | collective-permute-done | bytes 131104 | tf_op jit(solution)/shard_map/ppermute | solution.py:124
  127.7 8.3 %collective-permute-done.16 = bf16[2,384,256]{2,1,0:T(8,128)(2,1)S(1)} collective-permute-done((bf16[2,384,256]{2,1,0:T(8,128)(2,1)S(1)}, bf16[2,384,256]{2,1,0:T(8,128)(2,1)S(1)}, u32[]{:S(2)}, u32[]{:S(2)}) %collective-permute-start.16) | collective-permute-done | bytes 393248 | tf_op jit(solution)/shard_map/ppermute | solution.py:94
  137.4 5.6 %collective-permute-done.22 = bf16[2,64,1024]{2,1,0:T(8,128)(2,1)S(1)} collective-permute-done((bf16[2,64,1024]{2,1,0:T(8,128)(2,1)S(1)}, bf16[2,64,1024]{2,1,0:T(8,128)(2,1)S(1)}, u32[]{:S(2)}, u32[]{:S(2)}) %collective-permute-start.22) | collective-permute-done | bytes 262176 | tf_op jit(solution)/shard_map/ppermute | solution.py:124
  144.2 2.1 %collective-permute-done.17 = bf16[384,256]{1,0:T(8,128)(2,1)S(1)} collective-permute-done((bf16[384,256]{1,0:T(8,128)(2,1)S(1)}, bf16[384,256]{1,0:T(8,128)(2,1)S(1)}, u32[]{:S(2)}, u32[]{:S(2)}) %collective-permute-start.17) | collective-permute-done | bytes 196640 | tf_op jit(solution)/shard_map/ppermute | solution.py:94
  (114 shorter events, 34.3 us)
Async XLA Ops:
  0.7 3.2 %copy-start.11 = (s32[1,4,1024]{2,1,0:T(4,128)S(1)}, s32[1,4,1024]{2,1,0:T(4,128)}, u32[]{:S(2)}) copy-start(s32[1,4,1024]{2,1,0:T(4,128)} %param.11) | copy-start | bytes 49156
  8.8 39.1 %collective-permute-start.2 = (bf16[192,1024]{1,0:T(8,128)(2,1)}, bf16[192,1024]{1,0:T(8,128)(2,1)}, u32[]{:S(2)}, u32[]{:S(2)}) collective-permute-start(bf16[192,1024]{1,0:T(8,128)(2,1)} %bitcast.11), channel_id=1, source_target_pairs={{0,4},{4,8},{8,12},{12,0},{1,5},{5,9},{9,13},{13,1},{2,6},{6,10},{... | collective-permute-start | bytes 1179656 | tf_op jit(solution)/shard_map/ppermute | solution.py:185
  16.7 35.0 %collective-permute-start.1 = (bf16[192,1024]{1,0:T(8,128)(2,1)}, bf16[192,1024]{1,0:T(8,128)(2,1)}, u32[]{:S(2)}, u32[]{:S(2)}) collective-permute-start(bf16[192,1024]{1,0:T(8,128)(2,1)} %bitcast.7), channel_id=1, source_target_pairs={{0,8},{4,12},{8,0},{12,4},{1,9},{5,13},{9,1},{13,5},{2,10},{6,14},... | collective-permute-start | bytes 1179656 | tf_op jit(solution)/shard_map/ppermute | solution.py:185
  19.3 7.0 %copy-start.6 = (bf16[192,1024]{1,0:T(8,128)(2,1)S(1)}, bf16[192,1024]{1,0:T(8,128)(2,1)}, u32[]{:S(2)}) copy-start(bf16[192,1024]{1,0:T(8,128)(2,1)} %param.14) | copy-start | bytes 1179652
  23.5 31.6 %collective-permute-start = (bf16[192,1024]{1,0:T(8,128)(2,1)S(1)}, bf16[192,1024]{1,0:T(8,128)(2,1)}, u32[]{:S(2)}, u32[]{:S(2)}) collective-permute-start(bf16[192,1024]{1,0:T(8,128)(2,1)S(1)} %bitcast.149), channel_id=1, source_target_pairs={{0,12},{4,0},{8,4},{12,8},{1,13},{5,1},{9,5},{13,9},{2,14},{6,2},{... | collective-permute-start | bytes 1179656 | tf_op jit(solution)/shard_map/ppermute | solution.py:185
  24.9 15.0 %collective-permute-start.3 = (bf16[192,1024]{1,0:T(8,128)(2,1)}, bf16[192,1024]{1,0:T(8,128)(2,1)}, u32[]{:S(2)}, u32[]{:S(2)}) collective-permute-start(bf16[192,1024]{1,0:T(8,128)(2,1)} %param.13), channel_id=1, source_target_pairs={{0,2},{1,3},{2,0},{3,1},{4,6},{5,7},{6,4},{7,5},{8,10},{9,11},{10,... | collective-permute-start | bytes 1179656 | tf_op jit(solution)/shard_map/ppermute | solution.py:124
  26.4 19.3 %collective-permute-start.5 = (bf16[192,1024]{1,0:T(8,128)(2,1)S(1)}, bf16[192,1024]{1,0:T(8,128)(2,1)}, u32[]{:S(2)}, u32[]{:S(2)}) collective-permute-start(bf16[192,1024]{1,0:T(8,128)(2,1)S(1)} %copy-done.6), channel_id=1, source_target_pairs={{0,2},{1,3},{2,0},{3,1},{4,6},{5,7},{6,4},{7,5},{8,10},{9,11},{10,... | collective-permute-start | bytes 1179656 | tf_op jit(solution)/shard_map/ppermute | solution.py:124
  26.9 4.9 %copy-start.12 = (s32[1,4,1024]{2,1,0:T(4,128)S(1)}, s32[1,4,1024]{2,1,0:T(4,128)}, u32[]{:S(2)}) copy-start(s32[1,4,1024]{2,1,0:T(4,128)} %param.12) | copy-start | bytes 49156
  30.8 6.4 %copy-start.10 = (s32[256,15]{0,1:T(8,128)S(1)}, s32[256,15]{0,1:T(8,128)}, u32[]{:S(2)}) copy-start(s32[256,15]{0,1:T(8,128)} %param.18) | copy-start | bytes 46084
  32.4 13.3 %copy-start.7 = (bf16[192,1024]{1,0:T(8,128)(2,1)S(1)}, bf16[192,1024]{1,0:T(8,128)(2,1)}, u32[]{:S(2)}) copy-start(bf16[192,1024]{1,0:T(8,128)(2,1)} %param.13) | copy-start | bytes 1179652
  39.8 22.1 %collective-permute-start.10 = (bf16[256,1024]{1,0:T(8,128)(2,1)}, bf16[256,1024]{1,0:T(8,128)(2,1)}, u32[]{:S(2)}, u32[]{:S(2)}) collective-permute-start(bf16[256,1024]{1,0:T(8,128)(2,1)} %param.16), channel_id=1, source_target_pairs={{0,2},{1,3},{2,0},{3,1},{4,6},{5,7},{6,4},{7,5},{8,10},{9,11},{10,... | collective-permute-start | bytes 1572872 | tf_op jit(solution)/shard_map/ppermute | solution.py:124
  47.9 16.0 %collective-permute-start.6 = (bf16[2,192,1024]{2,1,0:T(8,128)(2,1)}, bf16[2,192,1024]{2,1,0:T(8,128)(2,1)}, u32[]{:S(2)}, u32[]{:S(2)}) collective-permute-start(bf16[2,192,1024]{2,1,0:T(8,128)(2,1)} %pad_maximum_fusion.5), channel_id=1, source_target_pairs={{0,1},{1,0},{2,3},{3,2},{4,5},{5,4},{6,7},{7,6},{8,9},{9,8},{10,11... | collective-permute-start | bytes 2359304 | tf_op jit(solution)/shard_map/ppermute | solution.py:124
  47.9 18.2 %collective-permute-start.4 = (bf16[2,192,1024]{2,1,0:T(8,128)(2,1)S(1)}, bf16[2,192,1024]{2,1,0:T(8,128)(2,1)}, u32[]{:S(2)}, u32[]{:S(2)}) collective-permute-start(bf16[2,192,1024]{2,1,0:T(8,128)(2,1)S(1)} %pad_maximum_fusion.4), channel_id=1, source_target_pairs={{0,1},{1,0},{2,3},{3,2},{4,5},{5,4},{6,7},{7,6},{8,9},{9,8},{10,11... | collective-permute-start | bytes 2359304 | tf_op jit(solution)/shard_map/ppermute | solution.py:124
  60.4 7.8 %collective-permute-start.8 = (bf16[384,256]{1,0:T(8,128)(2,1)S(1)}, bf16[384,256]{1,0:T(8,128)(2,1)S(1)}, u32[]{:S(2)}, u32[]{:S(2)}) collective-permute-start(bf16[384,256]{1,0:T(8,128)(2,1)S(1)} %get-tuple-element.33), channel_id=1, source_target_pairs={{0,2},{1,3},{2,0},{3,1},{4,6},{5,7},{6,4},{7,5},{8,10},{9,11},{10,... | collective-permute-start | bytes 589832 | tf_op jit(solution)/shard_map/ppermute | solution.py:197
  61.9 8.6 %collective-permute-start.9 = (bf16[384,256]{1,0:T(8,128)(2,1)S(1)}, bf16[384,256]{1,0:T(8,128)(2,1)S(1)}, u32[]{:S(2)}, u32[]{:S(2)}) collective-permute-start(bf16[384,256]{1,0:T(8,128)(2,1)S(1)} %get-tuple-element.34), channel_id=1, source_target_pairs={{0,3},{1,0},{2,1},{3,2},{4,7},{5,4},{6,5},{7,6},{8,11},{9,8},{10,9... | collective-permute-start | bytes 589832 | tf_op jit(solution)/shard_map/ppermute | solution.py:197
  61.9 9.5 %collective-permute-start.7 = (bf16[384,256]{1,0:T(8,128)(2,1)S(1)}, bf16[384,256]{1,0:T(8,128)(2,1)S(1)}, u32[]{:S(2)}, u32[]{:S(2)}) collective-permute-start(bf16[384,256]{1,0:T(8,128)(2,1)S(1)} %get-tuple-element.32), channel_id=1, source_target_pairs={{0,1},{1,2},{2,3},{3,0},{4,5},{5,6},{6,7},{7,4},{8,9},{9,10},{10,1... | collective-permute-start | bytes 589832 | tf_op jit(solution)/shard_map/ppermute | solution.py:197
  63.8 9.5 %collective-permute-start.11 = (bf16[2,256,1024]{2,1,0:T(8,128)(2,1)S(1)}, bf16[2,256,1024]{2,1,0:T(8,128)(2,1)S(1)}, u32[]{:S(2)}, u32[]{:S(2)}) collective-permute-start(bf16[2,256,1024]{2,1,0:T(8,128)(2,1)S(1)} %pad_maximum_fusion.3), channel_id=1, source_target_pairs={{0,1},{1,0},{2,3},{3,2},{4,5},{5,4},{6,7},{7,6},{8,9},{9,8},{10,11... | collective-permute-start | bytes 3145736 | tf_op jit(solution)/shard_map/ppermute | solution.py:124
  68.7 2.3 %copy-start.13 = (f32[1024]{0:T(1024)S(1)}, f32[1024]{0:T(1024)}, u32[]{:S(2)}) copy-start(f32[1024]{0:T(1024)} %param.15) | copy-start | bytes 12292
  79.9 5.2 %collective-permute-start.12 = (bf16[2,2,2,64,1024]{4,3,2,1,0:T(8,128)(2,1)}, bf16[2,2,2,64,1024]{4,3,2,1,0:T(8,128)(2,1)}, u32[]{:S(2)}, u32[]{:S(2)}) collective-permute-start(bf16[2,2,2,64,1024]{4,3,2,1,0:T(8,128)(2,1)} %fusion.2), channel_id=1, source_target_pairs={{0,1},{1,0},{2,3},{3,2},{4,5},{5,4},{6,7},{7,6},{8,9},{9,8},{10,11... | collective-permute-start | bytes 3145736 | tf_op jit(solution)/shard_map/ppermute | solution.py:94
  80.8 2.2 %copy-start.4 = (f32[256,1024]{1,0:T(8,128)S(1)}, f32[256,1024]{1,0:T(8,128)}, u32[]{:S(2)}) copy-start(f32[256,1024]{1,0:T(8,128)} %copy-done.3) | copy-start | bytes 3145732
  80.8 2.2 %copy-start.9 = (f32[256,256]{1,0:T(8,128)S(1)}, f32[256,256]{1,0:T(8,128)}, u32[]{:S(2)}) copy-start(f32[256,256]{1,0:T(8,128)} %convert_reduce_fusion) | copy-start | bytes 786436
  83.0 2.2 %copy-start.1 = (f32[1024,1024]{1,0:T(8,128)S(1)}, f32[1024,1024]{1,0:T(8,128)}, u32[]{:S(2)}) copy-start(f32[1024,1024]{1,0:T(8,128)} %copy-done) | copy-start | bytes 12582916
  86.8 14.0 %collective-permute-start.18 = (bf16[2,2,64,1024]{3,2,1,0:T(8,128)(2,1)S(1)}, bf16[2,2,64,1024]{3,2,1,0:T(8,128)(2,1)}, u32[]{:S(2)}, u32[]{:S(2)}) collective-permute-start(bf16[2,2,64,1024]{3,2,1,0:T(8,128)(2,1)S(1)} %fusion.17), channel_id=1, source_target_pairs={{0,4},{1,5},{2,6},{3,7},{4,0},{5,1},{6,2},{7,3},{8,12},{9,13},{10,... | collective-permute-start | bytes 1572872 | tf_op jit(solution)/shard_map/ppermute | solution.py:94
  87.6 30.2 %collective-permute-start.13 = (bf16[256,1024]{1,0:T(8,128)(2,1)}, bf16[256,1024]{1,0:T(8,128)(2,1)S(1)}, u32[]{:S(2)}, u32[]{:S(2)}) collective-permute-start(bf16[256,1024]{1,0:T(8,128)(2,1)} %multiply_convert_fusion), channel_id=1, source_target_pairs={{0,1},{1,0},{2,3},{3,2},{4,5},{5,4},{6,7},{7,6},{8,9},{9,8},{10,11... | collective-permute-start | bytes 1572872 | tf_op jit(solution)/shard_map/ppermute | solution.py:139
  87.6 14.7 %collective-permute-start.14 = (bf16[256,1024]{1,0:T(8,128)(2,1)}, bf16[256,1024]{1,0:T(8,128)(2,1)S(1)}, u32[]{:S(2)}, u32[]{:S(2)}) collective-permute-start(bf16[256,1024]{1,0:T(8,128)(2,1)} %multiply_convert_fusion), channel_id=1, source_target_pairs={{0,2},{1,3},{2,0},{3,1},{4,6},{5,7},{6,4},{7,5},{8,10},{9,11},{10,... | collective-permute-start | bytes 1572872 | tf_op jit(solution)/shard_map/ppermute | solution.py:139
  102.1 13.9 %collective-permute-start.19 = (bf16[2,64,1024]{2,1,0:T(8,128)(2,1)S(1)}, bf16[2,64,1024]{2,1,0:T(8,128)(2,1)S(1)}, u32[]{:S(2)}, u32[]{:S(2)}) collective-permute-start(bf16[2,64,1024]{2,1,0:T(8,128)(2,1)S(1)} %fusion.19), channel_id=1, source_target_pairs={{0,8},{1,9},{2,10},{3,11},{4,12},{5,13},{6,14},{7,15},{8,0},{9,1},... | collective-permute-start | bytes 786440 | tf_op jit(solution)/shard_map/ppermute | solution.py:94
  102.3 19.3 %collective-permute-start.15 = (bf16[256,1024]{1,0:T(8,128)(2,1)S(1)}, bf16[256,1024]{1,0:T(8,128)(2,1)S(1)}, u32[]{:S(2)}, u32[]{:S(2)}) collective-permute-start(bf16[256,1024]{1,0:T(8,128)(2,1)S(1)} %collective-permute-done.14), channel_id=1, source_target_pairs={{0,1},{1,0},{2,3},{3,2},{4,5},{5,4},{6,7},{7,6},{8,9},{9,8},{10,11... | collective-permute-start | bytes 1572872 | tf_op jit(solution)/shard_map/ppermute | solution.py:139
  116.2 5.4 %collective-permute-start.20 = (bf16[64,1024]{1,0:T(8,128)(2,1)S(1)}, bf16[64,1024]{1,0:T(8,128)(2,1)S(1)}, u32[]{:S(2)}, u32[]{:S(2)}) collective-permute-start(bf16[64,1024]{1,0:T(8,128)(2,1)S(1)} %fusion.39), channel_id=1, source_target_pairs={{0,2},{1,3},{2,0},{3,1},{4,6},{5,7},{6,4},{7,5},{8,10},{9,11},{10,... | collective-permute-start | bytes 393224 | tf_op jit(solution)/shard_map/ppermute | solution.py:94
  121.6 6.0 %collective-permute-start.21 = (bf16[64,1024]{1,0:T(8,128)(2,1)S(1)}, bf16[64,1024]{1,0:T(8,128)(2,1)S(1)}, u32[]{:S(2)}, u32[]{:S(2)}) collective-permute-start(bf16[64,1024]{1,0:T(8,128)(2,1)S(1)} %fusion.20), channel_id=1, source_target_pairs={{0,8},{4,12},{8,0},{12,4},{1,9},{5,13},{9,1},{13,5},{2,10},{6,14},... | collective-permute-start | bytes 393224 | tf_op jit(solution)/shard_map/ppermute | solution.py:124
  122.2 13.9 %collective-permute-start.16 = (bf16[2,384,256]{2,1,0:T(8,128)(2,1)S(1)}, bf16[2,384,256]{2,1,0:T(8,128)(2,1)S(1)}, u32[]{:S(2)}, u32[]{:S(2)}) collective-permute-start(bf16[2,384,256]{2,1,0:T(8,128)(2,1)S(1)} %fusion.18), channel_id=1, source_target_pairs={{0,4},{4,0},{8,12},{12,8},{1,5},{5,1},{9,13},{13,9},{2,6},{6,2},{1... | collective-permute-start | bytes 1179656 | tf_op jit(solution)/shard_map/ppermute | solution.py:94
  127.7 15.4 %collective-permute-start.22 = (bf16[2,64,1024]{2,1,0:T(8,128)(2,1)S(1)}, bf16[2,64,1024]{2,1,0:T(8,128)(2,1)S(1)}, u32[]{:S(2)}, u32[]{:S(2)}) collective-permute-start(bf16[2,64,1024]{2,1,0:T(8,128)(2,1)S(1)} %pad_maximum_fusion.6), channel_id=1, source_target_pairs={{0,4},{4,0},{8,12},{12,8},{1,5},{5,1},{9,13},{13,9},{2,6},{6,2},{1... | collective-permute-start | bytes 786440 | tf_op jit(solution)/shard_map/ppermute | solution.py:124
  136.2 10.1 %collective-permute-start.17 = (bf16[384,256]{1,0:T(8,128)(2,1)S(1)}, bf16[384,256]{1,0:T(8,128)(2,1)S(1)}, u32[]{:S(2)}, u32[]{:S(2)}) collective-permute-start(bf16[384,256]{1,0:T(8,128)(2,1)S(1)} %fusion.22), channel_id=1, source_target_pairs={{0,8},{4,12},{8,0},{12,4},{1,9},{5,13},{9,1},{13,5},{2,10},{6,14},... | collective-permute-start | bytes 589832 | tf_op jit(solution)/shard_map/ppermute | solution.py:94
  (6 other events, 7.2 us)

commit v18 on v17

--- a/solution.py
+++ b/solution.py
@@ -232,7 +232,15 @@
         slab_rows = all_gather_blocks(slope_one, "cols", n_cols).reshape(tgt_dev, hidden)
         stacked = jnp.dot(both_t, slab_rows, preferred_element_type=jnp.float32)
     dom_cols = hidden // n_dom
-    grad_upper = all_gather_blocks(upper_part.astype(jnp.bfloat16), "dom", n_dom)
+    if _is_pow2(n_dom):
+        upper_blocks = gather_block_list((upper_part.astype(jnp.bfloat16),), "dom", n_dom)
+        grad_upper = jnp.zeros((n_dom, dom_rows, hidden), jnp.float32)
+        for j, (block,) in enumerate(upper_blocks):
+            grad_upper = lax.dynamic_update_index_in_dim(
+                grad_upper, block.astype(jnp.float32), me_dom ^ j, 0
+            )
+    else:
+        grad_upper = all_gather_blocks(upper_part.astype(jnp.bfloat16), "dom", n_dom)
     grad_upper = grad_upper.reshape(up_rows, hidden).astype(jnp.float32)
     grad_layer = reduce_scatter_blocks(
         jnp.swapaxes(stacked.reshape(2 * width, n_dom, dom_cols), 0, 1),

time: 148 us -> 150 us (1.014)
  starting transfers between devices: 21.2 us -> 23.3 us
    ppermute x8 -> x6, waiting for transfers between devices: 14.5 us -> 4.3 us  [all_gather_blocks(): got = lax.ppermute(cur, axis, _xor_pairs(n, 1 << b))]
    ppermute x3 -> x6, waiting for transfers between devices: 0.01 us -> 6.31 us  [gather_block_list(): lax.ppermute(tuple((held[q] for q in keys)), axis, _xor_pairs(n, 1 << b))]
    ppermute x6, waiting for transfers between devices: 37.5 us -> 42.2 us  [_butterfly_reduce(): got = lax.ppermute(send.astype(send_dtype), axis, _xor_pairs(n, 1 << b))]
    ppermute x3 -> x6, starting transfers between devices: 1.52 us -> 3.86 us  [gather_block_list(): lax.ppermute(tuple((held[q] for q in keys)), axis, _xor_pairs(n, 1 << b))]
    ppermute x8 -> x6, starting transfers between devices: 5.34 us -> 5.2 us  [all_gather_blocks(): got = lax.ppermute(cur, axis, _xor_pairs(n, 1 << b))]
    another operation x14 -> x11, other arithmetic: 6.82 us -> 6.74 us  [join(): return jnp.stack([low, high], axis=k - 1 - b)]
    unnamed x31 -> x33, local copies, waits for them, and re-layouts: 6.3 us -> 6.3 us
  transfers between devices with their start and end apart: 23 -> 24, of which waited for: 10 -> 10; matrix products, arithmetic and copies ran while one was open for 27% -> 26% of each run, Pallas kernels for 9% -> 9%
where the time goes in v18:
time: 150 us; the launch traced here: 149 us
  waiting for transfers between devices  55 us (37%)
  local copies, waits for them, and re-layouts  30.7 us (20%)
  starting transfers between devices  23.3 us (16%)
  other arithmetic  13.4 us (9%)
  Pallas kernels  13.1 us (9%)
  matrix products  12.2 us (8%)
    ppermute x6, waiting for transfers between devices, _butterfly_reduce(): got = lax.ppermute(send.astype(send_dtype), axis, _xor_pairs(n, 1 << b))  42.2 us
    gather x8, local copies, waits for them, and re-layouts, local(): rows_t = features.at[slots].get(mode='promise_in_bounds').T  18.8 us
    pallas_call x4, Pallas kernels, accumulate(): pl.pallas_call(_accumulate_kernel, out_shape=[jax.ShapeDtypeStruct(acc_su...  13.1 us
    ppermute x3, starting transfers between devices, local(): rows_t = lax.ppermute(rows_t, 'dom', _shift_pairs(n_dom, shift))  7.01 us
    another operation x11, other arithmetic, join(): return jnp.stack([low, high], axis=k - 1 - b)  6.74 us
    ppermute x6, waiting for transfers between devices, gather_block_list(): lax.ppermute(tuple((held[q] for q in keys)), axis, _xor_pairs(n, 1 << b))  6.31 us
    unnamed x33, local copies, waits for them, and re-layouts  6.3 us
    ppermute x6, starting transfers between devices, all_gather_blocks(): got = lax.ppermute(cur, axis, _xor_pairs(n, 1 << b))  5.2 us
  transfers between devices with their start and end apart: 24, of which 10 were waited for; matrix products, arithmetic and copies ran while one was open for 26% of the time, Pallas kernels for 9%

profile of v18, /device:TPU:0, one launch (start us, length us, event | category | flops | bytes accessed | tf_op | source)
XLA Modules:
  0.0 148.9 jit_solution(9646292508873248489)
XLA Ops:
  0.7 3.2 %copy.44 = bf16[4096,192]{1,0:T(8,128)(2,1)S(1)} copy(bf16[4096,192]{0,1:T(8,128)(2,1)} %param.10) | data formatting | bytes 3145728 | tf_op args[0]
  3.9 3.9 %gather_fusion.2 = bf16[1024,192]{1,0:T(8,128)(2,1)S(1)} fusion(bf16[4096,192]{1,0:T(8,128)(2,1)S(1)} %copy.44, s32[1024]{0:T(1024)S(1)} %broadcast_clamp_fusion.1), kind=kCustom, calls=%fused_computation.2 | custom fusion | bytes 790528 | tf_op jit(solution)/shard_map/gather | solution.py:183
  8.8 3.0 %collective-permute-start.2 = (bf16[192,1024]{1,0:T(8,128)(2,1)}, bf16[192,1024]{1,0:T(8,128)(2,1)}, u32[]{:S(2)}, u32[]{:S(2)}) collective-permute-start(bf16[192,1024]{1,0:T(8,128)(2,1)} %bitcast.11), channel_id=1, source_target_pairs={{0,4},{4,8},{8,12},{12,0},{1,5},{5,9},{9,13},{13,1},{2,6},{6,10},{... | collective-permute-start | bytes 1179656 | tf_op jit(solution)/shard_map/ppermute | solution.py:185
  11.9 3.9 %gather_fusion.1 = bf16[1024,192]{1,0:T(8,128)(2,1)S(1)} fusion(bf16[4096,192]{1,0:T(8,128)(2,1)S(1)} %copy.44, s32[1024]{0:T(1024)S(1)} %broadcast_clamp_fusion.2), kind=kCustom, calls=%fused_computation.1 | custom fusion | bytes 790528 | tf_op jit(solution)/shard_map/gather | solution.py:183
  16.7 2.6 %collective-permute-start.1 = (bf16[192,1024]{1,0:T(8,128)(2,1)}, bf16[192,1024]{1,0:T(8,128)(2,1)}, u32[]{:S(2)}, u32[]{:S(2)}) collective-permute-start(bf16[192,1024]{1,0:T(8,128)(2,1)} %bitcast.7), channel_id=1, source_target_pairs={{0,8},{4,12},{8,0},{12,4},{1,9},{5,13},{9,1},{13,5},{2,10},{6,14},... | collective-permute-start | bytes 1179656 | tf_op jit(solution)/shard_map/ppermute | solution.py:185
  19.3 3.9 %gather_fusion = bf16[1024,192]{1,0:T(8,128)(2,1)S(1)} fusion(bf16[4096,192]{1,0:T(8,128)(2,1)S(1)} %copy.44, s32[1024]{0:T(1024)S(1)} %broadcast_clamp_fusion.3), kind=kCustom, calls=%fused_computation | custom fusion | bytes 790528 | tf_op jit(solution)/shard_map/gather | solution.py:183
  24.9 1.5 %collective-permute-start.3 = (bf16[192,1024]{1,0:T(8,128)(2,1)}, bf16[192,1024]{1,0:T(8,128)(2,1)}, u32[]{:S(2)}, u32[]{:S(2)}) collective-permute-start(bf16[192,1024]{1,0:T(8,128)(2,1)} %param.13), channel_id=1, source_target_pairs={{0,2},{1,3},{2,0},{3,1},{4,6},{5,7},{6,4},{7,5},{8,10},{9,11},{10,... | collective-permute-start | bytes 1179656 | tf_op jit(solution)/shard_map/ppermute | solution.py:124
  26.9 3.9 %gather_fusion.3 = bf16[1024,192]{1,0:T(8,128)(2,1)S(1)} fusion(bf16[4096,192]{1,0:T(8,128)(2,1)S(1)} %copy.44, s32[1024]{0:T(1024)S(1)} %broadcast_clamp_fusion), kind=kCustom, calls=%fused_computation.3 | custom fusion | bytes 790528 | tf_op jit(solution)/shard_map/gather | solution.py:183
  34.0 3.3 %shard_map.129 = (f32[192,1024]{1,0:T(8,128)}, f32[8,1024]{1,0:T(8,128)}) custom-call(s32[1,1024]{1,0:T(1,128)} %get-tuple-element.47.tgt_ref, bf16[192,1024]{1,0:T(8,128)(2,1)} %bitcast.155, f32[192,1024]{1,0:T(8,128)} %broadcast_in_dim.42.sum_in, f32[8,1024]{1,0:T(8,128)} %broadcast_in_dim.43.cnt_in), custom_call_target="tpu_custom_call", output_to_operand_aliasing={{0}: (2, {}), {1}: (3, {})} | custom-call | flops 419430400 | bytes 2035712 | tf_op jit(solution)/shard_map/pallas_call | solution.py:46
  37.3 1.5 %convert_reduce_fusion = f32[256,256]{1,0:T(8,128)} fusion(s32[256,15]{0,1:T(8,128)S(1)} %copy-done.11), kind=kLoop, calls=%fused_computation.12 | loop fusion | flops 2883584 | bytes 277504 | tf_op jit(solution)/shard_map/reduce_sum | solution.py:16
  39.8 1.6 %collective-permute-start.10 = (bf16[256,1024]{1,0:T(8,128)(2,1)}, bf16[256,1024]{1,0:T(8,128)(2,1)}, u32[]{:S(2)}, u32[]{:S(2)}) collective-permute-start(bf16[256,1024]{1,0:T(8,128)(2,1)} %param.16), channel_id=1, source_target_pairs={{0,2},{1,3},{2,0},{3,1},{4,6},{5,7},{6,4},{7,5},{8,10},{9,11},{10,... | collective-permute-start | bytes 1572872 | tf_op jit(solution)/shard_map/ppermute | solution.py:124
  41.4 4.3 %collective-permute-done.5 = bf16[192,1024]{1,0:T(8,128)(2,1)} collective-permute-done((bf16[192,1024]{1,0:T(8,128)(2,1)S(1)}, bf16[192,1024]{1,0:T(8,128)(2,1)}, u32[]{:S(2)}, u32[]{:S(2)}) %collective-permute-start.5) | collective-permute-done | bytes 393248 | tf_op jit(solution)/shard_map/ppermute | solution.py:124
  48.5 3.3 %shard_map.130 = (f32[192,1024]{1,0:T(8,128)}, f32[8,1024]{1,0:T(8,128)}) custom-call(s32[1,1024]{1,0:T(1,128)} %get-tuple-element.50.tgt_ref, bf16[192,1024]{1,0:T(8,128)(2,1)} %collective-permute-done.2.rec_ref, f32[192,1024]{1,0:T(8,128)} %get-tuple-element.14.sum_in, ...), custom_call_target="tpu_custom_call", output_to_operand_aliasing={{0}: (2, {}), {1}: (3, {})} | custom-call | flops 419430400 | bytes 2035712 | tf_op jit(solution)/shard_map/pallas_call | solution.py:46
  51.8 3.3 %shard_map.131 = (f32[192,1024]{1,0:T(8,128)}, f32[8,1024]{1,0:T(8,128)}) custom-call(s32[1,1024]{1,0:T(1,128)} %get-tuple-element.48.tgt_ref, bf16[192,1024]{1,0:T(8,128)(2,1)} %collective-permute-done.1.rec_ref, f32[192,1024]{1,0:T(8,128)} %get-tuple-element.16.sum_in, ...), custom_call_target="tpu_custom_call", output_to_operand_aliasing={{0}: (2, {}), {1}: (3, {})} | custom-call | flops 419430400 | bytes 2035712 | tf_op jit(solution)/shard_map/pallas_call | solution.py:46
  55.1 3.3 %shard_map.132 = (f32[192,1024]{1,0:T(8,128)}, f32[8,1024]{1,0:T(8,128)}) custom-call(s32[1,1024]{1,0:T(1,128)} %get-tuple-element.49.tgt_ref, bf16[192,1024]{1,0:T(8,128)(2,1)} %collective-permute-done.rec_ref, f32[192,1024]{1,0:T(8,128)} %get-tuple-element.18.sum_in, f32[8,1024]{1,0:T(8,128)} %get-tuple-element.19.cnt_in), custom_call_target="tpu_custom_call", output_to_operand_aliasing={{0}: (2, {}), {1}: (3, {})} | custom-call | flops 419430400 | bytes 2035712 | tf_op jit(solution)/shard_map/pallas_call | solution.py:46
  60.4 1.6 %collective-permute-start.8 = (bf16[384,256]{1,0:T(8,128)(2,1)S(1)}, bf16[384,256]{1,0:T(8,128)(2,1)S(1)}, u32[]{:S(2)}, u32[]{:S(2)}) collective-permute-start(bf16[384,256]{1,0:T(8,128)(2,1)S(1)} %get-tuple-element.35), channel_id=1, source_target_pairs={{0,2},{1,3},{2,0},{3,1},{4,6},{5,7},{6,4},{7,5},{8,10},{9,11},{10,... | collective-permute-start | bytes 589832 | tf_op jit(solution)/shard_map/ppermute | solution.py:197
  68.7 1.8 %collective-permute-done.9 = bf16[384,256]{1,0:T(8,128)(2,1)S(1)} collective-permute-done((bf16[384,256]{1,0:T(8,128)(2,1)S(1)}, bf16[384,256]{1,0:T(8,128)(2,1)S(1)}, u32[]{:S(2)}, u32[]{:S(2)}) %collective-permute-start.9) | collective-permute-done | bytes 196640 | tf_op jit(solution)/shard_map/ppermute | solution.py:197
  74.2 1.7 %multiply_convert_fusion.2 = (bf16[256,1024]{1,0:T(8,128)(2,1)}, f32[256,1024]{1,0:T(8,128)S(1)}) fusion(f32[1024]{0:T(1024)S(1)} %copy-done.15, bf16[256,1024]{1,0:T(8,128)(2,1)S(1)} %convolution_convert_fusion, bf16[1024,1024]{1,0:T(8,128)(2,1)S(1)} %bitcast.151), kind=kOutput, calls=%fused_computation.49 | convolution fusion | flops 538443776 | bytes 4198400 | tf_op jit(solution)/shard_map/dot_general | solution.py:205
  76.9 2.0 %copy-done = f32[1024,1024]{1,0:T(8,128)} copy-done((f32[1024,1024]{1,0:T(8,128)}, f32[1024,1024]{1,0:T(8,128)S(1)}, u32[]{:S(2)}) %copy-start) | copy-done | bytes 4194328
  80.8 2.2 %fusion.69 = f32[256,1024]{1,0:T(8,128)S(1)} fusion(bf16[1024,1024]{1,0:T(8,128)(2,1)S(1)} %bitcast.152, f32[256,1024]{1,0:T(8,128)} %copy-done.2, bf16[256,1024]{1,0:T(8,128)(2,1)S(1)} %copy-done.6), kind=kOutput, calls=%fused_computation.157 | convolution fusion | flops 539492352 | bytes 4718592 | tf_op jit(solution)/shard_map/dot_general | solution.py:210
  83.0 2.1 %multiply_convert_fusion = bf16[256,1024]{1,0:T(8,128)(2,1)} fusion(f32[256,1024]{1,0:T(8,128)S(1)} %copy-done.5, f32[256,1024]{1,0:T(8,128)S(1)} %fusion.69, f32[256,256]{1,0:T(8,128)S(1)} %copy-done.10), kind=kOutput, calls=%fused_computation.47 | convolution fusion | flops 807927808 | bytes 2883584 | tf_op jit(solution)/shard_map/dot_general | solution.py:213
  85.2 1.6 %bitcast_add_fusion = f32[2,2,2,64,1024]{4,3,2,1,0:T(8,128)S(1)} fusion(bf16[2,2,2,64,1024]{4,3,2,1,0:T(8,128)(2,1)} %collective-permute-done.12, f32[2,2,2,2,64,1024]{5,4,3,2,1,0:T(8,128)S(1)} %bitcast.147, s32[]{:T(128)S(6)} %select_n.333), kind=kLoop, calls=%fused_computation.15 | loop fusion | flops 1048576 | bytes 5242884 | tf_op jit(solution)/shard_map/add | solution.py:95
  87.6 1.5 %collective-permute-start.14 = (bf16[256,1024]{1,0:T(8,128)(2,1)}, bf16[256,1024]{1,0:T(8,128)(2,1)S(1)}, u32[]{:S(2)}, u32[]{:S(2)}) collective-permute-start(bf16[256,1024]{1,0:T(8,128)(2,1)} %multiply_convert_fusion), channel_id=1, source_target_pairs={{0,2},{1,3},{2,0},{3,1},{4,6},{5,7},{6,4},{7,5},{8,10},{9,11},{10,... | collective-permute-start | bytes 1572872 | tf_op jit(solution)/shard_map/ppermute | solution.py:139
  89.1 1.4 fusion.31
  90.5 10.3 %collective-permute-done.18 = bf16[2,2,64,1024]{3,2,1,0:T(8,128)(2,1)} collective-permute-done((bf16[2,2,64,1024]{3,2,1,0:T(8,128)(2,1)S(1)}, bf16[2,2,64,1024]{3,2,1,0:T(8,128)(2,1)}, u32[]{:S(2)}, u32[]{:S(2)}) %collective-permute-start.18) | collective-permute-done | bytes 524320 | tf_op jit(solution)/shard_map/ppermute | solution.py:94
  102.7 13.4 %collective-permute-done.19 = bf16[2,64,1024]{2,1,0:T(8,128)(2,1)S(1)} collective-permute-done((bf16[2,64,1024]{2,1,0:T(8,128)(2,1)S(1)}, bf16[2,64,1024]{2,1,0:T(8,128)(2,1)S(1)}, u32[]{:S(2)}, u32[]{:S(2)}) %collective-permute-start.19) | collective-permute-done | bytes 262176 | tf_op jit(solution)/shard_map/ppermute | solution.py:94
  116.2 1.6 %collective-permute-start.20 = (bf16[64,1024]{1,0:T(8,128)(2,1)S(1)}, bf16[64,1024]{1,0:T(8,128)(2,1)S(1)}, u32[]{:S(2)}, u32[]{:S(2)}) collective-permute-start(bf16[64,1024]{1,0:T(8,128)(2,1)S(1)} %fusion.39), channel_id=1, source_target_pairs={{0,2},{1,3},{2,0},{3,1},{4,6},{5,7},{6,4},{7,5},{8,10},{9,11},{10,... | collective-permute-start | bytes 393224 | tf_op jit(solution)/shard_map/ppermute | solution.py:94
  118.1 3.4 %collective-permute-done.20 = bf16[64,1024]{1,0:T(8,128)(2,1)S(1)} collective-permute-done((bf16[64,1024]{1,0:T(8,128)(2,1)S(1)}, bf16[64,1024]{1,0:T(8,128)(2,1)S(1)}, u32[]{:S(2)}, u32[]{:S(2)}) %collective-permute-start.20) | collective-permute-done | bytes 131104 | tf_op jit(solution)/shard_map/ppermute | solution.py:94
  124.4 5.1 %collective-permute-done.22 = bf16[64,1024]{1,0:T(8,128)(2,1)S(1)} collective-permute-done((bf16[64,1024]{1,0:T(8,128)(2,1)S(1)}, bf16[64,1024]{1,0:T(8,128)(2,1)S(1)}, u32[]{:S(2)}, u32[]{:S(2)}) %collective-permute-start.22) | collective-permute-done | bytes 131104 | tf_op jit(solution)/shard_map/ppermute | solution.py:139
  129.5 1.6 %collective-permute-start.23 = (bf16[64,1024]{1,0:T(8,128)(2,1)S(1)}, bf16[64,1024]{1,0:T(8,128)(2,1)S(1)}, u32[]{:S(2)}, u32[]{:S(2)}) collective-permute-start(bf16[64,1024]{1,0:T(8,128)(2,1)S(1)} %collective-permute-done.22), channel_id=1, source_target_pairs={{0,4},{4,0},{8,12},{12,8},{1,5},{5,1},{9,13},{13,9},{2,6},{6,2},{1... | collective-permute-start | bytes 393224 | tf_op jit(solution)/shard_map/ppermute | solution.py:139
  131.2 7.4 %collective-permute-done.16 = bf16[2,384,256]{2,1,0:T(8,128)(2,1)S(1)} collective-permute-done((bf16[2,384,256]{2,1,0:T(8,128)(2,1)S(1)}, bf16[2,384,256]{2,1,0:T(8,128)(2,1)S(1)}, u32[]{:S(2)}, u32[]{:S(2)}) %collective-permute-start.16) | collective-permute-done | bytes 393248 | tf_op jit(solution)/shard_map/ppermute | solution.py:94
  140.4 7.7 %collective-permute-done.17 = bf16[384,256]{1,0:T(8,128)(2,1)S(1)} collective-permute-done((bf16[384,256]{1,0:T(8,128)(2,1)S(1)}, bf16[384,256]{1,0:T(8,128)(2,1)S(1)}, u32[]{:S(2)}, u32[]{:S(2)}) %collective-permute-start.17) | collective-permute-done | bytes 196640 | tf_op jit(solution)/shard_map/ppermute | solution.py:94
  (117 shorter events, 35.0 us)
Async XLA Ops:
  0.7 3.2 %copy-start.12 = (s32[1,4,1024]{2,1,0:T(4,128)S(1)}, s32[1,4,1024]{2,1,0:T(4,128)}, u32[]{:S(2)}) copy-start(s32[1,4,1024]{2,1,0:T(4,128)} %param.11) | copy-start | bytes 49156
  8.8 39.1 %collective-permute-start.2 = (bf16[192,1024]{1,0:T(8,128)(2,1)}, bf16[192,1024]{1,0:T(8,128)(2,1)}, u32[]{:S(2)}, u32[]{:S(2)}) collective-permute-start(bf16[192,1024]{1,0:T(8,128)(2,1)} %bitcast.11), channel_id=1, source_target_pairs={{0,4},{4,8},{8,12},{12,0},{1,5},{5,9},{9,13},{13,1},{2,6},{6,10},{... | collective-permute-start | bytes 1179656 | tf_op jit(solution)/shard_map/ppermute | solution.py:185
  16.7 35.1 %collective-permute-start.1 = (bf16[192,1024]{1,0:T(8,128)(2,1)}, bf16[192,1024]{1,0:T(8,128)(2,1)}, u32[]{:S(2)}, u32[]{:S(2)}) collective-permute-start(bf16[192,1024]{1,0:T(8,128)(2,1)} %bitcast.7), channel_id=1, source_target_pairs={{0,8},{4,12},{8,0},{12,4},{1,9},{5,13},{9,1},{13,5},{2,10},{6,14},... | collective-permute-start | bytes 1179656 | tf_op jit(solution)/shard_map/ppermute | solution.py:185
  19.3 7.0 %copy-start.7 = (bf16[192,1024]{1,0:T(8,128)(2,1)S(1)}, bf16[192,1024]{1,0:T(8,128)(2,1)}, u32[]{:S(2)}) copy-start(bf16[192,1024]{1,0:T(8,128)(2,1)} %param.14) | copy-start | bytes 1179652
  23.5 31.6 %collective-permute-start = (bf16[192,1024]{1,0:T(8,128)(2,1)S(1)}, bf16[192,1024]{1,0:T(8,128)(2,1)}, u32[]{:S(2)}, u32[]{:S(2)}) collective-permute-start(bf16[192,1024]{1,0:T(8,128)(2,1)S(1)} %bitcast.154), channel_id=1, source_target_pairs={{0,12},{4,0},{8,4},{12,8},{1,13},{5,1},{9,5},{13,9},{2,14},{6,2},{... | collective-permute-start | bytes 1179656 | tf_op jit(solution)/shard_map/ppermute | solution.py:185
  24.9 14.9 %collective-permute-start.3 = (bf16[192,1024]{1,0:T(8,128)(2,1)}, bf16[192,1024]{1,0:T(8,128)(2,1)}, u32[]{:S(2)}, u32[]{:S(2)}) collective-permute-start(bf16[192,1024]{1,0:T(8,128)(2,1)} %param.13), channel_id=1, source_target_pairs={{0,2},{1,3},{2,0},{3,1},{4,6},{5,7},{6,4},{7,5},{8,10},{9,11},{10,... | collective-permute-start | bytes 1179656 | tf_op jit(solution)/shard_map/ppermute | solution.py:124
  26.4 19.3 %collective-permute-start.5 = (bf16[192,1024]{1,0:T(8,128)(2,1)S(1)}, bf16[192,1024]{1,0:T(8,128)(2,1)}, u32[]{:S(2)}, u32[]{:S(2)}) collective-permute-start(bf16[192,1024]{1,0:T(8,128)(2,1)S(1)} %copy-done.7), channel_id=1, source_target_pairs={{0,2},{1,3},{2,0},{3,1},{4,6},{5,7},{6,4},{7,5},{8,10},{9,11},{10,... | collective-permute-start | bytes 1179656 | tf_op jit(solution)/shard_map/ppermute | solution.py:124
  26.9 4.9 %copy-start.13 = (s32[1,4,1024]{2,1,0:T(4,128)S(1)}, s32[1,4,1024]{2,1,0:T(4,128)}, u32[]{:S(2)}) copy-start(s32[1,4,1024]{2,1,0:T(4,128)} %param.12) | copy-start | bytes 49156
  30.9 6.4 %copy-start.11 = (s32[256,15]{0,1:T(8,128)S(1)}, s32[256,15]{0,1:T(8,128)}, u32[]{:S(2)}) copy-start(s32[256,15]{0,1:T(8,128)} %param.18) | copy-start | bytes 46084
  32.4 13.3 %copy-start.8 = (bf16[192,1024]{1,0:T(8,128)(2,1)S(1)}, bf16[192,1024]{1,0:T(8,128)(2,1)}, u32[]{:S(2)}) copy-start(bf16[192,1024]{1,0:T(8,128)(2,1)} %param.13) | copy-start | bytes 1179652
  39.8 22.1 %collective-permute-start.10 = (bf16[256,1024]{1,0:T(8,128)(2,1)}, bf16[256,1024]{1,0:T(8,128)(2,1)}, u32[]{:S(2)}, u32[]{:S(2)}) collective-permute-start(bf16[256,1024]{1,0:T(8,128)(2,1)} %param.16), channel_id=1, source_target_pairs={{0,2},{1,3},{2,0},{3,1},{4,6},{5,7},{6,4},{7,5},{8,10},{9,11},{10,... | collective-permute-start | bytes 1572872 | tf_op jit(solution)/shard_map/ppermute | solution.py:124
  47.9 16.0 %collective-permute-start.6 = (bf16[2,192,1024]{2,1,0:T(8,128)(2,1)}, bf16[2,192,1024]{2,1,0:T(8,128)(2,1)}, u32[]{:S(2)}, u32[]{:S(2)}) collective-permute-start(bf16[2,192,1024]{2,1,0:T(8,128)(2,1)} %pad_maximum_fusion.5), channel_id=1, source_target_pairs={{0,1},{1,0},{2,3},{3,2},{4,5},{5,4},{6,7},{7,6},{8,9},{9,8},{10,11... | collective-permute-start | bytes 2359304 | tf_op jit(solution)/shard_map/ppermute | solution.py:124
  48.0 18.2 %collective-permute-start.4 = (bf16[2,192,1024]{2,1,0:T(8,128)(2,1)S(1)}, bf16[2,192,1024]{2,1,0:T(8,128)(2,1)}, u32[]{:S(2)}, u32[]{:S(2)}) collective-permute-start(bf16[2,192,1024]{2,1,0:T(8,128)(2,1)S(1)} %pad_maximum_fusion.4), channel_id=1, source_target_pairs={{0,1},{1,0},{2,3},{3,2},{4,5},{5,4},{6,7},{7,6},{8,9},{9,8},{10,11... | collective-permute-start | bytes 2359304 | tf_op jit(solution)/shard_map/ppermute | solution.py:124
  60.4 7.8 %collective-permute-start.8 = (bf16[384,256]{1,0:T(8,128)(2,1)S(1)}, bf16[384,256]{1,0:T(8,128)(2,1)S(1)}, u32[]{:S(2)}, u32[]{:S(2)}) collective-permute-start(bf16[384,256]{1,0:T(8,128)(2,1)S(1)} %get-tuple-element.35), channel_id=1, source_target_pairs={{0,2},{1,3},{2,0},{3,1},{4,6},{5,7},{6,4},{7,5},{8,10},{9,11},{10,... | collective-permute-start | bytes 589832 | tf_op jit(solution)/shard_map/ppermute | solution.py:197
  62.0 8.6 %collective-permute-start.9 = (bf16[384,256]{1,0:T(8,128)(2,1)S(1)}, bf16[384,256]{1,0:T(8,128)(2,1)S(1)}, u32[]{:S(2)}, u32[]{:S(2)}) collective-permute-start(bf16[384,256]{1,0:T(8,128)(2,1)S(1)} %get-tuple-element.36), channel_id=1, source_target_pairs={{0,3},{1,0},{2,1},{3,2},{4,7},{5,4},{6,5},{7,6},{8,11},{9,8},{10,9... | collective-permute-start | bytes 589832 | tf_op jit(solution)/shard_map/ppermute | solution.py:197
  62.0 9.5 %collective-permute-start.7 = (bf16[384,256]{1,0:T(8,128)(2,1)S(1)}, bf16[384,256]{1,0:T(8,128)(2,1)S(1)}, u32[]{:S(2)}, u32[]{:S(2)}) collective-permute-start(bf16[384,256]{1,0:T(8,128)(2,1)S(1)} %get-tuple-element.34), channel_id=1, source_target_pairs={{0,1},{1,2},{2,3},{3,0},{4,5},{5,6},{6,7},{7,4},{8,9},{9,10},{10,1... | collective-permute-start | bytes 589832 | tf_op jit(solution)/shard_map/ppermute | solution.py:197
  63.9 9.5 %collective-permute-start.11 = (bf16[2,256,1024]{2,1,0:T(8,128)(2,1)S(1)}, bf16[2,256,1024]{2,1,0:T(8,128)(2,1)S(1)}, u32[]{:S(2)}, u32[]{:S(2)}) collective-permute-start(bf16[2,256,1024]{2,1,0:T(8,128)(2,1)S(1)} %pad_maximum_fusion.3), channel_id=1, source_target_pairs={{0,1},{1,0},{2,3},{3,2},{4,5},{5,4},{6,7},{7,6},{8,9},{9,8},{10,11... | collective-permute-start | bytes 3145736 | tf_op jit(solution)/shard_map/ppermute | solution.py:124
  68.7 2.3 %copy-start.14 = (f32[1024]{0:T(1024)S(1)}, f32[1024]{0:T(1024)}, u32[]{:S(2)}) copy-start(f32[1024]{0:T(1024)} %param.15) | copy-start | bytes 12292
  80.0 5.2 %collective-permute-start.12 = (bf16[2,2,2,64,1024]{4,3,2,1,0:T(8,128)(2,1)}, bf16[2,2,2,64,1024]{4,3,2,1,0:T(8,128)(2,1)}, u32[]{:S(2)}, u32[]{:S(2)}) collective-permute-start(bf16[2,2,2,64,1024]{4,3,2,1,0:T(8,128)(2,1)} %fusion.2), channel_id=1, source_target_pairs={{0,1},{1,0},{2,3},{3,2},{4,5},{5,4},{6,7},{7,6},{8,9},{9,8},{10,11... | collective-permute-start | bytes 3145736 | tf_op jit(solution)/shard_map/ppermute | solution.py:94
  80.8 2.2 %copy-start.10 = (f32[256,256]{1,0:T(8,128)S(1)}, f32[256,256]{1,0:T(8,128)}, u32[]{:S(2)}) copy-start(f32[256,256]{1,0:T(8,128)} %convert_reduce_fusion) | copy-start | bytes 786436
  86.8 14.0 %collective-permute-start.18 = (bf16[2,2,64,1024]{3,2,1,0:T(8,128)(2,1)S(1)}, bf16[2,2,64,1024]{3,2,1,0:T(8,128)(2,1)}, u32[]{:S(2)}, u32[]{:S(2)}) collective-permute-start(bf16[2,2,64,1024]{3,2,1,0:T(8,128)(2,1)S(1)} %fusion.17), channel_id=1, source_target_pairs={{0,4},{1,5},{2,6},{3,7},{4,0},{5,1},{6,2},{7,3},{8,12},{9,13},{10,... | collective-permute-start | bytes 1572872 | tf_op jit(solution)/shard_map/ppermute | solution.py:94
  87.6 30.1 %collective-permute-start.13 = (bf16[256,1024]{1,0:T(8,128)(2,1)}, bf16[256,1024]{1,0:T(8,128)(2,1)S(1)}, u32[]{:S(2)}, u32[]{:S(2)}) collective-permute-start(bf16[256,1024]{1,0:T(8,128)(2,1)} %multiply_convert_fusion), channel_id=1, source_target_pairs={{0,1},{1,0},{2,3},{3,2},{4,5},{5,4},{6,7},{7,6},{8,9},{9,8},{10,11... | collective-permute-start | bytes 1572872 | tf_op jit(solution)/shard_map/ppermute | solution.py:139
  87.6 14.7 %collective-permute-start.14 = (bf16[256,1024]{1,0:T(8,128)(2,1)}, bf16[256,1024]{1,0:T(8,128)(2,1)S(1)}, u32[]{:S(2)}, u32[]{:S(2)}) collective-permute-start(bf16[256,1024]{1,0:T(8,128)(2,1)} %multiply_convert_fusion), channel_id=1, source_target_pairs={{0,2},{1,3},{2,0},{3,1},{4,6},{5,7},{6,4},{7,5},{8,10},{9,11},{10,... | collective-permute-start | bytes 1572872 | tf_op jit(solution)/shard_map/ppermute | solution.py:139
  102.1 13.9 %collective-permute-start.19 = (bf16[2,64,1024]{2,1,0:T(8,128)(2,1)S(1)}, bf16[2,64,1024]{2,1,0:T(8,128)(2,1)S(1)}, u32[]{:S(2)}, u32[]{:S(2)}) collective-permute-start(bf16[2,64,1024]{2,1,0:T(8,128)(2,1)S(1)} %fusion.19), channel_id=1, source_target_pairs={{0,8},{1,9},{2,10},{3,11},{4,12},{5,13},{6,14},{7,15},{8,0},{9,1},... | collective-permute-start | bytes 786440 | tf_op jit(solution)/shard_map/ppermute | solution.py:94
  102.3 20.1 %collective-permute-start.15 = (bf16[256,1024]{1,0:T(8,128)(2,1)S(1)}, bf16[256,1024]{1,0:T(8,128)(2,1)S(1)}, u32[]{:S(2)}, u32[]{:S(2)}) collective-permute-start(bf16[256,1024]{1,0:T(8,128)(2,1)S(1)} %collective-permute-done.14), channel_id=1, source_target_pairs={{0,1},{1,0},{2,3},{3,2},{4,5},{5,4},{6,7},{7,6},{8,9},{9,8},{10,11... | collective-permute-start | bytes 1572872 | tf_op jit(solution)/shard_map/ppermute | solution.py:139
  116.2 5.4 %collective-permute-start.20 = (bf16[64,1024]{1,0:T(8,128)(2,1)S(1)}, bf16[64,1024]{1,0:T(8,128)(2,1)S(1)}, u32[]{:S(2)}, u32[]{:S(2)}) collective-permute-start(bf16[64,1024]{1,0:T(8,128)(2,1)S(1)} %fusion.39), channel_id=1, source_target_pairs={{0,2},{1,3},{2,0},{3,1},{4,6},{5,7},{6,4},{7,5},{8,10},{9,11},{10,... | collective-permute-start | bytes 393224 | tf_op jit(solution)/shard_map/ppermute | solution.py:94
  121.7 9.4 %collective-permute-start.21 = (bf16[64,1024]{1,0:T(8,128)(2,1)S(1)}, bf16[64,1024]{1,0:T(8,128)(2,1)S(1)}, u32[]{:S(2)}, u32[]{:S(2)}) collective-permute-start(bf16[64,1024]{1,0:T(8,128)(2,1)S(1)} %get-tuple-element.25), channel_id=1, source_target_pairs={{0,4},{4,0},{8,12},{12,8},{1,5},{5,1},{9,13},{13,9},{2,6},{6,2},{1... | collective-permute-start | bytes 393224 | tf_op jit(solution)/shard_map/ppermute | solution.py:139
  121.8 7.7 %collective-permute-start.22 = (bf16[64,1024]{1,0:T(8,128)(2,1)S(1)}, bf16[64,1024]{1,0:T(8,128)(2,1)S(1)}, u32[]{:S(2)}, u32[]{:S(2)}) collective-permute-start(bf16[64,1024]{1,0:T(8,128)(2,1)S(1)} %get-tuple-element.25), channel_id=1, source_target_pairs={{0,8},{4,12},{8,0},{12,4},{1,9},{5,13},{9,1},{13,5},{2,10},{6,14},... | collective-permute-start | bytes 393224 | tf_op jit(solution)/shard_map/ppermute | solution.py:139
  123.0 15.6 %collective-permute-start.16 = (bf16[2,384,256]{2,1,0:T(8,128)(2,1)S(1)}, bf16[2,384,256]{2,1,0:T(8,128)(2,1)S(1)}, u32[]{:S(2)}, u32[]{:S(2)}) collective-permute-start(bf16[2,384,256]{2,1,0:T(8,128)(2,1)S(1)} %fusion.18), channel_id=1, source_target_pairs={{0,4},{4,0},{8,12},{12,8},{1,5},{5,1},{9,13},{13,9},{2,6},{6,2},{1... | collective-permute-start | bytes 1179656 | tf_op jit(solution)/shard_map/ppermute | solution.py:94
  129.5 10.9 %collective-permute-start.23 = (bf16[64,1024]{1,0:T(8,128)(2,1)S(1)}, bf16[64,1024]{1,0:T(8,128)(2,1)S(1)}, u32[]{:S(2)}, u32[]{:S(2)}) collective-permute-start(bf16[64,1024]{1,0:T(8,128)(2,1)S(1)} %collective-permute-done.22), channel_id=1, source_target_pairs={{0,4},{4,0},{8,12},{12,8},{1,5},{5,1},{9,13},{13,9},{2,6},{6,2},{1... | collective-permute-start | bytes 393224 | tf_op jit(solution)/shard_map/ppermute | solution.py:139
  138.7 9.4 %collective-permute-start.17 = (bf16[384,256]{1,0:T(8,128)(2,1)S(1)}, bf16[384,256]{1,0:T(8,128)(2,1)S(1)}, u32[]{:S(2)}, u32[]{:S(2)}) collective-permute-start(bf16[384,256]{1,0:T(8,128)(2,1)S(1)} %fusion.22), channel_id=1, source_target_pairs={{0,8},{4,12},{8,0},{12,4},{1,9},{5,13},{9,1},{13,5},{2,10},{6,14},... | collective-permute-start | bytes 589832 | tf_op jit(solution)/shard_map/ppermute | solution.py:94
  140.4 8.6 %copy-start.3 = (f32[4,64,1024]{2,1,0:T(8,128)}, f32[4,64,1024]{2,1,0:T(8,128)S(1)}, u32[]{:S(2)}) copy-start(f32[4,64,1024]{2,1,0:T(8,128)S(1)} %convert_dynamic-update-slice_fusion) | copy-start | bytes 3145732
  (8 other events, 11.6 us)

commit v19 on v17

--- a/solution.py
+++ b/solution.py
@@ -164,15 +164,28 @@
     w_rows = neigh_weight.shape[0]
     up_rows = upper_weight.shape[0]
 
-    neigh_full, self_full, full_upper = all_gather_blocks(
-        (neigh_weight, self_weight, upper_weight), "cols", n_cols
-    )
+    me_col = lax.axis_index("cols")
+    if _is_pow2(n_cols):
+        layer_weights = gather_block_list((neigh_weight, self_weight), "cols", n_cols)
+        full_upper = all_gather_blocks(upper_weight, "cols", n_cols)
+        partners = [(me_col ^ j, _xor_pairs(n_cols, j)) for j in range(n_cols)]
+    else:
+        neigh_full, self_full, full_upper = all_gather_blocks(
+            (neigh_weight, self_weight, upper_weight), "cols", n_cols
+        )
+        partners = [((me_col + j) % n_cols, _shift_pairs(n_cols, j)) for j in range(n_cols)]
+        layer_weights = [
+            tuple(
+                lax.dynamic_index_in_dim(full, (me_col - j) % n_cols, 0, keepdims=False)
+                for full in (neigh_full, self_full)
+            )
+            for j in range(n_cols)
+        ]
     full_upper = full_upper.reshape(n_cols * up_rows, hidden)
 
     me_dom = lax.axis_index("dom")
     me_col = lax.axis_index("cols")
     own_t = features[:tgt_dev].T
-    both_full = jnp.concatenate([neigh_full, self_full], axis=1)
 
     summed_t = jnp.zeros((width, tgt_dev), jnp.float32)
     counts = jnp.zeros((8, tgt_dev), jnp.float32)
@@ -189,14 +202,13 @@
     both_t = jnp.concatenate([mean_t, own_t], axis=0)
 
     pre_one = bias_one
-    for shift in range(n_cols):
-        dest = (me_col + shift) % n_cols
-        src = (me_col - shift) % n_cols
+    for j, (dest, pairs) in enumerate(partners):
         chunk = lax.dynamic_slice_in_dim(both_t, dest * tgt_loc, tgt_loc, axis=1)
-        if shift:
-            chunk = lax.ppermute(chunk, "cols", _shift_pairs(n_cols, shift))
-        weight = lax.dynamic_index_in_dim(both_full, src, 0, keepdims=False)
-        pre_one = pre_one + contract_rows(chunk, weight)
+        if j:
+            chunk = lax.ppermute(chunk, "cols", pairs)
+        neigh_j, self_j = layer_weights[j]
+        pre_one = pre_one + contract_rows(chunk[:width], neigh_j)
+        pre_one = pre_one + contract_rows(chunk[width:], self_j)
     hidden_one = jax.nn.silu(pre_one).astype(jnp.bfloat16)
     mix_matrix = mixing(upper_neighbours, tgt_loc)
     upper_input = jnp.dot(

time: 148 us -> 157 us (1.061)
  starting transfers between devices: 21.2 us -> 33.1 us
  other arithmetic: 13.5 us -> 7.31 us
  matrix products: 12.2 us -> 14.4 us
    ppermute x6, starting transfers between devices: 5.26 us -> 17 us  [_butterfly_reduce(): got = lax.ppermute(send.astype(send_dtype), axis, _xor_pairs(n, 1 << b))]
    another operation x14 -> x7, other arithmetic: 6.82 us -> 0.6 us  [join(): return jnp.stack([low, high], axis=k - 1 - b)]
    ppermute x3 -> x9, starting transfers between devices: 1.52 us -> 6.53 us  [gather_block_list(): lax.ppermute(tuple((held[q] for q in keys)), axis, _xor_pairs(n, 1 << b))]
    ppermute x3, waiting for transfers between devices: 2.21 us -> 6.8 us  [local(): chunk = lax.ppermute(chunk, 'cols', pairs)]
    dot_general x5 -> x9, matrix products: 2.83 us -> 6.68 us  [contract_rows(): lax.dot_general(left_mat, right_mat, (((0,), (0,)), ((), ())), preferred_...]
    ppermute x6, waiting for transfers between devices: 37.5 us -> 33.9 us  [_butterfly_reduce(): got = lax.ppermute(send.astype(send_dtype), axis, _xor_pairs(n, 1 << b))]
    ppermute x8 -> x4, starting transfers between devices: 5.34 us -> 3.1 us  [all_gather_blocks(): got = lax.ppermute(cur, axis, _xor_pairs(n, 1 << b))]
    unnamed x31 -> x35, local copies, waits for them, and re-layouts: 6.3 us -> 6.89 us
  transfers between devices with their start and end apart: 23 -> 25, of which waited for: 10 -> 10; matrix products, arithmetic and copies ran while one was open for 27% -> 28% of each run, Pallas kernels for 9% -> 8%
where the time goes in v19:
time: 157 us
  waiting for transfers between devices  55.8 us (36%)
  starting transfers between devices  33.1 us (21%)
  local copies, waits for them, and re-layouts  31.7 us (20%)
  matrix products  14.4 us (9%)
  Pallas kernels  13.1 us (8%)
  other arithmetic  7.31 us (5%)
    ppermute x6, waiting for transfers between devices, _butterfly_reduce(): got = lax.ppermute(send.astype(send_dtype), axis, _xor_pairs(n, 1 << b))  33.9 us
    gather x8, local copies, waits for them, and re-layouts, local(): rows_t = features.at[slots].get(mode='promise_in_bounds').T  18.2 us
    ppermute x6, starting transfers between devices, _butterfly_reduce(): got = lax.ppermute(send.astype(send_dtype), axis, _xor_pairs(n, 1 << b))  17 us
    ppermute x4, waiting for transfers between devices, all_gather_blocks(): got = lax.ppermute(cur, axis, _xor_pairs(n, 1 << b))  15.1 us
    pallas_call x4, Pallas kernels, accumulate(): pl.pallas_call(_accumulate_kernel, out_shape=[jax.ShapeDtypeStruct(acc_su...  13.1 us
    unnamed x35, local copies, waits for them, and re-layouts  6.89 us
    ppermute x3, waiting for transfers between devices, local(): chunk = lax.ppermute(chunk, 'cols', pairs)  6.8 us
    dot_general x9, matrix products, contract_rows(): lax.dot_general(left_mat, right_mat, (((0,), (0,)), ((), ())), preferred_...  6.68 us
  transfers between devices with their start and end apart: 25, of which 10 were waited for; matrix products, arithmetic and copies ran while one was open for 28% of the time, Pallas kernels for 8%

profile of v19, /device:TPU:0, one launch (start us, length us, event | category | flops | bytes accessed | tf_op | source)
XLA Modules:
  0.0 156.6 jit_solution(7535355361156458664)
XLA Ops:
  0.6 3.0 %collective-permute-start.8 = (bf16[192,1024]{1,0:T(8,128)(2,1)}, bf16[192,1024]{1,0:T(8,128)(2,1)}, u32[]{:S(2)}, u32[]{:S(2)}) collective-permute-start(bf16[192,1024]{1,0:T(8,128)(2,1)} %param.14), channel_id=1, source_target_pairs={{0,2},{1,3},{2,0},{3,1},{4,6},{5,7},{6,4},{7,5},{8,10},{9,11},{10,... | collective-permute-start | bytes 1179656 | tf_op jit(solution)/shard_map/ppermute | solution.py:139
  3.6 3.1 %copy.44 = bf16[4096,192]{1,0:T(8,128)(2,1)S(1)} copy(bf16[4096,192]{0,1:T(8,128)(2,1)} %param.10) | data formatting | bytes 3145728 | tf_op args[0]
  6.9 3.9 %gather_fusion.2 = bf16[1024,192]{1,0:T(8,128)(2,1)S(1)} fusion(bf16[4096,192]{1,0:T(8,128)(2,1)S(1)} %copy.44, s32[1024]{0:T(1024)S(1)} %broadcast_clamp_fusion.1), kind=kCustom, calls=%fused_computation.2 | custom fusion | bytes 790528 | tf_op jit(solution)/shard_map/gather | solution.py:196
  11.8 1.6 %collective-permute-start.2 = (bf16[192,1024]{1,0:T(8,128)(2,1)}, bf16[192,1024]{1,0:T(8,128)(2,1)}, u32[]{:S(2)}, u32[]{:S(2)}) collective-permute-start(bf16[192,1024]{1,0:T(8,128)(2,1)} %bitcast.11), channel_id=1, source_target_pairs={{0,4},{4,8},{8,12},{12,0},{1,5},{5,9},{9,13},{13,1},{2,6},{6,10},{... | collective-permute-start | bytes 1179656 | tf_op jit(solution)/shard_map/ppermute | solution.py:198
  13.4 3.9 %gather_fusion.1 = bf16[1024,192]{1,0:T(8,128)(2,1)S(1)} fusion(bf16[4096,192]{1,0:T(8,128)(2,1)S(1)} %copy.44, s32[1024]{0:T(1024)S(1)} %broadcast_clamp_fusion.2), kind=kCustom, calls=%fused_computation.1 | custom fusion | bytes 790528 | tf_op jit(solution)/shard_map/gather | solution.py:196
  17.5 2.7 %collective-permute-start.1 = (bf16[192,1024]{1,0:T(8,128)(2,1)S(1)}, bf16[192,1024]{1,0:T(8,128)(2,1)}, u32[]{:S(2)}, u32[]{:S(2)}) collective-permute-start(bf16[192,1024]{1,0:T(8,128)(2,1)S(1)} %bitcast.119), channel_id=1, source_target_pairs={{0,8},{4,12},{8,0},{12,4},{1,9},{5,13},{9,1},{13,5},{2,10},{6,14},... | collective-permute-start | bytes 1179656 | tf_op jit(solution)/shard_map/ppermute | solution.py:198
  20.2 3.9 %gather_fusion = bf16[1024,192]{1,0:T(8,128)(2,1)S(1)} fusion(bf16[4096,192]{1,0:T(8,128)(2,1)S(1)} %copy.44, s32[1024]{0:T(1024)S(1)} %broadcast_clamp_fusion.3), kind=kCustom, calls=%fused_computation | custom fusion | bytes 790528 | tf_op jit(solution)/shard_map/gather | solution.py:196
  27.8 4.1 %gather_fusion.3 = bf16[1024,192]{1,0:T(8,128)(2,1)S(1)} fusion(bf16[4096,192]{1,0:T(8,128)(2,1)S(1)} %copy.44, s32[1024]{0:T(1024)S(1)} %broadcast_clamp_fusion), kind=kCustom, calls=%fused_computation.3 | custom fusion | bytes 790528 | tf_op jit(solution)/shard_map/gather | solution.py:196
  34.5 3.3 %shard_map.129 = (f32[192,1024]{1,0:T(8,128)}, f32[8,1024]{1,0:T(8,128)}) custom-call(s32[1,1024]{1,0:T(1,128)} %get-tuple-element.42.tgt_ref, bf16[192,1024]{1,0:T(8,128)(2,1)} %bitcast.120, f32[192,1024]{1,0:T(8,128)} %broadcast_in_dim.4.sum_in, f32[8,1024]{1,0:T(8,128)} %broadcast_in_dim.5.cnt_in), custom_call_target="tpu_custom_call", output_to_operand_aliasing={{0}: (2, {}), {1}: (3, {})} | custom-call | flops 419430400 | bytes 2035712 | tf_op jit(solution)/shard_map/pallas_call | solution.py:46
  39.4 3.3 %shard_map.130 = (f32[192,1024]{1,0:T(8,128)}, f32[8,1024]{1,0:T(8,128)}) custom-call(s32[1,1024]{1,0:T(1,128)} %get-tuple-element.45.tgt_ref, bf16[192,1024]{1,0:T(8,128)(2,1)} %collective-permute-done.2.rec_ref, f32[192,1024]{1,0:T(8,128)} %get-tuple-element.14.sum_in, ...), custom_call_target="tpu_custom_call", output_to_operand_aliasing={{0}: (2, {}), {1}: (3, {})} | custom-call | flops 419430400 | bytes 2035712 | tf_op jit(solution)/shard_map/pallas_call | solution.py:46
  42.7 3.3 %shard_map.131 = (f32[192,1024]{1,0:T(8,128)}, f32[8,1024]{1,0:T(8,128)}) custom-call(s32[1,1024]{1,0:T(1,128)} %get-tuple-element.43.tgt_ref, bf16[192,1024]{1,0:T(8,128)(2,1)} %collective-permute-done.1.rec_ref, f32[192,1024]{1,0:T(8,128)} %get-tuple-element.16.sum_in, ...), custom_call_target="tpu_custom_call", output_to_operand_aliasing={{0}: (2, {}), {1}: (3, {})} | custom-call | flops 419430400 | bytes 2035712 | tf_op jit(solution)/shard_map/pallas_call | solution.py:46
  46.0 1.6 collective-permute-start.12
  47.5 3.3 %shard_map.132 = (f32[192,1024]{1,0:T(8,128)}, f32[8,1024]{1,0:T(8,128)}) custom-call(s32[1,1024]{1,0:T(1,128)} %get-tuple-element.44.tgt_ref, bf16[192,1024]{1,0:T(8,128)(2,1)} %collective-permute-done.rec_ref, f32[192,1024]{1,0:T(8,128)} %get-tuple-element.18.sum_in, f32[8,1024]{1,0:T(8,128)} %get-tuple-element.19.cnt_in), custom_call_target="tpu_custom_call", output_to_operand_aliasing={{0}: (2, {}), {1}: (3, {})} | custom-call | flops 419430400 | bytes 2035712 | tf_op jit(solution)/shard_map/pallas_call | solution.py:46
  54.8 6.3 %collective-permute-done.12 = bf16[256,1024]{1,0:T(8,128)(2,1)S(1)} collective-permute-done((bf16[256,1024]{1,0:T(8,128)(2,1)S(1)}, bf16[256,1024]{1,0:T(8,128)(2,1)S(1)}, u32[]{:S(2)}, u32[]{:S(2)}) %collective-permute-start.12) | collective-permute-done | bytes 524320 | tf_op jit(solution)/shard_map/ppermute | solution.py:124
  62.2 5.2 %collective-permute-done.6 = bf16[384,256]{1,0:T(8,128)(2,1)S(1)} collective-permute-done((bf16[384,256]{1,0:T(8,128)(2,1)S(1)}, bf16[384,256]{1,0:T(8,128)(2,1)S(1)}, u32[]{:S(2)}, u32[]{:S(2)}) %collective-permute-start.6) | collective-permute-done | bytes 196640 | tf_op jit(solution)/shard_map/ppermute | solution.py:208
  72.5 1.6 %collective-permute-done.9 = bf16[384,256]{1,0:T(8,128)(2,1)S(1)} collective-permute-done((bf16[384,256]{1,0:T(8,128)(2,1)S(1)}, bf16[384,256]{1,0:T(8,128)(2,1)S(1)}, u32[]{:S(2)}, u32[]{:S(2)}) %collective-permute-start.9) | collective-permute-done | bytes 196640 | tf_op jit(solution)/shard_map/ppermute | solution.py:208
  77.1 1.7 %multiply_convert_fusion.2 = (bf16[256,1024]{1,0:T(8,128)(2,1)}, f32[256,1024]{1,0:T(8,128)S(1)}) fusion(f32[1024]{0:T(1024)S(1)} %copy-done.16, bf16[256,1024]{1,0:T(8,128)(2,1)S(1)} %convolution_convert_fusion, bf16[1024,1024]{1,0:T(8,128)(2,1)S(1)} %bitcast.115), kind=kOutput, calls=%fused_computation.35 | convolution fusion | flops 538443776 | bytes 4198400 | tf_op jit(solution)/shard_map/dot_general | solution.py:217
  79.7 2.0 %copy-done = f32[1024,1024]{1,0:T(8,128)} copy-done((f32[1024,1024]{1,0:T(8,128)}, f32[1024,1024]{1,0:T(8,128)S(1)}, u32[]{:S(2)}) %copy-start) | copy-done | bytes 4194328
  82.8 2.3 %fusion.41 = f32[256,1024]{1,0:T(8,128)S(1)} fusion(bf16[1024,1024]{1,0:T(8,128)(2,1)S(1)} %bitcast.116, f32[256,1024]{1,0:T(8,128)} %copy-done.2, bf16[256,1024]{1,0:T(8,128)(2,1)} %param.19), kind=kOutput, calls=%fused_computation.114 | convolution fusion | flops 539492352 | bytes 4718592 | tf_op jit(solution)/shard_map/dot_general | solution.py:222
  85.1 1.5 multiply_convert_fusion
  87.3 1.6 bitcast_add_fusion
  88.9 5.9 %collective-permute-start.20 = (bf16[2,2,64,1024]{3,2,1,0:T(8,128)(2,1)S(1)}, bf16[2,2,64,1024]{3,2,1,0:T(8,128)(2,1)}, u32[]{:S(2)}, u32[]{:S(2)}) collective-permute-start(bf16[2,2,64,1024]{3,2,1,0:T(8,128)(2,1)S(1)} %fusion.5), channel_id=1, source_target_pairs={{0,4},{1,5},{2,6},{3,7},{4,0},{5,1},{6,2},{7,3},{8,12},{9,13},{10,... | collective-permute-start | bytes 1572872 | tf_op jit(solution)/shard_map/ppermute | solution.py:94
  96.8 10.7 %collective-permute-done.20 = bf16[2,2,64,1024]{3,2,1,0:T(8,128)(2,1)} collective-permute-done((bf16[2,2,64,1024]{3,2,1,0:T(8,128)(2,1)S(1)}, bf16[2,2,64,1024]{3,2,1,0:T(8,128)(2,1)}, u32[]{:S(2)}, u32[]{:S(2)}) %collective-permute-start.20) | collective-permute-done | bytes 524320 | tf_op jit(solution)/shard_map/ppermute | solution.py:94
  108.8 3.6 %collective-permute-start.21 = (bf16[2,64,1024]{2,1,0:T(8,128)(2,1)S(1)}, bf16[2,64,1024]{2,1,0:T(8,128)(2,1)S(1)}, u32[]{:S(2)}, u32[]{:S(2)}) collective-permute-start(bf16[2,64,1024]{2,1,0:T(8,128)(2,1)S(1)} %fusion.7), channel_id=1, source_target_pairs={{0,8},{1,9},{2,10},{3,11},{4,12},{5,13},{6,14},{7,15},{8,0},{9,1},... | collective-permute-start | bytes 786440 | tf_op jit(solution)/shard_map/ppermute | solution.py:94
  112.7 11.6 %collective-permute-done.21 = bf16[2,64,1024]{2,1,0:T(8,128)(2,1)S(1)} collective-permute-done((bf16[2,64,1024]{2,1,0:T(8,128)(2,1)S(1)}, bf16[2,64,1024]{2,1,0:T(8,128)(2,1)S(1)}, u32[]{:S(2)}, u32[]{:S(2)}) %collective-permute-start.21) | collective-permute-done | bytes 262176 | tf_op jit(solution)/shard_map/ppermute | solution.py:94
  126.2 3.3 %collective-permute-done.22 = bf16[64,1024]{1,0:T(8,128)(2,1)S(1)} collective-permute-done((bf16[64,1024]{1,0:T(8,128)(2,1)S(1)}, bf16[64,1024]{1,0:T(8,128)(2,1)S(1)}, u32[]{:S(2)}, u32[]{:S(2)}) %collective-permute-start.22) | collective-permute-done | bytes 131104 | tf_op jit(solution)/shard_map/ppermute | solution.py:94
  130.2 4.6 %collective-permute-start.18 = (bf16[2,384,256]{2,1,0:T(8,128)(2,1)S(1)}, bf16[2,384,256]{2,1,0:T(8,128)(2,1)S(1)}, u32[]{:S(2)}, u32[]{:S(2)}) collective-permute-start(bf16[2,384,256]{2,1,0:T(8,128)(2,1)S(1)} %fusion.6), channel_id=1, source_target_pairs={{0,4},{4,0},{8,12},{12,8},{1,5},{5,1},{9,13},{13,9},{2,6},{6,2},{1... | collective-permute-start | bytes 1179656 | tf_op jit(solution)/shard_map/ppermute | solution.py:94
  134.8 2.9 %collective-permute-done.23 = bf16[64,1024]{1,0:T(8,128)(2,1)S(1)} collective-permute-done((bf16[64,1024]{1,0:T(8,128)(2,1)S(1)}, bf16[64,1024]{1,0:T(8,128)(2,1)S(1)}, u32[]{:S(2)}, u32[]{:S(2)}) %collective-permute-start.23) | collective-permute-done | bytes 131104 | tf_op jit(solution)/shard_map/ppermute | solution.py:124
  138.7 6.8 %collective-permute-done.18 = bf16[2,384,256]{2,1,0:T(8,128)(2,1)S(1)} collective-permute-done((bf16[2,384,256]{2,1,0:T(8,128)(2,1)S(1)}, bf16[2,384,256]{2,1,0:T(8,128)(2,1)S(1)}, u32[]{:S(2)}, u32[]{:S(2)}) %collective-permute-start.18) | collective-permute-done | bytes 393248 | tf_op jit(solution)/shard_map/ppermute | solution.py:94
  145.6 1.6 %collective-permute-start.19 = (bf16[384,256]{1,0:T(8,128)(2,1)S(1)}, bf16[384,256]{1,0:T(8,128)(2,1)S(1)}, u32[]{:S(2)}, u32[]{:S(2)}) collective-permute-start(bf16[384,256]{1,0:T(8,128)(2,1)S(1)} %fusion.10), channel_id=1, source_target_pairs={{0,8},{4,12},{8,0},{12,4},{1,9},{5,13},{9,1},{13,5},{2,10},{6,14},... | collective-permute-start | bytes 589832 | tf_op jit(solution)/shard_map/ppermute | solution.py:94
  147.2 5.9 %collective-permute-done.24 = bf16[2,64,1024]{2,1,0:T(8,128)(2,1)S(1)} collective-permute-done((bf16[2,64,1024]{2,1,0:T(8,128)(2,1)S(1)}, bf16[2,64,1024]{2,1,0:T(8,128)(2,1)S(1)}, u32[]{:S(2)}, u32[]{:S(2)}) %collective-permute-start.24) | collective-permute-done | bytes 262176 | tf_op jit(solution)/shard_map/ppermute | solution.py:124
  154.3 1.5 collective-permute-done.19
  (118 shorter events, 34.2 us)
Async XLA Ops:
  0.6 6.2 %copy-start.13 = (s32[1,4,1024]{2,1,0:T(4,128)S(1)}, s32[1,4,1024]{2,1,0:T(4,128)}, u32[]{:S(2)}) copy-start(s32[1,4,1024]{2,1,0:T(4,128)} %param.11) | copy-start | bytes 49156
  0.6 61.4 %collective-permute-start.8 = (bf16[192,1024]{1,0:T(8,128)(2,1)}, bf16[192,1024]{1,0:T(8,128)(2,1)}, u32[]{:S(2)}, u32[]{:S(2)}) collective-permute-start(bf16[192,1024]{1,0:T(8,128)(2,1)} %param.14), channel_id=1, source_target_pairs={{0,2},{1,3},{2,0},{3,1},{4,6},{5,7},{6,4},{7,5},{8,10},{9,11},{10,... | collective-permute-start | bytes 1179656 | tf_op jit(solution)/shard_map/ppermute | solution.py:139
  3.6 66.6 %collective-permute-start.5 = (bf16[192,1024]{1,0:T(8,128)(2,1)}, bf16[192,1024]{1,0:T(8,128)(2,1)}, u32[]{:S(2)}, u32[]{:S(2)}) collective-permute-start(bf16[192,1024]{1,0:T(8,128)(2,1)} %param.14), channel_id=1, source_target_pairs={{0,1},{1,0},{2,3},{3,2},{4,5},{5,4},{6,7},{7,6},{8,9},{9,8},{10,11... | collective-permute-start | bytes 1179656 | tf_op jit(solution)/shard_map/ppermute | solution.py:139
  11.8 27.1 %collective-permute-start.2 = (bf16[192,1024]{1,0:T(8,128)(2,1)}, bf16[192,1024]{1,0:T(8,128)(2,1)}, u32[]{:S(2)}, u32[]{:S(2)}) collective-permute-start(bf16[192,1024]{1,0:T(8,128)(2,1)} %bitcast.11), channel_id=1, source_target_pairs={{0,4},{4,8},{8,12},{12,0},{1,5},{5,9},{9,13},{13,1},{2,6},{6,10},{... | collective-permute-start | bytes 1179656 | tf_op jit(solution)/shard_map/ppermute | solution.py:198
  17.5 25.2 %collective-permute-start.1 = (bf16[192,1024]{1,0:T(8,128)(2,1)S(1)}, bf16[192,1024]{1,0:T(8,128)(2,1)}, u32[]{:S(2)}, u32[]{:S(2)}) collective-permute-start(bf16[192,1024]{1,0:T(8,128)(2,1)S(1)} %bitcast.119), channel_id=1, source_target_pairs={{0,8},{4,12},{8,0},{12,4},{1,9},{5,13},{9,1},{13,5},{2,10},{6,14},... | collective-permute-start | bytes 1179656 | tf_op jit(solution)/shard_map/ppermute | solution.py:198
  20.2 7.0 %copy-start.14 = (s32[1,4,1024]{2,1,0:T(4,128)S(1)}, s32[1,4,1024]{2,1,0:T(4,128)}, u32[]{:S(2)}) copy-start(s32[1,4,1024]{2,1,0:T(4,128)} %param.12) | copy-start | bytes 49156
  24.3 21.7 %collective-permute-start = (bf16[192,1024]{1,0:T(8,128)(2,1)S(1)}, bf16[192,1024]{1,0:T(8,128)(2,1)}, u32[]{:S(2)}, u32[]{:S(2)}) collective-permute-start(bf16[192,1024]{1,0:T(8,128)(2,1)S(1)} %bitcast.118), channel_id=1, source_target_pairs={{0,12},{4,0},{8,4},{12,8},{1,13},{5,1},{9,5},{13,9},{2,14},{6,2},{... | collective-permute-start | bytes 1179656 | tf_op jit(solution)/shard_map/ppermute | solution.py:198
  37.7 8.2 %copy-start.7 = (bf16[256,1024]{1,0:T(8,128)(2,1)S(1)}, bf16[256,1024]{1,0:T(8,128)(2,1)}, u32[]{:S(2)}) copy-start(bf16[256,1024]{1,0:T(8,128)(2,1)} %param.16) | copy-start | bytes 1572868
  38.8 29.8 %collective-permute-start.7 = (bf16[192,1024]{1,0:T(8,128)(2,1)}, bf16[192,1024]{1,0:T(8,128)(2,1)S(1)}, u32[]{:S(2)}, u32[]{:S(2)}) collective-permute-start(bf16[192,1024]{1,0:T(8,128)(2,1)} %param.13), channel_id=1, source_target_pairs={{0,2},{1,3},{2,0},{3,1},{4,6},{5,7},{6,4},{7,5},{8,10},{9,11},{10,... | collective-permute-start | bytes 1179656 | tf_op jit(solution)/shard_map/ppermute | solution.py:139
  42.7 29.4 %collective-permute-start.4 = (bf16[192,1024]{1,0:T(8,128)(2,1)}, bf16[192,1024]{1,0:T(8,128)(2,1)S(1)}, u32[]{:S(2)}, u32[]{:S(2)}) collective-permute-start(bf16[192,1024]{1,0:T(8,128)(2,1)} %param.13), channel_id=1, source_target_pairs={{0,1},{1,0},{2,3},{3,2},{4,5},{5,4},{6,7},{7,6},{8,9},{9,8},{10,11... | collective-permute-start | bytes 1179656 | tf_op jit(solution)/shard_map/ppermute | solution.py:139
  46.0 15.1 %collective-permute-start.12 = (bf16[256,1024]{1,0:T(8,128)(2,1)S(1)}, bf16[256,1024]{1,0:T(8,128)(2,1)S(1)}, u32[]{:S(2)}, u32[]{:S(2)}) collective-permute-start(bf16[256,1024]{1,0:T(8,128)(2,1)S(1)} %copy-done.7), channel_id=1, source_target_pairs={{0,2},{1,3},{2,0},{3,1},{4,6},{5,7},{6,4},{7,5},{8,10},{9,11},{10,... | collective-permute-start | bytes 1572872 | tf_op jit(solution)/shard_map/ppermute | solution.py:124
  53.0 9.0 %copy-start.5 = (bf16[384,256]{1,0:T(8,128)(2,1)}, bf16[384,256]{1,0:T(8,128)(2,1)S(1)}, u32[]{:S(2)}) copy-start(bf16[384,256]{1,0:T(8,128)(2,1)S(1)} %get-tuple-element.30) | copy-start | bytes 589828
  53.0 9.1 %copy-start.3 = (bf16[384,256]{1,0:T(8,128)(2,1)}, bf16[384,256]{1,0:T(8,128)(2,1)S(1)}, u32[]{:S(2)}) copy-start(bf16[384,256]{1,0:T(8,128)(2,1)S(1)} %get-tuple-element.29) | copy-start | bytes 589828
  61.0 6.3 %collective-permute-start.6 = (bf16[384,256]{1,0:T(8,128)(2,1)S(1)}, bf16[384,256]{1,0:T(8,128)(2,1)S(1)}, u32[]{:S(2)}, u32[]{:S(2)}) collective-permute-start(bf16[384,256]{1,0:T(8,128)(2,1)S(1)} %get-tuple-element.30), channel_id=1, source_target_pairs={{0,2},{1,3},{2,0},{3,1},{4,6},{5,7},{6,4},{7,5},{8,10},{9,11},{10,... | collective-permute-start | bytes 589832 | tf_op jit(solution)/shard_map/ppermute | solution.py:208
  62.1 8.2 %collective-permute-start.3 = (bf16[384,256]{1,0:T(8,128)(2,1)S(1)}, bf16[384,256]{1,0:T(8,128)(2,1)S(1)}, u32[]{:S(2)}, u32[]{:S(2)}) collective-permute-start(bf16[384,256]{1,0:T(8,128)(2,1)S(1)} %get-tuple-element.29), channel_id=1, source_target_pairs={{0,1},{1,0},{2,3},{3,2},{4,5},{5,4},{6,7},{7,6},{8,9},{9,8},{10,11... | collective-permute-start | bytes 589832 | tf_op jit(solution)/shard_map/ppermute | solution.py:208
  67.4 6.8 %collective-permute-start.9 = (bf16[384,256]{1,0:T(8,128)(2,1)S(1)}, bf16[384,256]{1,0:T(8,128)(2,1)S(1)}, u32[]{:S(2)}, u32[]{:S(2)}) collective-permute-start(bf16[384,256]{1,0:T(8,128)(2,1)S(1)} %get-tuple-element.31), channel_id=1, source_target_pairs={{0,3},{1,2},{2,1},{3,0},{4,7},{5,6},{6,5},{7,4},{8,11},{9,10},{10,... | collective-permute-start | bytes 589832 | tf_op jit(solution)/shard_map/ppermute | solution.py:208
  68.7 5.5 %collective-permute-start.11 = (bf16[192,1024]{1,0:T(8,128)(2,1)}, bf16[192,1024]{1,0:T(8,128)(2,1)S(1)}, u32[]{:S(2)}, u32[]{:S(2)}) collective-permute-start(bf16[192,1024]{1,0:T(8,128)(2,1)} %collective-permute-done.8), channel_id=1, source_target_pairs={{0,1},{1,0},{2,3},{3,2},{4,5},{5,4},{6,7},{7,6},{8,9},{9,8},{10,11... | collective-permute-start | bytes 1179656 | tf_op jit(solution)/shard_map/ppermute | solution.py:139
  70.2 4.3 %collective-permute-start.10 = (bf16[192,1024]{1,0:T(8,128)(2,1)S(1)}, bf16[192,1024]{1,0:T(8,128)(2,1)S(1)}, u32[]{:S(2)}, u32[]{:S(2)}) collective-permute-start(bf16[192,1024]{1,0:T(8,128)(2,1)S(1)} %collective-permute-done.7), channel_id=1, source_target_pairs={{0,1},{1,0},{2,3},{3,2},{4,5},{5,4},{6,7},{7,6},{8,9},{9,8},{10,11... | collective-permute-start | bytes 1179656 | tf_op jit(solution)/shard_map/ppermute | solution.py:139
  70.3 5.9 %collective-permute-start.13 = (bf16[2,256,1024]{2,1,0:T(8,128)(2,1)S(1)}, bf16[2,256,1024]{2,1,0:T(8,128)(2,1)S(1)}, u32[]{:S(2)}, u32[]{:S(2)}) collective-permute-start(bf16[2,256,1024]{2,1,0:T(8,128)(2,1)S(1)} %pad_maximum_fusion.1), channel_id=1, source_target_pairs={{0,1},{1,0},{2,3},{3,2},{4,5},{5,4},{6,7},{7,6},{8,9},{9,8},{10,11... | collective-permute-start | bytes 3145736 | tf_op jit(solution)/shard_map/ppermute | solution.py:124
  82.8 3.8 %collective-permute-start.14 = (bf16[2,2,2,64,1024]{4,3,2,1,0:T(8,128)(2,1)}, bf16[2,2,2,64,1024]{4,3,2,1,0:T(8,128)(2,1)}, u32[]{:S(2)}, u32[]{:S(2)}) collective-permute-start(bf16[2,2,2,64,1024]{4,3,2,1,0:T(8,128)(2,1)} %fusion.4), channel_id=1, source_target_pairs={{0,1},{1,0},{2,3},{3,2},{4,5},{5,4},{6,7},{7,6},{8,9},{9,8},{10,11... | collective-permute-start | bytes 3145736 | tf_op jit(solution)/shard_map/ppermute | solution.py:94
  88.9 18.6 %collective-permute-start.20 = (bf16[2,2,64,1024]{3,2,1,0:T(8,128)(2,1)S(1)}, bf16[2,2,64,1024]{3,2,1,0:T(8,128)(2,1)}, u32[]{:S(2)}, u32[]{:S(2)}) collective-permute-start(bf16[2,2,64,1024]{3,2,1,0:T(8,128)(2,1)S(1)} %fusion.5), channel_id=1, source_target_pairs={{0,4},{1,5},{2,6},{3,7},{4,0},{5,1},{6,2},{7,3},{8,12},{9,13},{10,... | collective-permute-start | bytes 1572872 | tf_op jit(solution)/shard_map/ppermute | solution.py:94
  94.8 31.0 %collective-permute-start.15 = (bf16[256,1024]{1,0:T(8,128)(2,1)S(1)}, bf16[256,1024]{1,0:T(8,128)(2,1)S(1)}, u32[]{:S(2)}, u32[]{:S(2)}) collective-permute-start(bf16[256,1024]{1,0:T(8,128)(2,1)S(1)} %multiply_convert_fusion), channel_id=1, source_target_pairs={{0,1},{1,0},{2,3},{3,2},{4,5},{5,4},{6,7},{7,6},{8,9},{9,8},{10,11... | collective-permute-start | bytes 1572872 | tf_op jit(solution)/shard_map/ppermute | solution.py:139
  95.0 17.3 %collective-permute-start.16 = (bf16[256,1024]{1,0:T(8,128)(2,1)S(1)}, bf16[256,1024]{1,0:T(8,128)(2,1)S(1)}, u32[]{:S(2)}, u32[]{:S(2)}) collective-permute-start(bf16[256,1024]{1,0:T(8,128)(2,1)S(1)} %multiply_convert_fusion), channel_id=1, source_target_pairs={{0,2},{1,3},{2,0},{3,1},{4,6},{5,7},{6,4},{7,5},{8,10},{9,11},{10,... | collective-permute-start | bytes 1572872 | tf_op jit(solution)/shard_map/ppermute | solution.py:139
  96.8 15.5 %copy-start.6 = (bf16[384,256]{1,0:T(8,128)(2,1)S(1)}, bf16[384,256]{1,0:T(8,128)(2,1)}, u32[]{:S(2)}) copy-start(bf16[384,256]{1,0:T(8,128)(2,1)} %copy-done.5) | copy-start | bytes 589828
  108.7 17.1 %copy-start.4 = (bf16[384,256]{1,0:T(8,128)(2,1)S(1)}, bf16[384,256]{1,0:T(8,128)(2,1)}, u32[]{:S(2)}) copy-start(bf16[384,256]{1,0:T(8,128)(2,1)} %copy-done.3) | copy-start | bytes 589828
  108.8 15.6 %collective-permute-start.21 = (bf16[2,64,1024]{2,1,0:T(8,128)(2,1)S(1)}, bf16[2,64,1024]{2,1,0:T(8,128)(2,1)S(1)}, u32[]{:S(2)}, u32[]{:S(2)}) collective-permute-start(bf16[2,64,1024]{2,1,0:T(8,128)(2,1)S(1)} %fusion.7), channel_id=1, source_target_pairs={{0,8},{1,9},{2,10},{3,11},{4,12},{5,13},{6,14},{7,15},{8,0},{9,1},... | collective-permute-start | bytes 786440 | tf_op jit(solution)/shard_map/ppermute | solution.py:94
  112.4 17.3 %collective-permute-start.17 = (bf16[256,1024]{1,0:T(8,128)(2,1)S(1)}, bf16[256,1024]{1,0:T(8,128)(2,1)S(1)}, u32[]{:S(2)}, u32[]{:S(2)}) collective-permute-start(bf16[256,1024]{1,0:T(8,128)(2,1)S(1)} %collective-permute-done.16), channel_id=1, source_target_pairs={{0,1},{1,0},{2,3},{3,2},{4,5},{5,4},{6,7},{7,6},{8,9},{9,8},{10,11... | collective-permute-start | bytes 1572872 | tf_op jit(solution)/shard_map/ppermute | solution.py:139
  124.5 5.0 %collective-permute-start.22 = (bf16[64,1024]{1,0:T(8,128)(2,1)S(1)}, bf16[64,1024]{1,0:T(8,128)(2,1)S(1)}, u32[]{:S(2)}, u32[]{:S(2)}) collective-permute-start(bf16[64,1024]{1,0:T(8,128)(2,1)S(1)} %fusion.15), channel_id=1, source_target_pairs={{0,2},{1,3},{2,0},{3,1},{4,6},{5,7},{6,4},{7,5},{8,10},{9,11},{10,... | collective-permute-start | bytes 393224 | tf_op jit(solution)/shard_map/ppermute | solution.py:94
  129.5 8.1 %collective-permute-start.23 = (bf16[64,1024]{1,0:T(8,128)(2,1)S(1)}, bf16[64,1024]{1,0:T(8,128)(2,1)S(1)}, u32[]{:S(2)}, u32[]{:S(2)}) collective-permute-start(bf16[64,1024]{1,0:T(8,128)(2,1)S(1)} %fusion.8), channel_id=1, source_target_pairs={{0,8},{4,12},{8,0},{12,4},{1,9},{5,13},{9,1},{13,5},{2,10},{6,14},... | collective-permute-start | bytes 393224 | tf_op jit(solution)/shard_map/ppermute | solution.py:124
  130.2 15.3 %collective-permute-start.18 = (bf16[2,384,256]{2,1,0:T(8,128)(2,1)S(1)}, bf16[2,384,256]{2,1,0:T(8,128)(2,1)S(1)}, u32[]{:S(2)}, u32[]{:S(2)}) collective-permute-start(bf16[2,384,256]{2,1,0:T(8,128)(2,1)S(1)} %fusion.6), channel_id=1, source_target_pairs={{0,4},{4,0},{8,12},{12,8},{1,5},{5,1},{9,13},{13,9},{2,6},{6,2},{1... | collective-permute-start | bytes 1179656 | tf_op jit(solution)/shard_map/ppermute | solution.py:94
  137.7 15.4 %collective-permute-start.24 = (bf16[2,64,1024]{2,1,0:T(8,128)(2,1)S(1)}, bf16[2,64,1024]{2,1,0:T(8,128)(2,1)S(1)}, u32[]{:S(2)}, u32[]{:S(2)}) collective-permute-start(bf16[2,64,1024]{2,1,0:T(8,128)(2,1)S(1)} %pad_maximum_fusion.2), channel_id=1, source_target_pairs={{0,4},{4,0},{8,12},{12,8},{1,5},{5,1},{9,13},{13,9},{2,6},{6,2},{1... | collective-permute-start | bytes 786440 | tf_op jit(solution)/shard_map/ppermute | solution.py:124
  145.6 10.2 %collective-permute-start.19 = (bf16[384,256]{1,0:T(8,128)(2,1)S(1)}, bf16[384,256]{1,0:T(8,128)(2,1)S(1)}, u32[]{:S(2)}, u32[]{:S(2)}) collective-permute-start(bf16[384,256]{1,0:T(8,128)(2,1)S(1)} %fusion.10), channel_id=1, source_target_pairs={{0,8},{4,12},{8,0},{12,4},{1,9},{5,13},{9,1},{13,5},{2,10},{6,14},... | collective-permute-start | bytes 589832 | tf_op jit(solution)/shard_map/ppermute | solution.py:94
  (10 other events, 24.6 us)

commit v20 on v17

--- a/solution.py
+++ b/solution.py
@@ -239,6 +239,7 @@
         "dom",
         n_dom,
         jnp.bfloat16,
+        high_first=True,
     )
     grad_neigh = grad_layer[:w_rows]
     grad_self = grad_layer[w_rows:]

time: 148 us -> 156 us (1.054)
  waiting for transfers between devices: 54.3 us -> 59.5 us
  starting transfers between devices: 21.2 us -> 22.9 us
    ppermute x8, waiting for transfers between devices: 14.5 us -> 19.6 us  [all_gather_blocks(): got = lax.ppermute(cur, axis, _xor_pairs(n, 1 << b))]
  transfers between devices with their start and end apart: 23 -> 23, of which waited for: 10 -> 10; matrix products, arithmetic and copies ran while one was open for 27% -> 26% of each run, Pallas kernels for 9% -> 8%
where the time goes in v20:
time: 156 us; the launch traced here: 155 us
  waiting for transfers between devices  59.5 us (38%)
  local copies, waits for them, and re-layouts  32.7 us (21%)
  starting transfers between devices  22.9 us (15%)
  other arithmetic  13.5 us (9%)
  Pallas kernels  13.1 us (8%)
  matrix products  12.2 us (8%)
    ppermute x6, waiting for transfers between devices, _butterfly_reduce(): got = lax.ppermute(send.astype(send_dtype), axis, _xor_pairs(n, 1 << b))  37.7 us
    ppermute x8, waiting for transfers between devices, all_gather_blocks(): got = lax.ppermute(cur, axis, _xor_pairs(n, 1 << b))  19.6 us
    gather x8, local copies, waits for them, and re-layouts, local(): rows_t = features.at[slots].get(mode='promise_in_bounds').T  18.8 us
    pallas_call x4, Pallas kernels, accumulate(): pl.pallas_call(_accumulate_kernel, out_shape=[jax.ShapeDtypeStruct(acc_su...  13.1 us
    ppermute x3, starting transfers between devices, local(): rows_t = lax.ppermute(rows_t, 'dom', _shift_pairs(n_dom, shift))  7.01 us
    another operation x14, other arithmetic, join(): return jnp.stack([low, high], axis=k - 1 - b)  6.82 us
    unnamed x31, local copies, waits for them, and re-layouts  6.38 us
    ppermute x6, starting transfers between devices, _butterfly_reduce(): got = lax.ppermute(send.astype(send_dtype), axis, _xor_pairs(n, 1 << b))  6.3 us
  transfers between devices with their start and end apart: 23, of which 10 were waited for; matrix products, arithmetic and copies ran while one was open for 26% of the time, Pallas kernels for 8%

profile of v20, /device:TPU:0, one launch (start us, length us, event | category | flops | bytes accessed | tf_op | source)
XLA Modules:
  0.0 155.0 jit_solution(687368285929640768)
XLA Ops:
  0.7 3.2 %copy.47 = bf16[4096,192]{1,0:T(8,128)(2,1)S(1)} copy(bf16[4096,192]{0,1:T(8,128)(2,1)} %param.10) | data formatting | bytes 3145728 | tf_op args[0]
  3.9 3.9 %gather_fusion.2 = bf16[1024,192]{1,0:T(8,128)(2,1)S(1)} fusion(bf16[4096,192]{1,0:T(8,128)(2,1)S(1)} %copy.47, s32[1024]{0:T(1024)S(1)} %broadcast_clamp_fusion.1), kind=kCustom, calls=%fused_computation.2 | custom fusion | bytes 790528 | tf_op jit(solution)/shard_map/gather | solution.py:183
  8.8 3.0 %collective-permute-start.2 = (bf16[192,1024]{1,0:T(8,128)(2,1)}, bf16[192,1024]{1,0:T(8,128)(2,1)}, u32[]{:S(2)}, u32[]{:S(2)}) collective-permute-start(bf16[192,1024]{1,0:T(8,128)(2,1)} %bitcast.11), channel_id=1, source_target_pairs={{0,4},{4,8},{8,12},{12,0},{1,5},{5,9},{9,13},{13,1},{2,6},{6,10},{... | collective-permute-start | bytes 1179656 | tf_op jit(solution)/shard_map/ppermute | solution.py:185
  11.9 3.9 %gather_fusion.1 = bf16[1024,192]{1,0:T(8,128)(2,1)S(1)} fusion(bf16[4096,192]{1,0:T(8,128)(2,1)S(1)} %copy.47, s32[1024]{0:T(1024)S(1)} %broadcast_clamp_fusion.2), kind=kCustom, calls=%fused_computation.1 | custom fusion | bytes 790528 | tf_op jit(solution)/shard_map/gather | solution.py:183
  16.7 2.6 %collective-permute-start.1 = (bf16[192,1024]{1,0:T(8,128)(2,1)}, bf16[192,1024]{1,0:T(8,128)(2,1)}, u32[]{:S(2)}, u32[]{:S(2)}) collective-permute-start(bf16[192,1024]{1,0:T(8,128)(2,1)} %bitcast.7), channel_id=1, source_target_pairs={{0,8},{4,12},{8,0},{12,4},{1,9},{5,13},{9,1},{13,5},{2,10},{6,14},... | collective-permute-start | bytes 1179656 | tf_op jit(solution)/shard_map/ppermute | solution.py:185
  19.3 3.9 %gather_fusion = bf16[1024,192]{1,0:T(8,128)(2,1)S(1)} fusion(bf16[4096,192]{1,0:T(8,128)(2,1)S(1)} %copy.47, s32[1024]{0:T(1024)S(1)} %broadcast_clamp_fusion.3), kind=kCustom, calls=%fused_computation | custom fusion | bytes 790528 | tf_op jit(solution)/shard_map/gather | solution.py:183
  24.9 1.5 collective-permute-start.3
  26.9 3.9 %gather_fusion.3 = bf16[1024,192]{1,0:T(8,128)(2,1)S(1)} fusion(bf16[4096,192]{1,0:T(8,128)(2,1)S(1)} %copy.47, s32[1024]{0:T(1024)S(1)} %broadcast_clamp_fusion), kind=kCustom, calls=%fused_computation.3 | custom fusion | bytes 790528 | tf_op jit(solution)/shard_map/gather | solution.py:183
  34.0 3.3 %shard_map.129 = (f32[192,1024]{1,0:T(8,128)}, f32[8,1024]{1,0:T(8,128)}) custom-call(s32[1,1024]{1,0:T(1,128)} %get-tuple-element.49.tgt_ref, bf16[192,1024]{1,0:T(8,128)(2,1)} %bitcast.145, f32[192,1024]{1,0:T(8,128)} %broadcast_in_dim.4.sum_in, f32[8,1024]{1,0:T(8,128)} %broadcast_in_dim.5.cnt_in), custom_call_target="tpu_custom_call", output_to_operand_aliasing={{0}: (2, {}), {1}: (3, {})} | custom-call | flops 419430400 | bytes 2035712 | tf_op jit(solution)/shard_map/pallas_call | solution.py:46
  37.3 1.5 convert_reduce_fusion
  39.8 1.6 %collective-permute-start.10 = (bf16[256,1024]{1,0:T(8,128)(2,1)}, bf16[256,1024]{1,0:T(8,128)(2,1)}, u32[]{:S(2)}, u32[]{:S(2)}) collective-permute-start(bf16[256,1024]{1,0:T(8,128)(2,1)} %param.16), channel_id=1, source_target_pairs={{0,2},{1,3},{2,0},{3,1},{4,6},{5,7},{6,4},{7,5},{8,10},{9,11},{10,... | collective-permute-start | bytes 1572872 | tf_op jit(solution)/shard_map/ppermute | solution.py:124
  41.4 4.3 %collective-permute-done.5 = bf16[192,1024]{1,0:T(8,128)(2,1)} collective-permute-done((bf16[192,1024]{1,0:T(8,128)(2,1)S(1)}, bf16[192,1024]{1,0:T(8,128)(2,1)}, u32[]{:S(2)}, u32[]{:S(2)}) %collective-permute-start.5) | collective-permute-done | bytes 393248 | tf_op jit(solution)/shard_map/ppermute | solution.py:124
  48.5 3.3 %shard_map.130 = (f32[192,1024]{1,0:T(8,128)}, f32[8,1024]{1,0:T(8,128)}) custom-call(s32[1,1024]{1,0:T(1,128)} %get-tuple-element.52.tgt_ref, bf16[192,1024]{1,0:T(8,128)(2,1)} %collective-permute-done.2.rec_ref, f32[192,1024]{1,0:T(8,128)} %get-tuple-element.14.sum_in, ...), custom_call_target="tpu_custom_call", output_to_operand_aliasing={{0}: (2, {}), {1}: (3, {})} | custom-call | flops 419430400 | bytes 2035712 | tf_op jit(solution)/shard_map/pallas_call | solution.py:46
  51.8 3.3 %shard_map.131 = (f32[192,1024]{1,0:T(8,128)}, f32[8,1024]{1,0:T(8,128)}) custom-call(s32[1,1024]{1,0:T(1,128)} %get-tuple-element.50.tgt_ref, bf16[192,1024]{1,0:T(8,128)(2,1)} %collective-permute-done.1.rec_ref, f32[192,1024]{1,0:T(8,128)} %get-tuple-element.16.sum_in, ...), custom_call_target="tpu_custom_call", output_to_operand_aliasing={{0}: (2, {}), {1}: (3, {})} | custom-call | flops 419430400 | bytes 2035712 | tf_op jit(solution)/shard_map/pallas_call | solution.py:46
  55.0 3.3 %shard_map.132 = (f32[192,1024]{1,0:T(8,128)}, f32[8,1024]{1,0:T(8,128)}) custom-call(s32[1,1024]{1,0:T(1,128)} %get-tuple-element.51.tgt_ref, bf16[192,1024]{1,0:T(8,128)(2,1)} %collective-permute-done.rec_ref, f32[192,1024]{1,0:T(8,128)} %get-tuple-element.18.sum_in, f32[8,1024]{1,0:T(8,128)} %get-tuple-element.19.cnt_in), custom_call_target="tpu_custom_call", output_to_operand_aliasing={{0}: (2, {}), {1}: (3, {})} | custom-call | flops 419430400 | bytes 2035712 | tf_op jit(solution)/shard_map/pallas_call | solution.py:46
  60.4 1.6 %collective-permute-start.8 = (bf16[384,256]{1,0:T(8,128)(2,1)S(1)}, bf16[384,256]{1,0:T(8,128)(2,1)S(1)}, u32[]{:S(2)}, u32[]{:S(2)}) collective-permute-start(bf16[384,256]{1,0:T(8,128)(2,1)S(1)} %get-tuple-element.33), channel_id=1, source_target_pairs={{0,2},{1,3},{2,0},{3,1},{4,6},{5,7},{6,4},{7,5},{8,10},{9,11},{10,... | collective-permute-start | bytes 589832 | tf_op jit(solution)/shard_map/ppermute | solution.py:197
  68.7 1.8 %collective-permute-done.9 = bf16[384,256]{1,0:T(8,128)(2,1)S(1)} collective-permute-done((bf16[384,256]{1,0:T(8,128)(2,1)S(1)}, bf16[384,256]{1,0:T(8,128)(2,1)S(1)}, u32[]{:S(2)}, u32[]{:S(2)}) %collective-permute-start.9) | collective-permute-done | bytes 196640 | tf_op jit(solution)/shard_map/ppermute | solution.py:197
  74.2 1.7 %multiply_convert_fusion.2 = (bf16[256,1024]{1,0:T(8,128)(2,1)}, f32[256,1024]{1,0:T(8,128)S(1)}) fusion(f32[1024]{0:T(1024)S(1)} %copy-done.14, bf16[256,1024]{1,0:T(8,128)(2,1)S(1)} %convolution_convert_fusion, bf16[1024,1024]{1,0:T(8,128)(2,1)S(1)} %bitcast.141), kind=kOutput, calls=%fused_computation.48 | convolution fusion | flops 538443776 | bytes 4198400 | tf_op jit(solution)/shard_map/dot_general | solution.py:205
  76.9 2.0 %copy-done = f32[1024,1024]{1,0:T(8,128)} copy-done((f32[1024,1024]{1,0:T(8,128)}, f32[1024,1024]{1,0:T(8,128)S(1)}, u32[]{:S(2)}) %copy-start) | copy-done | bytes 4194328
  80.8 2.2 %fusion.69 = f32[256,1024]{1,0:T(8,128)S(1)} fusion(bf16[1024,1024]{1,0:T(8,128)(2,1)S(1)} %bitcast.142, f32[256,1024]{1,0:T(8,128)} %copy-done.2, bf16[256,1024]{1,0:T(8,128)(2,1)S(1)} %copy-done.5), kind=kOutput, calls=%fused_computation.158 | convolution fusion | flops 539492352 | bytes 4718592 | tf_op jit(solution)/shard_map/dot_general | solution.py:210
  83.0 2.1 %multiply_convert_fusion = bf16[256,1024]{1,0:T(8,128)(2,1)} fusion(f32[256,1024]{1,0:T(8,128)S(1)} %copy-done.4, f32[256,1024]{1,0:T(8,128)S(1)} %fusion.69, f32[256,256]{1,0:T(8,128)S(1)} %copy-done.9), kind=kOutput, calls=%fused_computation.46 | convolution fusion | flops 807927808 | bytes 2883584 | tf_op jit(solution)/shard_map/dot_general | solution.py:213
  85.2 1.6 %bitcast_add_fusion = f32[2,2,2,64,1024]{4,3,2,1,0:T(8,128)S(1)} fusion(bf16[2,2,2,64,1024]{4,3,2,1,0:T(8,128)(2,1)} %collective-permute-done.12, f32[2,2,2,2,64,1024]{5,4,3,2,1,0:T(8,128)S(1)} %bitcast.137, s32[]{:T(128)S(6)} %select_n.344), kind=kLoop, calls=%fused_computation.15 | loop fusion | flops 1048576 | bytes 5242884 | tf_op jit(solution)/shard_map/add | solution.py:95
  87.6 1.5 collective-permute-start.14
  90.5 10.3 %collective-permute-done.18 = bf16[2,2,64,1024]{3,2,1,0:T(8,128)(2,1)} collective-permute-done((bf16[2,2,64,1024]{3,2,1,0:T(8,128)(2,1)S(1)}, bf16[2,2,64,1024]{3,2,1,0:T(8,128)(2,1)}, u32[]{:S(2)}, u32[]{:S(2)}) %collective-permute-start.18) | collective-permute-done | bytes 524320 | tf_op jit(solution)/shard_map/ppermute | solution.py:94
  102.7 13.4 %collective-permute-done.19 = bf16[2,64,1024]{2,1,0:T(8,128)(2,1)S(1)} collective-permute-done((bf16[2,64,1024]{2,1,0:T(8,128)(2,1)S(1)}, bf16[2,64,1024]{2,1,0:T(8,128)(2,1)S(1)}, u32[]{:S(2)}, u32[]{:S(2)}) %collective-permute-start.19) | collective-permute-done | bytes 262176 | tf_op jit(solution)/shard_map/ppermute | solution.py:94
  116.2 1.5 collective-permute-start.20
  118.1 3.4 %collective-permute-done.20 = bf16[64,1024]{1,0:T(8,128)(2,1)S(1)} collective-permute-done((bf16[64,1024]{1,0:T(8,128)(2,1)S(1)}, bf16[64,1024]{1,0:T(8,128)(2,1)S(1)}, u32[]{:S(2)}, u32[]{:S(2)}) %collective-permute-start.20) | collective-permute-done | bytes 131104 | tf_op jit(solution)/shard_map/ppermute | solution.py:94
  123.2 3.0 %collective-permute-start.16 = (bf16[2,384,256]{2,1,0:T(8,128)(2,1)S(1)}, bf16[2,384,256]{2,1,0:T(8,128)(2,1)S(1)}, u32[]{:S(2)}, u32[]{:S(2)}) collective-permute-start(bf16[2,384,256]{2,1,0:T(8,128)(2,1)S(1)} %fusion.18), channel_id=1, source_target_pairs={{0,8},{4,12},{8,0},{12,4},{1,9},{5,13},{9,1},{13,5},{2,10},{6,14},... | collective-permute-start | bytes 1179656 | tf_op jit(solution)/shard_map/ppermute | solution.py:94
  126.1 9.9 %collective-permute-done.21 = bf16[64,1024]{1,0:T(8,128)(2,1)S(1)} collective-permute-done((bf16[64,1024]{1,0:T(8,128)(2,1)S(1)}, bf16[64,1024]{1,0:T(8,128)(2,1)S(1)}, u32[]{:S(2)}, u32[]{:S(2)}) %collective-permute-start.21) | collective-permute-done | bytes 131104 | tf_op jit(solution)/shard_map/ppermute | solution.py:124
  136.9 7.6 %collective-permute-done.16 = bf16[2,384,256]{2,1,0:T(8,128)(2,1)S(1)} collective-permute-done((bf16[2,384,256]{2,1,0:T(8,128)(2,1)S(1)}, bf16[2,384,256]{2,1,0:T(8,128)(2,1)S(1)}, u32[]{:S(2)}, u32[]{:S(2)}) %collective-permute-start.16) | collective-permute-done | bytes 393248 | tf_op jit(solution)/shard_map/ppermute | solution.py:94
  144.7 5.4 %collective-permute-done.22 = bf16[2,64,1024]{2,1,0:T(8,128)(2,1)S(1)} collective-permute-done((bf16[2,64,1024]{2,1,0:T(8,128)(2,1)S(1)}, bf16[2,64,1024]{2,1,0:T(8,128)(2,1)S(1)}, u32[]{:S(2)}, u32[]{:S(2)}) %collective-permute-start.22) | collective-permute-done | bytes 262176 | tf_op jit(solution)/shard_map/ppermute | solution.py:124
  151.3 2.9 %collective-permute-done.17 = bf16[384,256]{1,0:T(8,128)(2,1)S(1)} collective-permute-done((bf16[384,256]{1,0:T(8,128)(2,1)S(1)}, bf16[384,256]{1,0:T(8,128)(2,1)S(1)}, u32[]{:S(2)}, u32[]{:S(2)}) %collective-permute-start.17) | collective-permute-done | bytes 196640 | tf_op jit(solution)/shard_map/ppermute | solution.py:94
  (115 shorter events, 35.5 us)
Async XLA Ops:
  0.7 3.2 %copy-start.11 = (s32[1,4,1024]{2,1,0:T(4,128)S(1)}, s32[1,4,1024]{2,1,0:T(4,128)}, u32[]{:S(2)}) copy-start(s32[1,4,1024]{2,1,0:T(4,128)} %param.11) | copy-start | bytes 49156
  8.8 39.1 %collective-permute-start.2 = (bf16[192,1024]{1,0:T(8,128)(2,1)}, bf16[192,1024]{1,0:T(8,128)(2,1)}, u32[]{:S(2)}, u32[]{:S(2)}) collective-permute-start(bf16[192,1024]{1,0:T(8,128)(2,1)} %bitcast.11), channel_id=1, source_target_pairs={{0,4},{4,8},{8,12},{12,0},{1,5},{5,9},{9,13},{13,1},{2,6},{6,10},{... | collective-permute-start | bytes 1179656 | tf_op jit(solution)/shard_map/ppermute | solution.py:185
  16.7 35.0 %collective-permute-start.1 = (bf16[192,1024]{1,0:T(8,128)(2,1)}, bf16[192,1024]{1,0:T(8,128)(2,1)}, u32[]{:S(2)}, u32[]{:S(2)}) collective-permute-start(bf16[192,1024]{1,0:T(8,128)(2,1)} %bitcast.7), channel_id=1, source_target_pairs={{0,8},{4,12},{8,0},{12,4},{1,9},{5,13},{9,1},{13,5},{2,10},{6,14},... | collective-permute-start | bytes 1179656 | tf_op jit(solution)/shard_map/ppermute | solution.py:185
  19.3 7.0 %copy-start.6 = (bf16[192,1024]{1,0:T(8,128)(2,1)S(1)}, bf16[192,1024]{1,0:T(8,128)(2,1)}, u32[]{:S(2)}) copy-start(bf16[192,1024]{1,0:T(8,128)(2,1)} %param.14) | copy-start | bytes 1179652
  23.5 31.6 %collective-permute-start = (bf16[192,1024]{1,0:T(8,128)(2,1)S(1)}, bf16[192,1024]{1,0:T(8,128)(2,1)}, u32[]{:S(2)}, u32[]{:S(2)}) collective-permute-start(bf16[192,1024]{1,0:T(8,128)(2,1)S(1)} %bitcast.144), channel_id=1, source_target_pairs={{0,12},{4,0},{8,4},{12,8},{1,13},{5,1},{9,5},{13,9},{2,14},{6,2},{... | collective-permute-start | bytes 1179656 | tf_op jit(solution)/shard_map/ppermute | solution.py:185
  24.9 15.0 %collective-permute-start.3 = (bf16[192,1024]{1,0:T(8,128)(2,1)}, bf16[192,1024]{1,0:T(8,128)(2,1)}, u32[]{:S(2)}, u32[]{:S(2)}) collective-permute-start(bf16[192,1024]{1,0:T(8,128)(2,1)} %param.13), channel_id=1, source_target_pairs={{0,2},{1,3},{2,0},{3,1},{4,6},{5,7},{6,4},{7,5},{8,10},{9,11},{10,... | collective-permute-start | bytes 1179656 | tf_op jit(solution)/shard_map/ppermute | solution.py:124
  26.4 19.3 %collective-permute-start.5 = (bf16[192,1024]{1,0:T(8,128)(2,1)S(1)}, bf16[192,1024]{1,0:T(8,128)(2,1)}, u32[]{:S(2)}, u32[]{:S(2)}) collective-permute-start(bf16[192,1024]{1,0:T(8,128)(2,1)S(1)} %copy-done.6), channel_id=1, source_target_pairs={{0,2},{1,3},{2,0},{3,1},{4,6},{5,7},{6,4},{7,5},{8,10},{9,11},{10,... | collective-permute-start | bytes 1179656 | tf_op jit(solution)/shard_map/ppermute | solution.py:124
  26.9 4.9 %copy-start.12 = (s32[1,4,1024]{2,1,0:T(4,128)S(1)}, s32[1,4,1024]{2,1,0:T(4,128)}, u32[]{:S(2)}) copy-start(s32[1,4,1024]{2,1,0:T(4,128)} %param.12) | copy-start | bytes 49156
  30.8 6.4 %copy-start.10 = (s32[256,15]{0,1:T(8,128)S(1)}, s32[256,15]{0,1:T(8,128)}, u32[]{:S(2)}) copy-start(s32[256,15]{0,1:T(8,128)} %param.18) | copy-start | bytes 46084
  32.4 13.3 %copy-start.7 = (bf16[192,1024]{1,0:T(8,128)(2,1)S(1)}, bf16[192,1024]{1,0:T(8,128)(2,1)}, u32[]{:S(2)}) copy-start(bf16[192,1024]{1,0:T(8,128)(2,1)} %param.13) | copy-start | bytes 1179652
  39.8 22.1 %collective-permute-start.10 = (bf16[256,1024]{1,0:T(8,128)(2,1)}, bf16[256,1024]{1,0:T(8,128)(2,1)}, u32[]{:S(2)}, u32[]{:S(2)}) collective-permute-start(bf16[256,1024]{1,0:T(8,128)(2,1)} %param.16), channel_id=1, source_target_pairs={{0,2},{1,3},{2,0},{3,1},{4,6},{5,7},{6,4},{7,5},{8,10},{9,11},{10,... | collective-permute-start | bytes 1572872 | tf_op jit(solution)/shard_map/ppermute | solution.py:124
  47.9 16.0 %collective-permute-start.6 = (bf16[2,192,1024]{2,1,0:T(8,128)(2,1)}, bf16[2,192,1024]{2,1,0:T(8,128)(2,1)}, u32[]{:S(2)}, u32[]{:S(2)}) collective-permute-start(bf16[2,192,1024]{2,1,0:T(8,128)(2,1)} %pad_maximum_fusion.5), channel_id=1, source_target_pairs={{0,1},{1,0},{2,3},{3,2},{4,5},{5,4},{6,7},{7,6},{8,9},{9,8},{10,11... | collective-permute-start | bytes 2359304 | tf_op jit(solution)/shard_map/ppermute | solution.py:124
  47.9 18.2 %collective-permute-start.4 = (bf16[2,192,1024]{2,1,0:T(8,128)(2,1)S(1)}, bf16[2,192,1024]{2,1,0:T(8,128)(2,1)}, u32[]{:S(2)}, u32[]{:S(2)}) collective-permute-start(bf16[2,192,1024]{2,1,0:T(8,128)(2,1)S(1)} %pad_maximum_fusion.4), channel_id=1, source_target_pairs={{0,1},{1,0},{2,3},{3,2},{4,5},{5,4},{6,7},{7,6},{8,9},{9,8},{10,11... | collective-permute-start | bytes 2359304 | tf_op jit(solution)/shard_map/ppermute | solution.py:124
  60.4 7.8 %collective-permute-start.8 = (bf16[384,256]{1,0:T(8,128)(2,1)S(1)}, bf16[384,256]{1,0:T(8,128)(2,1)S(1)}, u32[]{:S(2)}, u32[]{:S(2)}) collective-permute-start(bf16[384,256]{1,0:T(8,128)(2,1)S(1)} %get-tuple-element.33), channel_id=1, source_target_pairs={{0,2},{1,3},{2,0},{3,1},{4,6},{5,7},{6,4},{7,5},{8,10},{9,11},{10,... | collective-permute-start | bytes 589832 | tf_op jit(solution)/shard_map/ppermute | solution.py:197
  61.9 8.6 %collective-permute-start.9 = (bf16[384,256]{1,0:T(8,128)(2,1)S(1)}, bf16[384,256]{1,0:T(8,128)(2,1)S(1)}, u32[]{:S(2)}, u32[]{:S(2)}) collective-permute-start(bf16[384,256]{1,0:T(8,128)(2,1)S(1)} %get-tuple-element.34), channel_id=1, source_target_pairs={{0,3},{1,0},{2,1},{3,2},{4,7},{5,4},{6,5},{7,6},{8,11},{9,8},{10,9... | collective-permute-start | bytes 589832 | tf_op jit(solution)/shard_map/ppermute | solution.py:197
  61.9 9.5 %collective-permute-start.7 = (bf16[384,256]{1,0:T(8,128)(2,1)S(1)}, bf16[384,256]{1,0:T(8,128)(2,1)S(1)}, u32[]{:S(2)}, u32[]{:S(2)}) collective-permute-start(bf16[384,256]{1,0:T(8,128)(2,1)S(1)} %get-tuple-element.32), channel_id=1, source_target_pairs={{0,1},{1,2},{2,3},{3,0},{4,5},{5,6},{6,7},{7,4},{8,9},{9,10},{10,1... | collective-permute-start | bytes 589832 | tf_op jit(solution)/shard_map/ppermute | solution.py:197
  63.8 9.5 %collective-permute-start.11 = (bf16[2,256,1024]{2,1,0:T(8,128)(2,1)S(1)}, bf16[2,256,1024]{2,1,0:T(8,128)(2,1)S(1)}, u32[]{:S(2)}, u32[]{:S(2)}) collective-permute-start(bf16[2,256,1024]{2,1,0:T(8,128)(2,1)S(1)} %pad_maximum_fusion.3), channel_id=1, source_target_pairs={{0,1},{1,0},{2,3},{3,2},{4,5},{5,4},{6,7},{7,6},{8,9},{9,8},{10,11... | collective-permute-start | bytes 3145736 | tf_op jit(solution)/shard_map/ppermute | solution.py:124
  68.7 2.3 %copy-start.13 = (f32[1024]{0:T(1024)S(1)}, f32[1024]{0:T(1024)}, u32[]{:S(2)}) copy-start(f32[1024]{0:T(1024)} %param.15) | copy-start | bytes 12292
  80.0 5.2 %collective-permute-start.12 = (bf16[2,2,2,64,1024]{4,3,2,1,0:T(8,128)(2,1)}, bf16[2,2,2,64,1024]{4,3,2,1,0:T(8,128)(2,1)}, u32[]{:S(2)}, u32[]{:S(2)}) collective-permute-start(bf16[2,2,2,64,1024]{4,3,2,1,0:T(8,128)(2,1)} %fusion.2), channel_id=1, source_target_pairs={{0,1},{1,0},{2,3},{3,2},{4,5},{5,4},{6,7},{7,6},{8,9},{9,8},{10,11... | collective-permute-start | bytes 3145736 | tf_op jit(solution)/shard_map/ppermute | solution.py:94
  80.8 2.2 %copy-start.4 = (f32[256,1024]{1,0:T(8,128)S(1)}, f32[256,1024]{1,0:T(8,128)}, u32[]{:S(2)}) copy-start(f32[256,1024]{1,0:T(8,128)} %copy-done.3) | copy-start | bytes 3145732
  80.8 2.2 %copy-start.9 = (f32[256,256]{1,0:T(8,128)S(1)}, f32[256,256]{1,0:T(8,128)}, u32[]{:S(2)}) copy-start(f32[256,256]{1,0:T(8,128)} %convert_reduce_fusion) | copy-start | bytes 786436
  83.0 2.2 %copy-start.1 = (f32[1024,1024]{1,0:T(8,128)S(1)}, f32[1024,1024]{1,0:T(8,128)}, u32[]{:S(2)}) copy-start(f32[1024,1024]{1,0:T(8,128)} %copy-done) | copy-start | bytes 12582916
  86.8 14.0 %collective-permute-start.18 = (bf16[2,2,64,1024]{3,2,1,0:T(8,128)(2,1)S(1)}, bf16[2,2,64,1024]{3,2,1,0:T(8,128)(2,1)}, u32[]{:S(2)}, u32[]{:S(2)}) collective-permute-start(bf16[2,2,64,1024]{3,2,1,0:T(8,128)(2,1)S(1)} %fusion.17), channel_id=1, source_target_pairs={{0,4},{1,5},{2,6},{3,7},{4,0},{5,1},{6,2},{7,3},{8,12},{9,13},{10,... | collective-permute-start | bytes 1572872 | tf_op jit(solution)/shard_map/ppermute | solution.py:94
  87.6 30.1 %collective-permute-start.13 = (bf16[256,1024]{1,0:T(8,128)(2,1)}, bf16[256,1024]{1,0:T(8,128)(2,1)S(1)}, u32[]{:S(2)}, u32[]{:S(2)}) collective-permute-start(bf16[256,1024]{1,0:T(8,128)(2,1)} %multiply_convert_fusion), channel_id=1, source_target_pairs={{0,1},{1,0},{2,3},{3,2},{4,5},{5,4},{6,7},{7,6},{8,9},{9,8},{10,11... | collective-permute-start | bytes 1572872 | tf_op jit(solution)/shard_map/ppermute | solution.py:139
  87.6 14.7 %collective-permute-start.14 = (bf16[256,1024]{1,0:T(8,128)(2,1)}, bf16[256,1024]{1,0:T(8,128)(2,1)S(1)}, u32[]{:S(2)}, u32[]{:S(2)}) collective-permute-start(bf16[256,1024]{1,0:T(8,128)(2,1)} %multiply_convert_fusion), channel_id=1, source_target_pairs={{0,2},{1,3},{2,0},{3,1},{4,6},{5,7},{6,4},{7,5},{8,10},{9,11},{10,... | collective-permute-start | bytes 1572872 | tf_op jit(solution)/shard_map/ppermute | solution.py:139
  102.1 13.9 %collective-permute-start.19 = (bf16[2,64,1024]{2,1,0:T(8,128)(2,1)S(1)}, bf16[2,64,1024]{2,1,0:T(8,128)(2,1)S(1)}, u32[]{:S(2)}, u32[]{:S(2)}) collective-permute-start(bf16[2,64,1024]{2,1,0:T(8,128)(2,1)S(1)} %fusion.19), channel_id=1, source_target_pairs={{0,8},{1,9},{2,10},{3,11},{4,12},{5,13},{6,14},{7,15},{8,0},{9,1},... | collective-permute-start | bytes 786440 | tf_op jit(solution)/shard_map/ppermute | solution.py:94
  102.3 19.3 %collective-permute-start.15 = (bf16[256,1024]{1,0:T(8,128)(2,1)S(1)}, bf16[256,1024]{1,0:T(8,128)(2,1)S(1)}, u32[]{:S(2)}, u32[]{:S(2)}) collective-permute-start(bf16[256,1024]{1,0:T(8,128)(2,1)S(1)} %collective-permute-done.14), channel_id=1, source_target_pairs={{0,1},{1,0},{2,3},{3,2},{4,5},{5,4},{6,7},{7,6},{8,9},{9,8},{10,11... | collective-permute-start | bytes 1572872 | tf_op jit(solution)/shard_map/ppermute | solution.py:139
  116.2 5.4 %collective-permute-start.20 = (bf16[64,1024]{1,0:T(8,128)(2,1)S(1)}, bf16[64,1024]{1,0:T(8,128)(2,1)S(1)}, u32[]{:S(2)}, u32[]{:S(2)}) collective-permute-start(bf16[64,1024]{1,0:T(8,128)(2,1)S(1)} %fusion.39), channel_id=1, source_target_pairs={{0,2},{1,3},{2,0},{3,1},{4,6},{5,7},{6,4},{7,5},{8,10},{9,11},{10,... | collective-permute-start | bytes 393224 | tf_op jit(solution)/shard_map/ppermute | solution.py:94
  121.6 14.5 %collective-permute-start.21 = (bf16[64,1024]{1,0:T(8,128)(2,1)S(1)}, bf16[64,1024]{1,0:T(8,128)(2,1)S(1)}, u32[]{:S(2)}, u32[]{:S(2)}) collective-permute-start(bf16[64,1024]{1,0:T(8,128)(2,1)S(1)} %fusion.20), channel_id=1, source_target_pairs={{0,8},{4,12},{8,0},{12,4},{1,9},{5,13},{9,1},{13,5},{2,10},{6,14},... | collective-permute-start | bytes 393224 | tf_op jit(solution)/shard_map/ppermute | solution.py:124
  123.2 21.3 %collective-permute-start.16 = (bf16[2,384,256]{2,1,0:T(8,128)(2,1)S(1)}, bf16[2,384,256]{2,1,0:T(8,128)(2,1)S(1)}, u32[]{:S(2)}, u32[]{:S(2)}) collective-permute-start(bf16[2,384,256]{2,1,0:T(8,128)(2,1)S(1)} %fusion.18), channel_id=1, source_target_pairs={{0,8},{4,12},{8,0},{12,4},{1,9},{5,13},{9,1},{13,5},{2,10},{6,14},... | collective-permute-start | bytes 1179656 | tf_op jit(solution)/shard_map/ppermute | solution.py:94
  136.1 14.0 %collective-permute-start.22 = (bf16[2,64,1024]{2,1,0:T(8,128)(2,1)S(1)}, bf16[2,64,1024]{2,1,0:T(8,128)(2,1)S(1)}, u32[]{:S(2)}, u32[]{:S(2)}) collective-permute-start(bf16[2,64,1024]{2,1,0:T(8,128)(2,1)S(1)} %pad_maximum_fusion.6), channel_id=1, source_target_pairs={{0,4},{4,0},{8,12},{12,8},{1,5},{5,1},{9,13},{13,9},{2,6},{6,2},{1... | collective-permute-start | bytes 786440 | tf_op jit(solution)/shard_map/ppermute | solution.py:124
  144.6 9.6 %collective-permute-start.17 = (bf16[384,256]{1,0:T(8,128)(2,1)S(1)}, bf16[384,256]{1,0:T(8,128)(2,1)S(1)}, u32[]{:S(2)}, u32[]{:S(2)}) collective-permute-start(bf16[384,256]{1,0:T(8,128)(2,1)S(1)} %fusion.22), channel_id=1, source_target_pairs={{0,4},{4,0},{8,12},{12,8},{1,5},{5,1},{9,13},{13,9},{2,6},{6,2},{1... | collective-permute-start | bytes 589832 | tf_op jit(solution)/shard_map/ppermute | solution.py:94
  (6 other events, 7.2 us)

commit v21 on v17

--- a/solution.py
+++ b/solution.py
@@ -28,16 +28,15 @@
 def _accumulate_kernel(tgt_ref, rec_ref, sum_in, cnt_in, sum_ref, cnt_ref):
     targets = tgt_ref[...]
     n_tgt = sum_ref.shape[1]
+    width = sum_ref.shape[0]
     rows = lax.broadcasted_iota(jnp.int32, (n_tgt, targets.shape[1]), 0)
     hot = (rows == targets).astype(jnp.bfloat16)
+    ones = jnp.ones((cnt_ref.shape[0], targets.shape[1]), jnp.bfloat16)
+    extended = jnp.concatenate([rec_ref[...], ones], axis=0)
     dims = (((1,), (1,)), ((), ()))
-    sum_ref[...] = sum_in[...] + lax.dot_general(
-        rec_ref[...], hot, dims, preferred_element_type=jnp.float32
-    )
-    ones = jnp.ones((cnt_ref.shape[0], targets.shape[1]), jnp.bfloat16)
-    cnt_ref[...] = cnt_in[...] + lax.dot_general(
-        ones, hot, dims, preferred_element_type=jnp.float32
-    )
+    both = lax.dot_general(extended, hot, dims, preferred_element_type=jnp.float32)
+    sum_ref[...] = sum_in[...] + both[:width]
+    cnt_ref[...] = cnt_in[...] + both[width:]
 
 
 def accumulate(targets, rec_t, acc_sum, acc_cnt):

time: 148 us -> 147 us (level)
  transfers between devices with their start and end apart: 23 -> 23, of which waited for: 10 -> 10; matrix products, arithmetic and copies ran while one was open for 27% -> 27% of each run, Pallas kernels for 9% -> 8%
where the time goes in v21:
time: 147 us; the launch traced here: 146 us
  waiting for transfers between devices  54.6 us (37%)
  local copies, waits for them, and re-layouts  31.7 us (22%)
  starting transfers between devices  21.2 us (14%)
  other arithmetic  13.5 us (9%)
  matrix products  12.2 us (8%)
  Pallas kernels  11.9 us (8%)
    ppermute x6, waiting for transfers between devices, _butterfly_reduce(): got = lax.ppermute(send.astype(send_dtype), axis, _xor_pairs(n, 1 << b))  37.5 us
    gather x8, local copies, waits for them, and re-layouts, local(): rows_t = features.at[slots].get(mode='promise_in_bounds').T  18.8 us
    ppermute x8, waiting for transfers between devices, all_gather_blocks(): got = lax.ppermute(cur, axis, _xor_pairs(n, 1 << b))  14.8 us
    pallas_call x4, Pallas kernels, accumulate(): pl.pallas_call(_accumulate_kernel, out_shape=[jax.ShapeDtypeStruct(acc_su...  11.9 us
    ppermute x3, starting transfers between devices, local(): rows_t = lax.ppermute(rows_t, 'dom', _shift_pairs(n_dom, shift))  7.01 us
    another operation x14, other arithmetic, join(): return jnp.stack([low, high], axis=k - 1 - b)  6.82 us
    unnamed x31, local copies, waits for them, and re-layouts  6.3 us
    ppermute x8, starting transfers between devices, all_gather_blocks(): got = lax.ppermute(cur, axis, _xor_pairs(n, 1 << b))  5.33 us
  transfers between devices with their start and end apart: 23, of which 10 were waited for; matrix products, arithmetic and copies ran while one was open for 27% of the time, Pallas kernels for 8%

profile of v21, /device:TPU:0, one launch (start us, length us, event | category | flops | bytes accessed | tf_op | source)
XLA Modules:
  0.0 146.2 jit_solution(15826134016971260309)
XLA Ops:
  0.7 3.2 %copy.46 = bf16[4096,192]{1,0:T(8,128)(2,1)S(1)} copy(bf16[4096,192]{0,1:T(8,128)(2,1)} %param.10) | data formatting | bytes 3145728 | tf_op args[0]
  3.9 3.9 %gather_fusion.2 = bf16[1024,192]{1,0:T(8,128)(2,1)S(1)} fusion(bf16[4096,192]{1,0:T(8,128)(2,1)S(1)} %copy.46, s32[1024]{0:T(1024)S(1)} %broadcast_clamp_fusion.1), kind=kCustom, calls=%fused_computation.2 | custom fusion | bytes 790528 | tf_op jit(solution)/shard_map/gather | solution.py:182
  8.8 3.0 %collective-permute-start.2 = (bf16[192,1024]{1,0:T(8,128)(2,1)}, bf16[192,1024]{1,0:T(8,128)(2,1)}, u32[]{:S(2)}, u32[]{:S(2)}) collective-permute-start(bf16[192,1024]{1,0:T(8,128)(2,1)} %bitcast.11), channel_id=1, source_target_pairs={{0,4},{4,8},{8,12},{12,0},{1,5},{5,9},{9,13},{13,1},{2,6},{6,10},{... | collective-permute-start | bytes 1179656 | tf_op jit(solution)/shard_map/ppermute | solution.py:184
  11.9 3.9 %gather_fusion.1 = bf16[1024,192]{1,0:T(8,128)(2,1)S(1)} fusion(bf16[4096,192]{1,0:T(8,128)(2,1)S(1)} %copy.46, s32[1024]{0:T(1024)S(1)} %broadcast_clamp_fusion.2), kind=kCustom, calls=%fused_computation.1 | custom fusion | bytes 790528 | tf_op jit(solution)/shard_map/gather | solution.py:182
  16.7 2.6 %collective-permute-start.1 = (bf16[192,1024]{1,0:T(8,128)(2,1)}, bf16[192,1024]{1,0:T(8,128)(2,1)}, u32[]{:S(2)}, u32[]{:S(2)}) collective-permute-start(bf16[192,1024]{1,0:T(8,128)(2,1)} %bitcast.7), channel_id=1, source_target_pairs={{0,8},{4,12},{8,0},{12,4},{1,9},{5,13},{9,1},{13,5},{2,10},{6,14},... | collective-permute-start | bytes 1179656 | tf_op jit(solution)/shard_map/ppermute | solution.py:184
  19.3 3.9 %gather_fusion = bf16[1024,192]{1,0:T(8,128)(2,1)S(1)} fusion(bf16[4096,192]{1,0:T(8,128)(2,1)S(1)} %copy.46, s32[1024]{0:T(1024)S(1)} %broadcast_clamp_fusion.3), kind=kCustom, calls=%fused_computation | custom fusion | bytes 790528 | tf_op jit(solution)/shard_map/gather | solution.py:182
  24.9 1.5 %collective-permute-start.3 = (bf16[192,1024]{1,0:T(8,128)(2,1)}, bf16[192,1024]{1,0:T(8,128)(2,1)}, u32[]{:S(2)}, u32[]{:S(2)}) collective-permute-start(bf16[192,1024]{1,0:T(8,128)(2,1)} %param.13), channel_id=1, source_target_pairs={{0,2},{1,3},{2,0},{3,1},{4,6},{5,7},{6,4},{7,5},{8,10},{9,11},{10,... | collective-permute-start | bytes 1179656 | tf_op jit(solution)/shard_map/ppermute | solution.py:123
  26.9 3.9 %gather_fusion.3 = bf16[1024,192]{1,0:T(8,128)(2,1)S(1)} fusion(bf16[4096,192]{1,0:T(8,128)(2,1)S(1)} %copy.46, s32[1024]{0:T(1024)S(1)} %broadcast_clamp_fusion), kind=kCustom, calls=%fused_computation.3 | custom fusion | bytes 790528 | tf_op jit(solution)/shard_map/gather | solution.py:182
  34.0 3.0 %shard_map.129 = (f32[192,1024]{1,0:T(8,128)}, f32[8,1024]{1,0:T(8,128)}) custom-call(s32[1,1024]{1,0:T(1,128)} %get-tuple-element.49.tgt_ref, bf16[192,1024]{1,0:T(8,128)(2,1)} %bitcast.150, f32[192,1024]{1,0:T(8,128)} %broadcast_in_dim.4.sum_in, f32[8,1024]{1,0:T(8,128)} %broadcast_in_dim.5.cnt_in), custom_call_target="tpu_custom_call", output_to_operand_aliasing={{0}: (2, {}), {1}: (3, {})} | custom-call | flops 419430400 | bytes 2035712 | tf_op jit(solution)/shard_map/pallas_call | solution.py:45
  37.0 1.5 %convert_reduce_fusion = f32[256,256]{1,0:T(8,128)} fusion(s32[256,15]{0,1:T(8,128)S(1)} %copy-done.10), kind=kLoop, calls=%fused_computation.12 | loop fusion | flops 2883584 | bytes 277504 | tf_op jit(solution)/shard_map/reduce_sum | solution.py:16
  39.5 1.6 %collective-permute-start.10 = (bf16[256,1024]{1,0:T(8,128)(2,1)}, bf16[256,1024]{1,0:T(8,128)(2,1)}, u32[]{:S(2)}, u32[]{:S(2)}) collective-permute-start(bf16[256,1024]{1,0:T(8,128)(2,1)} %param.16), channel_id=1, source_target_pairs={{0,2},{1,3},{2,0},{3,1},{4,6},{5,7},{6,4},{7,5},{8,10},{9,11},{10,... | collective-permute-start | bytes 1572872 | tf_op jit(solution)/shard_map/ppermute | solution.py:123
  41.1 4.6 %collective-permute-done.5 = bf16[192,1024]{1,0:T(8,128)(2,1)} collective-permute-done((bf16[192,1024]{1,0:T(8,128)(2,1)S(1)}, bf16[192,1024]{1,0:T(8,128)(2,1)}, u32[]{:S(2)}, u32[]{:S(2)}) %collective-permute-start.5) | collective-permute-done | bytes 393248 | tf_op jit(solution)/shard_map/ppermute | solution.py:123
  48.5 3.0 %shard_map.130 = (f32[192,1024]{1,0:T(8,128)}, f32[8,1024]{1,0:T(8,128)}) custom-call(s32[1,1024]{1,0:T(1,128)} %get-tuple-element.52.tgt_ref, bf16[192,1024]{1,0:T(8,128)(2,1)} %collective-permute-done.2.rec_ref, f32[192,1024]{1,0:T(8,128)} %get-tuple-element.14.sum_in, ...), custom_call_target="tpu_custom_call", output_to_operand_aliasing={{0}: (2, {}), {1}: (3, {})} | custom-call | flops 419430400 | bytes 2035712 | tf_op jit(solution)/shard_map/pallas_call | solution.py:45
  51.5 3.0 %shard_map.131 = (f32[192,1024]{1,0:T(8,128)}, f32[8,1024]{1,0:T(8,128)}) custom-call(s32[1,1024]{1,0:T(1,128)} %get-tuple-element.50.tgt_ref, bf16[192,1024]{1,0:T(8,128)(2,1)} %collective-permute-done.1.rec_ref, f32[192,1024]{1,0:T(8,128)} %get-tuple-element.16.sum_in, ...), custom_call_target="tpu_custom_call", output_to_operand_aliasing={{0}: (2, {}), {1}: (3, {})} | custom-call | flops 419430400 | bytes 2035712 | tf_op jit(solution)/shard_map/pallas_call | solution.py:45
  54.4 3.0 %shard_map.132 = (f32[192,1024]{1,0:T(8,128)}, f32[8,1024]{1,0:T(8,128)}) custom-call(s32[1,1024]{1,0:T(1,128)} %get-tuple-element.51.tgt_ref, bf16[192,1024]{1,0:T(8,128)(2,1)} %collective-permute-done.rec_ref, f32[192,1024]{1,0:T(8,128)} %get-tuple-element.18.sum_in, f32[8,1024]{1,0:T(8,128)} %get-tuple-element.19.cnt_in), custom_call_target="tpu_custom_call", output_to_operand_aliasing={{0}: (2, {}), {1}: (3, {})} | custom-call | flops 419430400 | bytes 2035712 | tf_op jit(solution)/shard_map/pallas_call | solution.py:45
  59.5 1.6 %collective-permute-start.8 = (bf16[384,256]{1,0:T(8,128)(2,1)S(1)}, bf16[384,256]{1,0:T(8,128)(2,1)S(1)}, u32[]{:S(2)}, u32[]{:S(2)}) collective-permute-start(bf16[384,256]{1,0:T(8,128)(2,1)S(1)} %get-tuple-element.33), channel_id=1, source_target_pairs={{0,2},{1,3},{2,0},{3,1},{4,6},{5,7},{6,4},{7,5},{8,10},{9,11},{10,... | collective-permute-start | bytes 589832 | tf_op jit(solution)/shard_map/ppermute | solution.py:196
  67.8 1.8 %collective-permute-done.9 = bf16[384,256]{1,0:T(8,128)(2,1)S(1)} collective-permute-done((bf16[384,256]{1,0:T(8,128)(2,1)S(1)}, bf16[384,256]{1,0:T(8,128)(2,1)S(1)}, u32[]{:S(2)}, u32[]{:S(2)}) %collective-permute-start.9) | collective-permute-done | bytes 196640 | tf_op jit(solution)/shard_map/ppermute | solution.py:196
  73.3 1.7 %multiply_convert_fusion.2 = (bf16[256,1024]{1,0:T(8,128)(2,1)}, f32[256,1024]{1,0:T(8,128)S(1)}) fusion(f32[1024]{0:T(1024)S(1)} %copy-done.14, bf16[256,1024]{1,0:T(8,128)(2,1)S(1)} %convolution_convert_fusion, bf16[1024,1024]{1,0:T(8,128)(2,1)S(1)} %bitcast.146), kind=kOutput, calls=%fused_computation.49 | convolution fusion | flops 538443776 | bytes 4198400 | tf_op jit(solution)/shard_map/dot_general | solution.py:204
  75.9 2.0 %copy-done = f32[1024,1024]{1,0:T(8,128)} copy-done((f32[1024,1024]{1,0:T(8,128)}, f32[1024,1024]{1,0:T(8,128)S(1)}, u32[]{:S(2)}) %copy-start) | copy-done | bytes 4194328
  79.9 2.2 %fusion.69 = f32[256,1024]{1,0:T(8,128)S(1)} fusion(bf16[1024,1024]{1,0:T(8,128)(2,1)S(1)} %bitcast.147, f32[256,1024]{1,0:T(8,128)} %copy-done.2, bf16[256,1024]{1,0:T(8,128)(2,1)S(1)} %copy-done.5), kind=kOutput, calls=%fused_computation.159 | convolution fusion | flops 539492352 | bytes 4718592 | tf_op jit(solution)/shard_map/dot_general | solution.py:209
  82.1 2.1 %multiply_convert_fusion = bf16[256,1024]{1,0:T(8,128)(2,1)} fusion(f32[256,1024]{1,0:T(8,128)S(1)} %copy-done.4, f32[256,1024]{1,0:T(8,128)S(1)} %fusion.69, f32[256,256]{1,0:T(8,128)S(1)} %copy-done.9), kind=kOutput, calls=%fused_computation.47 | convolution fusion | flops 807927808 | bytes 2883584 | tf_op jit(solution)/shard_map/dot_general | solution.py:212
  84.3 1.6 %bitcast_add_fusion = f32[2,2,2,64,1024]{4,3,2,1,0:T(8,128)S(1)} fusion(bf16[2,2,2,64,1024]{4,3,2,1,0:T(8,128)(2,1)} %collective-permute-done.12, f32[2,2,2,2,64,1024]{5,4,3,2,1,0:T(8,128)S(1)} %bitcast.142, s32[]{:T(128)S(6)} %select_n.344), kind=kLoop, calls=%fused_computation.15 | loop fusion | flops 1048576 | bytes 5242884 | tf_op jit(solution)/shard_map/add | solution.py:94
  86.7 1.5 %collective-permute-start.14 = (bf16[256,1024]{1,0:T(8,128)(2,1)}, bf16[256,1024]{1,0:T(8,128)(2,1)S(1)}, u32[]{:S(2)}, u32[]{:S(2)}) collective-permute-start(bf16[256,1024]{1,0:T(8,128)(2,1)} %multiply_convert_fusion), channel_id=1, source_target_pairs={{0,2},{1,3},{2,0},{3,1},{4,6},{5,7},{6,4},{7,5},{8,10},{9,11},{10,... | collective-permute-start | bytes 1572872 | tf_op jit(solution)/shard_map/ppermute | solution.py:138
  88.2 1.4 fusion.31
  89.6 10.3 %collective-permute-done.18 = bf16[2,2,64,1024]{3,2,1,0:T(8,128)(2,1)} collective-permute-done((bf16[2,2,64,1024]{3,2,1,0:T(8,128)(2,1)S(1)}, bf16[2,2,64,1024]{3,2,1,0:T(8,128)(2,1)}, u32[]{:S(2)}, u32[]{:S(2)}) %collective-permute-start.18) | collective-permute-done | bytes 524320 | tf_op jit(solution)/shard_map/ppermute | solution.py:93
  101.8 13.4 %collective-permute-done.19 = bf16[2,64,1024]{2,1,0:T(8,128)(2,1)S(1)} collective-permute-done((bf16[2,64,1024]{2,1,0:T(8,128)(2,1)S(1)}, bf16[2,64,1024]{2,1,0:T(8,128)(2,1)S(1)}, u32[]{:S(2)}, u32[]{:S(2)}) %collective-permute-start.19) | collective-permute-done | bytes 262176 | tf_op jit(solution)/shard_map/ppermute | solution.py:93
  115.3 1.6 %collective-permute-start.20 = (bf16[64,1024]{1,0:T(8,128)(2,1)S(1)}, bf16[64,1024]{1,0:T(8,128)(2,1)S(1)}, u32[]{:S(2)}, u32[]{:S(2)}) collective-permute-start(bf16[64,1024]{1,0:T(8,128)(2,1)S(1)} %fusion.39), channel_id=1, source_target_pairs={{0,2},{1,3},{2,0},{3,1},{4,6},{5,7},{6,4},{7,5},{8,10},{9,11},{10,... | collective-permute-start | bytes 393224 | tf_op jit(solution)/shard_map/ppermute | solution.py:93
  117.2 3.4 %collective-permute-done.20 = bf16[64,1024]{1,0:T(8,128)(2,1)S(1)} collective-permute-done((bf16[64,1024]{1,0:T(8,128)(2,1)S(1)}, bf16[64,1024]{1,0:T(8,128)(2,1)S(1)}, u32[]{:S(2)}, u32[]{:S(2)}) %collective-permute-start.20) | collective-permute-done | bytes 131104 | tf_op jit(solution)/shard_map/ppermute | solution.py:93
  122.0 4.7 %collective-permute-done.21 = bf16[64,1024]{1,0:T(8,128)(2,1)S(1)} collective-permute-done((bf16[64,1024]{1,0:T(8,128)(2,1)S(1)}, bf16[64,1024]{1,0:T(8,128)(2,1)S(1)}, u32[]{:S(2)}, u32[]{:S(2)}) %collective-permute-start.21) | collective-permute-done | bytes 131104 | tf_op jit(solution)/shard_map/ppermute | solution.py:123
  126.8 8.3 %collective-permute-done.16 = bf16[2,384,256]{2,1,0:T(8,128)(2,1)S(1)} collective-permute-done((bf16[2,384,256]{2,1,0:T(8,128)(2,1)S(1)}, bf16[2,384,256]{2,1,0:T(8,128)(2,1)S(1)}, u32[]{:S(2)}, u32[]{:S(2)}) %collective-permute-start.16) | collective-permute-done | bytes 393248 | tf_op jit(solution)/shard_map/ppermute | solution.py:93
  136.5 5.6 %collective-permute-done.22 = bf16[2,64,1024]{2,1,0:T(8,128)(2,1)S(1)} collective-permute-done((bf16[2,64,1024]{2,1,0:T(8,128)(2,1)S(1)}, bf16[2,64,1024]{2,1,0:T(8,128)(2,1)S(1)}, u32[]{:S(2)}, u32[]{:S(2)}) %collective-permute-start.22) | collective-permute-done | bytes 262176 | tf_op jit(solution)/shard_map/ppermute | solution.py:123
  143.3 2.1 %collective-permute-done.17 = bf16[384,256]{1,0:T(8,128)(2,1)S(1)} collective-permute-done((bf16[384,256]{1,0:T(8,128)(2,1)S(1)}, bf16[384,256]{1,0:T(8,128)(2,1)S(1)}, u32[]{:S(2)}, u32[]{:S(2)}) %collective-permute-start.17) | collective-permute-done | bytes 196640 | tf_op jit(solution)/shard_map/ppermute | solution.py:93
  (114 shorter events, 34.4 us)
Async XLA Ops:
  0.7 3.2 %copy-start.11 = (s32[1,4,1024]{2,1,0:T(4,128)S(1)}, s32[1,4,1024]{2,1,0:T(4,128)}, u32[]{:S(2)}) copy-start(s32[1,4,1024]{2,1,0:T(4,128)} %param.11) | copy-start | bytes 49156
  8.8 39.1 %collective-permute-start.2 = (bf16[192,1024]{1,0:T(8,128)(2,1)}, bf16[192,1024]{1,0:T(8,128)(2,1)}, u32[]{:S(2)}, u32[]{:S(2)}) collective-permute-start(bf16[192,1024]{1,0:T(8,128)(2,1)} %bitcast.11), channel_id=1, source_target_pairs={{0,4},{4,8},{8,12},{12,0},{1,5},{5,9},{9,13},{13,1},{2,6},{6,10},{... | collective-permute-start | bytes 1179656 | tf_op jit(solution)/shard_map/ppermute | solution.py:184
  16.7 34.7 %collective-permute-start.1 = (bf16[192,1024]{1,0:T(8,128)(2,1)}, bf16[192,1024]{1,0:T(8,128)(2,1)}, u32[]{:S(2)}, u32[]{:S(2)}) collective-permute-start(bf16[192,1024]{1,0:T(8,128)(2,1)} %bitcast.7), channel_id=1, source_target_pairs={{0,8},{4,12},{8,0},{12,4},{1,9},{5,13},{9,1},{13,5},{2,10},{6,14},... | collective-permute-start | bytes 1179656 | tf_op jit(solution)/shard_map/ppermute | solution.py:184
  19.3 7.0 %copy-start.6 = (bf16[192,1024]{1,0:T(8,128)(2,1)S(1)}, bf16[192,1024]{1,0:T(8,128)(2,1)}, u32[]{:S(2)}) copy-start(bf16[192,1024]{1,0:T(8,128)(2,1)} %param.14) | copy-start | bytes 1179652
  23.5 31.0 %collective-permute-start = (bf16[192,1024]{1,0:T(8,128)(2,1)S(1)}, bf16[192,1024]{1,0:T(8,128)(2,1)}, u32[]{:S(2)}, u32[]{:S(2)}) collective-permute-start(bf16[192,1024]{1,0:T(8,128)(2,1)S(1)} %bitcast.149), channel_id=1, source_target_pairs={{0,12},{4,0},{8,4},{12,8},{1,13},{5,1},{9,5},{13,9},{2,14},{6,2},{... | collective-permute-start | bytes 1179656 | tf_op jit(solution)/shard_map/ppermute | solution.py:184
  24.9 14.7 %collective-permute-start.3 = (bf16[192,1024]{1,0:T(8,128)(2,1)}, bf16[192,1024]{1,0:T(8,128)(2,1)}, u32[]{:S(2)}, u32[]{:S(2)}) collective-permute-start(bf16[192,1024]{1,0:T(8,128)(2,1)} %param.13), channel_id=1, source_target_pairs={{0,2},{1,3},{2,0},{3,1},{4,6},{5,7},{6,4},{7,5},{8,10},{9,11},{10,... | collective-permute-start | bytes 1179656 | tf_op jit(solution)/shard_map/ppermute | solution.py:123
  26.4 19.3 %collective-permute-start.5 = (bf16[192,1024]{1,0:T(8,128)(2,1)S(1)}, bf16[192,1024]{1,0:T(8,128)(2,1)}, u32[]{:S(2)}, u32[]{:S(2)}) collective-permute-start(bf16[192,1024]{1,0:T(8,128)(2,1)S(1)} %copy-done.6), channel_id=1, source_target_pairs={{0,2},{1,3},{2,0},{3,1},{4,6},{5,7},{6,4},{7,5},{8,10},{9,11},{10,... | collective-permute-start | bytes 1179656 | tf_op jit(solution)/shard_map/ppermute | solution.py:123
  26.9 4.9 %copy-start.12 = (s32[1,4,1024]{2,1,0:T(4,128)S(1)}, s32[1,4,1024]{2,1,0:T(4,128)}, u32[]{:S(2)}) copy-start(s32[1,4,1024]{2,1,0:T(4,128)} %param.12) | copy-start | bytes 49156
  30.8 6.1 %copy-start.10 = (s32[256,15]{0,1:T(8,128)S(1)}, s32[256,15]{0,1:T(8,128)}, u32[]{:S(2)}) copy-start(s32[256,15]{0,1:T(8,128)} %param.18) | copy-start | bytes 46084
  32.4 13.3 %copy-start.7 = (bf16[192,1024]{1,0:T(8,128)(2,1)S(1)}, bf16[192,1024]{1,0:T(8,128)(2,1)}, u32[]{:S(2)}) copy-start(bf16[192,1024]{1,0:T(8,128)(2,1)} %param.13) | copy-start | bytes 1179652
  39.5 21.5 %collective-permute-start.10 = (bf16[256,1024]{1,0:T(8,128)(2,1)}, bf16[256,1024]{1,0:T(8,128)(2,1)}, u32[]{:S(2)}, u32[]{:S(2)}) collective-permute-start(bf16[256,1024]{1,0:T(8,128)(2,1)} %param.16), channel_id=1, source_target_pairs={{0,2},{1,3},{2,0},{3,1},{4,6},{5,7},{6,4},{7,5},{8,10},{9,11},{10,... | collective-permute-start | bytes 1572872 | tf_op jit(solution)/shard_map/ppermute | solution.py:123
  47.9 15.1 %collective-permute-start.6 = (bf16[2,192,1024]{2,1,0:T(8,128)(2,1)}, bf16[2,192,1024]{2,1,0:T(8,128)(2,1)}, u32[]{:S(2)}, u32[]{:S(2)}) collective-permute-start(bf16[2,192,1024]{2,1,0:T(8,128)(2,1)} %pad_maximum_fusion.5), channel_id=1, source_target_pairs={{0,1},{1,0},{2,3},{3,2},{4,5},{5,4},{6,7},{7,6},{8,9},{9,8},{10,11... | collective-permute-start | bytes 2359304 | tf_op jit(solution)/shard_map/ppermute | solution.py:123
  47.9 17.3 %collective-permute-start.4 = (bf16[2,192,1024]{2,1,0:T(8,128)(2,1)S(1)}, bf16[2,192,1024]{2,1,0:T(8,128)(2,1)}, u32[]{:S(2)}, u32[]{:S(2)}) collective-permute-start(bf16[2,192,1024]{2,1,0:T(8,128)(2,1)S(1)} %pad_maximum_fusion.4), channel_id=1, source_target_pairs={{0,1},{1,0},{2,3},{3,2},{4,5},{5,4},{6,7},{7,6},{8,9},{9,8},{10,11... | collective-permute-start | bytes 2359304 | tf_op jit(solution)/shard_map/ppermute | solution.py:123
  59.5 7.8 %collective-permute-start.8 = (bf16[384,256]{1,0:T(8,128)(2,1)S(1)}, bf16[384,256]{1,0:T(8,128)(2,1)S(1)}, u32[]{:S(2)}, u32[]{:S(2)}) collective-permute-start(bf16[384,256]{1,0:T(8,128)(2,1)S(1)} %get-tuple-element.33), channel_id=1, source_target_pairs={{0,2},{1,3},{2,0},{3,1},{4,6},{5,7},{6,4},{7,5},{8,10},{9,11},{10,... | collective-permute-start | bytes 589832 | tf_op jit(solution)/shard_map/ppermute | solution.py:196
  61.0 8.6 %collective-permute-start.9 = (bf16[384,256]{1,0:T(8,128)(2,1)S(1)}, bf16[384,256]{1,0:T(8,128)(2,1)S(1)}, u32[]{:S(2)}, u32[]{:S(2)}) collective-permute-start(bf16[384,256]{1,0:T(8,128)(2,1)S(1)} %get-tuple-element.34), channel_id=1, source_target_pairs={{0,3},{1,0},{2,1},{3,2},{4,7},{5,4},{6,5},{7,6},{8,11},{9,8},{10,9... | collective-permute-start | bytes 589832 | tf_op jit(solution)/shard_map/ppermute | solution.py:196
  61.0 9.5 %collective-permute-start.7 = (bf16[384,256]{1,0:T(8,128)(2,1)S(1)}, bf16[384,256]{1,0:T(8,128)(2,1)S(1)}, u32[]{:S(2)}, u32[]{:S(2)}) collective-permute-start(bf16[384,256]{1,0:T(8,128)(2,1)S(1)} %get-tuple-element.32), channel_id=1, source_target_pairs={{0,1},{1,2},{2,3},{3,0},{4,5},{5,6},{6,7},{7,4},{8,9},{9,10},{10,1... | collective-permute-start | bytes 589832 | tf_op jit(solution)/shard_map/ppermute | solution.py:196
  62.9 9.5 %collective-permute-start.11 = (bf16[2,256,1024]{2,1,0:T(8,128)(2,1)S(1)}, bf16[2,256,1024]{2,1,0:T(8,128)(2,1)S(1)}, u32[]{:S(2)}, u32[]{:S(2)}) collective-permute-start(bf16[2,256,1024]{2,1,0:T(8,128)(2,1)S(1)} %pad_maximum_fusion.3), channel_id=1, source_target_pairs={{0,1},{1,0},{2,3},{3,2},{4,5},{5,4},{6,7},{7,6},{8,9},{9,8},{10,11... | collective-permute-start | bytes 3145736 | tf_op jit(solution)/shard_map/ppermute | solution.py:123
  67.8 2.3 %copy-start.13 = (f32[1024]{0:T(1024)S(1)}, f32[1024]{0:T(1024)}, u32[]{:S(2)}) copy-start(f32[1024]{0:T(1024)} %param.15) | copy-start | bytes 12292
  79.0 5.2 %collective-permute-start.12 = (bf16[2,2,2,64,1024]{4,3,2,1,0:T(8,128)(2,1)}, bf16[2,2,2,64,1024]{4,3,2,1,0:T(8,128)(2,1)}, u32[]{:S(2)}, u32[]{:S(2)}) collective-permute-start(bf16[2,2,2,64,1024]{4,3,2,1,0:T(8,128)(2,1)} %fusion.2), channel_id=1, source_target_pairs={{0,1},{1,0},{2,3},{3,2},{4,5},{5,4},{6,7},{7,6},{8,9},{9,8},{10,11... | collective-permute-start | bytes 3145736 | tf_op jit(solution)/shard_map/ppermute | solution.py:93
  79.9 2.2 %copy-start.4 = (f32[256,1024]{1,0:T(8,128)S(1)}, f32[256,1024]{1,0:T(8,128)}, u32[]{:S(2)}) copy-start(f32[256,1024]{1,0:T(8,128)} %copy-done.3) | copy-start | bytes 3145732
  79.9 2.2 %copy-start.9 = (f32[256,256]{1,0:T(8,128)S(1)}, f32[256,256]{1,0:T(8,128)}, u32[]{:S(2)}) copy-start(f32[256,256]{1,0:T(8,128)} %convert_reduce_fusion) | copy-start | bytes 786436
  82.1 2.2 %copy-start.1 = (f32[1024,1024]{1,0:T(8,128)S(1)}, f32[1024,1024]{1,0:T(8,128)}, u32[]{:S(2)}) copy-start(f32[1024,1024]{1,0:T(8,128)} %copy-done) | copy-start | bytes 12582916
  85.9 14.0 %collective-permute-start.18 = (bf16[2,2,64,1024]{3,2,1,0:T(8,128)(2,1)S(1)}, bf16[2,2,64,1024]{3,2,1,0:T(8,128)(2,1)}, u32[]{:S(2)}, u32[]{:S(2)}) collective-permute-start(bf16[2,2,64,1024]{3,2,1,0:T(8,128)(2,1)S(1)} %fusion.17), channel_id=1, source_target_pairs={{0,4},{1,5},{2,6},{3,7},{4,0},{5,1},{6,2},{7,3},{8,12},{9,13},{10,... | collective-permute-start | bytes 1572872 | tf_op jit(solution)/shard_map/ppermute | solution.py:93
  86.7 30.1 %collective-permute-start.13 = (bf16[256,1024]{1,0:T(8,128)(2,1)}, bf16[256,1024]{1,0:T(8,128)(2,1)S(1)}, u32[]{:S(2)}, u32[]{:S(2)}) collective-permute-start(bf16[256,1024]{1,0:T(8,128)(2,1)} %multiply_convert_fusion), channel_id=1, source_target_pairs={{0,1},{1,0},{2,3},{3,2},{4,5},{5,4},{6,7},{7,6},{8,9},{9,8},{10,11... | collective-permute-start | bytes 1572872 | tf_op jit(solution)/shard_map/ppermute | solution.py:138
  86.7 14.7 %collective-permute-start.14 = (bf16[256,1024]{1,0:T(8,128)(2,1)}, bf16[256,1024]{1,0:T(8,128)(2,1)S(1)}, u32[]{:S(2)}, u32[]{:S(2)}) collective-permute-start(bf16[256,1024]{1,0:T(8,128)(2,1)} %multiply_convert_fusion), channel_id=1, source_target_pairs={{0,2},{1,3},{2,0},{3,1},{4,6},{5,7},{6,4},{7,5},{8,10},{9,11},{10,... | collective-permute-start | bytes 1572872 | tf_op jit(solution)/shard_map/ppermute | solution.py:138
  101.2 13.9 %collective-permute-start.19 = (bf16[2,64,1024]{2,1,0:T(8,128)(2,1)S(1)}, bf16[2,64,1024]{2,1,0:T(8,128)(2,1)S(1)}, u32[]{:S(2)}, u32[]{:S(2)}) collective-permute-start(bf16[2,64,1024]{2,1,0:T(8,128)(2,1)S(1)} %fusion.19), channel_id=1, source_target_pairs={{0,8},{1,9},{2,10},{3,11},{4,12},{5,13},{6,14},{7,15},{8,0},{9,1},... | collective-permute-start | bytes 786440 | tf_op jit(solution)/shard_map/ppermute | solution.py:93
  101.4 19.3 %collective-permute-start.15 = (bf16[256,1024]{1,0:T(8,128)(2,1)S(1)}, bf16[256,1024]{1,0:T(8,128)(2,1)S(1)}, u32[]{:S(2)}, u32[]{:S(2)}) collective-permute-start(bf16[256,1024]{1,0:T(8,128)(2,1)S(1)} %collective-permute-done.14), channel_id=1, source_target_pairs={{0,1},{1,0},{2,3},{3,2},{4,5},{5,4},{6,7},{7,6},{8,9},{9,8},{10,11... | collective-permute-start | bytes 1572872 | tf_op jit(solution)/shard_map/ppermute | solution.py:138
  115.3 5.4 %collective-permute-start.20 = (bf16[64,1024]{1,0:T(8,128)(2,1)S(1)}, bf16[64,1024]{1,0:T(8,128)(2,1)S(1)}, u32[]{:S(2)}, u32[]{:S(2)}) collective-permute-start(bf16[64,1024]{1,0:T(8,128)(2,1)S(1)} %fusion.39), channel_id=1, source_target_pairs={{0,2},{1,3},{2,0},{3,1},{4,6},{5,7},{6,4},{7,5},{8,10},{9,11},{10,... | collective-permute-start | bytes 393224 | tf_op jit(solution)/shard_map/ppermute | solution.py:93
  120.7 6.0 %collective-permute-start.21 = (bf16[64,1024]{1,0:T(8,128)(2,1)S(1)}, bf16[64,1024]{1,0:T(8,128)(2,1)S(1)}, u32[]{:S(2)}, u32[]{:S(2)}) collective-permute-start(bf16[64,1024]{1,0:T(8,128)(2,1)S(1)} %fusion.20), channel_id=1, source_target_pairs={{0,8},{4,12},{8,0},{12,4},{1,9},{5,13},{9,1},{13,5},{2,10},{6,14},... | collective-permute-start | bytes 393224 | tf_op jit(solution)/shard_map/ppermute | solution.py:123
  121.3 13.9 %collective-permute-start.16 = (bf16[2,384,256]{2,1,0:T(8,128)(2,1)S(1)}, bf16[2,384,256]{2,1,0:T(8,128)(2,1)S(1)}, u32[]{:S(2)}, u32[]{:S(2)}) collective-permute-start(bf16[2,384,256]{2,1,0:T(8,128)(2,1)S(1)} %fusion.18), channel_id=1, source_target_pairs={{0,4},{4,0},{8,12},{12,8},{1,5},{5,1},{9,13},{13,9},{2,6},{6,2},{1... | collective-permute-start | bytes 1179656 | tf_op jit(solution)/shard_map/ppermute | solution.py:93
  126.8 15.4 %collective-permute-start.22 = (bf16[2,64,1024]{2,1,0:T(8,128)(2,1)S(1)}, bf16[2,64,1024]{2,1,0:T(8,128)(2,1)S(1)}, u32[]{:S(2)}, u32[]{:S(2)}) collective-permute-start(bf16[2,64,1024]{2,1,0:T(8,128)(2,1)S(1)} %pad_maximum_fusion.6), channel_id=1, source_target_pairs={{0,4},{4,0},{8,12},{12,8},{1,5},{5,1},{9,13},{13,9},{2,6},{6,2},{1... | collective-permute-start | bytes 786440 | tf_op jit(solution)/shard_map/ppermute | solution.py:123
  135.3 10.1 %collective-permute-start.17 = (bf16[384,256]{1,0:T(8,128)(2,1)S(1)}, bf16[384,256]{1,0:T(8,128)(2,1)S(1)}, u32[]{:S(2)}, u32[]{:S(2)}) collective-permute-start(bf16[384,256]{1,0:T(8,128)(2,1)S(1)} %fusion.22), channel_id=1, source_target_pairs={{0,8},{4,12},{8,0},{12,4},{1,9},{5,13},{9,1},{13,5},{2,10},{6,14},... | collective-permute-start | bytes 589832 | tf_op jit(solution)/shard_map/ppermute | solution.py:93
  (6 other events, 7.2 us)
